TPU v7x, 256 devices: a whole 4x4x8 slice. The times are simulated.
256 devices in a mesh: req: 64 (over z, x, core), tp: 4 (over y).
Axes of the slice: x: 4, y: 4, z: 8, core: 2. Of those that a mesh axis runs over, the one named last changes fastest.
Arguments:
- hidden: bfloat16 [16384, 2048], P('req'), may hold values from -10.5 to 10.5
- lengths: int32 [64], replicated, may hold values from 1 to 1024, 16384 in all
- dealing: int32 [64], replicated, may hold values from 0 to 63, each once
- norm_gain: bfloat16 [2048], replicated, may hold values from 0.5 to 1.5
- w_query: bfloat16 [2048, 2048], P(None, 'tp'), may hold values from -0.125 to 0.125
- w_key: bfloat16 [2048, 1024], P(None, 'tp'), may hold values from -0.125 to 0.125
- w_value: bfloat16 [2048, 1024], P(None, 'tp'), may hold values from -0.125 to 0.125
- query_gain: bfloat16 [128], replicated, may hold values from 0.5 to 8
- key_gain: bfloat16 [128], replicated, may hold values from 0.5 to 8
- w_out: bfloat16 [2048, 2048], P(None, 'tp'), may hold values from -0.125 to 0.125
Outputs:
- hidden_out: bfloat16 [16384, 2048], P('req', 'tp')
- kv_cache: bfloat16 [2, 64, 1024, 1024], P(None, 'req', None, 'tp')
Inputs may be any that keep to these rules, and one draw needn't show every extreme that they name: The lengths sum to 16384; the largest is exactly 1024. A permutation: dealt slot j, on device j of req, holds prompt dealing[j].
All inputs are finite; a program needn't handle non-finite values.
Results may differ from a plain program's by a relative error of at most 0.012.
The roundings to bfloat16 on the way count: a program that leaves them out, or rounds other values in their place, can miss the bound.
Values may be sent and summed in bfloat16 or wider, within the bound.
No kernel may reach another device: no remote copies, remote signals or barrier semaphores. Data moves between devices by JAX's collectives and lax.ppermute only.
A program may use at most 128 MiB of HBM per device.

v0:
```python
import jax
import jax.numpy as jnp
from jax import lax
from jax.sharding import PartitionSpec as P

EPS = 1e-06
THETA = 1000000.0


def rms_rows(values, scale_gain):
    inv_rms = lax.rsqrt(jnp.mean(values * values, axis=-1, keepdims=True) + EPS)
    return values * inv_rms * scale_gain


def rotate(values, positions):
    features = values.shape[-1]
    half_width = features // 2
    frequency = THETA ** (-(jnp.arange(half_width).astype(jnp.float32) * 2.0) / features)
    angles = positions.astype(jnp.float32)[:, None] * frequency[None, :]
    cosine = jnp.cos(angles)[:, None, :]
    sine_part = jnp.sin(angles)[:, None, :]
    first_half = values[..., :half_width]
    second_half = values[..., half_width:]
    return jnp.concatenate(
        [
            first_half * cosine - second_half * sine_part,
            second_half * cosine + first_half * sine_part,
        ],
        axis=-1,
    )


def project(normed, w_query, w_key, w_value, query_gain, key_gain, positions):
    head_dim = query_gain.shape[0]
    row_count = normed.shape[0]
    query_rows = jnp.dot(normed, w_query, preferred_element_type=jnp.float32).reshape(
        row_count, -1, head_dim
    )
    key_rows = jnp.dot(normed, w_key, preferred_element_type=jnp.float32).reshape(
        row_count, -1, head_dim
    )
    value_rows = jnp.dot(normed, w_value, preferred_element_type=jnp.float32).astype(jnp.bfloat16)
    query_rows = rotate(rms_rows(query_rows, query_gain.astype(jnp.float32)), positions).astype(
        jnp.bfloat16
    )
    key_rows = rotate(rms_rows(key_rows, key_gain.astype(jnp.float32)), positions).astype(
        jnp.bfloat16
    )
    return (query_rows.reshape(row_count, -1), key_rows.reshape(row_count, -1), value_rows)


def attend(query_slot, key_slot, value_slot, prompt_length, head_dim):
    slot_len, query_width = query_slot.shape
    kv_heads = key_slot.shape[1] // head_dim
    group_size = query_width // head_dim // kv_heads
    queries = query_slot.reshape(slot_len, kv_heads, group_size, head_dim)
    keys_split = key_slot.reshape(slot_len, kv_heads, head_dim)
    values_split = value_slot.reshape(slot_len, kv_heads, head_dim)
    scores = jnp.einsum(
        "qkgd,skd->kgqs", queries, keys_split, preferred_element_type=jnp.float32
    ) * head_dim ** (-0.5)
    offsets = jnp.arange(slot_len, dtype=jnp.int32)
    allowed = (offsets[None, :] <= offsets[:, None]) & (offsets[None, :] < prompt_length)
    scores = jnp.where(allowed[None, None], scores, -jnp.inf)
    row_max = jnp.max(scores, axis=-1, keepdims=True)
    weights = jnp.exp(scores - row_max)
    weights = (weights / jnp.sum(weights, axis=-1, keepdims=True)).astype(jnp.bfloat16)
    mixture = jnp.einsum(
        "kgqs,skd->qkgd", weights, values_split, preferred_element_type=jnp.float32
    )
    return mixture.astype(jnp.bfloat16).reshape(slot_len, query_width)


def on_device(
    hidden, lengths, dealing, norm_gain, w_query, w_key, w_value, query_gain, key_gain, w_out
):
    devices = lax.axis_size("req")
    home_index = lax.axis_index("req")
    slice_index = lax.axis_index("tp")
    tok_rows, features = hidden.shape
    head_dim = query_gain.shape[0]
    out_width = w_out.shape[1]
    slot_len = 4 * tok_rows
    capacity = slot_len // devices
    prompt_total = lengths.shape[0]
    prompt_ids = jnp.arange(prompt_total, dtype=jnp.int32)
    prompt_ends = jnp.cumsum(lengths)
    starts = prompt_ends - lengths
    packed_ids = jnp.arange(tok_rows, dtype=jnp.int32) * devices + home_index
    segment = jnp.sum((packed_ids[:, None] >= prompt_ends[None, :]).astype(jnp.int32), axis=1)
    seg_onehot = (segment[:, None] == prompt_ids[None, :]).astype(jnp.int32)
    positions = packed_ids - jnp.sum(seg_onehot * starts[None, :], axis=1)
    inverse = jnp.zeros((prompt_total,), jnp.int32).at[dealing].set(prompt_ids)
    deal_hot = (dealing[:, None] == prompt_ids[None, :]).astype(jnp.int32)
    dealt_starts = jnp.sum(deal_hot * starts[None, :], axis=1)
    dealt_lengths = jnp.sum(deal_hot * lengths[None, :], axis=1)
    first_offset = jnp.mod(home_index - dealt_starts, devices)
    ranks = jnp.arange(capacity, dtype=jnp.int32)
    slot_offset = first_offset[None, :] + ranks[:, None] * devices
    send_valid = slot_offset < dealt_lengths[None, :]
    send_rows = jnp.where(
        send_valid, (dealt_starts[None, :] + slot_offset - home_index) // devices, 0
    ).reshape(-1)
    my_start = lax.dynamic_index_in_dim(dealt_starts, home_index, 0, keepdims=False)
    my_length = lax.dynamic_index_in_dim(dealt_lengths, home_index, 0, keepdims=False)
    roll_shift = jnp.mod(my_start, devices)
    my_slots = jnp.sum(seg_onehot * inverse[None, :], axis=1)
    back_rows = positions // devices * devices + my_slots
    offsets = jnp.arange(slot_len, dtype=jnp.int32)
    gain_values = norm_gain.astype(jnp.float32)
    picked = jnp.take(hidden, send_rows, axis=0).reshape(capacity, devices, hidden.shape[1])
    arrived = lax.all_to_all(
        jnp.where(send_valid[:, :, None], picked, jnp.zeros((), hidden.dtype)),
        "req",
        split_axis=1,
        concat_axis=1,
        tiled=True,
    )
    slot_hidden = jnp.roll(arrived, -roll_shift, axis=1).reshape(slot_len, arrived.shape[2])
    normed = rms_rows(slot_hidden.astype(jnp.float32), gain_values).astype(jnp.bfloat16)
    query_slot, key_slot, value_slot = project(
        normed, w_query, w_key, w_value, query_gain, key_gain, offsets
    )
    mixture = attend(query_slot, key_slot, value_slot, my_length, head_dim)
    sendback = jnp.roll(mixture.reshape(capacity, devices, mixture.shape[1]), roll_shift, axis=1)
    returned = lax.all_to_all(sendback, "req", split_axis=1, concat_axis=1, tiled=True)
    attended = jnp.take(returned.reshape(capacity * devices, -1), back_rows, axis=0)
    kv_cache = jnp.stack([key_slot, value_slot])[:, None]
    summed = jnp.dot(
        lax.all_gather(attended, "tp", axis=1, tiled=True),
        w_out,
        preferred_element_type=jnp.float32,
    )
    branch = lax.optimization_barrier(summed.astype(jnp.bfloat16))
    residual = lax.dynamic_slice_in_dim(hidden, slice_index * out_width, out_width, 1)
    hidden_out = (residual.astype(jnp.float32) + branch.astype(jnp.float32)).astype(jnp.bfloat16)
    return (hidden_out, kv_cache)


def solution(mesh):
    in_specs = (
        P("req", None),
        P(),
        P(),
        P(),
        P(None, "tp"),
        P(None, "tp"),
        P(None, "tp"),
        P(),
        P(),
        P(None, "tp"),
    )
    out_specs = (P("req", "tp"), P(None, "req", None, "tp"))
    return jax.shard_map(
        on_device, mesh=mesh, in_specs=in_specs, out_specs=out_specs, check_vma=False
    )
```

profile of v0, /device:TPU:1, one launch (start us, length us, event | category | flops | bytes accessed | tf_op | source)
XLA Modules:
  0.0 271.2 jit_solution(343829114084428690)
XLA Ops:
  7.2 0.9 copy.58
  8.3 0.7 sub.85
  9.0 0.8 select_reduce_fusion.2
  9.8 0.7 compare_select_fusion.7
  11.1 10.2 %gather_fusion = bf16[1024,2048]{1,0:T(8,128)(2,1)} fusion(bf16[256,2048]{1,0:T(8,128)(2,1)} %param.10, s32[1024]{0:T(1024)S(1)} %broadcast_clamp_fusion), kind=kCustom, calls=%fused_computation | custom fusion | bytes 8392704 | tf_op jit(solution)/shard_map/jit(_take)/gather | solution.py:111
  21.3 9.6 %fusion.10 = bf16[16,64,2048]{2,0,1:T(8,128)(2,1)} fusion(bf16[16,64,2048]{2,1,0:T(8,128)(2,1)} %bitcast.70, pred[16,64]{0,1:T(8,128)(4,1)S(1)} %copy.60, pred[16,64]{0,1:T(8,128)(4,1)S(1)} %copy.59), kind=kLoop, calls=%fused_computation.22 | loop fusion | flops 4194304 | bytes 8390656 | tf_op jit(solution)/shard_map/jit(_where)/select_n | solution.py:113
  30.9 13.3 %all-to-all-start = ((bf16[16,64,2048]{2,0,1:T(8,128)(2,1)}), bf16[16,64,2048]{2,0,1:T(8,128)(2,1)}, u32[]{:S(2)}, u32[]{:S(2)}) async-start(bf16[16,64,2048]{2,0,1:T(8,128)(2,1)} %fusion.10), calls=%async_computation | async-start | bytes 8388608 | tf_op jit(solution)/shard_map/all_to_all | solution.py:112
  44.2 0.6 dynamic_slice.19
  46.8 0.6 dynamic_slice.21
  47.4 4.0 %copy.80 = bf16[512,2048]{1,0:T(8,128)(2,1)} copy(bf16[512,2048]{0,1:T(8,128)(2,1)} %bitcast.76) | data formatting | bytes 4194304 | tf_op jit(solution)/shard_map/dot_general | solution.py:36
  51.4 1.4 copy.77
  52.8 0.7 iota_compare_fusion.3
  53.5 1.0 multiply_cosine_fusion
  54.5 1.3 fusion.11
  55.8 83.1 %all-to-all-done = bf16[16,64,2048]{2,0,1:T(8,128)(2,1)} async-done(((bf16[16,64,2048]{2,0,1:T(8,128)(2,1)}), bf16[16,64,2048]{2,0,1:T(8,128)(2,1)}, u32[]{:S(2)}, u32[]{:S(2)}) %all-to-all-start) | async-done | bytes 4194336 | tf_op jit(solution)/shard_map/all_to_all | solution.py:112
  138.9 4.5 %copy.62 = bf16[16,64,2048]{2,1,0:T(8,128)(2,1)S(1)} copy(bf16[16,64,2048]{2,0,1:T(8,128)(2,1)} %all-to-all-done) | data formatting | bytes 8388608 | tf_op jit(solution)/shard_map/all_to_all | solution.py:112
  143.4 6.5 %multiply_reduce_fusion = (f32[16,64]{1,0:T(8,128)S(1)}, f32[16,64,2048]{2,1,0:T(8,128)}) fusion(s32[]{:T(128)S(6)} %select_n.166, bf16[16,64,2048]{2,1,0:T(8,128)(2,1)S(1)} %copy.62), kind=kLoop, calls=%fused_computation.16 | loop fusion | flops 12581888 | bytes 12587012 | tf_op jit(solution)/shard_map/reduce_sum | solution.py:11
  149.9 4.3 %multiply_convert_fusion = bf16[16,64,2048]{2,1,0:T(8,128)(2,1)S(1)} fusion(f32[16,64,2048]{2,1,0:T(8,128)} %get-tuple-element.17, f32[2048]{0:T(1024)S(1)} %convert_element_type.122, f32[16,64]{1,0:T(8,128)S(1)} %add_rsqrt_fusion.2), kind=kLoop, calls=%fused_computation.15 | loop fusion | flops 6291456 | bytes 12595200 | tf_op jit(solution)/shard_map/convert_element_type | solution.py:120
  154.2 1.5 copy-done.1
  155.7 2.7 fusion.3
  158.4 0.7 copy-done.3
  159.1 2.4 multiply_reduce_fusion.1
  161.5 0.5 multiply_multiply_fusion
  162.0 1.2 subtract_convert_fusion
  163.2 2.4 copy.67
  165.6 1.4 copy.66
  167.0 3.9 %multiply_reduce_fusion.2 = (f32[1024,2]{0,1:T(2,128)S(1)}, f32[1024,2,128]{0,2,1:T(8,128)S(1)}) fusion(bf16[1024,2048,1]{1,0,2:T(8,128)(2,1)} %bitcast.73, bf16[2,128,2048]{2,1,0:T(8,128)(2,1)} %bitcast.80), kind=kOutput, calls=%fused_computation.41 | convolution fusion | flops 1074264064 | bytes 6299648 | tf_op jit(solution)/shard_map/dot_general | solution.py:39
  171.1 0.9 multiply_subtract_fusion
  172.0 1.2 copy-done.2
  173.1 2.1 convolution_convert_fusion
  175.2 11.5 %fusion.38 = (f32[2,2,1024]{2,1,0:T(2,128)S(1)}, f32[2,2,1024,1024]{2,3,1,0:T(8,128)}) fusion(pred[1024,1024]{0,1:T(8,128)(4,1)S(1)} %copy-done.5, bf16[1024,2,2,64]{3,0,2,1:T(8,128)(2,1)} %copy.67, bf16[1024,2,2,64]{3,0,2,1:T(8,128)(2,1)} %copy.66, bf16[1024,2,64]{0,2,1:T(8,128)(2,1)} %get-tuple-element.21, bf16[1024,2,64]{0,2,1:T(8,128)(2,1)S(1)} %get-tuple-element.20), kind=kOutput, calls=%fused_computation.108 | convolution fusion | flops 1093665792 | bytes 19415040 | tf_op jit(solution)/shard_map/sub | solution.py:66
  186.7 7.2 %fusion.15 = bf16[1024,2,2,128]{0,3,2,1:T(8,128)(2,1)S(1)} fusion(bf16[1024,2,128,1]{0,2,3,1:T(8,128)(2,1)} %bitcast.81, f32[2,2,1024,1024]{2,3,1,0:T(8,128)} %get-tuple-element.31, f32[2,2,1024]{2,1,0:T(2,128)S(1)} %get-tuple-element.30), kind=kOutput, calls=%fused_computation.31 | convolution fusion | flops 1082654720 | bytes 18366464 | tf_op jit(solution)/shard_map/kgqs,skd->qkgd/dot_general | solution.py:68
  194.0 2.0 copy.70
  196.0 1.5 reshape_reshape.4
  197.5 0.8 fusion.16
  198.3 1.5 copy.71
  199.8 7.0 %all-to-all-start.1 = ((bf16[16,64,512]{2,0,1:T(8,128)(2,1)}), bf16[16,64,512]{2,0,1:T(8,128)(2,1)}, u32[]{:S(2)}, u32[]{:S(2)}) async-start(bf16[16,64,512]{2,0,1:T(8,128)(2,1)} %copy.71), calls=%async_computation.1 | async-start | bytes 2097152 | tf_op jit(solution)/shard_map/all_to_all | solution.py:126
  206.9 0.8 scatter_custom_fusion
  208.0 26.9 %all-to-all-done.1 = bf16[16,64,512]{2,0,1:T(8,128)(2,1)} async-done(((bf16[16,64,512]{2,0,1:T(8,128)(2,1)}), bf16[16,64,512]{2,0,1:T(8,128)(2,1)}, u32[]{:S(2)}, u32[]{:S(2)}) %all-to-all-start.1) | async-done | bytes 1048608 | tf_op jit(solution)/shard_map/all_to_all | solution.py:126
  234.8 1.8 copy.72
  236.6 1.2 gather_fusion.1
  237.8 0.8 broadcast_select_fusion
  238.6 1.1 maximum_convert_fusion
  239.7 1.1 maximum_bitcast_fusion
  240.9 1.3 copy.73
  242.2 18.5 %all-gather.2.cloned.1.call-done = bf16[256,2048]{1,0:T(8,128)(2,1)} async-done(((bf16[256,512]{1,0:T(8,128)(2,1)}), bf16[256,2048]{1,0:T(8,128)(2,1)}) %all-gather.2.cloned.1.call-update) | async-done | bytes 1048592 | tf_op jit(solution)/shard_map/all_gather | solution.py:130
  260.7 1.9 convolution_convert_fusion.1
  262.6 1.7 add_convert_fusion.1
  (51 shorter events, 1.4 us)
Async XLA Ops:
  7.2 253.5 %copy-start = (bf16[2048,512]{1,0:T(8,128)(2,1)S(1)}, bf16[2048,512]{1,0:T(8,128)(2,1)}, u32[]{:S(2)}) copy-start(bf16[2048,512]{1,0:T(8,128)(2,1)} %param.19) | copy-start | bytes 6291460
  30.9 16.5 %copy-start.8 = (bf16[2048]{0:T(1024)(128)(2,1)S(1)}, bf16[2048]{0:T(1024)(128)(2,1)}, u32[]{:S(2)}) copy-start(bf16[2048]{0:T(1024)(128)(2,1)} %param.13) | copy-start | bytes 12292
  30.9 108.0 %all-to-all-start = ((bf16[16,64,2048]{2,0,1:T(8,128)(2,1)}), bf16[16,64,2048]{2,0,1:T(8,128)(2,1)}, u32[]{:S(2)}, u32[]{:S(2)}) async-start(bf16[16,64,2048]{2,0,1:T(8,128)(2,1)} %fusion.10), calls=%async_computation | async-start | bytes 8388608 | tf_op jit(solution)/shard_map/all_to_all | solution.py:112
  44.2 7.2 %copy-start.10 = (bf16[128]{0:T(256)(128)(2,1)S(1)}, bf16[128]{0:T(256)(128)(2,1)}, u32[]{:S(2)}) copy-start(bf16[128]{0:T(256)(128)(2,1)} %param.17) | copy-start | bytes 772
  44.2 7.2 %copy-start.6 = (bf16[2048,256]{1,0:T(8,128)(2,1)S(1)}, bf16[2048,256]{1,0:T(8,128)(2,1)}, u32[]{:S(2)}) copy-start(bf16[2048,256]{1,0:T(8,128)(2,1)} %param.15) | copy-start | bytes 3145732
  44.2 8.6 %copy-start.11 = (bf16[128]{0:T(256)(128)(2,1)S(1)}, bf16[128]{0:T(256)(128)(2,1)}, u32[]{:S(2)}) copy-start(bf16[128]{0:T(256)(128)(2,1)} %param.18) | copy-start | bytes 772
  149.9 5.8 %copy-start.1 = (f32[16,64,2048]{2,1,0:T(8,128)S(1)}, f32[16,64,2048]{2,1,0:T(8,128)}, u32[]{:S(2)}) copy-start(f32[16,64,2048]{2,1,0:T(8,128)} %get-tuple-element.17) | copy-start | bytes 25165828
  155.7 3.4 %copy-start.3 = (bf16[16,64,2048]{2,1,0:T(8,128)(2,1)}, bf16[16,64,2048]{2,1,0:T(8,128)(2,1)S(1)}, u32[]{:S(2)}) copy-start(bf16[16,64,2048]{2,1,0:T(8,128)(2,1)S(1)} %multiply_convert_fusion) | copy-start | bytes 12582916
  155.7 3.4 %copy-start.4 = (bf16[512,2048]{1,0:T(8,128)(2,1)S(1)}, bf16[512,2048]{1,0:T(8,128)(2,1)}, u32[]{:S(2)}) copy-start(bf16[512,2048]{1,0:T(8,128)(2,1)} %copy.80) | copy-start | bytes 6291460
  167.0 5.0 %copy-start.9 = (bf16[2048,256]{1,0:T(8,128)(2,1)S(1)}, bf16[2048,256]{1,0:T(8,128)(2,1)}, u32[]{:S(2)}) copy-start(bf16[2048,256]{1,0:T(8,128)(2,1)} %param.16) | copy-start | bytes 3145732
  170.8 2.3 copy-start.2
  173.1 2.1 copy-start.7
  173.1 2.1 copy-start.5
  199.8 35.0 %all-to-all-start.1 = ((bf16[16,64,512]{2,0,1:T(8,128)(2,1)}), bf16[16,64,512]{2,0,1:T(8,128)(2,1)}, u32[]{:S(2)}, u32[]{:S(2)}) async-start(bf16[16,64,512]{2,0,1:T(8,128)(2,1)} %copy.71), calls=%async_computation.1 | async-start | bytes 2097152 | tf_op jit(solution)/shard_map/all_to_all | solution.py:126
  206.9 53.8 %all-gather.2.cloned.1.call-start = ((), (), s32[]{:S(2)}) async-start(), calls=%async_computation.2 | async-start | bytes 1310720 | tf_op jit(solution)/shard_map/all_gather | solution.py:130
Sparse Core Ops, SparseCore 0:
  238.8 21.8 all-gather.1
where the time goes:
time: 273 us; the launch traced here: 271 us
  waiting for transfers between devices  128 us (47%)
  local copies, waits for them, and re-layouts  39.9 us (15%)
  other arithmetic  37.2 us (14%)
  matrix products  29 us (11%)
  starting transfers between devices  20.4 us (7%)
  between operations  16.3 us (6%)
    all_to_all x1, waiting for transfers between devices, on_device(): lax.all_to_all(jnp.where(send_valid[:, :, None], picked, jnp.zeros((), hi...  83.1 us
    all_to_all x1, waiting for transfers between devices, on_device(): lax.all_to_all(sendback, 'req', split_axis=1, concat_axis=1, tiled=True)  26.9 us
    all_gather x1, waiting for transfers between devices, on_device(): lax.all_gather(attended, 'tp', axis=1, tiled=True)  18.5 us
    all_to_all x1, starting transfers between devices, on_device(): lax.all_to_all(jnp.where(send_valid[:, :, None], picked, jnp.zeros((), hi...  13.3 us
    sub x1, matrix products, attend(): weights = jnp.exp(scores - row_max)  11.5 us
    gather x1, local copies, waits for them, and re-layouts, on_device(): jnp.take(hidden, send_rows, axis=0)  10.2 us
    select_n x1, other arithmetic, on_device(): jnp.where(send_valid[:, :, None], picked, jnp.zeros((), hidden.dtype))  9.61 us
    dot_general x1, matrix products, attend(): jnp.einsum('kgqs,skd->qkgd', weights, values_split, preferred_element_typ...  7.24 us
  transfers between devices with their start and end apart: 3, of which 3 were waited for; matrix products, arithmetic and copies ran while one was open for 5% of the time, Pallas kernels for 0%

commit v1 on v0

--- a/solution.py
+++ b/solution.py
@@ -80,6 +80,8 @@
     tok_rows, features = hidden.shape
     head_dim = query_gain.shape[0]
     out_width = w_out.shape[1]
+    q_width = w_query.shape[1]
+    k_width = w_key.shape[1]
     slot_len = 4 * tok_rows
     capacity = slot_len // devices
     prompt_total = lengths.shape[0]
@@ -106,21 +108,24 @@
     roll_shift = jnp.mod(my_start, devices)
     my_slots = jnp.sum(seg_onehot * inverse[None, :], axis=1)
     back_rows = positions // devices * devices + my_slots
-    offsets = jnp.arange(slot_len, dtype=jnp.int32)
     gain_values = norm_gain.astype(jnp.float32)
-    picked = jnp.take(hidden, send_rows, axis=0).reshape(capacity, devices, hidden.shape[1])
+    normed = rms_rows(hidden.astype(jnp.float32), gain_values).astype(jnp.bfloat16)
+    query_rows, key_rows, value_rows = project(
+        normed, w_query, w_key, w_value, query_gain, key_gain, positions
+    )
+    qkv_rows = jnp.concatenate([query_rows, key_rows, value_rows], axis=1)
+    picked = jnp.take(qkv_rows, send_rows, axis=0).reshape(capacity, devices, qkv_rows.shape[1])
     arrived = lax.all_to_all(
-        jnp.where(send_valid[:, :, None], picked, jnp.zeros((), hidden.dtype)),
+        jnp.where(send_valid[:, :, None], picked, jnp.zeros((), qkv_rows.dtype)),
         "req",
         split_axis=1,
         concat_axis=1,
         tiled=True,
     )
-    slot_hidden = jnp.roll(arrived, -roll_shift, axis=1).reshape(slot_len, arrived.shape[2])
-    normed = rms_rows(slot_hidden.astype(jnp.float32), gain_values).astype(jnp.bfloat16)
-    query_slot, key_slot, value_slot = project(
-        normed, w_query, w_key, w_value, query_gain, key_gain, offsets
-    )
+    slot_rows = jnp.roll(arrived, -roll_shift, axis=1).reshape(slot_len, arrived.shape[2])
+    query_slot = slot_rows[:, :q_width]
+    key_slot = slot_rows[:, q_width : q_width + k_width]
+    value_slot = slot_rows[:, q_width + k_width :]
     mixture = attend(query_slot, key_slot, value_slot, my_length, head_dim)
     sendback = jnp.roll(mixture.reshape(capacity, devices, mixture.shape[1]), roll_shift, axis=1)
     returned = lax.all_to_all(sendback, "req", split_axis=1, concat_axis=1, tiled=True)

time: 273 us -> 213 us (0.78)
  waiting for transfers between devices: 128 us -> 92 us
  other arithmetic: 37.2 us -> 23.7 us
  local copies, waits for them, and re-layouts: 39.9 us -> 30.5 us
    all_to_all x1, waiting for transfers between devices: 83.1 us -> 44.4 us  [on_device(): lax.all_to_all(jnp.where(send_valid[:, :, None], picked, jnp.zeros((), qk...]
    convert_element_type x3 -> x0, other arithmetic: 8.05 us -> none  [the longest x2 6.98 us: on_device(): rms_rows(slot_hidden.astype(jnp.float32), gain_values).astype(jnp.bfloat16)]
    select_n x2, other arithmetic: 9.64 us -> 4.07 us  [the longest x1 4.04 us: on_device(): jnp.where(send_valid[:, :, None], picked, jnp.zeros((), qkv_rows.dtype))]
    slice x0 -> x4, local copies, waits for them, and re-layouts: none -> 5.53 us  [the longest x1 2.07 us: on_device(): key_slot = slot_rows[:, q_width:q_width + k_width]]
    dot_general x2 -> x0, local copies, waits for them, and re-layouts: 5.42 us -> none  [the longest x1 3.98 us: project(): jnp.dot(normed, w_query, preferred_element_type=jnp.float32)]
    gather x1, local copies, waits for them, and re-layouts: 10.2 us -> 5.39 us  [on_device(): jnp.take(qkv_rows, send_rows, axis=0)]
    reduce_sum x1 -> x2, other arithmetic: 6.46 us -> 1.94 us  [rms_rows(): inv_rms = lax.rsqrt(jnp.mean(values * values, axis=-1, keepdims=True) + EPS)]
    unnamed x25 -> x35, local copies, waits for them, and re-layouts: 4.72 us -> 0.69 us
  transfers between devices with their start and end apart: 3 -> 3, of which waited for: 3 -> 3; matrix products, arithmetic and copies ran while one was open for 5% -> 3% of each run, Pallas kernels for 0% -> 0%
where the time goes in v1:
time: 213 us; the launch traced here: 211 us
  waiting for transfers between devices  92 us (43%)
  local copies, waits for them, and re-layouts  30.5 us (14%)
  matrix products  28.1 us (13%)
  other arithmetic  23.7 us (11%)
  starting transfers between devices  20.5 us (10%)
  between operations  16.4 us (8%)
    all_to_all x1, waiting for transfers between devices, on_device(): lax.all_to_all(jnp.where(send_valid[:, :, None], picked, jnp.zeros((), qk...  44.4 us
    all_to_all x1, waiting for transfers between devices, on_device(): lax.all_to_all(sendback, 'req', split_axis=1, concat_axis=1, tiled=True)  28 us
    all_gather x1, waiting for transfers between devices, on_device(): lax.all_gather(attended, 'tp', axis=1, tiled=True)  19.6 us
    all_to_all x1, starting transfers between devices, on_device(): lax.all_to_all(jnp.where(send_valid[:, :, None], picked, jnp.zeros((), qk...  13.3 us
    sub x1, matrix products, attend(): weights = jnp.exp(scores - row_max)  11.2 us
    dot_general x1, matrix products, attend(): jnp.einsum('kgqs,skd->qkgd', weights, values_split, preferred_element_typ...  7.24 us
    all_to_all x1, starting transfers between devices, on_device(): lax.all_to_all(sendback, 'req', split_axis=1, concat_axis=1, tiled=True)  7.13 us
    gather x1, local copies, waits for them, and re-layouts, on_device(): jnp.take(qkv_rows, send_rows, axis=0)  5.39 us
  transfers between devices with their start and end apart: 3, of which 3 were waited for; matrix products, arithmetic and copies ran while one was open for 3% of the time, Pallas kernels for 0%

profile of v1, /device:TPU:1, one launch (start us, length us, event | category | flops | bytes accessed | tf_op | source)
XLA Modules:
  0.0 211.2 jit_solution(9252795499204256088)
XLA Ops:
  7.2 0.9 copy.123
  8.3 0.7 sub.88
  9.0 0.8 select_reduce_fusion.2
  9.8 0.7 compare_select_fusion.7
  10.6 0.6 compare_and_fusion
  11.2 0.7 lt.124
  12.0 0.7 convert_element_type.73
  12.7 1.6 fusion.7
  14.3 2.2 %convolution_convert_fusion.1 = bf16[256,256]{0,1:T(8,128)(2,1)S(1)} fusion(bf16[2048,256]{1,0:T(8,128)(2,1)} %param.16, bf16[256,2048]{1,0:T(8,128)(2,1)} %param.10, f32[2048]{0:T(1024)S(1)} %convert_element_type.73, f32[256]{0:T(256)S(1)} %add_rsqrt_fusion.2), kind=kOutput, calls=%fused_computation.30 | convolution fusion | flops 270598144 | bytes 2237440 | tf_op jit(solution)/shard_map/dot_general | solution.py:42
  16.6 0.7 copy.131
  17.3 0.6 convert_element_type.79
  17.9 2.6 %multiply_reduce_fusion.1 = (f32[256,2]{0,1:T(2,128)S(1)}, f32[256,256]{0,1:T(8,128)}) fusion(bf16[2048,256]{1,0:T(8,128)(2,1)} %param.15, bf16[256,2048]{1,0:T(8,128)(2,1)S(1)} %copy-done.1, f32[2048]{0:T(1024)S(1)} %convert_element_type.73, f32[256]{0:T(256)S(1)} %add_rsqrt_fusion.2), kind=kOutput, calls=%fused_computation.42 | convolution fusion | flops 270663168 | bytes 2370560 | tf_op jit(solution)/shard_map/dot_general | solution.py:39
  20.5 0.6 add_rsqrt_fusion.1
  21.1 0.8 scatter_custom_fusion
  21.9 0.6 select_reduce_fusion
  23.7 1.1 multiply_multiply_fusion.1
  24.8 0.8 copy.149
  25.6 2.3 %fusion.29 = f32[256,512]{1,0:T(8,128)} fusion(bf16[2048,512]{1,0:T(8,128)(2,1)S(1)} %copy-done, bf16[256,2048]{1,0:T(8,128)(2,1)S(1)} %copy-done.1, f32[2048]{0:T(1024)} %copy-done.9, f32[256]{0:T(256)} %copy-done.14), kind=kOutput, calls=%fused_computation.107 | convolution fusion | flops 538968064 | bytes 3679232 | tf_op jit(solution)/shard_map/dot_general | solution.py:36
  27.8 1.2 reshape.456
  31.1 5.4 %gather_fusion = bf16[1024,1024]{1,0:T(8,128)(2,1)} fusion(bf16[256,1024]{1,0:T(8,128)(2,1)S(1)} %pad_maximum_fusion, s32[1024]{0:T(1024)S(1)} %broadcast_clamp_fusion), kind=kCustom, calls=%fused_computation | custom fusion | bytes 4198400 | tf_op jit(solution)/shard_map/jit(_take)/gather | solution.py:117
  36.5 4.0 %fusion.11 = bf16[16,64,1024]{2,0,1:T(8,128)(2,1)} fusion(bf16[16,64,1024]{2,1,0:T(8,128)(2,1)} %bitcast.61, pred[16,64]{0,1:T(8,128)(4,1)S(1)} %copy.125, pred[16,64]{0,1:T(8,128)(4,1)S(1)} %copy.124), kind=kLoop, calls=%fused_computation.25 | loop fusion | flops 2097152 | bytes 4196352 | tf_op jit(solution)/shard_map/jit(_where)/select_n | solution.py:119
  40.5 13.3 %all-to-all-start = ((bf16[16,64,1024]{2,0,1:T(8,128)(2,1)}), bf16[16,64,1024]{2,0,1:T(8,128)(2,1)}, u32[]{:S(2)}, u32[]{:S(2)}) async-start(bf16[16,64,1024]{2,0,1:T(8,128)(2,1)} %fusion.11), calls=%async_computation | async-start | bytes 4194304 | tf_op jit(solution)/shard_map/all_to_all | solution.py:118
  53.8 0.6 dynamic_slice.19
  56.4 0.6 dynamic_slice.21
  57.0 0.6 iota_compare_fusion.3
  57.7 1.3 fusion.6
  59.0 44.4 %all-to-all-done = bf16[16,64,1024]{2,0,1:T(8,128)(2,1)} async-done(((bf16[16,64,1024]{2,0,1:T(8,128)(2,1)}), bf16[16,64,1024]{2,0,1:T(8,128)(2,1)}, u32[]{:S(2)}, u32[]{:S(2)}) %all-to-all-start) | async-done | bytes 2097184 | tf_op jit(solution)/shard_map/all_to_all | solution.py:118
  103.4 2.7 %copy.133 = bf16[16,64,1024]{2,1,0:T(8,128)(2,1)S(1)} copy(bf16[16,64,1024]{2,0,1:T(8,128)(2,1)} %all-to-all-done) | data formatting | bytes 4194304 | tf_op jit(solution)/shard_map/all_to_all | solution.py:118
  106.2 1.6 fusion.10
  107.8 1.4 slice_bitcast_fusion
  109.3 2.0 copy.135
  111.4 2.1 copy.136
  113.4 1.3 copy.137
  114.8 11.2 %fusion.31 = (f32[2,2,1024]{2,1,0:T(2,128)S(1)}, f32[2,2,1024,1024]{2,3,1,0:T(8,128)}) fusion(pred[1024,1024]{0,1:T(8,128)(4,1)} %fusion.6, bf16[1024,2,128,1]{0,2,3,1:T(8,128)(2,1)} %bitcast.68, bf16[1024,2,2,128]{0,3,2,1:T(8,128)(2,1)} %bitcast.65), kind=kOutput, calls=%fused_computation.108 | convolution fusion | flops 1090520064 | bytes 19415040 | tf_op jit(solution)/shard_map/sub | solution.py:66
  126.0 7.2 %fusion.15 = bf16[1024,2,2,128]{0,3,2,1:T(8,128)(2,1)S(1)} fusion(bf16[1024,2,128,1]{0,2,3,1:T(8,128)(2,1)} %bitcast.67, f32[2,2,1024,1024]{2,3,1,0:T(8,128)} %get-tuple-element.35, f32[2,2,1024]{2,1,0:T(2,128)S(1)} %get-tuple-element.34), kind=kOutput, calls=%fused_computation.28 | convolution fusion | flops 1082654720 | bytes 18366464 | tf_op jit(solution)/shard_map/kgqs,skd->qkgd/dot_general | solution.py:68
  133.2 2.0 copy.141
  135.3 1.5 reshape_reshape.3
  136.7 0.8 fusion.16
  137.6 1.5 copy.142
  139.1 7.1 %all-to-all-start.1 = ((bf16[16,64,512]{2,0,1:T(8,128)(2,1)}), bf16[16,64,512]{2,0,1:T(8,128)(2,1)}, u32[]{:S(2)}, u32[]{:S(2)}) async-start(bf16[16,64,512]{2,0,1:T(8,128)(2,1)} %copy.142), calls=%async_computation.1 | async-start | bytes 2097152 | tf_op jit(solution)/shard_map/all_to_all | solution.py:131
  146.4 28.0 %all-to-all-done.1 = bf16[16,64,512]{2,0,1:T(8,128)(2,1)} async-done(((bf16[16,64,512]{2,0,1:T(8,128)(2,1)}), bf16[16,64,512]{2,0,1:T(8,128)(2,1)}, u32[]{:S(2)}, u32[]{:S(2)}) %all-to-all-start.1) | async-done | bytes 1048608 | tf_op jit(solution)/shard_map/all_to_all | solution.py:131
  174.3 1.8 copy.143
  176.1 1.2 gather_fusion.1
  177.3 0.8 broadcast_select_fusion
  178.1 2.3 %maximum_bitcast_fusion = bf16[2,1,1024,256]{3,2,1,0:T(8,128)(2,1)} fusion(bf16[1,1024,256]{2,1,0:T(8,128)(2,1)} %get-tuple-element.21, bf16[1,1024,256]{2,1,0:T(8,128)(2,1)} %get-tuple-element.20), kind=kLoop, calls=%fused_computation.32 | loop fusion | flops 524288 | bytes 2097152
  180.4 19.6 %all-gather.2.cloned.1.call-done = bf16[256,2048]{1,0:T(8,128)(2,1)} async-done(((bf16[256,512]{1,0:T(8,128)(2,1)}), bf16[256,2048]{1,0:T(8,128)(2,1)}) %all-gather.2.cloned.1.call-update) | async-done | bytes 1048592 | tf_op jit(solution)/shard_map/all_gather | solution.py:135
  200.0 2.6 %convolution_convert_fusion = bf16[256,512]{1,0:T(8,128)(2,1)S(1)} fusion(bf16[256,2048]{1,0:T(8,128)(2,1)} %all-gather.2.cloned.1.call-done, bf16[2048,512]{1,0:T(8,128)(2,1)} %param.19), kind=kOutput, calls=%fused_computation.29 | convolution fusion | flops 537001984 | bytes 3407872 | tf_op jit(solution)/shard_map/dot_general | solution.py:134
  202.6 1.7 add_convert_fusion
  (68 shorter events, 3.8 us)
Async XLA Ops:
  7.2 18.4 %copy-start = (bf16[2048,512]{1,0:T(8,128)(2,1)S(1)}, bf16[2048,512]{1,0:T(8,128)(2,1)}, u32[]{:S(2)}) copy-start(bf16[2048,512]{1,0:T(8,128)(2,1)} %param.14) | copy-start | bytes 6291460
  9.8 2.2 %copy-start.10 = (s32[64]{0:T(128)}, s32[64]{0:T(128)S(1)}, u32[]{:S(2)}) copy-start(s32[64]{0:T(128)S(1)} %get-tuple-element.19) | copy-start | bytes 772
  9.8 7.5 %copy-start.12 = (s32[64]{0:T(128)}, s32[64]{0:T(128)S(1)}, u32[]{:S(2)}) copy-start(s32[64]{0:T(128)S(1)} %get-tuple-element.18) | copy-start | bytes 772
  12.7 5.2 %copy-start.9 = (f32[2048]{0:T(1024)}, f32[2048]{0:T(1024)S(1)}, u32[]{:S(2)}) copy-start(f32[2048]{0:T(1024)S(1)} %convert_element_type.73) | copy-start | bytes 24580
  12.7 4.6 %copy-start.15 = (bf16[128]{0:T(256)(128)(2,1)S(1)}, bf16[128]{0:T(256)(128)(2,1)}, u32[]{:S(2)}) copy-start(bf16[128]{0:T(256)(128)(2,1)} %param.18) | copy-start | bytes 772
  12.7 5.2 %copy-start.1 = (bf16[256,2048]{1,0:T(8,128)(2,1)S(1)}, bf16[256,2048]{1,0:T(8,128)(2,1)}, u32[]{:S(2)}) copy-start(bf16[256,2048]{1,0:T(8,128)(2,1)} %param.10) | copy-start | bytes 3145732
  14.3 6.1 %copy-start.14 = (f32[256]{0:T(256)}, f32[256]{0:T(256)S(1)}, u32[]{:S(2)}) copy-start(f32[256]{0:T(256)S(1)} %add_rsqrt_fusion.2) | copy-start | bytes 3076
  22.6 0.6 copy-start.5
  25.6 3.5 %copy-start.16 = (bf16[128]{0:T(256)(128)(2,1)S(1)}, bf16[128]{0:T(256)(128)(2,1)}, u32[]{:S(2)}) copy-start(bf16[128]{0:T(256)(128)(2,1)} %param.17) | copy-start | bytes 772
  29.4 1.4 copy-start.4
  29.4 1.4 copy-start.8
  29.5 1.5 copy-start.2
  29.5 1.5 copy-start.3
  40.5 13.3 %copy-start.11 = (s32[64]{0:T(128)S(1)}, s32[64]{0:T(128)}, u32[]{:S(2)}) copy-start(s32[64]{0:T(128)} %copy-done.10) | copy-start | bytes 772
  40.5 15.9 %copy-start.13 = (s32[64]{0:T(128)S(1)}, s32[64]{0:T(128)}, u32[]{:S(2)}) copy-start(s32[64]{0:T(128)} %copy-done.12) | copy-start | bytes 772
  40.5 62.9 %all-to-all-start = ((bf16[16,64,1024]{2,0,1:T(8,128)(2,1)}), bf16[16,64,1024]{2,0,1:T(8,128)(2,1)}, u32[]{:S(2)}, u32[]{:S(2)}) async-start(bf16[16,64,1024]{2,0,1:T(8,128)(2,1)} %fusion.11), calls=%async_computation | async-start | bytes 4194304 | tf_op jit(solution)/shard_map/all_to_all | solution.py:118
  137.5 8.8 %copy-start.6 = (s32[256]{0:T(256)S(1)}, s32[256]{0:T(256)}, u32[]{:S(2)}) copy-start(s32[256]{0:T(256)} %copy-done.5) | copy-start | bytes 3076
  137.6 8.8 %copy-start.7 = (s32[256]{0:T(256)S(1)}, s32[256]{0:T(256)}, u32[]{:S(2)}) copy-start(s32[256]{0:T(256)} %get-tuple-element.16) | copy-start | bytes 3076
  139.1 35.2 %all-to-all-start.1 = ((bf16[16,64,512]{2,0,1:T(8,128)(2,1)}), bf16[16,64,512]{2,0,1:T(8,128)(2,1)}, u32[]{:S(2)}, u32[]{:S(2)}) async-start(bf16[16,64,512]{2,0,1:T(8,128)(2,1)} %copy.142), calls=%async_computation.1 | async-start | bytes 2097152 | tf_op jit(solution)/shard_map/all_to_all | solution.py:131
  146.3 53.7 %all-gather.2.cloned.1.call-start = ((), (), s32[]{:S(2)}) async-start(), calls=%async_computation.2 | async-start | bytes 1310720 | tf_op jit(solution)/shard_map/all_gather | solution.py:135
Sparse Core Ops, SparseCore 0:
  178.2 21.6 all-gather.1

commit v2 on v1

--- a/solution.py
+++ b/solution.py
@@ -1,6 +1,8 @@
 import jax
 import jax.numpy as jnp
 from jax import lax
+from jax.experimental import pallas as pl
+from jax.experimental.pallas import tpu as pltpu
 from jax.sharding import PartitionSpec as P
 
 EPS = 1e-06
@@ -49,26 +51,58 @@
     return (query_rows.reshape(row_count, -1), key_rows.reshape(row_count, -1), value_rows)
 
 
-def attend(query_slot, key_slot, value_slot, prompt_length, head_dim):
-    slot_len, query_width = query_slot.shape
-    kv_heads = key_slot.shape[1] // head_dim
-    group_size = query_width // head_dim // kv_heads
-    queries = query_slot.reshape(slot_len, kv_heads, group_size, head_dim)
-    keys_split = key_slot.reshape(slot_len, kv_heads, head_dim)
-    values_split = value_slot.reshape(slot_len, kv_heads, head_dim)
-    scores = jnp.einsum(
-        "qkgd,skd->kgqs", queries, keys_split, preferred_element_type=jnp.float32
-    ) * head_dim ** (-0.5)
-    offsets = jnp.arange(slot_len, dtype=jnp.int32)
-    allowed = (offsets[None, :] <= offsets[:, None]) & (offsets[None, :] < prompt_length)
-    scores = jnp.where(allowed[None, None], scores, -jnp.inf)
-    row_max = jnp.max(scores, axis=-1, keepdims=True)
-    weights = jnp.exp(scores - row_max)
-    weights = (weights / jnp.sum(weights, axis=-1, keepdims=True)).astype(jnp.bfloat16)
-    mixture = jnp.einsum(
-        "kgqs,skd->qkgd", weights, values_split, preferred_element_type=jnp.float32
-    )
-    return mixture.astype(jnp.bfloat16).reshape(slot_len, query_width)
+def attention_kernel(qkv_ref, qpos_ref, kpos_ref, out_ref, *, q_width, k_width, head_dim, blocks):
+    rows = qkv_ref.shape[0]
+    block = rows // blocks
+    kv_heads = k_width // head_dim
+    group = q_width // head_dim // kv_heads
+    scale = head_dim ** (-0.5)
+    for i in range(blocks):
+        key_rows = block * (i + 1)
+        rows_here = pl.ds(i * block, block)
+        allowed = kpos_ref[:, :key_rows] <= qpos_ref[rows_here, :]
+        for h in range(kv_heads):
+            k_col = q_width + h * head_dim
+            v_col = q_width + k_width + h * head_dim
+            keys = qkv_ref[:key_rows, k_col : k_col + head_dim]
+            values = qkv_ref[:key_rows, v_col : v_col + head_dim]
+            for g in range(group):
+                q_col = (h * group + g) * head_dim
+                queries = qkv_ref[rows_here, q_col : q_col + head_dim]
+                scores = lax.dot_general(
+                    queries,
+                    keys,
+                    (((1,), (1,)), ((), ())),
+                    preferred_element_type=jnp.float32,
+                ) * scale
+                scores = jnp.where(allowed, scores, -jnp.inf)
+                row_max = jnp.max(scores, axis=-1, keepdims=True)
+                weights = jnp.exp(scores - row_max)
+                weights = (weights / jnp.sum(weights, axis=-1, keepdims=True)).astype(jnp.bfloat16)
+                mixed = jnp.dot(weights, values, preferred_element_type=jnp.float32)
+                out_ref[rows_here, q_col : q_col + head_dim] = mixed.astype(out_ref.dtype)
+
+
+def attend(qkv_slot, query_pos, key_pos, q_width, k_width, head_dim):
+    rows = qkv_slot.shape[0]
+    blocks = 4
+    heads = q_width // head_dim
+    causal_pairs = blocks * (blocks + 1) // 2
+    pair_flops = 4 * (rows // blocks) ** 2 * head_dim
+    vmem = pl.BlockSpec(memory_space=pltpu.VMEM)
+    return pl.pallas_call(
+        lambda *refs: attention_kernel(
+            *refs, q_width=q_width, k_width=k_width, head_dim=head_dim, blocks=blocks
+        ),
+        out_shape=jax.ShapeDtypeStruct((rows, q_width), jnp.bfloat16),
+        in_specs=[vmem, vmem, vmem],
+        out_specs=vmem,
+        cost_estimate=pl.CostEstimate(
+            flops=heads * causal_pairs * pair_flops,
+            transcendentals=heads * causal_pairs * (rows // blocks) ** 2,
+            bytes_accessed=qkv_slot.size * 2 + rows * q_width * 2,
+        ),
+    )(qkv_slot, query_pos[:, None], key_pos[None, :])
 
 
 def on_device(
@@ -114,28 +148,53 @@
         normed, w_query, w_key, w_value, query_gain, key_gain, positions
     )
     qkv_rows = jnp.concatenate([query_rows, key_rows, value_rows], axis=1)
-    picked = jnp.take(qkv_rows, send_rows, axis=0).reshape(capacity, devices, qkv_rows.shape[1])
+    chosen = jnp.where(send_valid, send_rows.reshape(capacity, devices), -1).reshape(-1)
+    one_hot = (chosen[:, None] == jnp.arange(tok_rows, dtype=jnp.int32)[None, :]).astype(
+        qkv_rows.dtype
+    )
+    picked = jnp.dot(one_hot, qkv_rows, preferred_element_type=jnp.float32).astype(qkv_rows.dtype)
     arrived = lax.all_to_all(
-        jnp.where(send_valid[:, :, None], picked, jnp.zeros((), qkv_rows.dtype)),
+        picked.reshape(capacity, devices, qkv_rows.shape[1]),
         "req",
         split_axis=1,
         concat_axis=1,
         tiled=True,
     )
-    slot_rows = jnp.roll(arrived, -roll_shift, axis=1).reshape(slot_len, arrived.shape[2])
-    query_slot = slot_rows[:, :q_width]
-    key_slot = slot_rows[:, q_width : q_width + k_width]
-    value_slot = slot_rows[:, q_width + k_width :]
-    mixture = attend(query_slot, key_slot, value_slot, my_length, head_dim)
-    sendback = jnp.roll(mixture.reshape(capacity, devices, mixture.shape[1]), roll_shift, axis=1)
-    returned = lax.all_to_all(sendback, "req", split_axis=1, concat_axis=1, tiled=True)
+    source_ids = jnp.arange(devices, dtype=jnp.int32)
+    arrived_pos = (
+        ranks[:, None] * devices + jnp.mod(source_ids[None, :] - my_start, devices)
+    ).reshape(-1)
+    key_pos = jnp.where(arrived_pos < my_length, arrived_pos, 1 << 30)
+    mixture = attend(
+        arrived.reshape(slot_len, arrived.shape[2]), arrived_pos, key_pos, q_width, k_width, head_dim
+    )
+    returned = lax.all_to_all(
+        mixture.reshape(capacity, devices, mixture.shape[1]),
+        "req",
+        split_axis=1,
+        concat_axis=1,
+        tiled=True,
+    )
     attended = jnp.take(returned.reshape(capacity * devices, -1), back_rows, axis=0)
-    kv_cache = jnp.stack([key_slot, value_slot])[:, None]
+    kv_rows = jnp.roll(arrived[:, :, q_width:], -roll_shift, axis=1).reshape(slot_len, -1)
+    kv_cache = jnp.stack([kv_rows[:, :k_width], kv_rows[:, k_width:]])[:, None]
+    tp_size = lax.axis_size("tp")
+    w_rows = w_out.shape[0] // tp_size
     summed = jnp.dot(
-        lax.all_gather(attended, "tp", axis=1, tiled=True),
-        w_out,
+        attended,
+        lax.dynamic_slice_in_dim(w_out, slice_index * w_rows, w_rows, 0),
         preferred_element_type=jnp.float32,
     )
+    for shift in range(1, tp_size):
+        passed = lax.ppermute(
+            attended, "tp", perm=[(i, (i + shift) % tp_size) for i in range(tp_size)]
+        )
+        source = jnp.mod(slice_index - shift, tp_size)
+        summed = summed + jnp.dot(
+            passed,
+            lax.dynamic_slice_in_dim(w_out, source * w_rows, w_rows, 0),
+            preferred_element_type=jnp.float32,
+        )
     branch = lax.optimization_barrier(summed.astype(jnp.bfloat16))
     residual = lax.dynamic_slice_in_dim(hidden, slice_index * out_width, out_width, 1)
     hidden_out = (residual.astype(jnp.float32) + branch.astype(jnp.float32)).astype(jnp.bfloat16)

time: 213 us -> 166 us (0.78)
  matrix products: 28.1 us -> 9.87 us
  between operations: 16.4 us -> 2.75 us
  waiting for transfers between devices: 92 us -> 79.3 us
  Pallas kernels: 0 us -> 10.4 us
  local copies, waits for them, and re-layouts: 30.5 us -> 21.2 us
  other arithmetic: 23.7 us -> 15.1 us
  starting transfers between devices: 20.5 us -> 24.8 us
    all_gather x1 -> x0, waiting for transfers between devices: 19.6 us -> none  [on_device(): lax.all_gather(attended, 'tp', axis=1, tiled=True)]
    sub x1 -> x0, matrix products: 11.2 us -> none  [attend(): weights = jnp.exp(scores - row_max)]
    pallas_call x0 -> x1, Pallas kernels: none -> 10.4 us  [attend(): pl.pallas_call(lambda *refs: attention_kernel(*refs, q_width=q_width, k_w...]
    ppermute x0 -> x3, waiting for transfers between devices: none -> 9.73 us  [on_device(): lax.ppermute(attended, 'tp', perm=[(i, (i + shift) % tp_size) for i in ra...]
    dot_general x2 -> x5, matrix products: 9.86 us -> 1.93 us  [the longest x3 0.88 us: on_device(): jnp.dot(passed, lax.dynamic_slice_in_dim(w_out, source * w_rows, w_rows,...]
    gather x1 -> x0, local copies, waits for them, and re-layouts: 5.39 us -> none  [on_device(): jnp.take(qkv_rows, send_rows, axis=0)]
    reshape x0 -> x2, local copies, waits for them, and re-layouts: none -> 5.29 us  [the longest x1 2.78 us: on_device(): mixture.reshape(capacity, devices, mixture.shape[1])]
    ppermute x0 -> x3, starting transfers between devices: none -> 4.47 us  [on_device(): lax.ppermute(attended, 'tp', perm=[(i, (i + shift) % tp_size) for i in ra...]
  transfers between devices with their start and end apart: 3 -> 5, of which waited for: 3 -> 5; matrix products, arithmetic and copies ran while one was open for 3% -> 6% of each run, Pallas kernels for 0% -> 0%
where the time goes in v2:
time: 166 us; the launch traced here: 163 us
  waiting for transfers between devices  79.3 us (48%)
  starting transfers between devices  24.8 us (15%)
  local copies, waits for them, and re-layouts  21.2 us (13%)
  other arithmetic  15.1 us (9%)
  Pallas kernels  10.4 us (6%)
  matrix products  9.87 us (6%)
  between operations  2.75 us (2%)
    all_to_all x1, waiting for transfers between devices, on_device(): lax.all_to_all(picked.reshape(capacity, devices, qkv_rows.shape[1]), 'req...  46.4 us
    all_to_all x1, waiting for transfers between devices, on_device(): lax.all_to_all(mixture.reshape(capacity, devices, mixture.shape[1]), 'req...  23.1 us
    all_to_all x1, starting transfers between devices, on_device(): lax.all_to_all(picked.reshape(capacity, devices, qkv_rows.shape[1]), 'req...  13.2 us
    pallas_call x1, Pallas kernels, attend(): pl.pallas_call(lambda *refs: attention_kernel(*refs, q_width=q_width, k_w...  10.4 us
    ppermute x3, waiting for transfers between devices, on_device(): lax.ppermute(attended, 'tp', perm=[(i, (i + shift) % tp_size) for i in ra...  9.73 us
    all_to_all x1, starting transfers between devices, on_device(): lax.all_to_all(mixture.reshape(capacity, devices, mixture.shape[1]), 'req...  7.16 us
    ppermute x3, starting transfers between devices, on_device(): lax.ppermute(attended, 'tp', perm=[(i, (i + shift) % tp_size) for i in ra...  4.47 us
    all_to_all x1, local copies, waits for them, and re-layouts, on_device(): lax.all_to_all(picked.reshape(capacity, devices, qkv_rows.shape[1]), 'req...  4.09 us
  transfers between devices with their start and end apart: 5, of which 5 were waited for; matrix products, arithmetic and copies ran while one was open for 6% of the time, Pallas kernels for 0%

profile of v2, /device:TPU:1, one launch (start us, length us, event | category | flops | bytes accessed | tf_op | source)
XLA Modules:
  0.0 163.5 jit_solution(14628899968477144419)
XLA Ops:
  0.7 0.8 convert_element_type.68
  1.5 1.6 fusion
  3.1 2.2 %convolution_convert_fusion.1 = bf16[256,256]{0,1:T(8,128)(2,1)S(1)} fusion(bf16[2048,256]{1,0:T(8,128)(2,1)} %param.16, bf16[256,2048]{1,0:T(8,128)(2,1)} %param.10, f32[2048]{0:T(1024)S(1)} %convert_element_type.68, f32[256]{0:T(256)S(1)} %add_rsqrt_fusion.2), kind=kOutput, calls=%fused_computation.14 | convolution fusion | flops 270598144 | bytes 2237440 | tf_op jit(solution)/shard_map/dot_general | solution.py:44
  5.4 0.7 copy.74
  6.1 0.5 convert_element_type.74
  6.6 2.6 %multiply_reduce_fusion.1 = (f32[256,2]{0,1:T(2,128)S(1)}, f32[256,256]{0,1:T(8,128)}) fusion(bf16[2048,256]{1,0:T(8,128)(2,1)} %param.15, bf16[256,2048]{1,0:T(8,128)(2,1)S(1)} %copy-done.1, f32[2048]{0:T(1024)S(1)} %convert_element_type.68, f32[256]{0:T(256)S(1)} %add_rsqrt_fusion.2), kind=kOutput, calls=%fused_computation.40 | convolution fusion | flops 270663168 | bytes 2370560 | tf_op jit(solution)/shard_map/dot_general | solution.py:41
  9.6 0.7 select_reduce_fusion.3
  10.3 0.5 and_select_fusion.2
  10.8 0.6 dynamic_slice.27
  11.4 1.1 compare_select_fusion.3
  12.6 0.8 scatter_custom_fusion
  13.5 0.3 multiply_cosine_fusion
  14.0 1.1 multiply_multiply_fusion.1
  15.1 0.8 copy.73
  15.9 3.2 %fusion.33 = f32[256,512]{1,0:T(8,128)} fusion(bf16[2048,512]{1,0:T(8,128)(2,1)} %param.14, bf16[256,2048]{1,0:T(8,128)(2,1)S(1)} %copy-done.1, f32[2048]{0:T(1024)} %copy-done.4, f32[256]{0:T(256)} %copy-done.12), kind=kOutput, calls=%fused_computation.103 | convolution fusion | flops 538968064 | bytes 3679232 | tf_op jit(solution)/shard_map/dot_general | solution.py:38
  19.1 1.2 reshape.380
  20.3 0.3 multiply_reduce_fusion
  20.7 0.3 multiply_multiply_fusion
  21.1 0.5 subtract_convert_fusion
  21.6 0.4 pad_maximum_fusion
  22.4 0.7 convolution_convert_fusion
  23.1 2.5 %copy.75 = bf16[16,64,1024]{2,0,1:T(8,128)(2,1)} copy(bf16[16,64,1024]{2,1,0:T(8,128)(2,1)S(1)} %bitcast.37) | data formatting | bytes 4194304 | tf_op jit(solution)/shard_map/reshape | solution.py:157
  25.6 13.2 %all-to-all-start = ((bf16[16,64,1024]{2,0,1:T(8,128)(2,1)}), bf16[16,64,1024]{2,0,1:T(8,128)(2,1)}, u32[]{:S(2)}, u32[]{:S(2)}) async-start(bf16[16,64,1024]{2,0,1:T(8,128)(2,1)} %copy.75), calls=%async_computation | async-start | bytes 4194304 | tf_op jit(solution)/shard_map/all_to_all | solution.py:156
  38.8 1.3 add.308.refs_1_
  40.2 0.6 dynamic_slice.28
  40.7 1.2 compare_select_fusion.refs_2_
  42.0 46.4 %all-to-all-done = bf16[16,64,1024]{2,0,1:T(8,128)(2,1)} async-done(((bf16[16,64,1024]{2,0,1:T(8,128)(2,1)}), bf16[16,64,1024]{2,0,1:T(8,128)(2,1)}, u32[]{:S(2)}, u32[]{:S(2)}) %all-to-all-start) | async-done | bytes 2097184 | tf_op jit(solution)/shard_map/all_to_all | solution.py:156
  88.4 4.1 %copy.76 = bf16[16,64,1024]{2,1,0:T(8,128)(2,1)} copy(bf16[16,64,1024]{2,0,1:T(8,128)(2,1)} %all-to-all-done) | data formatting | bytes 4194304 | tf_op jit(solution)/shard_map/all_to_all | solution.py:156
  92.5 10.4 %shard_map.113 = bf16[1024,512]{1,0:T(8,128)(2,1)} custom-call(bf16[1024,1024]{1,0:T(8,128)(2,1)} %bitcast.35, s32[1024,1]{1,0:T(8,128)} %add.308.refs_1_, s32[1,1024]{1,0:T(1,128)} %compare_select_fusion.refs_2_), custom_call_target="tpu_custom_call" | custom-call | flops 1342177280 | bytes 3145728 | tf_op jit(solution)/shard_map/pallas_call | solution.py:93
  103.0 2.8 %copy.78 = bf16[16,64,512]{2,0,1:T(8,128)(2,1)} copy(bf16[16,64,512]{2,1,0:T(8,128)(2,1)} %bitcast.39) | data formatting | bytes 2097152 | tf_op jit(solution)/shard_map/reshape | solution.py:172
  105.8 7.2 %all-to-all-start.1 = ((bf16[16,64,512]{2,0,1:T(8,128)(2,1)}), bf16[16,64,512]{2,0,1:T(8,128)(2,1)}, u32[]{:S(2)}, u32[]{:S(2)}) async-start(bf16[16,64,512]{2,0,1:T(8,128)(2,1)} %copy.78), calls=%async_computation.1 | async-start | bytes 2097152 | tf_op jit(solution)/shard_map/all_to_all | solution.py:171
  114.7 1.3 slice.34
  116.0 0.8 fusion.5
  116.8 1.1 slice_bitcast_fusion.1
  117.9 23.1 %all-to-all-done.1 = bf16[16,64,512]{2,0,1:T(8,128)(2,1)} async-done(((bf16[16,64,512]{2,0,1:T(8,128)(2,1)}), bf16[16,64,512]{2,0,1:T(8,128)(2,1)}, u32[]{:S(2)}, u32[]{:S(2)}) %all-to-all-start.1) | async-done | bytes 1048608 | tf_op jit(solution)/shard_map/all_to_all | solution.py:171
  141.0 1.8 %copy.79 = bf16[16,64,512]{2,1,0:T(8,128)(2,1)S(1)} copy(bf16[16,64,512]{2,0,1:T(8,128)(2,1)} %all-to-all-done.1) | data formatting | bytes 2097152 | tf_op jit(solution)/shard_map/all_to_all | solution.py:171
  142.8 1.2 gather_fusion
  144.1 2.8 %collective-permute-start.2 = (bf16[256,512]{1,0:T(8,128)(2,1)S(1)}, bf16[256,512]{1,0:T(8,128)(2,1)S(1)}, u32[]{:S(2)}, u32[]{:S(2)}) collective-permute-start(bf16[256,512]{1,0:T(8,128)(2,1)S(1)} %broadcast_select_fusion), channel_id=1, source_target_pairs={{0,3},{1,0},{2,1},{3,2},{4,7},{5,4},{6,5},{7,6},{8,11},{9,8},{10,9... | collective-permute-start | bytes 786440 | tf_op jit(solution)/shard_map/ppermute | solution.py:189
  146.9 2.3 %maximum_bitcast_fusion = bf16[2,1,1024,256]{3,2,1,0:T(8,128)(2,1)} fusion(bf16[1,1024,256]{2,1,0:T(8,128)(2,1)} %get-tuple-element.15, bf16[1,1024,256]{2,1,0:T(8,128)(2,1)} %get-tuple-element.14), kind=kLoop, calls=%fused_computation.16 | loop fusion | flops 524288 | bytes 2097152
  149.2 1.6 %collective-permute-start.1 = (bf16[256,512]{1,0:T(8,128)(2,1)S(1)}, bf16[256,512]{1,0:T(8,128)(2,1)S(1)}, u32[]{:S(2)}, u32[]{:S(2)}) collective-permute-start(bf16[256,512]{1,0:T(8,128)(2,1)S(1)} %broadcast_select_fusion), channel_id=1, source_target_pairs={{0,2},{1,3},{2,0},{3,1},{4,6},{5,7},{6,4},{7,5},{8,10},{9,11},{10,... | collective-permute-start | bytes 786440 | tf_op jit(solution)/shard_map/ppermute | solution.py:189
  150.8 0.3 fusion.15
  151.1 0.3 collective-permute-done.2
  151.4 0.3 fusion.11
  151.7 6.1 %collective-permute-done = bf16[256,512]{1,0:T(8,128)(2,1)S(1)} collective-permute-done((bf16[256,512]{1,0:T(8,128)(2,1)S(1)}, bf16[256,512]{1,0:T(8,128)(2,1)S(1)}, u32[]{:S(2)}, u32[]{:S(2)}) %collective-permute-start) | collective-permute-done | bytes 262176 | tf_op jit(solution)/shard_map/ppermute | solution.py:189
  157.8 0.3 convolution_add_fusion.1
  158.1 3.3 %collective-permute-done.1 = bf16[256,512]{1,0:T(8,128)(2,1)S(1)} collective-permute-done((bf16[256,512]{1,0:T(8,128)(2,1)S(1)}, bf16[256,512]{1,0:T(8,128)(2,1)S(1)}, u32[]{:S(2)}, u32[]{:S(2)}) %collective-permute-start.1) | collective-permute-done | bytes 262176 | tf_op jit(solution)/shard_map/ppermute | solution.py:189
  161.4 0.3 fusion.4
  161.7 1.7 %add_convert_fusion = bf16[256,512]{1,0:T(8,128)(2,1)} fusion(bf16[256,512]{1,0:T(8,128)(2,1)S(1)} %fusion.4, bf16[256,2048]{1,0:T(8,128)(2,1)} %param.10, s32[]{:T(128)S(6)} %select_n.143), kind=kLoop, calls=%fused_computation.25 | loop fusion | flops 524288 | bytes 786436 | tf_op jit(solution)/shard_map/convert_element_type | solution.py:200
  (61 shorter events, 1.5 us)
Async XLA Ops:
  0.6 150.2 %copy-start = (bf16[2048,512]{1,0:T(8,128)(2,1)S(1)}, bf16[2048,512]{1,0:T(8,128)(2,1)}, u32[]{:S(2)}) copy-start(bf16[2048,512]{1,0:T(8,128)(2,1)} %param.19) | copy-start | bytes 6291460
  1.5 5.1 %copy-start.4 = (f32[2048]{0:T(1024)}, f32[2048]{0:T(1024)S(1)}, u32[]{:S(2)}) copy-start(f32[2048]{0:T(1024)S(1)} %convert_element_type.68) | copy-start | bytes 24580
  1.5 4.6 %copy-start.13 = (bf16[128]{0:T(256)(128)(2,1)S(1)}, bf16[128]{0:T(256)(128)(2,1)}, u32[]{:S(2)}) copy-start(bf16[128]{0:T(256)(128)(2,1)} %param.18) | copy-start | bytes 772
  1.5 5.1 %copy-start.1 = (bf16[256,2048]{1,0:T(8,128)(2,1)S(1)}, bf16[256,2048]{1,0:T(8,128)(2,1)}, u32[]{:S(2)}) copy-start(bf16[256,2048]{1,0:T(8,128)(2,1)} %param.10) | copy-start | bytes 3145732
  3.1 6.1 %copy-start.12 = (f32[256]{0:T(256)}, f32[256]{0:T(256)S(1)}, u32[]{:S(2)}) copy-start(f32[256]{0:T(256)S(1)} %add_rsqrt_fusion.2) | copy-start | bytes 3076
  5.3 3.9 %copy-start.5 = (s32[64]{0:T(128)S(1)}, s32[64]{0:T(128)}, u32[]{:S(2)}) copy-start(s32[64]{0:T(128)} %param.11) | copy-start | bytes 772
  5.4 4.2 %copy-start.10 = (s32[64]{0:T(128)S(1)}, s32[64]{0:T(128)}, u32[]{:S(2)}) copy-start(s32[64]{0:T(128)} %param.12) | copy-start | bytes 772
  10.3 1.1 copy-start.7
  15.9 4.4 %copy-start.14 = (bf16[128]{0:T(256)(128)(2,1)S(1)}, bf16[128]{0:T(256)(128)(2,1)}, u32[]{:S(2)}) copy-start(bf16[128]{0:T(256)(128)(2,1)} %param.17) | copy-start | bytes 772
  20.7 1.3 copy-start.6
  20.7 1.3 copy-start.9
  20.7 1.5 copy-start.8
  20.7 1.5 copy-start.11
  20.7 1.6 %copy-start.2 = (bf16[256,256]{1,0:T(8,128)(2,1)S(1)}, bf16[256,256]{1,0:T(8,128)(2,1)}, u32[]{:S(2)}) copy-start(bf16[256,256]{1,0:T(8,128)(2,1)} %copy.74) | copy-start | bytes 393220
  20.7 1.6 %copy-start.3 = (bf16[256,256]{1,0:T(8,128)(2,1)S(1)}, bf16[256,256]{1,0:T(8,128)(2,1)}, u32[]{:S(2)}) copy-start(bf16[256,256]{1,0:T(8,128)(2,1)} %copy.73) | copy-start | bytes 393220
  25.6 62.8 %all-to-all-start = ((bf16[16,64,1024]{2,0,1:T(8,128)(2,1)}), bf16[16,64,1024]{2,0,1:T(8,128)(2,1)}, u32[]{:S(2)}, u32[]{:S(2)}) async-start(bf16[16,64,1024]{2,0,1:T(8,128)(2,1)} %copy.75), calls=%async_computation | async-start | bytes 4194304 | tf_op jit(solution)/shard_map/all_to_all | solution.py:156
  105.8 35.2 %all-to-all-start.1 = ((bf16[16,64,512]{2,0,1:T(8,128)(2,1)}), bf16[16,64,512]{2,0,1:T(8,128)(2,1)}, u32[]{:S(2)}, u32[]{:S(2)}) async-start(bf16[16,64,512]{2,0,1:T(8,128)(2,1)} %copy.78), calls=%async_computation.1 | async-start | bytes 2097152 | tf_op jit(solution)/shard_map/all_to_all | solution.py:171
  144.1 7.3 %collective-permute-start.2 = (bf16[256,512]{1,0:T(8,128)(2,1)S(1)}, bf16[256,512]{1,0:T(8,128)(2,1)S(1)}, u32[]{:S(2)}, u32[]{:S(2)}) collective-permute-start(bf16[256,512]{1,0:T(8,128)(2,1)S(1)} %broadcast_select_fusion), channel_id=1, source_target_pairs={{0,3},{1,0},{2,1},{3,2},{4,7},{5,4},{6,5},{7,6},{8,11},{9,8},{10,9... | collective-permute-start | bytes 786440 | tf_op jit(solution)/shard_map/ppermute | solution.py:189
  149.2 8.7 %collective-permute-start = (bf16[256,512]{1,0:T(8,128)(2,1)S(1)}, bf16[256,512]{1,0:T(8,128)(2,1)S(1)}, u32[]{:S(2)}, u32[]{:S(2)}) collective-permute-start(bf16[256,512]{1,0:T(8,128)(2,1)S(1)} %broadcast_select_fusion), channel_id=1, source_target_pairs={{0,1},{1,2},{2,3},{3,0},{4,5},{5,6},{6,7},{7,4},{8,9},{9,10},{10,1... | collective-permute-start | bytes 786440 | tf_op jit(solution)/shard_map/ppermute | solution.py:189
  149.2 12.3 %collective-permute-start.1 = (bf16[256,512]{1,0:T(8,128)(2,1)S(1)}, bf16[256,512]{1,0:T(8,128)(2,1)S(1)}, u32[]{:S(2)}, u32[]{:S(2)}) collective-permute-start(bf16[256,512]{1,0:T(8,128)(2,1)S(1)} %broadcast_select_fusion), channel_id=1, source_target_pairs={{0,2},{1,3},{2,0},{3,1},{4,6},{5,7},{6,4},{7,5},{8,10},{9,11},{10,... | collective-permute-start | bytes 786440 | tf_op jit(solution)/shard_map/ppermute | solution.py:189

commit v3 on v2

--- a/solution.py
+++ b/solution.py
@@ -179,22 +179,18 @@
     kv_rows = jnp.roll(arrived[:, :, q_width:], -roll_shift, axis=1).reshape(slot_len, -1)
     kv_cache = jnp.stack([kv_rows[:, :k_width], kv_rows[:, k_width:]])[:, None]
     tp_size = lax.axis_size("tp")
-    w_rows = w_out.shape[0] // tp_size
+    gathered = lax.all_to_all(
+        jnp.broadcast_to(attended[None], (tp_size,) + attended.shape),
+        "tp",
+        split_axis=0,
+        concat_axis=0,
+        tiled=True,
+    )
     summed = jnp.dot(
-        attended,
-        lax.dynamic_slice_in_dim(w_out, slice_index * w_rows, w_rows, 0),
+        gathered.transpose(1, 0, 2).reshape(attended.shape[0], -1),
+        w_out,
         preferred_element_type=jnp.float32,
     )
-    for shift in range(1, tp_size):
-        passed = lax.ppermute(
-            attended, "tp", perm=[(i, (i + shift) % tp_size) for i in range(tp_size)]
-        )
-        source = jnp.mod(slice_index - shift, tp_size)
-        summed = summed + jnp.dot(
-            passed,
-            lax.dynamic_slice_in_dim(w_out, source * w_rows, w_rows, 0),
-            preferred_element_type=jnp.float32,
-        )
     branch = lax.optimization_barrier(summed.astype(jnp.bfloat16))
     residual = lax.dynamic_slice_in_dim(hidden, slice_index * out_width, out_width, 1)
     hidden_out = (residual.astype(jnp.float32) + branch.astype(jnp.float32)).astype(jnp.bfloat16)

time: 166 us -> 169 us (1.018)
  waiting for transfers between devices: 79.3 us -> 83.3 us
    ppermute x3 -> x0, waiting for transfers between devices: 9.73 us -> none  [on_device(): lax.ppermute(attended, 'tp', perm=[(i, (i + shift) % tp_size) for i in ra...]
    all_to_all x0 -> x1, waiting for transfers between devices: none -> 8.82 us  [on_device(): lax.all_to_all(jnp.broadcast_to(attended[None], (tp_size,) + attended.sha...]
    all_to_all x1, waiting for transfers between devices: 23.1 us -> 28 us  [on_device(): lax.all_to_all(mixture.reshape(capacity, devices, mixture.shape[1]), 'req...]
    ppermute x3 -> x0, starting transfers between devices: 4.47 us -> none  [on_device(): lax.ppermute(attended, 'tp', perm=[(i, (i + shift) % tp_size) for i in ra...]
    all_to_all x0 -> x1, starting transfers between devices: none -> 4.19 us  [on_device(): lax.all_to_all(jnp.broadcast_to(attended[None], (tp_size,) + attended.sha...]
  transfers between devices with their start and end apart: 5 -> 3, of which waited for: 5 -> 3; matrix products, arithmetic and copies ran while one was open for 6% -> 4% of each run, Pallas kernels for 0% -> 0%
where the time goes in v3:
time: 169 us; the launch traced here: 168 us
  waiting for transfers between devices  83.3 us (49%)
  starting transfers between devices  24.5 us (14%)
  local copies, waits for them, and re-layouts  21.4 us (13%)
  other arithmetic  14.6 us (9%)
  matrix products  11 us (7%)
  Pallas kernels  10.4 us (6%)
  between operations  2.65 us (2%)
    all_to_all x1, waiting for transfers between devices, on_device(): lax.all_to_all(picked.reshape(capacity, devices, qkv_rows.shape[1]), 'req...  46.4 us
    all_to_all x1, waiting for transfers between devices, on_device(): lax.all_to_all(mixture.reshape(capacity, devices, mixture.shape[1]), 'req...  28 us
    all_to_all x1, starting transfers between devices, on_device(): lax.all_to_all(picked.reshape(capacity, devices, qkv_rows.shape[1]), 'req...  13.2 us
    pallas_call x1, Pallas kernels, attend(): pl.pallas_call(lambda *refs: attention_kernel(*refs, q_width=q_width, k_w...  10.4 us
    all_to_all x1, waiting for transfers between devices, on_device(): lax.all_to_all(jnp.broadcast_to(attended[None], (tp_size,) + attended.sha...  8.82 us
    all_to_all x1, starting transfers between devices, on_device(): lax.all_to_all(mixture.reshape(capacity, devices, mixture.shape[1]), 'req...  7.15 us
    all_to_all x1, starting transfers between devices, on_device(): lax.all_to_all(jnp.broadcast_to(attended[None], (tp_size,) + attended.sha...  4.19 us
    all_to_all x1, local copies, waits for them, and re-layouts, on_device(): lax.all_to_all(picked.reshape(capacity, devices, qkv_rows.shape[1]), 'req...  4.09 us
  transfers between devices with their start and end apart: 3, of which 3 were waited for; matrix products, arithmetic and copies ran while one was open for 4% of the time, Pallas kernels for 0%

profile of v3, /device:TPU:1, one launch (start us, length us, event | category | flops | bytes accessed | tf_op | source)
XLA Modules:
  0.0 167.8 jit_solution(15657453210008783803)
XLA Ops:
  0.7 0.8 convert_element_type.68
  1.5 1.6 fusion
  3.1 2.2 %convolution_convert_fusion.2 = bf16[256,256]{0,1:T(8,128)(2,1)S(1)} fusion(bf16[2048,256]{1,0:T(8,128)(2,1)} %param.16, bf16[256,2048]{1,0:T(8,128)(2,1)} %param.10, f32[2048]{0:T(1024)S(1)} %convert_element_type.68, f32[256]{0:T(256)S(1)} %add_rsqrt_fusion.2), kind=kOutput, calls=%fused_computation.11 | convolution fusion | flops 270598144 | bytes 2237440 | tf_op jit(solution)/shard_map/dot_general | solution.py:44
  5.4 0.7 copy.79
  6.1 0.5 convert_element_type.74
  6.6 2.6 %multiply_reduce_fusion.1 = (f32[256,2]{0,1:T(2,128)S(1)}, f32[256,256]{0,1:T(8,128)}) fusion(bf16[2048,256]{1,0:T(8,128)(2,1)} %param.15, bf16[256,2048]{1,0:T(8,128)(2,1)S(1)} %copy-done.1, f32[2048]{0:T(1024)S(1)} %convert_element_type.68, f32[256]{0:T(256)S(1)} %add_rsqrt_fusion.2), kind=kOutput, calls=%fused_computation.31 | convolution fusion | flops 270663168 | bytes 2370560 | tf_op jit(solution)/shard_map/dot_general | solution.py:41
  9.2 0.1 copy.73
  9.3 0.1 reduce-window.8
  9.4 0.1 reduce
  9.6 0.7 select_reduce_fusion.3
  10.3 0.5 and_select_fusion.2
  10.8 0.6 dynamic_slice.15
  11.4 1.1 compare_select_fusion.3
  12.6 0.8 scatter_custom_fusion
  13.5 0.3 multiply_cosine_fusion
  14.0 1.1 multiply_multiply_fusion.1
  15.1 0.8 copy.78
  15.9 2.3 %fusion.21 = f32[256,512]{1,0:T(8,128)} fusion(bf16[2048,512]{1,0:T(8,128)(2,1)S(1)} %copy-done, bf16[256,2048]{1,0:T(8,128)(2,1)S(1)} %copy-done.1, f32[2048]{0:T(1024)} %copy-done.3, f32[256]{0:T(256)} %copy-done.9), kind=kOutput, calls=%fused_computation.90 | convolution fusion | flops 538968064 | bytes 3679232 | tf_op jit(solution)/shard_map/dot_general | solution.py:38
  18.2 1.2 reshape.395
  19.4 0.3 multiply_reduce_fusion
  19.8 0.3 multiply_multiply_fusion
  20.1 0.5 subtract_convert_fusion
  20.6 0.4 pad_maximum_fusion
  21.2 0.7 broadcast_add_fusion
  22.1 1.7 convolution_convert_fusion
  23.7 2.5 %copy.80 = bf16[16,64,1024]{2,0,1:T(8,128)(2,1)} copy(bf16[16,64,1024]{2,1,0:T(8,128)(2,1)S(1)} %bitcast.38) | data formatting | bytes 4194304 | tf_op jit(solution)/shard_map/reshape | solution.py:157
  26.2 13.2 %all-to-all-start = ((bf16[16,64,1024]{2,0,1:T(8,128)(2,1)}), bf16[16,64,1024]{2,0,1:T(8,128)(2,1)}, u32[]{:S(2)}, u32[]{:S(2)}) async-start(bf16[16,64,1024]{2,0,1:T(8,128)(2,1)} %copy.80), calls=%async_computation | async-start | bytes 4194304 | tf_op jit(solution)/shard_map/all_to_all | solution.py:156
  39.4 1.3 add.268.refs_1_
  40.8 0.6 dynamic_slice.16
  41.3 1.2 compare_select_fusion.refs_2_
  42.6 46.4 %all-to-all-done = bf16[16,64,1024]{2,0,1:T(8,128)(2,1)} async-done(((bf16[16,64,1024]{2,0,1:T(8,128)(2,1)}), bf16[16,64,1024]{2,0,1:T(8,128)(2,1)}, u32[]{:S(2)}, u32[]{:S(2)}) %all-to-all-start) | async-done | bytes 2097184 | tf_op jit(solution)/shard_map/all_to_all | solution.py:156
  89.0 4.1 %copy.81 = bf16[16,64,1024]{2,1,0:T(8,128)(2,1)} copy(bf16[16,64,1024]{2,0,1:T(8,128)(2,1)} %all-to-all-done) | data formatting | bytes 4194304 | tf_op jit(solution)/shard_map/all_to_all | solution.py:156
  93.1 10.4 %shard_map.113 = bf16[1024,512]{1,0:T(8,128)(2,1)} custom-call(bf16[1024,1024]{1,0:T(8,128)(2,1)} %bitcast.36, s32[1024,1]{1,0:T(8,128)} %add.268.refs_1_, s32[1,1024]{1,0:T(1,128)} %compare_select_fusion.refs_2_), custom_call_target="tpu_custom_call" | custom-call | flops 1342177280 | bytes 3145728 | tf_op jit(solution)/shard_map/pallas_call | solution.py:93
  103.6 2.8 %copy.83 = bf16[16,64,512]{2,0,1:T(8,128)(2,1)} copy(bf16[16,64,512]{2,1,0:T(8,128)(2,1)} %bitcast.41) | data formatting | bytes 2097152 | tf_op jit(solution)/shard_map/reshape | solution.py:172
  106.3 7.1 %all-to-all-start.1 = ((bf16[16,64,512]{2,0,1:T(8,128)(2,1)}), bf16[16,64,512]{2,0,1:T(8,128)(2,1)}, u32[]{:S(2)}, u32[]{:S(2)}) async-start(bf16[16,64,512]{2,0,1:T(8,128)(2,1)} %copy.83), calls=%async_computation.1 | async-start | bytes 2097152 | tf_op jit(solution)/shard_map/all_to_all | solution.py:171
  113.6 28.0 %all-to-all-done.1 = bf16[16,64,512]{2,0,1:T(8,128)(2,1)} async-done(((bf16[16,64,512]{2,0,1:T(8,128)(2,1)}), bf16[16,64,512]{2,0,1:T(8,128)(2,1)}, u32[]{:S(2)}, u32[]{:S(2)}) %all-to-all-start.1) | async-done | bytes 1048608 | tf_op jit(solution)/shard_map/all_to_all | solution.py:171
  141.6 1.8 %copy.84 = bf16[16,64,512]{2,1,0:T(8,128)(2,1)S(1)} copy(bf16[16,64,512]{2,0,1:T(8,128)(2,1)} %all-to-all-done.1) | data formatting | bytes 2097152 | tf_op jit(solution)/shard_map/all_to_all | solution.py:171
  143.4 1.2 gather_fusion
  144.5 0.1 broadcast_select_fusion
  144.7 0.1 copy.85
  144.8 1.1 broadcast_in_dim.23
  145.8 4.2 %all-to-all-start.2 = ((bf16[4,256,512]{1,2,0:T(8,128)(2,1)}), bf16[4,256,512]{1,2,0:T(8,128)(2,1)S(1)}, u32[]{:S(2)}, u32[]{:S(2)}) async-start(bf16[4,256,512]{1,2,0:T(8,128)(2,1)} %broadcast_in_dim.23), calls=%async_computation.2 | async-start | bytes 2097152 | tf_op jit(solution)/shard_map/all_to_all | solution.py:182
  151.7 1.3 slice.34
  153.0 0.8 fusion.3
  153.9 1.1 maximum_bitcast_fusion
  155.0 8.8 %all-to-all-done.2 = bf16[4,256,512]{1,2,0:T(8,128)(2,1)S(1)} async-done(((bf16[4,256,512]{1,2,0:T(8,128)(2,1)}), bf16[4,256,512]{1,2,0:T(8,128)(2,1)S(1)}, u32[]{:S(2)}, u32[]{:S(2)}) %all-to-all-start.2) | async-done | bytes 1048608 | tf_op jit(solution)/shard_map/all_to_all | solution.py:182
  163.8 2.3 %convolution_convert_fusion.1 = bf16[256,512]{1,0:T(8,128)(2,1)S(1)} fusion(bf16[256,2048]{0,1:T(8,128)(2,1)S(1)} %bitcast.40, bf16[2048,512]{1,0:T(8,128)(2,1)} %param.19), kind=kOutput, calls=%fused_computation.10 | convolution fusion | flops 537001984 | bytes 3407872 | tf_op jit(solution)/shard_map/dot_general | solution.py:189
  166.1 1.7 %add_convert_fusion = bf16[256,512]{1,0:T(8,128)(2,1)} fusion(bf16[256,512]{1,0:T(8,128)(2,1)S(1)} %convolution_convert_fusion.1, bf16[256,2048]{1,0:T(8,128)(2,1)} %param.10, s32[]{:T(128)S(6)} %select_n.125), kind=kLoop, calls=%fused_computation.22 | loop fusion | flops 524288 | bytes 786436 | tf_op jit(solution)/shard_map/convert_element_type | solution.py:196
  (50 shorter events, 1.0 us)
Async XLA Ops:
  0.6 15.3 %copy-start = (bf16[2048,512]{1,0:T(8,128)(2,1)S(1)}, bf16[2048,512]{1,0:T(8,128)(2,1)}, u32[]{:S(2)}) copy-start(bf16[2048,512]{1,0:T(8,128)(2,1)} %param.14) | copy-start | bytes 6291460
  1.5 5.1 %copy-start.3 = (f32[2048]{0:T(1024)}, f32[2048]{0:T(1024)S(1)}, u32[]{:S(2)}) copy-start(f32[2048]{0:T(1024)S(1)} %convert_element_type.68) | copy-start | bytes 24580
  1.5 4.6 %copy-start.10 = (bf16[128]{0:T(256)(128)(2,1)S(1)}, bf16[128]{0:T(256)(128)(2,1)}, u32[]{:S(2)}) copy-start(bf16[128]{0:T(256)(128)(2,1)} %param.18) | copy-start | bytes 772
  1.5 5.1 %copy-start.1 = (bf16[256,2048]{1,0:T(8,128)(2,1)S(1)}, bf16[256,2048]{1,0:T(8,128)(2,1)}, u32[]{:S(2)}) copy-start(bf16[256,2048]{1,0:T(8,128)(2,1)} %param.10) | copy-start | bytes 3145732
  3.1 6.1 %copy-start.9 = (f32[256]{0:T(256)}, f32[256]{0:T(256)S(1)}, u32[]{:S(2)}) copy-start(f32[256]{0:T(256)S(1)} %add_rsqrt_fusion.2) | copy-start | bytes 3076
  5.3 3.9 %copy-start.4 = (s32[64]{0:T(128)S(1)}, s32[64]{0:T(128)}, u32[]{:S(2)}) copy-start(s32[64]{0:T(128)} %param.11) | copy-start | bytes 772
  5.4 4.2 %copy-start.8 = (s32[64]{0:T(128)S(1)}, s32[64]{0:T(128)}, u32[]{:S(2)}) copy-start(s32[64]{0:T(128)} %param.12) | copy-start | bytes 772
  10.3 1.1 copy-start.6
  15.9 3.5 %copy-start.11 = (bf16[128]{0:T(256)(128)(2,1)S(1)}, bf16[128]{0:T(256)(128)(2,1)}, u32[]{:S(2)}) copy-start(bf16[128]{0:T(256)(128)(2,1)} %param.17) | copy-start | bytes 772
  19.8 1.3 copy-start.5
  19.8 1.3 copy-start.7
  19.8 2.3 %copy-start.2 = (bf16[256,256]{1,0:T(8,128)(2,1)S(1)}, bf16[256,256]{1,0:T(8,128)(2,1)}, u32[]{:S(2)}) copy-start(bf16[256,256]{1,0:T(8,128)(2,1)} %copy.79) | copy-start | bytes 393220
  26.2 62.8 %all-to-all-start = ((bf16[16,64,1024]{2,0,1:T(8,128)(2,1)}), bf16[16,64,1024]{2,0,1:T(8,128)(2,1)}, u32[]{:S(2)}, u32[]{:S(2)}) async-start(bf16[16,64,1024]{2,0,1:T(8,128)(2,1)} %copy.80), calls=%async_computation | async-start | bytes 4194304 | tf_op jit(solution)/shard_map/all_to_all | solution.py:156
  106.3 35.2 %all-to-all-start.1 = ((bf16[16,64,512]{2,0,1:T(8,128)(2,1)}), bf16[16,64,512]{2,0,1:T(8,128)(2,1)}, u32[]{:S(2)}, u32[]{:S(2)}) async-start(bf16[16,64,512]{2,0,1:T(8,128)(2,1)} %copy.83), calls=%async_computation.1 | async-start | bytes 2097152 | tf_op jit(solution)/shard_map/all_to_all | solution.py:171
  145.8 18.0 %all-to-all-start.2 = ((bf16[4,256,512]{1,2,0:T(8,128)(2,1)}), bf16[4,256,512]{1,2,0:T(8,128)(2,1)S(1)}, u32[]{:S(2)}, u32[]{:S(2)}) async-start(bf16[4,256,512]{1,2,0:T(8,128)(2,1)} %broadcast_in_dim.23), calls=%async_computation.2 | async-start | bytes 2097152 | tf_op jit(solution)/shard_map/all_to_all | solution.py:182

commit v4 on v2

--- a/solution.py
+++ b/solution.py
@@ -49,6 +49,96 @@
         jnp.bfloat16
     )
     return (query_rows.reshape(row_count, -1), key_rows.reshape(row_count, -1), value_rows)
+
+
+def prep_kernel(
+    hidden_ref,
+    norm_gain_ref,
+    wq_ref,
+    wk_ref,
+    wv_ref,
+    qgain_ref,
+    kgain_ref,
+    cos_ref,
+    sin_ref,
+    chosen_ref,
+    out_ref,
+    qkv_ref,
+    *,
+    head_dim,
+    row_blocks,
+):
+    values = hidden_ref[...].astype(jnp.float32)
+    inv_rms = lax.rsqrt(jnp.mean(values * values, axis=-1, keepdims=True) + EPS)
+    normed = (values * inv_rms * norm_gain_ref[...]).astype(jnp.bfloat16)
+    cosine = cos_ref[...]
+    sine = sin_ref[...]
+    column = 0
+    for w_ref, gain_ref in ((wq_ref, qgain_ref), (wk_ref, kgain_ref)):
+        rows = jnp.dot(normed, w_ref[...], preferred_element_type=jnp.float32)
+        gain = gain_ref[...]
+        for h in range(rows.shape[1] // head_dim):
+            head = rows[:, h * head_dim : (h + 1) * head_dim]
+            head_inv = lax.rsqrt(jnp.mean(head * head, axis=-1, keepdims=True) + EPS)
+            head = head * head_inv * gain
+            swapped = pltpu.roll(head, head_dim // 2, 1)
+            qkv_ref[:, column : column + head_dim] = (head * cosine + swapped * sine).astype(
+                jnp.bfloat16
+            )
+            column += head_dim
+    v_width = wv_ref.shape[1]
+    qkv_ref[:, column : column + v_width] = jnp.dot(
+        normed, wv_ref[...], preferred_element_type=jnp.float32
+    ).astype(jnp.bfloat16)
+    tok_rows = qkv_ref.shape[0]
+    out_rows = out_ref.shape[0]
+    block = out_rows // row_blocks
+    qkv = qkv_ref[...]
+    token_ids = lax.broadcasted_iota(jnp.int32, (block, tok_rows), 1)
+    for b in range(row_blocks):
+        rows_here = pl.ds(b * block, block)
+        one_hot = (chosen_ref[rows_here, :] == token_ids).astype(jnp.bfloat16)
+        out_ref[rows_here, :] = jnp.dot(
+            one_hot, qkv, preferred_element_type=jnp.float32
+        ).astype(out_ref.dtype)
+
+
+def prepare(hidden, norm_gain, w_query, w_key, w_value, query_gain, key_gain, positions, chosen):
+    tok_rows, features = hidden.shape
+    head_dim = query_gain.shape[0]
+    half_width = head_dim // 2
+    width = w_query.shape[1] + w_key.shape[1] + w_value.shape[1]
+    frequency = THETA ** (-(jnp.arange(half_width).astype(jnp.float32) * 2.0) / head_dim)
+    angles = positions.astype(jnp.float32)[:, None] * frequency[None, :]
+    cosine = jnp.cos(angles)
+    sine = jnp.sin(angles)
+    cos_full = jnp.concatenate([cosine, cosine], axis=1)
+    sin_signed = jnp.concatenate([-sine, sine], axis=1)
+    out_rows = chosen.shape[0]
+    vmem = pl.BlockSpec(memory_space=pltpu.VMEM)
+    return pl.pallas_call(
+        lambda *refs: prep_kernel(*refs, head_dim=head_dim, row_blocks=4),
+        out_shape=jax.ShapeDtypeStruct((out_rows, width), jnp.bfloat16),
+        in_specs=[vmem] * 10,
+        out_specs=vmem,
+        scratch_shapes=[pltpu.VMEM((tok_rows, width), jnp.bfloat16)],
+        cost_estimate=pl.CostEstimate(
+            flops=2 * tok_rows * features * width + 2 * out_rows * tok_rows * width,
+            transcendentals=tok_rows * 8,
+            bytes_accessed=hidden.size * 2 + features * width * 2 + out_rows * width * 2,
+        ),
+    )(
+        hidden,
+        norm_gain.astype(jnp.float32)[None, :],
+        w_query,
+        w_key,
+        w_value,
+        query_gain.astype(jnp.float32)[None, :],
+        key_gain.astype(jnp.float32)[None, :],
+        cos_full,
+        sin_signed,
+        chosen[:, None],
+    )
 
 
 def attention_kernel(qkv_ref, qpos_ref, kpos_ref, out_ref, *, q_width, k_width, head_dim, blocks):
@@ -142,24 +232,17 @@
     roll_shift = jnp.mod(my_start, devices)
     my_slots = jnp.sum(seg_onehot * inverse[None, :], axis=1)
     back_rows = positions // devices * devices + my_slots
-    gain_values = norm_gain.astype(jnp.float32)
-    normed = rms_rows(hidden.astype(jnp.float32), gain_values).astype(jnp.bfloat16)
-    query_rows, key_rows, value_rows = project(
-        normed, w_query, w_key, w_value, query_gain, key_gain, positions
-    )
-    qkv_rows = jnp.concatenate([query_rows, key_rows, value_rows], axis=1)
-    chosen = jnp.where(send_valid, send_rows.reshape(capacity, devices), -1).reshape(-1)
-    one_hot = (chosen[:, None] == jnp.arange(tok_rows, dtype=jnp.int32)[None, :]).astype(
-        qkv_rows.dtype
-    )
-    picked = jnp.dot(one_hot, qkv_rows, preferred_element_type=jnp.float32).astype(qkv_rows.dtype)
+    chosen = jnp.where(send_valid, send_rows.reshape(capacity, devices), -1).T.reshape(-1)
+    picked = prepare(
+        hidden, norm_gain, w_query, w_key, w_value, query_gain, key_gain, positions, chosen
+    )
     arrived = lax.all_to_all(
-        picked.reshape(capacity, devices, qkv_rows.shape[1]),
+        picked.reshape(devices, capacity, picked.shape[1]),
         "req",
-        split_axis=1,
-        concat_axis=1,
+        split_axis=0,
+        concat_axis=0,
         tiled=True,
-    )
+    ).transpose(1, 0, 2)
     source_ids = jnp.arange(devices, dtype=jnp.int32)
     arrived_pos = (
         ranks[:, None] * devices + jnp.mod(source_ids[None, :] - my_start, devices)

time: 166 us -> 159 us (0.958)
  matrix products: 9.87 us -> 1.18 us
  Pallas kernels: 10.4 us -> 16.8 us
  local copies, waits for them, and re-layouts: 21.2 us -> 16.8 us
    dot_general x4 -> x0, matrix products: 8.69 us -> none  [the longest x1 3.16 us: project(): jnp.dot(normed, w_query, preferred_element_type=jnp.float32)]
    pallas_call x0 -> x1, Pallas kernels: none -> 6.37 us  [prepare(): pl.pallas_call(lambda *refs: prep_kernel(*refs, head_dim=head_dim, row_bl...]
    reshape x2 -> x0, local copies, waits for them, and re-layouts: 3.71 us -> none  [the longest x1 2.5 us: on_device(): picked.reshape(capacity, devices, qkv_rows.shape[1])]
    broadcast_in_dim x0 -> x2, other arithmetic: none -> 2.68 us  [the longest x1 1.43 us: prepare(): norm_gain.astype(jnp.float32)[None, :]]
    reduce_sum x2 -> x0, other arithmetic: 1.94 us -> none  [rms_rows(): inv_rms = lax.rsqrt(jnp.mean(values * values, axis=-1, keepdims=True) + EPS)]
where the time goes in v4:
time: 159 us; the launch traced here: 157 us
  waiting for transfers between devices  79.2 us (50%)
  starting transfers between devices  24.8 us (16%)
  local copies, waits for them, and re-layouts  16.8 us (11%)
  Pallas kernels  16.8 us (11%)
  other arithmetic  15.5 us (10%)
  between operations  2.55 us (2%)
    all_to_all x1, waiting for transfers between devices, on_device(): lax.all_to_all(picked.reshape(devices, capacity, picked.shape[1]), 'req',...  46.4 us
    all_to_all x1, waiting for transfers between devices, on_device(): lax.all_to_all(mixture.reshape(capacity, devices, mixture.shape[1]), 'req...  23.1 us
    all_to_all x1, starting transfers between devices, on_device(): lax.all_to_all(picked.reshape(devices, capacity, picked.shape[1]), 'req',...  13.2 us
    pallas_call x1, Pallas kernels, attend(): pl.pallas_call(lambda *refs: attention_kernel(*refs, q_width=q_width, k_w...  10.4 us
    ppermute x3, waiting for transfers between devices, on_device(): lax.ppermute(attended, 'tp', perm=[(i, (i + shift) % tp_size) for i in ra...  9.73 us
    all_to_all x1, starting transfers between devices, on_device(): lax.all_to_all(mixture.reshape(capacity, devices, mixture.shape[1]), 'req...  7.17 us
    pallas_call x1, Pallas kernels, prepare(): pl.pallas_call(lambda *refs: prep_kernel(*refs, head_dim=head_dim, row_bl...  6.37 us
    ppermute x3, starting transfers between devices, on_device(): lax.ppermute(attended, 'tp', perm=[(i, (i + shift) % tp_size) for i in ra...  4.47 us
  transfers between devices with their start and end apart: 5, of which 5 were waited for; matrix products, arithmetic and copies ran while one was open for 6% of the time, Pallas kernels for 0%

profile of v4, /device:TPU:1, one launch (start us, length us, event | category | flops | bytes accessed | tf_op | source)
XLA Modules:
  0.0 156.8 jit_solution(4021774169893413737)
XLA Ops:
  0.7 1.4 broadcast_in_dim.68
  2.1 0.7 copy.46
  2.8 0.1 reduce-window.8
  2.9 0.1 reduce
  3.1 0.7 sub.85
  3.7 0.8 select_reduce_fusion.3
  4.6 0.6 dynamic_slice.27
  5.1 1.2 compare_select_fusion.3
  6.4 0.1 convert_reduce_fusion
  6.5 0.8 scatter_custom_fusion
  7.2 0.1 select_reduce_fusion
  7.3 0.5 fusion.11
  7.9 0.8 pad_maximum_fusion.refs_7_
  8.7 0.1 add_compare_fusion
  8.8 0.3 lt.133
  9.2 0.3 sub.102
  9.5 1.3 bitcast_convert_fusion
  10.7 0.8 pad_maximum_fusion.1.refs_8_
  11.5 1.2 select_select_fusion.refs_9_
  12.6 6.4 %shard_map.113 = bf16[1024,1024]{1,0:T(8,128)(2,1)} custom-call(bf16[256,2048]{1,0:T(8,128)(2,1)} %refs_0_.1, f32[1,2048]{1,0:T(1,128)} %bitcast.40, bf16[2048,512]{1,0:T(8,128)(2,1)} %refs_2_.1, bf16[2048,256]{1,0:T(8,128)(2,1)} %refs_3_.1, bf16[2048,256]{1,0:T(8,128)(2,1)} %refs_4_.1, f32[1,128]{1,0:T(1,128)} %get-tuple-element.20.refs_5_, ...), custom_call_target="tpu_custom_call" | custom-call | flops 1610612736 | bytes 7340032 | tf_op jit(solution)/shard_map/pallas_call | solution.py:119
  19.0 13.2 %all-to-all-start = ((bf16[64,16,1024]{2,1,0:T(8,128)(2,1)}), bf16[64,16,1024]{2,1,0:T(8,128)(2,1)}, u32[]{:S(2)}, u32[]{:S(2)}) async-start(bf16[64,16,1024]{2,1,0:T(8,128)(2,1)} %bitcast.35), calls=%async_computation | async-start | bytes 4194304 | tf_op jit(solution)/shard_map/all_to_all | solution.py:239
  32.3 1.3 add.274.refs_1_
  33.5 0.1 add.255
  33.6 0.6 dynamic_slice.28
  34.2 1.2 compare_select_fusion.refs_2_
  35.4 46.4 %all-to-all-done = bf16[64,16,1024]{2,1,0:T(8,128)(2,1)} async-done(((bf16[64,16,1024]{2,1,0:T(8,128)(2,1)}), bf16[64,16,1024]{2,1,0:T(8,128)(2,1)}, u32[]{:S(2)}, u32[]{:S(2)}) %all-to-all-start) | async-done | bytes 2097184 | tf_op jit(solution)/shard_map/all_to_all | solution.py:239
  81.8 4.1 %copy.60 = bf16[64,16,1024]{2,0,1:T(8,128)(2,1)} copy(bf16[64,16,1024]{2,1,0:T(8,128)(2,1)} %all-to-all-done) | data formatting | bytes 4194304 | tf_op jit(solution)/shard_map/all_to_all | solution.py:239
  85.9 10.4 %shard_map.114 = bf16[1024,512]{1,0:T(8,128)(2,1)} custom-call(bf16[1024,1024]{1,0:T(8,128)(2,1)} %bitcast.36, s32[1024,1]{1,0:T(8,128)} %add.274.refs_1_, s32[1,1024]{1,0:T(1,128)} %compare_select_fusion.refs_2_), custom_call_target="tpu_custom_call" | custom-call | flops 1342177280 | bytes 3145728 | tf_op jit(solution)/shard_map/pallas_call | solution.py:183
  96.3 2.8 %copy.55 = bf16[16,64,512]{2,0,1:T(8,128)(2,1)} copy(bf16[16,64,512]{2,1,0:T(8,128)(2,1)} %bitcast.39) | data formatting | bytes 2097152 | tf_op jit(solution)/shard_map/reshape | solution.py:255
  99.1 7.2 %all-to-all-start.1 = ((bf16[16,64,512]{2,0,1:T(8,128)(2,1)}), bf16[16,64,512]{2,0,1:T(8,128)(2,1)}, u32[]{:S(2)}, u32[]{:S(2)}) async-start(bf16[16,64,512]{2,0,1:T(8,128)(2,1)} %copy.55), calls=%async_computation.1 | async-start | bytes 2097152 | tf_op jit(solution)/shard_map/all_to_all | solution.py:254
  108.1 1.3 slice.14
  109.4 0.8 fusion.2
  110.2 1.1 slice_bitcast_fusion.1
  111.2 23.1 %all-to-all-done.1 = bf16[16,64,512]{2,0,1:T(8,128)(2,1)} async-done(((bf16[16,64,512]{2,0,1:T(8,128)(2,1)}), bf16[16,64,512]{2,0,1:T(8,128)(2,1)}, u32[]{:S(2)}, u32[]{:S(2)}) %all-to-all-start.1) | async-done | bytes 1048608 | tf_op jit(solution)/shard_map/all_to_all | solution.py:254
  134.4 1.8 %copy.56 = bf16[16,64,512]{2,1,0:T(8,128)(2,1)S(1)} copy(bf16[16,64,512]{2,0,1:T(8,128)(2,1)} %all-to-all-done.1) | data formatting | bytes 2097152 | tf_op jit(solution)/shard_map/all_to_all | solution.py:254
  136.2 1.2 gather_fusion
  137.3 0.1 broadcast_select_fusion
  137.4 2.8 %collective-permute-start.2 = (bf16[256,512]{1,0:T(8,128)(2,1)S(1)}, bf16[256,512]{1,0:T(8,128)(2,1)S(1)}, u32[]{:S(2)}, u32[]{:S(2)}) collective-permute-start(bf16[256,512]{1,0:T(8,128)(2,1)S(1)} %broadcast_select_fusion), channel_id=1, source_target_pairs={{0,3},{1,0},{2,1},{3,2},{4,7},{5,4},{6,5},{7,6},{8,11},{9,8},{10,9... | collective-permute-start | bytes 786440 | tf_op jit(solution)/shard_map/ppermute | solution.py:272
  140.2 2.3 %maximum_bitcast_fusion = bf16[2,1,1024,256]{3,2,1,0:T(8,128)(2,1)} fusion(bf16[1,1024,256]{2,1,0:T(8,128)(2,1)} %get-tuple-element.13, bf16[1,1024,256]{2,1,0:T(8,128)(2,1)} %get-tuple-element.12), kind=kLoop, calls=%fused_computation.9 | loop fusion | flops 524288 | bytes 2097152
  142.5 1.6 %collective-permute-start.1 = (bf16[256,512]{1,0:T(8,128)(2,1)S(1)}, bf16[256,512]{1,0:T(8,128)(2,1)S(1)}, u32[]{:S(2)}, u32[]{:S(2)}) collective-permute-start(bf16[256,512]{1,0:T(8,128)(2,1)S(1)} %broadcast_select_fusion), channel_id=1, source_target_pairs={{0,2},{1,3},{2,0},{3,1},{4,6},{5,7},{6,4},{7,5},{8,10},{9,11},{10,... | collective-permute-start | bytes 786440 | tf_op jit(solution)/shard_map/ppermute | solution.py:272
  144.2 0.3 fusion.8
  144.5 0.3 collective-permute-done.2
  144.8 0.3 fusion.4
  145.1 6.1 %collective-permute-done = bf16[256,512]{1,0:T(8,128)(2,1)S(1)} collective-permute-done((bf16[256,512]{1,0:T(8,128)(2,1)S(1)}, bf16[256,512]{1,0:T(8,128)(2,1)S(1)}, u32[]{:S(2)}, u32[]{:S(2)}) %collective-permute-start) | collective-permute-done | bytes 262176 | tf_op jit(solution)/shard_map/ppermute | solution.py:272
  151.2 0.3 convolution_add_fusion.1
  151.5 3.3 %collective-permute-done.1 = bf16[256,512]{1,0:T(8,128)(2,1)S(1)} collective-permute-done((bf16[256,512]{1,0:T(8,128)(2,1)S(1)}, bf16[256,512]{1,0:T(8,128)(2,1)S(1)}, u32[]{:S(2)}, u32[]{:S(2)}) %collective-permute-start.1) | collective-permute-done | bytes 262176 | tf_op jit(solution)/shard_map/ppermute | solution.py:272
  154.8 0.3 fusion.1
  155.1 1.7 %add_convert_fusion = bf16[256,512]{1,0:T(8,128)(2,1)} fusion(bf16[256,512]{1,0:T(8,128)(2,1)S(1)} %fusion.1, bf16[256,2048]{1,0:T(8,128)(2,1)} %refs_0_.1, s32[]{:T(128)S(6)} %select_n.155), kind=kLoop, calls=%fused_computation.18 | loop fusion | flops 524288 | bytes 786436 | tf_op jit(solution)/shard_map/convert_element_type | solution.py:283
  (14 shorter events, 0.2 us)
Async XLA Ops:
  0.6 143.5 %copy-start = (bf16[2048,512]{1,0:T(8,128)(2,1)S(1)}, bf16[2048,512]{1,0:T(8,128)(2,1)}, u32[]{:S(2)}) copy-start(bf16[2048,512]{1,0:T(8,128)(2,1)} %param.19) | copy-start | bytes 6291460
  19.0 62.8 %all-to-all-start = ((bf16[64,16,1024]{2,1,0:T(8,128)(2,1)}), bf16[64,16,1024]{2,1,0:T(8,128)(2,1)}, u32[]{:S(2)}, u32[]{:S(2)}) async-start(bf16[64,16,1024]{2,1,0:T(8,128)(2,1)} %bitcast.35), calls=%async_computation | async-start | bytes 4194304 | tf_op jit(solution)/shard_map/all_to_all | solution.py:239
  99.1 35.2 %all-to-all-start.1 = ((bf16[16,64,512]{2,0,1:T(8,128)(2,1)}), bf16[16,64,512]{2,0,1:T(8,128)(2,1)}, u32[]{:S(2)}, u32[]{:S(2)}) async-start(bf16[16,64,512]{2,0,1:T(8,128)(2,1)} %copy.55), calls=%async_computation.1 | async-start | bytes 2097152 | tf_op jit(solution)/shard_map/all_to_all | solution.py:254
  137.4 7.3 %collective-permute-start.2 = (bf16[256,512]{1,0:T(8,128)(2,1)S(1)}, bf16[256,512]{1,0:T(8,128)(2,1)S(1)}, u32[]{:S(2)}, u32[]{:S(2)}) collective-permute-start(bf16[256,512]{1,0:T(8,128)(2,1)S(1)} %broadcast_select_fusion), channel_id=1, source_target_pairs={{0,3},{1,0},{2,1},{3,2},{4,7},{5,4},{6,5},{7,6},{8,11},{9,8},{10,9... | collective-permute-start | bytes 786440 | tf_op jit(solution)/shard_map/ppermute | solution.py:272
  142.5 8.7 %collective-permute-start = (bf16[256,512]{1,0:T(8,128)(2,1)S(1)}, bf16[256,512]{1,0:T(8,128)(2,1)S(1)}, u32[]{:S(2)}, u32[]{:S(2)}) collective-permute-start(bf16[256,512]{1,0:T(8,128)(2,1)S(1)} %broadcast_select_fusion), channel_id=1, source_target_pairs={{0,1},{1,2},{2,3},{3,0},{4,5},{5,6},{6,7},{7,4},{8,9},{9,10},{10,1... | collective-permute-start | bytes 786440 | tf_op jit(solution)/shard_map/ppermute | solution.py:272
  142.5 12.3 %collective-permute-start.1 = (bf16[256,512]{1,0:T(8,128)(2,1)S(1)}, bf16[256,512]{1,0:T(8,128)(2,1)S(1)}, u32[]{:S(2)}, u32[]{:S(2)}) collective-permute-start(bf16[256,512]{1,0:T(8,128)(2,1)S(1)} %broadcast_select_fusion), channel_id=1, source_target_pairs={{0,2},{1,3},{2,0},{3,1},{4,6},{5,7},{6,4},{7,5},{8,10},{9,11},{10,... | collective-permute-start | bytes 786440 | tf_op jit(solution)/shard_map/ppermute | solution.py:272

commit v5 on v4

--- a/solution.py
+++ b/solution.py
@@ -141,56 +141,62 @@
     )
 
 
-def attention_kernel(qkv_ref, qpos_ref, kpos_ref, out_ref, *, q_width, k_width, head_dim, blocks):
+def attention_kernel(
+    qkv_ref, qpos_ref, kpos_ref, out_ref, *, q_width, k_width, head_dim, blocks, kv_head
+):
     rows = qkv_ref.shape[0]
     block = rows // blocks
     kv_heads = k_width // head_dim
     group = q_width // head_dim // kv_heads
     scale = head_dim ** (-0.5)
+    k_col = q_width + kv_head * head_dim
+    v_col = q_width + k_width + kv_head * head_dim
     for i in range(blocks):
         key_rows = block * (i + 1)
         rows_here = pl.ds(i * block, block)
         allowed = kpos_ref[:, :key_rows] <= qpos_ref[rows_here, :]
-        for h in range(kv_heads):
-            k_col = q_width + h * head_dim
-            v_col = q_width + k_width + h * head_dim
-            keys = qkv_ref[:key_rows, k_col : k_col + head_dim]
-            values = qkv_ref[:key_rows, v_col : v_col + head_dim]
-            for g in range(group):
-                q_col = (h * group + g) * head_dim
-                queries = qkv_ref[rows_here, q_col : q_col + head_dim]
-                scores = lax.dot_general(
-                    queries,
-                    keys,
-                    (((1,), (1,)), ((), ())),
-                    preferred_element_type=jnp.float32,
-                ) * scale
-                scores = jnp.where(allowed, scores, -jnp.inf)
-                row_max = jnp.max(scores, axis=-1, keepdims=True)
-                weights = jnp.exp(scores - row_max)
-                weights = (weights / jnp.sum(weights, axis=-1, keepdims=True)).astype(jnp.bfloat16)
-                mixed = jnp.dot(weights, values, preferred_element_type=jnp.float32)
-                out_ref[rows_here, q_col : q_col + head_dim] = mixed.astype(out_ref.dtype)
-
-
-def attend(qkv_slot, query_pos, key_pos, q_width, k_width, head_dim):
+        keys = qkv_ref[:key_rows, k_col : k_col + head_dim]
+        values = qkv_ref[:key_rows, v_col : v_col + head_dim]
+        for g in range(group):
+            q_col = (kv_head * group + g) * head_dim
+            queries = qkv_ref[rows_here, q_col : q_col + head_dim]
+            scores = lax.dot_general(
+                queries,
+                keys,
+                (((1,), (1,)), ((), ())),
+                preferred_element_type=jnp.float32,
+            ) * scale
+            scores = jnp.where(allowed, scores, -jnp.inf)
+            row_max = jnp.max(scores, axis=-1, keepdims=True)
+            weights = jnp.exp(scores - row_max)
+            weights = (weights / jnp.sum(weights, axis=-1, keepdims=True)).astype(jnp.bfloat16)
+            mixed = jnp.dot(weights, values, preferred_element_type=jnp.float32)
+            out_ref[rows_here, g * head_dim : (g + 1) * head_dim] = mixed.astype(out_ref.dtype)
+
+
+def attend(qkv_slot, query_pos, key_pos, q_width, k_width, head_dim, kv_head):
     rows = qkv_slot.shape[0]
     blocks = 4
-    heads = q_width // head_dim
+    heads = q_width // k_width
     causal_pairs = blocks * (blocks + 1) // 2
     pair_flops = 4 * (rows // blocks) ** 2 * head_dim
     vmem = pl.BlockSpec(memory_space=pltpu.VMEM)
     return pl.pallas_call(
         lambda *refs: attention_kernel(
-            *refs, q_width=q_width, k_width=k_width, head_dim=head_dim, blocks=blocks
+            *refs,
+            q_width=q_width,
+            k_width=k_width,
+            head_dim=head_dim,
+            blocks=blocks,
+            kv_head=kv_head,
         ),
-        out_shape=jax.ShapeDtypeStruct((rows, q_width), jnp.bfloat16),
+        out_shape=jax.ShapeDtypeStruct((rows, heads * head_dim), jnp.bfloat16),
         in_specs=[vmem, vmem, vmem],
         out_specs=vmem,
         cost_estimate=pl.CostEstimate(
             flops=heads * causal_pairs * pair_flops,
             transcendentals=heads * causal_pairs * (rows // blocks) ** 2,
-            bytes_accessed=qkv_slot.size * 2 + rows * q_width * 2,
+            bytes_accessed=qkv_slot.size * 2 + rows * heads * head_dim * 2,
         ),
     )(qkv_slot, query_pos[:, None], key_pos[None, :])
 
@@ -248,36 +254,47 @@
         ranks[:, None] * devices + jnp.mod(source_ids[None, :] - my_start, devices)
     ).reshape(-1)
     key_pos = jnp.where(arrived_pos < my_length, arrived_pos, 1 << 30)
-    mixture = attend(
-        arrived.reshape(slot_len, arrived.shape[2]), arrived_pos, key_pos, q_width, k_width, head_dim
-    )
-    returned = lax.all_to_all(
-        mixture.reshape(capacity, devices, mixture.shape[1]),
-        "req",
-        split_axis=1,
-        concat_axis=1,
-        tiled=True,
-    )
-    attended = jnp.take(returned.reshape(capacity * devices, -1), back_rows, axis=0)
+    qkv_slot = arrived.reshape(slot_len, arrived.shape[2])
+    kv_heads = k_width // head_dim
+    tp_size = lax.axis_size("tp")
+    w_rows = w_out.shape[0] // tp_size
+    part_width = q_width // kv_heads
+    mixtures = [
+        attend(qkv_slot, arrived_pos, key_pos, q_width, k_width, head_dim, h)
+        for h in range(kv_heads)
+    ]
+    summed = None
+    attended = None
+    for h in range(kv_heads):
+        mixture = mixtures[h]
+        if attended is not None:
+            attended, mixture = lax.optimization_barrier((attended, mixture))
+        returned = lax.all_to_all(
+            mixture.reshape(capacity, devices, part_width),
+            "req",
+            split_axis=1,
+            concat_axis=1,
+            tiled=True,
+        )
+        attended = jnp.take(returned.reshape(capacity * devices, -1), back_rows, axis=0)
+        for shift in range(tp_size):
+            if shift == 0:
+                passed = attended
+            else:
+                passed = lax.ppermute(
+                    attended, "tp", perm=[(i, (i + shift) % tp_size) for i in range(tp_size)]
+                )
+            source = jnp.mod(slice_index - shift, tp_size)
+            product = jnp.dot(
+                passed,
+                lax.dynamic_slice_in_dim(
+                    w_out, source * w_rows + h * part_width, part_width, 0
+                ),
+                preferred_element_type=jnp.float32,
+            )
+            summed = product if summed is None else summed + product
     kv_rows = jnp.roll(arrived[:, :, q_width:], -roll_shift, axis=1).reshape(slot_len, -1)
     kv_cache = jnp.stack([kv_rows[:, :k_width], kv_rows[:, k_width:]])[:, None]
-    tp_size = lax.axis_size("tp")
-    w_rows = w_out.shape[0] // tp_size
-    summed = jnp.dot(
-        attended,
-        lax.dynamic_slice_in_dim(w_out, slice_index * w_rows, w_rows, 0),
-        preferred_element_type=jnp.float32,
-    )
-    for shift in range(1, tp_size):
-        passed = lax.ppermute(
-            attended, "tp", perm=[(i, (i + shift) % tp_size) for i in range(tp_size)]
-        )
-        source = jnp.mod(slice_index - shift, tp_size)
-        summed = summed + jnp.dot(
-            passed,
-            lax.dynamic_slice_in_dim(w_out, source * w_rows, w_rows, 0),
-            preferred_element_type=jnp.float32,
-        )
     branch = lax.optimization_barrier(summed.astype(jnp.bfloat16))
     residual = lax.dynamic_slice_in_dim(hidden, slice_index * out_width, out_width, 1)
     hidden_out = (residual.astype(jnp.float32) + branch.astype(jnp.float32)).astype(jnp.bfloat16)

time: 159 us -> 162 us (1.019)
  waiting for transfers between devices: 79.2 us -> 65.7 us
  starting transfers between devices: 24.8 us -> 35.1 us
  Pallas kernels: 16.8 us -> 20.1 us
  local copies, waits for them, and re-layouts: 16.8 us -> 19.4 us
  matrix products: 1.18 us -> 3.66 us
    all_to_all x1 -> x2, waiting for transfers between devices: 23.1 us -> 15.1 us  [on_device(): lax.all_to_all(mixture.reshape(capacity, devices, part_width), 'req', spl...]
    all_to_all x1 -> x2, starting transfers between devices: 7.17 us -> 13 us  [on_device(): lax.all_to_all(mixture.reshape(capacity, devices, part_width), 'req', spl...]
    ppermute x3 -> x6, waiting for transfers between devices: 9.73 us -> 4.31 us  [on_device(): lax.ppermute(attended, 'tp', perm=[(i, (i + shift) % tp_size) for i in ra...]
    ppermute x3 -> x6, starting transfers between devices: 4.47 us -> 8.85 us  [on_device(): lax.ppermute(attended, 'tp', perm=[(i, (i + shift) % tp_size) for i in ra...]
    pallas_call x1 -> x2, Pallas kernels: 10.4 us -> 13.7 us  [attend(): pl.pallas_call(lambda *refs: attention_kernel(*refs, q_width=q_width, k_w...]
    dot_general x4 -> x8, matrix products: 1.18 us -> 3.66 us  [on_device(): jnp.dot(passed, lax.dynamic_slice_in_dim(w_out, source * w_rows + h * par...]
    reshape x1 -> x2, local copies, waits for them, and re-layouts: 2.78 us -> 4.31 us  [on_device(): mixture.reshape(capacity, devices, part_width)]
  transfers between devices with their start and end apart: 5 -> 9, of which waited for: 5 -> 7; matrix products, arithmetic and copies ran while one was open for 6% -> 8% of each run, Pallas kernels for 0% -> 4%
where the time goes in v5:
time: 162 us; the launch traced here: 161 us
  waiting for transfers between devices  65.7 us (41%)
  starting transfers between devices  35.1 us (22%)
  Pallas kernels  20.1 us (12%)
  local copies, waits for them, and re-layouts  19.4 us (12%)
  other arithmetic  14.6 us (9%)
  matrix products  3.66 us (2%)
  between operations  2.88 us (2%)
    all_to_all x1, waiting for transfers between devices, on_device(): lax.all_to_all(picked.reshape(devices, capacity, picked.shape[1]), 'req',...  46.2 us
    all_to_all x2, waiting for transfers between devices, on_device(): lax.all_to_all(mixture.reshape(capacity, devices, part_width), 'req', spl...  15.1 us
    pallas_call x2, Pallas kernels, attend(): pl.pallas_call(lambda *refs: attention_kernel(*refs, q_width=q_width, k_w...  13.7 us
    all_to_all x1, starting transfers between devices, on_device(): lax.all_to_all(picked.reshape(devices, capacity, picked.shape[1]), 'req',...  13.2 us
    all_to_all x2, starting transfers between devices, on_device(): lax.all_to_all(mixture.reshape(capacity, devices, part_width), 'req', spl...  13 us
    ppermute x6, starting transfers between devices, on_device(): lax.ppermute(attended, 'tp', perm=[(i, (i + shift) % tp_size) for i in ra...  8.85 us
    pallas_call x1, Pallas kernels, prepare(): pl.pallas_call(lambda *refs: prep_kernel(*refs, head_dim=head_dim, row_bl...  6.36 us
    reshape x2, local copies, waits for them, and re-layouts, on_device(): mixture.reshape(capacity, devices, part_width)  4.31 us
  transfers between devices with their start and end apart: 9, of which 7 were waited for; matrix products, arithmetic and copies ran while one was open for 8% of the time, Pallas kernels for 4%

profile of v5, /device:TPU:1, one launch (start us, length us, event | category | flops | bytes accessed | tf_op | source)
XLA Modules:
  0.0 161.4 jit_solution(10796230869173859198)
XLA Ops:
  0.7 0.9 copy.53
  1.8 0.7 sub.76
  2.5 0.8 select_reduce_fusion.3
  3.3 0.6 dynamic_slice.39
  4.0 1.3 compare_select_fusion.2
  5.3 0.8 scatter_custom_fusion
  6.2 0.5 fusion.21
  6.8 0.8 pad_maximum_fusion.refs_7_
  7.6 0.3 sub.91
  8.0 0.3 lt.158
  8.3 1.3 broadcast_in_dim.69
  9.6 0.8 pad_maximum_fusion.1.refs_8_
  10.4 1.2 select_select_fusion.refs_9_
  11.6 0.6 bitcast_convert_fusion
  12.1 6.4 %shard_map.113 = bf16[1024,1024]{1,0:T(8,128)(2,1)} custom-call(bf16[256,2048]{1,0:T(8,128)(2,1)} %refs_0_.1, f32[1,2048]{1,0:T(1,128)} %bitcast.46, bf16[2048,512]{1,0:T(8,128)(2,1)} %refs_2_.1, bf16[2048,256]{1,0:T(8,128)(2,1)} %refs_3_.1, bf16[2048,256]{1,0:T(8,128)(2,1)} %refs_4_.1, f32[1,128]{1,0:T(1,128)} %get-tuple-element.25.refs_5_, ...), custom_call_target="tpu_custom_call" | custom-call | flops 1610612736 | bytes 7340032 | tf_op jit(solution)/shard_map/pallas_call | solution.py:119
  18.5 13.2 %all-to-all-start = ((bf16[64,16,1024]{2,1,0:T(8,128)(2,1)}), bf16[64,16,1024]{2,1,0:T(8,128)(2,1)}, u32[]{:S(2)}, u32[]{:S(2)}) async-start(bf16[64,16,1024]{2,1,0:T(8,128)(2,1)} %bitcast.40), calls=%async_computation | async-start | bytes 4194304 | tf_op jit(solution)/shard_map/all_to_all | solution.py:245
  31.7 0.7 dynamic_slice.40
  32.5 1.3 add.290.refs_1_
  33.8 1.3 compare_select_fusion.refs_2_
  35.0 46.2 %all-to-all-done = bf16[64,16,1024]{2,1,0:T(8,128)(2,1)} async-done(((bf16[64,16,1024]{2,1,0:T(8,128)(2,1)}), bf16[64,16,1024]{2,1,0:T(8,128)(2,1)}, u32[]{:S(2)}, u32[]{:S(2)}) %all-to-all-start) | async-done | bytes 2097184 | tf_op jit(solution)/shard_map/all_to_all | solution.py:245
  81.3 4.1 %copy.70 = bf16[64,16,1024]{2,0,1:T(8,128)(2,1)} copy(bf16[64,16,1024]{2,1,0:T(8,128)(2,1)} %all-to-all-done) | data formatting | bytes 4194304 | tf_op jit(solution)/shard_map/all_to_all | solution.py:245
  85.4 6.9 %shard_map.114 = bf16[1024,256]{1,0:T(8,128)(2,1)} custom-call(bf16[1024,1024]{1,0:T(8,128)(2,1)} %bitcast.37, s32[1024,1]{1,0:T(8,128)} %add.290.refs_1_, s32[1,1024]{1,0:T(1,128)} %compare_select_fusion.refs_2_), custom_call_target="tpu_custom_call" | custom-call | flops 671088640 | bytes 2621440 | tf_op jit(solution)/shard_map/pallas_call | solution.py:184
  92.2 2.1 %copy.62 = bf16[16,64,256]{2,0,1:T(8,128)(2,1)} copy(bf16[16,64,256]{2,1,0:T(8,128)(2,1)} %bitcast.45) | data formatting | bytes 1048576 | tf_op jit(solution)/shard_map/reshape | solution.py:273
  94.4 7.2 %all-to-all-start.1 = ((bf16[16,64,256]{2,0,1:T(8,128)(2,1)}), bf16[16,64,256]{2,0,1:T(8,128)(2,1)}, u32[]{:S(2)}, u32[]{:S(2)}) async-start(bf16[16,64,256]{2,0,1:T(8,128)(2,1)} %copy.62), calls=%async_computation.1 | async-start | bytes 1048576 | tf_op jit(solution)/shard_map/all_to_all | solution.py:272
  103.5 1.3 slice.16
  104.9 6.8 %shard_map.115 = bf16[1024,256]{1,0:T(8,128)(2,1)} custom-call(bf16[1024,1024]{1,0:T(8,128)(2,1)} %bitcast.39, s32[1024,1]{1,0:T(8,128)} %add.290.refs_1_, s32[1,1024]{1,0:T(1,128)} %compare_select_fusion.refs_2_), custom_call_target="tpu_custom_call" | custom-call | flops 671088640 | bytes 2621440 | tf_op jit(solution)/shard_map/pallas_call | solution.py:184
  111.7 1.8 %fusion.5 = bf16[16,64,512]{2,1,0:T(8,128)(2,1)} fusion(s32[]{:T(128)S(6)} %select_n.181, bf16[16,64,512]{2,1,0:T(8,128)(2,1)S(1)} %slice.16), kind=kLoop, calls=%fused_computation.13 | loop fusion | flops 2097152 | bytes 2097156 | tf_op jit(solution)/shard_map/jit(_roll_dynamic)/concatenate | solution.py:296
  113.5 5.7 %all-to-all-done.1 = bf16[16,64,256]{2,0,1:T(8,128)(2,1)} async-done(((bf16[16,64,256]{2,0,1:T(8,128)(2,1)}), bf16[16,64,256]{2,0,1:T(8,128)(2,1)}, u32[]{:S(2)}, u32[]{:S(2)}) %all-to-all-start.1) | async-done | bytes 524320 | tf_op jit(solution)/shard_map/all_to_all | solution.py:272
  119.1 1.2 copy.63
  120.3 1.2 gather_fusion
  121.6 2.2 %copy.65 = bf16[16,64,256]{2,0,1:T(8,128)(2,1)} copy(bf16[16,64,256]{2,1,0:T(8,128)(2,1)} %bitcast.44) | data formatting | bytes 1048576 | tf_op jit(solution)/shard_map/reshape | solution.py:273
  123.8 5.9 %all-to-all-start.2 = ((bf16[16,64,256]{2,0,1:T(8,128)(2,1)}), bf16[16,64,256]{2,0,1:T(8,128)(2,1)}, u32[]{:S(2)}, u32[]{:S(2)}) async-start(bf16[16,64,256]{2,0,1:T(8,128)(2,1)} %copy.65), calls=%async_computation.2 | async-start | bytes 1048576 | tf_op jit(solution)/shard_map/all_to_all | solution.py:272
  129.8 1.1 maximum_bitcast_fusion
  130.8 1.3 collective-permute-start
  132.1 1.4 collective-permute-start.2
  133.6 1.6 %collective-permute-start.1 = (bf16[256,256]{1,0:T(8,128)(2,1)S(1)}, bf16[256,256]{1,0:T(8,128)(2,1)S(1)}, u32[]{:S(2)}, u32[]{:S(2)}) collective-permute-start(bf16[256,256]{1,0:T(8,128)(2,1)S(1)} %broadcast_select_fusion.1), channel_id=1, source_target_pairs={{0,2},{1,3},{2,0},{3,1},{4,6},{5,7},{6,4},{7,5},{8,10},{9,11},{10,... | collective-permute-start | bytes 393224 | tf_op jit(solution)/shard_map/ppermute | solution.py:284
  135.4 1.0 collective-permute-done.2
  136.8 1.0 convolution_add_fusion.2
  137.9 9.4 %all-to-all-done.2 = bf16[16,64,256]{2,0,1:T(8,128)(2,1)} async-done(((bf16[16,64,256]{2,0,1:T(8,128)(2,1)}), bf16[16,64,256]{2,0,1:T(8,128)(2,1)}, u32[]{:S(2)}, u32[]{:S(2)}) %all-to-all-start.2) | async-done | bytes 524320 | tf_op jit(solution)/shard_map/all_to_all | solution.py:272
  147.3 1.2 copy.66
  148.5 1.2 gather_fusion.1
  149.8 3.0 %collective-permute-start.4 = (bf16[256,256]{1,0:T(8,128)(2,1)S(1)}, bf16[256,256]{1,0:T(8,128)(2,1)S(1)}, u32[]{:S(2)}, u32[]{:S(2)}) collective-permute-start(bf16[256,256]{1,0:T(8,128)(2,1)S(1)} %broadcast_select_fusion), channel_id=1, source_target_pairs={{0,2},{1,3},{2,0},{3,1},{4,6},{5,7},{6,4},{7,5},{8,10},{9,11},{10,... | collective-permute-start | bytes 393224 | tf_op jit(solution)/shard_map/ppermute | solution.py:284
  152.8 0.8 collective-permute-start.5
  153.5 0.7 collective-permute-start.3
  154.5 1.3 fusion.3
  155.8 0.2 collective-permute-done.4
  156.2 2.9 %collective-permute-done.5 = bf16[256,256]{1,0:T(8,128)(2,1)S(1)} collective-permute-done((bf16[256,256]{1,0:T(8,128)(2,1)S(1)}, bf16[256,256]{1,0:T(8,128)(2,1)S(1)}, u32[]{:S(2)}, u32[]{:S(2)}) %collective-permute-start.5) | collective-permute-done | bytes 131104 | tf_op jit(solution)/shard_map/ppermute | solution.py:284
  159.6 1.7 %add_convert_fusion = bf16[256,512]{1,0:T(8,128)(2,1)} fusion(bf16[256,512]{1,0:T(8,128)(2,1)S(1)} %fusion.4, bf16[256,2048]{1,0:T(8,128)(2,1)} %refs_0_.1, s32[]{:T(128)S(6)} %select_n.157), kind=kLoop, calls=%fused_computation.23 | loop fusion | flops 524288 | bytes 786436 | tf_op jit(solution)/shard_map/convert_element_type | solution.py:300
  (36 shorter events, 2.5 us)
Async XLA Ops:
  0.6 134.6 %copy-start = (bf16[2048,512]{1,0:T(8,128)(2,1)S(1)}, bf16[2048,512]{1,0:T(8,128)(2,1)}, u32[]{:S(2)}) copy-start(bf16[2048,512]{1,0:T(8,128)(2,1)} %param.21) | copy-start | bytes 6291460
  0.6 10.9 %copy-start.3 = (bf16[128]{0:T(256)(128)(2,1)S(1)}, bf16[128]{0:T(256)(128)(2,1)}, u32[]{:S(2)}) copy-start(bf16[128]{0:T(256)(128)(2,1)} %param.19) | copy-start | bytes 772
  0.7 10.9 %copy-start.2 = (bf16[128]{0:T(256)(128)(2,1)S(1)}, bf16[128]{0:T(256)(128)(2,1)}, u32[]{:S(2)}) copy-start(bf16[128]{0:T(256)(128)(2,1)} %param.20) | copy-start | bytes 772
  18.5 62.8 %all-to-all-start = ((bf16[64,16,1024]{2,1,0:T(8,128)(2,1)}), bf16[64,16,1024]{2,1,0:T(8,128)(2,1)}, u32[]{:S(2)}, u32[]{:S(2)}) async-start(bf16[64,16,1024]{2,1,0:T(8,128)(2,1)} %bitcast.40), calls=%async_computation | async-start | bytes 4194304 | tf_op jit(solution)/shard_map/all_to_all | solution.py:245
  94.4 24.8 %all-to-all-start.1 = ((bf16[16,64,256]{2,0,1:T(8,128)(2,1)}), bf16[16,64,256]{2,0,1:T(8,128)(2,1)}, u32[]{:S(2)}, u32[]{:S(2)}) async-start(bf16[16,64,256]{2,0,1:T(8,128)(2,1)} %copy.62), calls=%async_computation.1 | async-start | bytes 1048576 | tf_op jit(solution)/shard_map/all_to_all | solution.py:272
  121.5 8.2 %copy-start.1 = (bf16[16,64,512]{2,1,0:T(8,128)(2,1)S(1)}, bf16[16,64,512]{2,1,0:T(8,128)(2,1)}, u32[]{:S(2)}) copy-start(bf16[16,64,512]{2,1,0:T(8,128)(2,1)} %fusion.5) | copy-start | bytes 3145732
  123.8 23.5 %all-to-all-start.2 = ((bf16[16,64,256]{2,0,1:T(8,128)(2,1)}), bf16[16,64,256]{2,0,1:T(8,128)(2,1)}, u32[]{:S(2)}, u32[]{:S(2)}) async-start(bf16[16,64,256]{2,0,1:T(8,128)(2,1)} %copy.65), calls=%async_computation.2 | async-start | bytes 1048576 | tf_op jit(solution)/shard_map/all_to_all | solution.py:272
  130.8 6.0 %collective-permute-start = (bf16[256,256]{1,0:T(8,128)(2,1)S(1)}, bf16[256,256]{1,0:T(8,128)(2,1)S(1)}, u32[]{:S(2)}, u32[]{:S(2)}) collective-permute-start(bf16[256,256]{1,0:T(8,128)(2,1)S(1)} %broadcast_select_fusion.1), channel_id=1, source_target_pairs={{0,1},{1,2},{2,3},{3,0},{4,5},{5,6},{6,7},{7,4},{8,9},{9,10},{10,1... | collective-permute-start | bytes 393224 | tf_op jit(solution)/shard_map/ppermute | solution.py:284
  132.1 4.3 %collective-permute-start.2 = (bf16[256,256]{1,0:T(8,128)(2,1)S(1)}, bf16[256,256]{1,0:T(8,128)(2,1)S(1)}, u32[]{:S(2)}, u32[]{:S(2)}) collective-permute-start(bf16[256,256]{1,0:T(8,128)(2,1)S(1)} %broadcast_select_fusion.1), channel_id=1, source_target_pairs={{0,3},{1,0},{2,1},{3,2},{4,7},{5,4},{6,5},{7,6},{8,11},{9,8},{10,9... | collective-permute-start | bytes 393224 | tf_op jit(solution)/shard_map/ppermute | solution.py:284
  133.6 20.9 %collective-permute-start.1 = (bf16[256,256]{1,0:T(8,128)(2,1)S(1)}, bf16[256,256]{1,0:T(8,128)(2,1)S(1)}, u32[]{:S(2)}, u32[]{:S(2)}) collective-permute-start(bf16[256,256]{1,0:T(8,128)(2,1)S(1)} %broadcast_select_fusion.1), channel_id=1, source_target_pairs={{0,2},{1,3},{2,0},{3,1},{4,6},{5,7},{6,4},{7,5},{8,10},{9,11},{10,... | collective-permute-start | bytes 393224 | tf_op jit(solution)/shard_map/ppermute | solution.py:284
  149.8 6.3 %collective-permute-start.4 = (bf16[256,256]{1,0:T(8,128)(2,1)S(1)}, bf16[256,256]{1,0:T(8,128)(2,1)S(1)}, u32[]{:S(2)}, u32[]{:S(2)}) collective-permute-start(bf16[256,256]{1,0:T(8,128)(2,1)S(1)} %broadcast_select_fusion), channel_id=1, source_target_pairs={{0,2},{1,3},{2,0},{3,1},{4,6},{5,7},{6,4},{7,5},{8,10},{9,11},{10,... | collective-permute-start | bytes 393224 | tf_op jit(solution)/shard_map/ppermute | solution.py:284
  152.8 6.4 %collective-permute-start.5 = (bf16[256,256]{1,0:T(8,128)(2,1)S(1)}, bf16[256,256]{1,0:T(8,128)(2,1)S(1)}, u32[]{:S(2)}, u32[]{:S(2)}) collective-permute-start(bf16[256,256]{1,0:T(8,128)(2,1)S(1)} %broadcast_select_fusion), channel_id=1, source_target_pairs={{0,3},{1,0},{2,1},{3,2},{4,7},{5,4},{6,5},{7,6},{8,11},{9,8},{10,9... | collective-permute-start | bytes 393224 | tf_op jit(solution)/shard_map/ppermute | solution.py:284
  153.5 5.9 %collective-permute-start.3 = (bf16[256,256]{1,0:T(8,128)(2,1)S(1)}, bf16[256,256]{1,0:T(8,128)(2,1)S(1)}, u32[]{:S(2)}, u32[]{:S(2)}) collective-permute-start(bf16[256,256]{1,0:T(8,128)(2,1)S(1)} %broadcast_select_fusion), channel_id=1, source_target_pairs={{0,1},{1,2},{2,3},{3,0},{4,5},{5,6},{6,7},{7,4},{8,9},{9,10},{10,1... | collective-permute-start | bytes 393224 | tf_op jit(solution)/shard_map/ppermute | solution.py:284

commit v6 on v4

--- a/solution.py
+++ b/solution.py
@@ -52,6 +52,9 @@
 
 
 def prep_kernel(
+    lengths_ref,
+    dealing_ref,
+    home_ref,
     hidden_ref,
     norm_gain_ref,
     wq_ref,
@@ -61,22 +64,50 @@
     kgain_ref,
     cos_ref,
     sin_ref,
-    chosen_ref,
     out_ref,
     qkv_ref,
+    pick_ref,
+    starts_ref,
     *,
     head_dim,
-    row_blocks,
+    capacity,
 ):
+    devices = dealing_ref.shape[0]
+    prompt_total = lengths_ref.shape[0]
+    tok_rows = qkv_ref.shape[0]
+
+    def running(p, total):
+        starts_ref[p] = total
+        return total + lengths_ref[p]
+
+    lax.fori_loop(0, prompt_total, running, jnp.int32(0))
+    home = home_ref[0]
+    rank_ids = lax.broadcasted_iota(jnp.int32, (capacity, tok_rows), 0)
+    row_gap = lax.broadcasted_iota(jnp.int32, (capacity, tok_rows), 1) - rank_ids
+
+    def pick_rows(d, carry):
+        prompt = dealing_ref[d]
+        start = starts_ref[prompt]
+        length = lengths_ref[prompt]
+        first = lax.rem(lax.rem(home - start, devices) + devices, devices)
+        first_row = lax.div(start + first - home, devices)
+        count = jnp.minimum(lax.div(length - first + devices - 1, devices), capacity)
+        hits = (row_gap == first_row) & (rank_ids < count)
+        pick_ref[pl.ds(pl.multiple_of(d * capacity, capacity), capacity), :] = hits.astype(
+            pick_ref.dtype
+        )
+        return carry
+
+    lax.fori_loop(0, devices, pick_rows, 0)
     values = hidden_ref[...].astype(jnp.float32)
     inv_rms = lax.rsqrt(jnp.mean(values * values, axis=-1, keepdims=True) + EPS)
-    normed = (values * inv_rms * norm_gain_ref[...]).astype(jnp.bfloat16)
+    normed = (values * inv_rms * norm_gain_ref[...].astype(jnp.float32)).astype(jnp.bfloat16)
     cosine = cos_ref[...]
     sine = sin_ref[...]
     column = 0
     for w_ref, gain_ref in ((wq_ref, qgain_ref), (wk_ref, kgain_ref)):
         rows = jnp.dot(normed, w_ref[...], preferred_element_type=jnp.float32)
-        gain = gain_ref[...]
+        gain = gain_ref[...].astype(jnp.float32)
         for h in range(rows.shape[1] // head_dim):
             head = rows[:, h * head_dim : (h + 1) * head_dim]
             head_inv = lax.rsqrt(jnp.mean(head * head, axis=-1, keepdims=True) + EPS)
@@ -90,54 +121,62 @@
     qkv_ref[:, column : column + v_width] = jnp.dot(
         normed, wv_ref[...], preferred_element_type=jnp.float32
     ).astype(jnp.bfloat16)
-    tok_rows = qkv_ref.shape[0]
+    qkv = qkv_ref[...]
     out_rows = out_ref.shape[0]
-    block = out_rows // row_blocks
-    qkv = qkv_ref[...]
-    token_ids = lax.broadcasted_iota(jnp.int32, (block, tok_rows), 1)
-    for b in range(row_blocks):
+    block = out_rows // 4
+    for b in range(4):
         rows_here = pl.ds(b * block, block)
-        one_hot = (chosen_ref[rows_here, :] == token_ids).astype(jnp.bfloat16)
         out_ref[rows_here, :] = jnp.dot(
-            one_hot, qkv, preferred_element_type=jnp.float32
+            pick_ref[rows_here, :], qkv, preferred_element_type=jnp.float32
         ).astype(out_ref.dtype)
 
 
-def prepare(hidden, norm_gain, w_query, w_key, w_value, query_gain, key_gain, positions, chosen):
+def prepare(
+    hidden, lengths, dealing, home, norm_gain, w_query, w_key, w_value, query_gain, key_gain,
+    positions, capacity,
+):
     tok_rows, features = hidden.shape
     head_dim = query_gain.shape[0]
     half_width = head_dim // 2
     width = w_query.shape[1] + w_key.shape[1] + w_value.shape[1]
+    devices = dealing.shape[0]
+    out_rows = devices * capacity
     frequency = THETA ** (-(jnp.arange(half_width).astype(jnp.float32) * 2.0) / head_dim)
+    frequency = jnp.concatenate([frequency, frequency])
     angles = positions.astype(jnp.float32)[:, None] * frequency[None, :]
-    cosine = jnp.cos(angles)
-    sine = jnp.sin(angles)
-    cos_full = jnp.concatenate([cosine, cosine], axis=1)
-    sin_signed = jnp.concatenate([-sine, sine], axis=1)
-    out_rows = chosen.shape[0]
+    sign = jnp.where(jnp.arange(head_dim) < half_width, -1.0, 1.0).astype(jnp.float32)
+    cos_full = jnp.cos(angles)
+    sin_signed = jnp.sin(angles) * sign[None, :]
     vmem = pl.BlockSpec(memory_space=pltpu.VMEM)
+    smem = pl.BlockSpec(memory_space=pltpu.SMEM)
     return pl.pallas_call(
-        lambda *refs: prep_kernel(*refs, head_dim=head_dim, row_blocks=4),
+        lambda *refs: prep_kernel(*refs, head_dim=head_dim, capacity=capacity),
         out_shape=jax.ShapeDtypeStruct((out_rows, width), jnp.bfloat16),
-        in_specs=[vmem] * 10,
+        in_specs=[smem] * 3 + [vmem] * 9,
         out_specs=vmem,
-        scratch_shapes=[pltpu.VMEM((tok_rows, width), jnp.bfloat16)],
+        scratch_shapes=[
+            pltpu.VMEM((tok_rows, width), jnp.bfloat16),
+            pltpu.VMEM((out_rows, tok_rows), jnp.bfloat16),
+            pltpu.SMEM((lengths.shape[0],), jnp.int32),
+        ],
         cost_estimate=pl.CostEstimate(
             flops=2 * tok_rows * features * width + 2 * out_rows * tok_rows * width,
             transcendentals=tok_rows * 8,
             bytes_accessed=hidden.size * 2 + features * width * 2 + out_rows * width * 2,
         ),
     )(
+        lengths,
+        dealing,
+        home,
         hidden,
-        norm_gain.astype(jnp.float32)[None, :],
+        norm_gain[None, :],
         w_query,
         w_key,
         w_value,
-        query_gain.astype(jnp.float32)[None, :],
-        key_gain.astype(jnp.float32)[None, :],
+        query_gain[None, :],
+        key_gain[None, :],
         cos_full,
         sin_signed,
-        chosen[:, None],
     )
 
 
@@ -220,21 +259,25 @@
     deal_hot = (dealing[:, None] == prompt_ids[None, :]).astype(jnp.int32)
     dealt_starts = jnp.sum(deal_hot * starts[None, :], axis=1)
     dealt_lengths = jnp.sum(deal_hot * lengths[None, :], axis=1)
-    first_offset = jnp.mod(home_index - dealt_starts, devices)
     ranks = jnp.arange(capacity, dtype=jnp.int32)
-    slot_offset = first_offset[None, :] + ranks[:, None] * devices
-    send_valid = slot_offset < dealt_lengths[None, :]
-    send_rows = jnp.where(
-        send_valid, (dealt_starts[None, :] + slot_offset - home_index) // devices, 0
-    ).reshape(-1)
     my_start = lax.dynamic_index_in_dim(dealt_starts, home_index, 0, keepdims=False)
     my_length = lax.dynamic_index_in_dim(dealt_lengths, home_index, 0, keepdims=False)
     roll_shift = jnp.mod(my_start, devices)
     my_slots = jnp.sum(seg_onehot * inverse[None, :], axis=1)
     back_rows = positions // devices * devices + my_slots
-    chosen = jnp.where(send_valid, send_rows.reshape(capacity, devices), -1).T.reshape(-1)
     picked = prepare(
-        hidden, norm_gain, w_query, w_key, w_value, query_gain, key_gain, positions, chosen
+        hidden,
+        lengths,
+        dealing,
+        jnp.reshape(home_index, (1,)).astype(jnp.int32),
+        norm_gain,
+        w_query,
+        w_key,
+        w_value,
+        query_gain,
+        key_gain,
+        positions,
+        capacity,
     )
     arrived = lax.all_to_all(
         picked.reshape(devices, capacity, picked.shape[1]),

time: 159 us -> 157 us (0.987)
  other arithmetic: 15.5 us -> 10.8 us
  Pallas kernels: 16.8 us -> 18.5 us
    broadcast_in_dim x2 -> x0, other arithmetic: 2.68 us -> none  [the longest x1 1.43 us: prepare(): norm_gain.astype(jnp.float32)[None, :]]
    pallas_call x1, Pallas kernels: 6.37 us -> 8.04 us  [prepare(): pl.pallas_call(lambda *refs: prep_kernel(*refs, head_dim=head_dim, capaci...]
where the time goes in v6:
time: 157 us; the launch traced here: 155 us
  waiting for transfers between devices  78.9 us (50%)
  starting transfers between devices  24.8 us (16%)
  Pallas kernels  18.5 us (12%)
  local copies, waits for them, and re-layouts  17.7 us (11%)
  other arithmetic  10.8 us (7%)
  between operations  2.77 us (2%)
    all_to_all x1, waiting for transfers between devices, on_device(): lax.all_to_all(picked.reshape(devices, capacity, picked.shape[1]), 'req',...  46.4 us
    all_to_all x1, waiting for transfers between devices, on_device(): lax.all_to_all(mixture.reshape(capacity, devices, mixture.shape[1]), 'req...  22.9 us
    all_to_all x1, starting transfers between devices, on_device(): lax.all_to_all(picked.reshape(devices, capacity, picked.shape[1]), 'req',...  13.2 us
    pallas_call x1, Pallas kernels, attend(): pl.pallas_call(lambda *refs: attention_kernel(*refs, q_width=q_width, k_w...  10.4 us
    ppermute x3, waiting for transfers between devices, on_device(): lax.ppermute(attended, 'tp', perm=[(i, (i + shift) % tp_size) for i in ra...  9.73 us
    pallas_call x1, Pallas kernels, prepare(): pl.pallas_call(lambda *refs: prep_kernel(*refs, head_dim=head_dim, capaci...  8.04 us
    all_to_all x1, starting transfers between devices, on_device(): lax.all_to_all(mixture.reshape(capacity, devices, mixture.shape[1]), 'req...  7.17 us
    ppermute x3, starting transfers between devices, on_device(): lax.ppermute(attended, 'tp', perm=[(i, (i + shift) % tp_size) for i in ra...  4.46 us
  transfers between devices with their start and end apart: 5, of which 5 were waited for; matrix products, arithmetic and copies ran while one was open for 6% of the time, Pallas kernels for 0%

profile of v6, /device:TPU:1, one launch (start us, length us, event | category | flops | bytes accessed | tf_op | source)
XLA Modules:
  0.0 154.7 jit_solution(6194585286217306831)
XLA Ops:
  0.6 0.0 copy-start
  0.7 1.4 broadcast_in_dim.55.refs_4_
  2.1 0.1 compare_select_fusion.9
  2.2 0.7 copy.28
  2.9 0.1 reduce-window.8
  3.0 0.1 reduce
  3.1 0.7 sub.52
  3.8 0.8 select_reduce_fusion.2
  4.6 0.7 dynamic_slice.27
  5.3 1.3 compare_select_fusion.3
  6.6 0.1 convert_reduce_fusion
  6.7 0.8 scatter_custom_fusion
  7.5 0.1 select_reduce_fusion
  7.6 1.2 fusion.9
  8.8 8.0 %shard_map.113 = bf16[1024,1024]{1,0:T(8,128)(2,1)} custom-call(s32[64]{0:T(128)} %refs_0_.1, s32[64]{0:T(128)} %refs_1_.1, s32[1]{0:T(128)} %bitcast.1.refs_2_, bf16[256,2048]{1,0:T(8,128)(2,1)} %refs_3_.1, bf16[1,2048]{1,0:T(2,128)(2,1)} %broadcast_in_dim.55.refs_4_, bf16[2048,512]{1,0:T(8,128)(2,1)} %refs_5_.1, bf16[2048,256]{1,0:T(8,128)(2,1)} %refs_6_.1, ...), custom_call_target="tpu_custom_call" | custom-call | flops 1610612736 | bytes 7340032 | tf_op jit(solution)/shard_map/pallas_call | solution.py:152
  16.9 13.2 %all-to-all-start = ((bf16[64,16,1024]{2,1,0:T(8,128)(2,1)}), bf16[64,16,1024]{2,1,0:T(8,128)(2,1)}, u32[]{:S(2)}, u32[]{:S(2)}) async-start(bf16[64,16,1024]{2,1,0:T(8,128)(2,1)} %bitcast.31), calls=%async_computation | async-start | bytes 4194304 | tf_op jit(solution)/shard_map/all_to_all | solution.py:282
  30.1 0.1 broadcast_add_fusion
  30.1 1.3 add.210.refs_1_
  31.4 0.1 add.191
  31.5 0.6 dynamic_slice.28
  32.1 1.2 compare_select_fusion.refs_2_
  33.3 46.4 %all-to-all-done = bf16[64,16,1024]{2,1,0:T(8,128)(2,1)} async-done(((bf16[64,16,1024]{2,1,0:T(8,128)(2,1)}), bf16[64,16,1024]{2,1,0:T(8,128)(2,1)}, u32[]{:S(2)}, u32[]{:S(2)}) %all-to-all-start) | async-done | bytes 2097184 | tf_op jit(solution)/shard_map/all_to_all | solution.py:282
  79.7 4.1 %copy.36 = bf16[64,16,1024]{2,0,1:T(8,128)(2,1)} copy(bf16[64,16,1024]{2,1,0:T(8,128)(2,1)} %all-to-all-done) | data formatting | bytes 4194304 | tf_op jit(solution)/shard_map/all_to_all | solution.py:282
  83.8 10.4 %shard_map.114 = bf16[1024,512]{1,0:T(8,128)(2,1)} custom-call(bf16[1024,1024]{1,0:T(8,128)(2,1)} %bitcast.32, s32[1024,1]{1,0:T(8,128)} %add.210.refs_1_, s32[1,1024]{1,0:T(1,128)} %compare_select_fusion.refs_2_), custom_call_target="tpu_custom_call" | custom-call | flops 1342177280 | bytes 3145728 | tf_op jit(solution)/shard_map/pallas_call | solution.py:222
  94.2 2.8 %copy.31 = bf16[16,64,512]{2,0,1:T(8,128)(2,1)} copy(bf16[16,64,512]{2,1,0:T(8,128)(2,1)} %bitcast.35) | data formatting | bytes 2097152 | tf_op jit(solution)/shard_map/reshape | solution.py:298
  97.0 7.2 %all-to-all-start.1 = ((bf16[16,64,512]{2,0,1:T(8,128)(2,1)}), bf16[16,64,512]{2,0,1:T(8,128)(2,1)}, u32[]{:S(2)}, u32[]{:S(2)}) async-start(bf16[16,64,512]{2,0,1:T(8,128)(2,1)} %copy.31), calls=%async_computation.1 | async-start | bytes 2097152 | tf_op jit(solution)/shard_map/all_to_all | solution.py:297
  106.2 1.3 slice.14
  107.5 0.8 fusion.2
  108.3 1.1 slice_bitcast_fusion.1
  109.4 22.9 %all-to-all-done.1 = bf16[16,64,512]{2,0,1:T(8,128)(2,1)} async-done(((bf16[16,64,512]{2,0,1:T(8,128)(2,1)}), bf16[16,64,512]{2,0,1:T(8,128)(2,1)}, u32[]{:S(2)}, u32[]{:S(2)}) %all-to-all-start.1) | async-done | bytes 1048608 | tf_op jit(solution)/shard_map/all_to_all | solution.py:297
  132.2 1.8 %copy.32 = bf16[16,64,512]{2,1,0:T(8,128)(2,1)S(1)} copy(bf16[16,64,512]{2,0,1:T(8,128)(2,1)} %all-to-all-done.1) | data formatting | bytes 2097152 | tf_op jit(solution)/shard_map/all_to_all | solution.py:297
  134.0 1.2 gather_fusion
  135.2 0.1 broadcast_select_fusion
  135.3 2.8 %collective-permute-start.2 = (bf16[256,512]{1,0:T(8,128)(2,1)S(1)}, bf16[256,512]{1,0:T(8,128)(2,1)S(1)}, u32[]{:S(2)}, u32[]{:S(2)}) collective-permute-start(bf16[256,512]{1,0:T(8,128)(2,1)S(1)} %broadcast_select_fusion), channel_id=1, source_target_pairs={{0,3},{1,0},{2,1},{3,2},{4,7},{5,4},{6,5},{7,6},{8,11},{9,8},{10,9... | collective-permute-start | bytes 786440 | tf_op jit(solution)/shard_map/ppermute | solution.py:315
  138.1 2.3 %maximum_bitcast_fusion = bf16[2,1,1024,256]{3,2,1,0:T(8,128)(2,1)} fusion(bf16[1,1024,256]{2,1,0:T(8,128)(2,1)} %get-tuple-element.13, bf16[1,1024,256]{2,1,0:T(8,128)(2,1)} %get-tuple-element.12), kind=kLoop, calls=%fused_computation.9 | loop fusion | flops 524288 | bytes 2097152
  140.4 0.0 collective-permute-start
  140.4 1.6 %collective-permute-start.1 = (bf16[256,512]{1,0:T(8,128)(2,1)S(1)}, bf16[256,512]{1,0:T(8,128)(2,1)S(1)}, u32[]{:S(2)}, u32[]{:S(2)}) collective-permute-start(bf16[256,512]{1,0:T(8,128)(2,1)S(1)} %broadcast_select_fusion), channel_id=1, source_target_pairs={{0,2},{1,3},{2,0},{3,1},{4,6},{5,7},{6,4},{7,5},{8,10},{9,11},{10,... | collective-permute-start | bytes 786440 | tf_op jit(solution)/shard_map/ppermute | solution.py:315
  142.0 0.0 copy-done
  142.0 0.3 fusion.7
  142.3 0.3 collective-permute-done.2
  142.6 0.3 fusion.3
  142.9 6.1 %collective-permute-done = bf16[256,512]{1,0:T(8,128)(2,1)S(1)} collective-permute-done((bf16[256,512]{1,0:T(8,128)(2,1)S(1)}, bf16[256,512]{1,0:T(8,128)(2,1)S(1)}, u32[]{:S(2)}, u32[]{:S(2)}) %collective-permute-start) | collective-permute-done | bytes 262176 | tf_op jit(solution)/shard_map/ppermute | solution.py:315
  149.0 0.3 convolution_add_fusion.1
  149.3 3.3 %collective-permute-done.1 = bf16[256,512]{1,0:T(8,128)(2,1)S(1)} collective-permute-done((bf16[256,512]{1,0:T(8,128)(2,1)S(1)}, bf16[256,512]{1,0:T(8,128)(2,1)S(1)}, u32[]{:S(2)}, u32[]{:S(2)}) %collective-permute-start.1) | collective-permute-done | bytes 262176 | tf_op jit(solution)/shard_map/ppermute | solution.py:315
  152.7 0.3 fusion.1
  153.0 1.7 %add_convert_fusion = bf16[256,512]{1,0:T(8,128)(2,1)} fusion(bf16[256,512]{1,0:T(8,128)(2,1)S(1)} %fusion.1, bf16[256,2048]{1,0:T(8,128)(2,1)} %refs_3_.1, s32[]{:T(128)S(6)} %select_n.117), kind=kLoop, calls=%fused_computation.12 | loop fusion | flops 524288 | bytes 786436 | tf_op jit(solution)/shard_map/convert_element_type | solution.py:326
  (8 shorter events, 0.1 us)
Async XLA Ops:
  0.6 141.4 %copy-start = (bf16[2048,512]{1,0:T(8,128)(2,1)S(1)}, bf16[2048,512]{1,0:T(8,128)(2,1)}, u32[]{:S(2)}) copy-start(bf16[2048,512]{1,0:T(8,128)(2,1)} %param.19) | copy-start | bytes 6291460
  16.9 62.8 %all-to-all-start = ((bf16[64,16,1024]{2,1,0:T(8,128)(2,1)}), bf16[64,16,1024]{2,1,0:T(8,128)(2,1)}, u32[]{:S(2)}, u32[]{:S(2)}) async-start(bf16[64,16,1024]{2,1,0:T(8,128)(2,1)} %bitcast.31), calls=%async_computation | async-start | bytes 4194304 | tf_op jit(solution)/shard_map/all_to_all | solution.py:282
  97.0 35.2 %all-to-all-start.1 = ((bf16[16,64,512]{2,0,1:T(8,128)(2,1)}), bf16[16,64,512]{2,0,1:T(8,128)(2,1)}, u32[]{:S(2)}, u32[]{:S(2)}) async-start(bf16[16,64,512]{2,0,1:T(8,128)(2,1)} %copy.31), calls=%async_computation.1 | async-start | bytes 2097152 | tf_op jit(solution)/shard_map/all_to_all | solution.py:297
  135.3 7.3 %collective-permute-start.2 = (bf16[256,512]{1,0:T(8,128)(2,1)S(1)}, bf16[256,512]{1,0:T(8,128)(2,1)S(1)}, u32[]{:S(2)}, u32[]{:S(2)}) collective-permute-start(bf16[256,512]{1,0:T(8,128)(2,1)S(1)} %broadcast_select_fusion), channel_id=1, source_target_pairs={{0,3},{1,0},{2,1},{3,2},{4,7},{5,4},{6,5},{7,6},{8,11},{9,8},{10,9... | collective-permute-start | bytes 786440 | tf_op jit(solution)/shard_map/ppermute | solution.py:315
  140.4 8.7 %collective-permute-start = (bf16[256,512]{1,0:T(8,128)(2,1)S(1)}, bf16[256,512]{1,0:T(8,128)(2,1)S(1)}, u32[]{:S(2)}, u32[]{:S(2)}) collective-permute-start(bf16[256,512]{1,0:T(8,128)(2,1)S(1)} %broadcast_select_fusion), channel_id=1, source_target_pairs={{0,1},{1,2},{2,3},{3,0},{4,5},{5,6},{6,7},{7,4},{8,9},{9,10},{10,1... | collective-permute-start | bytes 786440 | tf_op jit(solution)/shard_map/ppermute | solution.py:315
  140.4 12.3 %collective-permute-start.1 = (bf16[256,512]{1,0:T(8,128)(2,1)S(1)}, bf16[256,512]{1,0:T(8,128)(2,1)S(1)}, u32[]{:S(2)}, u32[]{:S(2)}) collective-permute-start(bf16[256,512]{1,0:T(8,128)(2,1)S(1)} %broadcast_select_fusion), channel_id=1, source_target_pairs={{0,2},{1,3},{2,0},{3,1},{4,6},{5,7},{6,4},{7,5},{8,10},{9,11},{10,... | collective-permute-start | bytes 786440 | tf_op jit(solution)/shard_map/ppermute | solution.py:315

commit v7 on v6

--- a/solution.py
+++ b/solution.py
@@ -64,14 +64,12 @@
     kgain_ref,
     cos_ref,
     sin_ref,
-    out_ref,
-    qkv_ref,
-    pick_ref,
-    starts_ref,
-    *,
+    *refs,
     head_dim,
     capacity,
 ):
+    qkv_ref, pick_ref, starts_ref = refs[-3:]
+    out_refs = refs[:-3]
     devices = dealing_ref.shape[0]
     prompt_total = lengths_ref.shape[0]
     tok_rows = qkv_ref.shape[0]
@@ -121,14 +119,28 @@
     qkv_ref[:, column : column + v_width] = jnp.dot(
         normed, wv_ref[...], preferred_element_type=jnp.float32
     ).astype(jnp.bfloat16)
-    qkv = qkv_ref[...]
-    out_rows = out_ref.shape[0]
+    q_width = wq_ref.shape[1]
+    k_width = wk_ref.shape[1]
+    kv_heads = k_width // head_dim
+    q_part = q_width // kv_heads
+    out_rows = out_refs[0].shape[0]
     block = out_rows // 4
-    for b in range(4):
-        rows_here = pl.ds(b * block, block)
-        out_ref[rows_here, :] = jnp.dot(
-            pick_ref[rows_here, :], qkv, preferred_element_type=jnp.float32
-        ).astype(out_ref.dtype)
+    for h, out_ref in enumerate(out_refs):
+        part = jnp.concatenate(
+            [
+                qkv_ref[:, h * q_part : (h + 1) * q_part],
+                qkv_ref[:, q_width + h * head_dim : q_width + (h + 1) * head_dim],
+                qkv_ref[
+                    :, q_width + k_width + h * head_dim : q_width + k_width + (h + 1) * head_dim
+                ],
+            ],
+            axis=1,
+        )
+        for b in range(4):
+            rows_here = pl.ds(b * block, block)
+            out_ref[rows_here, :] = jnp.dot(
+                pick_ref[rows_here, :], part, preferred_element_type=jnp.float32
+            ).astype(out_ref.dtype)
 
 
 def prepare(
@@ -141,6 +153,7 @@
     width = w_query.shape[1] + w_key.shape[1] + w_value.shape[1]
     devices = dealing.shape[0]
     out_rows = devices * capacity
+    kv_heads = w_key.shape[1] // head_dim
     frequency = THETA ** (-(jnp.arange(half_width).astype(jnp.float32) * 2.0) / head_dim)
     frequency = jnp.concatenate([frequency, frequency])
     angles = positions.astype(jnp.float32)[:, None] * frequency[None, :]
@@ -151,9 +164,9 @@
     smem = pl.BlockSpec(memory_space=pltpu.SMEM)
     return pl.pallas_call(
         lambda *refs: prep_kernel(*refs, head_dim=head_dim, capacity=capacity),
-        out_shape=jax.ShapeDtypeStruct((out_rows, width), jnp.bfloat16),
+        out_shape=[jax.ShapeDtypeStruct((out_rows, width // kv_heads), jnp.bfloat16)] * kv_heads,
         in_specs=[smem] * 3 + [vmem] * 9,
-        out_specs=vmem,
+        out_specs=[vmem] * kv_heads,
         scratch_shapes=[
             pltpu.VMEM((tok_rows, width), jnp.bfloat16),
             pltpu.VMEM((out_rows, tok_rows), jnp.bfloat16),
@@ -265,7 +278,7 @@
     roll_shift = jnp.mod(my_start, devices)
     my_slots = jnp.sum(seg_onehot * inverse[None, :], axis=1)
     back_rows = positions // devices * devices + my_slots
-    picked = prepare(
+    parts = prepare(
         hidden,
         lengths,
         dealing,
@@ -279,48 +292,68 @@
         positions,
         capacity,
     )
-    arrived = lax.all_to_all(
-        picked.reshape(devices, capacity, picked.shape[1]),
-        "req",
-        split_axis=0,
-        concat_axis=0,
-        tiled=True,
-    ).transpose(1, 0, 2)
     source_ids = jnp.arange(devices, dtype=jnp.int32)
     arrived_pos = (
         ranks[:, None] * devices + jnp.mod(source_ids[None, :] - my_start, devices)
     ).reshape(-1)
     key_pos = jnp.where(arrived_pos < my_length, arrived_pos, 1 << 30)
-    mixture = attend(
-        arrived.reshape(slot_len, arrived.shape[2]), arrived_pos, key_pos, q_width, k_width, head_dim
-    )
-    returned = lax.all_to_all(
-        mixture.reshape(capacity, devices, mixture.shape[1]),
-        "req",
-        split_axis=1,
-        concat_axis=1,
-        tiled=True,
-    )
-    attended = jnp.take(returned.reshape(capacity * devices, -1), back_rows, axis=0)
-    kv_rows = jnp.roll(arrived[:, :, q_width:], -roll_shift, axis=1).reshape(slot_len, -1)
-    kv_cache = jnp.stack([kv_rows[:, :k_width], kv_rows[:, k_width:]])[:, None]
+    kv_heads = k_width // head_dim
+    q_part = q_width // kv_heads
     tp_size = lax.axis_size("tp")
     w_rows = w_out.shape[0] // tp_size
-    summed = jnp.dot(
-        attended,
-        lax.dynamic_slice_in_dim(w_out, slice_index * w_rows, w_rows, 0),
-        preferred_element_type=jnp.float32,
-    )
-    for shift in range(1, tp_size):
-        passed = lax.ppermute(
-            attended, "tp", perm=[(i, (i + shift) % tp_size) for i in range(tp_size)]
+    summed = None
+    passes = []
+    key_parts = []
+    value_parts = []
+    for h in range(kv_heads):
+        arrived = lax.all_to_all(
+            parts[h].reshape(devices, capacity, parts[h].shape[1]),
+            "req",
+            split_axis=0,
+            concat_axis=0,
+            tiled=True,
+        ).transpose(1, 0, 2)
+        mixture = attend(
+            arrived.reshape(slot_len, arrived.shape[2]),
+            arrived_pos,
+            key_pos,
+            q_part,
+            head_dim,
+            head_dim,
         )
-        source = jnp.mod(slice_index - shift, tp_size)
-        summed = summed + jnp.dot(
-            passed,
-            lax.dynamic_slice_in_dim(w_out, source * w_rows, w_rows, 0),
-            preferred_element_type=jnp.float32,
+        kv_rows = jnp.roll(arrived[:, :, q_part:], -roll_shift, axis=1).reshape(slot_len, -1)
+        key_parts.append(kv_rows[:, :head_dim])
+        value_parts.append(kv_rows[:, head_dim:])
+        if h > 0:
+            attended, mixture = lax.optimization_barrier((attended, mixture))
+            passes.append(attended)
+        returned = lax.all_to_all(
+            mixture.reshape(capacity, devices, q_part),
+            "req",
+            split_axis=1,
+            concat_axis=1,
+            tiled=True,
         )
+        attended = jnp.take(returned.reshape(capacity * devices, -1), back_rows, axis=0)
+    passes.append(attended)
+    for h, attended in enumerate(passes):
+        for shift in range(tp_size):
+            if shift == 0:
+                passed = attended
+            else:
+                passed = lax.ppermute(
+                    attended, "tp", perm=[(i, (i + shift) % tp_size) for i in range(tp_size)]
+                )
+            source = jnp.mod(slice_index - shift, tp_size)
+            product = jnp.dot(
+                passed,
+                lax.dynamic_slice_in_dim(w_out, source * w_rows + h * q_part, q_part, 0),
+                preferred_element_type=jnp.float32,
+            )
+            summed = product if summed is None else summed + product
+    kv_cache = jnp.stack(
+        [jnp.concatenate(key_parts, axis=1), jnp.concatenate(value_parts, axis=1)]
+    )[:, None]
     branch = lax.optimization_barrier(summed.astype(jnp.bfloat16))
     residual = lax.dynamic_slice_in_dim(hidden, slice_index * out_width, out_width, 1)
     hidden_out = (residual.astype(jnp.float32) + branch.astype(jnp.float32)).astype(jnp.bfloat16)

time: 157 us -> 159 us (1.013)
  waiting for transfers between devices: 78.9 us -> 28 us
  blocking collectives: 0 us -> 41.2 us
  matrix products: 1.18 us -> 4.49 us
  local copies, waits for them, and re-layouts: 17.7 us -> 20.9 us
  starting transfers between devices: 24.8 us -> 27.3 us
  Pallas kernels: 18.5 us -> 20.6 us
  other arithmetic: 10.8 us -> 12.6 us
    all_to_all x2 -> x3, waiting for transfers between devices: 69.2 us -> 23.9 us  [the longest x2 12.2 us: on_device(): lax.all_to_all(mixture.reshape(capacity, devices, q_part), 'req', split_a...]
    all_to_all x0 -> x1, blocking collectives: none -> 41.2 us  [on_device(): lax.all_to_all(parts[h].reshape(devices, capacity, parts[h].shape[1]), 'r...]
    ppermute x3 -> x6, waiting for transfers between devices: 9.73 us -> 4.17 us  [on_device(): lax.ppermute(attended, 'tp', perm=[(i, (i + shift) % tp_size) for i in ra...]
    ppermute x3 -> x6, starting transfers between devices: 4.46 us -> 8.88 us  [on_device(): lax.ppermute(attended, 'tp', perm=[(i, (i + shift) % tp_size) for i in ra...]
    dot_general x4 -> x8, matrix products: 1.18 us -> 4.49 us  [on_device(): jnp.dot(passed, lax.dynamic_slice_in_dim(w_out, source * w_rows + h * q_p...]
    pallas_call x1 -> x2, Pallas kernels: 10.4 us -> 12.8 us  [attend(): pl.pallas_call(lambda *refs: attention_kernel(*refs, q_width=q_width, k_w...]
    slice x1 -> x4, local copies, waits for them, and re-layouts: 1.29 us -> 3.46 us  [the longest x2 1.91 us: on_device(): arrived[:, :, q_part:]]
    another operation x2 -> x4, other arithmetic: 0.2 us -> 2.3 us  [the longest x2 2.1 us: on_device(): jnp.stack([jnp.concatenate(key_parts, axis=1), jnp.concatenate(value_part...]
  transfers between devices with their start and end apart: 5 -> 9, of which waited for: 5 -> 6; matrix products, arithmetic and copies ran while one was open for 6% -> 14% of each run, Pallas kernels for 0% -> 8%
where the time goes in v7:
time: 159 us; the launch traced here: 158 us
  blocking collectives  41.2 us (26%)
  waiting for transfers between devices  28 us (18%)
  starting transfers between devices  27.3 us (17%)
  local copies, waits for them, and re-layouts  20.9 us (13%)
  Pallas kernels  20.6 us (13%)
  other arithmetic  12.6 us (8%)
  matrix products  4.49 us (3%)
  between operations  2.78 us (2%)
    all_to_all x1, blocking collectives, on_device(): lax.all_to_all(parts[h].reshape(devices, capacity, parts[h].shape[1]), 'r...  41.2 us
    pallas_call x2, Pallas kernels, attend(): pl.pallas_call(lambda *refs: attention_kernel(*refs, q_width=q_width, k_w...  12.8 us
    all_to_all x2, starting transfers between devices, on_device(): lax.all_to_all(mixture.reshape(capacity, devices, q_part), 'req', split_a...  12.2 us
    all_to_all x2, waiting for transfers between devices, on_device(): lax.all_to_all(mixture.reshape(capacity, devices, q_part), 'req', split_a...  12.2 us
    all_to_all x1, waiting for transfers between devices, on_device(): lax.all_to_all(parts[h].reshape(devices, capacity, parts[h].shape[1]), 'r...  11.7 us
    ppermute x6, starting transfers between devices, on_device(): lax.ppermute(attended, 'tp', perm=[(i, (i + shift) % tp_size) for i in ra...  8.88 us
    pallas_call x1, Pallas kernels, prepare(): pl.pallas_call(lambda *refs: prep_kernel(*refs, head_dim=head_dim, capaci...  7.78 us
    all_to_all x1, starting transfers between devices, on_device(): lax.all_to_all(parts[h].reshape(devices, capacity, parts[h].shape[1]), 'r...  6.27 us
  transfers between devices with their start and end apart: 9, of which 6 were waited for; matrix products, arithmetic and copies ran while one was open for 14% of the time, Pallas kernels for 8%

profile of v7, /device:TPU:1, one launch (start us, length us, event | category | flops | bytes accessed | tf_op | source)
XLA Modules:
  0.0 157.9 jit_solution(3780505382647134328)
XLA Ops:
  0.7 0.9 copy.39
  1.8 0.7 sub.42
  2.4 0.8 select_reduce_fusion.2
  3.3 0.6 dynamic_slice.38
  3.9 1.3 compare_select_fusion.2
  5.3 0.8 scatter_custom_fusion
  6.3 1.3 broadcast_in_dim.28.refs_4_
  7.6 1.2 fusion.20
  8.8 7.8 %shard_map.113 = (bf16[1024,512]{1,0:T(8,128)(2,1)}, bf16[1024,512]{1,0:T(8,128)(2,1)}) custom-call(s32[64]{0:T(128)} %refs_0_.1, s32[64]{0:T(128)} %refs_1_.1, s32[1]{0:T(128)} %bitcast.1.refs_2_, bf16[256,2048]{1,0:T(8,128)(2,1)} %refs_3_.1, bf16[1,2048]{1,0:T(2,128)(2,1)} %broadcast_in_dim.28.refs_4_, bf16[2048,512]{1,0:T(8,128)(2,1)} %refs_5_.1, ...), custom_call_target="tpu_custom_call" | custom-call | flops 1610612736 | bytes 7340032 | tf_op jit(solution)/shard_map/pallas_call | solution.py:165
  16.6 41.2 %all_to_all.20 = bf16[64,16,512]{2,1,0:T(8,128)(2,1)} all-to-all(bf16[64,16,512]{2,1,0:T(8,128)(2,1)} %bitcast.49), channel_id=1, replica_groups=mesh['req'=64,'tp'=4] {'req'}, dimensions={0} | all-to-all | bytes 2097152 | tf_op jit(solution)/shard_map/all_to_all | solution.py:309
  57.8 6.3 %all-to-all-start.2 = ((bf16[64,16,512]{2,1,0:T(8,128)(2,1)}), bf16[64,16,512]{2,1,0:T(8,128)(2,1)S(1)}, u32[]{:S(2)}, u32[]{:S(2)}) async-start(bf16[64,16,512]{2,1,0:T(8,128)(2,1)} %bitcast.48), calls=%async_computation.2 | async-start | bytes 2097152 | tf_op jit(solution)/shard_map/all_to_all | solution.py:309
  66.1 1.3 add.228.refs_1_
  67.4 0.6 dynamic_slice.39
  68.0 1.2 compare_select_fusion.refs_2_
  69.2 2.8 %copy.54 = bf16[64,16,512]{2,0,1:T(8,128)(2,1)} copy(bf16[64,16,512]{2,1,0:T(8,128)(2,1)} %all_to_all.20) | data formatting | bytes 2097152 | tf_op jit(solution)/shard_map/all_to_all | solution.py:309
  72.0 6.4 %shard_map.114 = bf16[1024,256]{1,0:T(8,128)(2,1)} custom-call(bf16[1024,512]{1,0:T(8,128)(2,1)} %bitcast.42, s32[1024,1]{1,0:T(8,128)} %add.228.refs_1_, s32[1,1024]{1,0:T(1,128)} %compare_select_fusion.refs_2_), custom_call_target="tpu_custom_call" | custom-call | flops 671088640 | bytes 1572864 | tf_op jit(solution)/shard_map/pallas_call | solution.py:235
  78.4 2.1 %copy.42 = bf16[16,64,256]{2,0,1:T(8,128)(2,1)} copy(bf16[16,64,256]{2,1,0:T(8,128)(2,1)} %bitcast.51) | data formatting | bytes 1048576 | tf_op jit(solution)/shard_map/reshape | solution.py:331
  80.5 11.7 %all-to-all-done.2 = bf16[64,16,512]{2,1,0:T(8,128)(2,1)S(1)} async-done(((bf16[64,16,512]{2,1,0:T(8,128)(2,1)}), bf16[64,16,512]{2,1,0:T(8,128)(2,1)S(1)}, u32[]{:S(2)}, u32[]{:S(2)}) %all-to-all-start.2) | async-done | bytes 1048608 | tf_op jit(solution)/shard_map/all_to_all | solution.py:309
  92.3 6.5 %all-to-all-start.1 = ((bf16[16,64,256]{2,0,1:T(8,128)(2,1)}), bf16[16,64,256]{2,0,1:T(8,128)(2,1)}, u32[]{:S(2)}, u32[]{:S(2)}) async-start(bf16[16,64,256]{2,0,1:T(8,128)(2,1)} %copy.42), calls=%async_computation.1 | async-start | bytes 1048576 | tf_op jit(solution)/shard_map/all_to_all | solution.py:330
  98.8 1.9 %slice.28 = bf16[16,64,256]{2,1,0:T(8,128)(2,1)} slice(bf16[16,64,512]{2,1,0:T(8,128)(2,1)} %bitcast.43), slice={[0:16], [0:64], [256:512]} | slice | bytes 1048576 | tf_op jit(solution)/shard_map/slice | solution.py:324
  100.7 0.6 copy.53
  101.3 1.0 copy-done.1
  102.3 6.4 %shard_map.115 = bf16[1024,256]{1,0:T(8,128)(2,1)} custom-call(bf16[1024,512]{1,0:T(8,128)(2,1)} %bitcast.45, s32[1024,1]{1,0:T(8,128)} %add.228.refs_1_, s32[1,1024]{1,0:T(1,128)} %compare_select_fusion.refs_2_), custom_call_target="tpu_custom_call" | custom-call | flops 671088640 | bytes 1572864 | tf_op jit(solution)/shard_map/pallas_call | solution.py:235
  109.5 0.7 fusion.32
  110.2 0.8 fusion.33
  111.0 5.3 %all-to-all-done.1 = bf16[16,64,256]{2,0,1:T(8,128)(2,1)} async-done(((bf16[16,64,256]{2,0,1:T(8,128)(2,1)}), bf16[16,64,256]{2,0,1:T(8,128)(2,1)}, u32[]{:S(2)}, u32[]{:S(2)}) %all-to-all-start.1) | async-done | bytes 524320 | tf_op jit(solution)/shard_map/all_to_all | solution.py:330
  116.3 1.2 copy.43
  117.5 1.8 %gather_fusion = bf16[256,256]{1,0:T(8,128)(2,1)} fusion(bf16[1024,256]{1,0:T(8,128)(2,1)S(1)} %bitcast.41, s32[1024]{0:T(1024)S(1)} %pad_clamp_fusion), kind=kCustom, calls=%fused_computation.clone | custom fusion | bytes 263168 | tf_op jit(solution)/shard_map/jit(_take)/gather | solution.py:337
  119.3 1.0 broadcast_select_fusion.1
  120.4 1.1 copy.46
  121.4 5.7 %all-to-all-start.3 = ((bf16[16,64,256]{2,0,1:T(8,128)(2,1)}), bf16[16,64,256]{2,0,1:T(8,128)(2,1)S(1)}, u32[]{:S(2)}, u32[]{:S(2)}) async-start(bf16[16,64,256]{2,0,1:T(8,128)(2,1)} %copy.46), calls=%async_computation.3 | async-start | bytes 1048576 | tf_op jit(solution)/shard_map/all_to_all | solution.py:330
  127.1 1.1 maximum_bitcast_fusion.1
  128.2 1.0 maximum_bitcast_fusion.2
  129.2 1.1 maximum_bitcast_fusion
  130.3 1.3 collective-permute-start
  131.6 1.4 collective-permute-start.2
  133.1 1.6 %collective-permute-start.1 = (bf16[256,256]{1,0:T(8,128)(2,1)S(1)}, bf16[256,256]{1,0:T(8,128)(2,1)S(1)}, u32[]{:S(2)}, u32[]{:S(2)}) collective-permute-start(bf16[256,256]{1,0:T(8,128)(2,1)S(1)} %broadcast_select_fusion.1), channel_id=1, source_target_pairs={{0,2},{1,3},{2,0},{3,1},{4,6},{5,7},{6,4},{7,5},{8,10},{9,11},{10,... | collective-permute-start | bytes 393224 | tf_op jit(solution)/shard_map/ppermute | solution.py:344
  134.9 1.0 collective-permute-done.2
  135.9 1.0 fusion.14
  137.0 1.0 convolution_add_fusion.2
  138.0 6.8 %all-to-all-done.3 = bf16[16,64,256]{2,0,1:T(8,128)(2,1)S(1)} async-done(((bf16[16,64,256]{2,0,1:T(8,128)(2,1)}), bf16[16,64,256]{2,0,1:T(8,128)(2,1)S(1)}, u32[]{:S(2)}, u32[]{:S(2)}) %all-to-all-start.3) | async-done | bytes 524320 | tf_op jit(solution)/shard_map/all_to_all | solution.py:330
  145.0 1.2 gather_fusion.1
  146.3 3.0 %collective-permute-start.4 = (bf16[256,256]{1,0:T(8,128)(2,1)S(1)}, bf16[256,256]{1,0:T(8,128)(2,1)S(1)}, u32[]{:S(2)}, u32[]{:S(2)}) collective-permute-start(bf16[256,256]{1,0:T(8,128)(2,1)S(1)} %broadcast_select_fusion), channel_id=1, source_target_pairs={{0,2},{1,3},{2,0},{3,1},{4,6},{5,7},{6,4},{7,5},{8,10},{9,11},{10,... | collective-permute-start | bytes 393224 | tf_op jit(solution)/shard_map/ppermute | solution.py:344
  149.3 0.8 collective-permute-start.5
  150.1 0.7 collective-permute-start.3
  151.0 1.3 fusion.3
  152.7 2.9 %collective-permute-done.5 = bf16[256,256]{1,0:T(8,128)(2,1)S(1)} collective-permute-done((bf16[256,256]{1,0:T(8,128)(2,1)S(1)}, bf16[256,256]{1,0:T(8,128)(2,1)S(1)}, u32[]{:S(2)}, u32[]{:S(2)}) %collective-permute-start.5) | collective-permute-done | bytes 131104 | tf_op jit(solution)/shard_map/ppermute | solution.py:344
  156.2 1.7 %add_convert_fusion = bf16[256,512]{1,0:T(8,128)(2,1)} fusion(bf16[256,512]{1,0:T(8,128)(2,1)S(1)} %fusion.4, bf16[256,2048]{1,0:T(8,128)(2,1)} %refs_3_.1, s32[]{:T(128)S(6)} %select_n.116), kind=kLoop, calls=%fused_computation.20 | loop fusion | flops 524288 | bytes 786436 | tf_op jit(solution)/shard_map/convert_element_type | solution.py:359
  (37 shorter events, 3.1 us)
Async XLA Ops:
  0.6 134.1 %copy-start = (bf16[2048,512]{1,0:T(8,128)(2,1)S(1)}, bf16[2048,512]{1,0:T(8,128)(2,1)}, u32[]{:S(2)}) copy-start(bf16[2048,512]{1,0:T(8,128)(2,1)} %param.23) | copy-start | bytes 6291460
  57.8 34.4 %all-to-all-start.2 = ((bf16[64,16,512]{2,1,0:T(8,128)(2,1)}), bf16[64,16,512]{2,1,0:T(8,128)(2,1)S(1)}, u32[]{:S(2)}, u32[]{:S(2)}) async-start(bf16[64,16,512]{2,1,0:T(8,128)(2,1)} %bitcast.48), calls=%async_computation.2 | async-start | bytes 2097152 | tf_op jit(solution)/shard_map/all_to_all | solution.py:309
  92.3 24.1 %all-to-all-start.1 = ((bf16[16,64,256]{2,0,1:T(8,128)(2,1)}), bf16[16,64,256]{2,0,1:T(8,128)(2,1)}, u32[]{:S(2)}, u32[]{:S(2)}) async-start(bf16[16,64,256]{2,0,1:T(8,128)(2,1)} %copy.42), calls=%async_computation.1 | async-start | bytes 1048576 | tf_op jit(solution)/shard_map/all_to_all | solution.py:330
  101.2 1.0 copy-start.1
  101.3 7.4 %copy-start.2 = (bf16[16,64,256]{2,1,0:T(8,128)(2,1)S(1)}, bf16[16,64,256]{2,1,0:T(8,128)(2,1)}, u32[]{:S(2)}) copy-start(bf16[16,64,256]{2,1,0:T(8,128)(2,1)} %slice.28) | copy-start | bytes 1572868
  109.5 10.9 %copy-start.4 = (bf16[1024,256]{1,0:T(8,128)(2,1)S(1)}, bf16[1024,256]{1,0:T(8,128)(2,1)}, u32[]{:S(2)}) copy-start(bf16[1024,256]{1,0:T(8,128)(2,1)} %shard_map.115) | copy-start | bytes 1572868
  121.4 23.4 %all-to-all-start.3 = ((bf16[16,64,256]{2,0,1:T(8,128)(2,1)}), bf16[16,64,256]{2,0,1:T(8,128)(2,1)S(1)}, u32[]{:S(2)}, u32[]{:S(2)}) async-start(bf16[16,64,256]{2,0,1:T(8,128)(2,1)} %copy.46), calls=%async_computation.3 | async-start | bytes 1048576 | tf_op jit(solution)/shard_map/all_to_all | solution.py:330
  130.3 6.7 %collective-permute-start = (bf16[256,256]{1,0:T(8,128)(2,1)S(1)}, bf16[256,256]{1,0:T(8,128)(2,1)S(1)}, u32[]{:S(2)}, u32[]{:S(2)}) collective-permute-start(bf16[256,256]{1,0:T(8,128)(2,1)S(1)} %broadcast_select_fusion.1), channel_id=1, source_target_pairs={{0,1},{1,2},{2,3},{3,0},{4,5},{5,6},{6,7},{7,4},{8,9},{9,10},{10,1... | collective-permute-start | bytes 393224 | tf_op jit(solution)/shard_map/ppermute | solution.py:344
  131.6 4.3 %collective-permute-start.2 = (bf16[256,256]{1,0:T(8,128)(2,1)S(1)}, bf16[256,256]{1,0:T(8,128)(2,1)S(1)}, u32[]{:S(2)}, u32[]{:S(2)}) collective-permute-start(bf16[256,256]{1,0:T(8,128)(2,1)S(1)} %broadcast_select_fusion.1), channel_id=1, source_target_pairs={{0,3},{1,0},{2,1},{3,2},{4,7},{5,4},{6,5},{7,6},{8,11},{9,8},{10,9... | collective-permute-start | bytes 393224 | tf_op jit(solution)/shard_map/ppermute | solution.py:344
  133.1 17.9 %collective-permute-start.1 = (bf16[256,256]{1,0:T(8,128)(2,1)S(1)}, bf16[256,256]{1,0:T(8,128)(2,1)S(1)}, u32[]{:S(2)}, u32[]{:S(2)}) collective-permute-start(bf16[256,256]{1,0:T(8,128)(2,1)S(1)} %broadcast_select_fusion.1), channel_id=1, source_target_pairs={{0,2},{1,3},{2,0},{3,1},{4,6},{5,7},{6,4},{7,5},{8,10},{9,11},{10,... | collective-permute-start | bytes 393224 | tf_op jit(solution)/shard_map/ppermute | solution.py:344
  145.0 6.0 %copy-start.3 = (f32[256,512]{1,0:T(8,128)S(1)}, f32[256,512]{1,0:T(8,128)}, u32[]{:S(2)}) copy-start(f32[256,512]{1,0:T(8,128)} %fusion.14) | copy-start | bytes 1572868
  146.3 6.3 %collective-permute-start.4 = (bf16[256,256]{1,0:T(8,128)(2,1)S(1)}, bf16[256,256]{1,0:T(8,128)(2,1)S(1)}, u32[]{:S(2)}, u32[]{:S(2)}) collective-permute-start(bf16[256,256]{1,0:T(8,128)(2,1)S(1)} %broadcast_select_fusion), channel_id=1, source_target_pairs={{0,2},{1,3},{2,0},{3,1},{4,6},{5,7},{6,4},{7,5},{8,10},{9,11},{10,... | collective-permute-start | bytes 393224 | tf_op jit(solution)/shard_map/ppermute | solution.py:344
  149.3 6.4 %collective-permute-start.5 = (bf16[256,256]{1,0:T(8,128)(2,1)S(1)}, bf16[256,256]{1,0:T(8,128)(2,1)S(1)}, u32[]{:S(2)}, u32[]{:S(2)}) collective-permute-start(bf16[256,256]{1,0:T(8,128)(2,1)S(1)} %broadcast_select_fusion), channel_id=1, source_target_pairs={{0,3},{1,0},{2,1},{3,2},{4,7},{5,4},{6,5},{7,6},{8,11},{9,8},{10,9... | collective-permute-start | bytes 393224 | tf_op jit(solution)/shard_map/ppermute | solution.py:344
  150.1 5.9 %collective-permute-start.3 = (bf16[256,256]{1,0:T(8,128)(2,1)S(1)}, bf16[256,256]{1,0:T(8,128)(2,1)S(1)}, u32[]{:S(2)}, u32[]{:S(2)}) collective-permute-start(bf16[256,256]{1,0:T(8,128)(2,1)S(1)} %broadcast_select_fusion), channel_id=1, source_target_pairs={{0,1},{1,2},{2,3},{3,0},{4,5},{5,6},{6,7},{7,4},{8,9},{9,10},{10,1... | collective-permute-start | bytes 393224 | tf_op jit(solution)/shard_map/ppermute | solution.py:344

commit v8 on v6

--- a/solution.py
+++ b/solution.py
@@ -255,16 +255,6 @@
     segment = jnp.sum((packed_ids[:, None] >= prompt_ends[None, :]).astype(jnp.int32), axis=1)
     seg_onehot = (segment[:, None] == prompt_ids[None, :]).astype(jnp.int32)
     positions = packed_ids - jnp.sum(seg_onehot * starts[None, :], axis=1)
-    inverse = jnp.zeros((prompt_total,), jnp.int32).at[dealing].set(prompt_ids)
-    deal_hot = (dealing[:, None] == prompt_ids[None, :]).astype(jnp.int32)
-    dealt_starts = jnp.sum(deal_hot * starts[None, :], axis=1)
-    dealt_lengths = jnp.sum(deal_hot * lengths[None, :], axis=1)
-    ranks = jnp.arange(capacity, dtype=jnp.int32)
-    my_start = lax.dynamic_index_in_dim(dealt_starts, home_index, 0, keepdims=False)
-    my_length = lax.dynamic_index_in_dim(dealt_lengths, home_index, 0, keepdims=False)
-    roll_shift = jnp.mod(my_start, devices)
-    my_slots = jnp.sum(seg_onehot * inverse[None, :], axis=1)
-    back_rows = positions // devices * devices + my_slots
     picked = prepare(
         hidden,
         lengths,
@@ -279,6 +269,19 @@
         positions,
         capacity,
     )
+    picked, lengths, dealing, starts, seg_onehot = lax.optimization_barrier(
+        (picked, lengths, dealing, starts, seg_onehot)
+    )
+    inverse = jnp.zeros((prompt_total,), jnp.int32).at[dealing].set(prompt_ids)
+    deal_hot = (dealing[:, None] == prompt_ids[None, :]).astype(jnp.int32)
+    dealt_starts = jnp.sum(deal_hot * starts[None, :], axis=1)
+    dealt_lengths = jnp.sum(deal_hot * lengths[None, :], axis=1)
+    ranks = jnp.arange(capacity, dtype=jnp.int32)
+    my_start = lax.dynamic_index_in_dim(dealt_starts, home_index, 0, keepdims=False)
+    my_length = lax.dynamic_index_in_dim(dealt_lengths, home_index, 0, keepdims=False)
+    roll_shift = jnp.mod(my_start, devices)
+    my_slots = jnp.sum(seg_onehot * inverse[None, :], axis=1)
+    back_rows = my_slots * capacity + positions // devices
     arrived = lax.all_to_all(
         picked.reshape(devices, capacity, picked.shape[1]),
         "req",
@@ -295,10 +298,10 @@
         arrived.reshape(slot_len, arrived.shape[2]), arrived_pos, key_pos, q_width, k_width, head_dim
     )
     returned = lax.all_to_all(
-        mixture.reshape(capacity, devices, mixture.shape[1]),
+        mixture.reshape(capacity, devices, mixture.shape[1]).transpose(1, 0, 2),
         "req",
-        split_axis=1,
-        concat_axis=1,
+        split_axis=0,
+        concat_axis=0,
         tiled=True,
     )
     attended = jnp.take(returned.reshape(capacity * devices, -1), back_rows, axis=0)

time: 157 us -> 153 us (0.975); the launches traced: 155 us -> 153 us
  local copies, waits for them, and re-layouts: 17.7 us -> 15.9 us
  waiting for transfers between devices: 78.9 us -> 80.6 us
    ppermute x3, waiting for transfers between devices: 9.73 us -> 13.7 us  [on_device(): lax.ppermute(attended, 'tp', perm=[(i, (i + shift) % tp_size) for i in ra...]
    all_to_all x1 -> x0, local copies, waits for them, and re-layouts: 1.8 us -> none  [on_device(): lax.all_to_all(mixture.reshape(capacity, devices, mixture.shape[1]), 'req...]
  transfers between devices with their start and end apart: 5 -> 5, of which waited for: 5 -> 4; matrix products, arithmetic and copies ran while one was open for 6% -> 8% of each run, Pallas kernels for 0% -> 0%
where the time goes in v8:
time: 153 us
  waiting for transfers between devices  80.6 us (53%)
  starting transfers between devices  24.4 us (16%)
  Pallas kernels  18.5 us (12%)
  local copies, waits for them, and re-layouts  15.9 us (10%)
  other arithmetic  9.6 us (6%)
  between operations  2.81 us (2%)
    all_to_all x1, waiting for transfers between devices, on_device(): lax.all_to_all(picked.reshape(devices, capacity, picked.shape[1]), 'req',...  44.9 us
    all_to_all x1, waiting for transfers between devices, on_device(): lax.all_to_all(mixture.reshape(capacity, devices, mixture.shape[1]).trans...  22 us
    ppermute x3, waiting for transfers between devices, on_device(): lax.ppermute(attended, 'tp', perm=[(i, (i + shift) % tp_size) for i in ra...  13.7 us
    all_to_all x1, starting transfers between devices, on_device(): lax.all_to_all(picked.reshape(devices, capacity, picked.shape[1]), 'req',...  13.3 us
    pallas_call x1, Pallas kernels, attend(): pl.pallas_call(lambda *refs: attention_kernel(*refs, q_width=q_width, k_w...  10.4 us
    pallas_call x1, Pallas kernels, prepare(): pl.pallas_call(lambda *refs: prep_kernel(*refs, head_dim=head_dim, capaci...  8.03 us
    all_to_all x1, starting transfers between devices, on_device(): lax.all_to_all(mixture.reshape(capacity, devices, mixture.shape[1]).trans...  6.97 us
    all_to_all x1, local copies, waits for them, and re-layouts, on_device(): lax.all_to_all(picked.reshape(devices, capacity, picked.shape[1]), 'req',...  4.09 us
  transfers between devices with their start and end apart: 5, of which 4 were waited for; matrix products, arithmetic and copies ran while one was open for 8% of the time, Pallas kernels for 0%

profile of v8, /device:TPU:1, one launch (start us, length us, event | category | flops | bytes accessed | tf_op | source)
XLA Modules:
  0.0 152.9 jit_solution(3914021247794655406)
XLA Ops:
  0.6 0.0 copy-start
  0.7 0.1 compare_select_fusion.9
  0.7 1.4 broadcast_in_dim.32.refs_4_
  2.2 0.7 copy.28
  2.9 0.1 reduce-window.8
  3.0 0.1 reduce
  3.1 0.7 sub.52
  3.8 0.1 convert_reduce_fusion
  3.9 0.1 select_reduce_fusion
  4.0 1.2 fusion.9
  5.2 8.0 %shard_map.113 = bf16[1024,1024]{1,0:T(8,128)(2,1)} custom-call(s32[64]{0:T(128)} %refs_0_.1, s32[64]{0:T(128)} %refs_1_.1, s32[1]{0:T(128)} %bitcast.refs_2_, bf16[256,2048]{1,0:T(8,128)(2,1)} %refs_3_.1, bf16[1,2048]{1,0:T(2,128)(2,1)} %broadcast_in_dim.32.refs_4_, bf16[2048,512]{1,0:T(8,128)(2,1)} %refs_5_.1, bf16[2048,256]{1,0:T(8,128)(2,1)} %refs_6_.1, ...), custom_call_target="tpu_custom_call" | custom-call | flops 1610612736 | bytes 7340032 | tf_op jit(solution)/shard_map/pallas_call | solution.py:152
  13.3 13.3 %all-to-all-start = ((bf16[64,16,1024]{2,1,0:T(8,128)(2,1)}), bf16[64,16,1024]{2,1,0:T(8,128)(2,1)}, u32[]{:S(2)}, u32[]{:S(2)}) async-start(bf16[64,16,1024]{2,1,0:T(8,128)(2,1)} %bitcast.35), calls=%async_computation | async-start | bytes 4194304 | tf_op jit(solution)/shard_map/all_to_all | solution.py:285
  26.6 0.0 copy-done.1
  26.6 0.0 copy-done.2
  26.6 0.2 select_reduce_fusion.1
  26.8 0.7 dynamic_slice.27
  27.4 0.6 and_select_fusion.1
  28.1 0.1 broadcast_add_fusion
  28.2 0.1 add.191
  28.2 1.3 add.210.refs_1_
  29.5 0.6 dynamic_slice.28
  30.1 1.2 compare_select_fusion.refs_2_
  31.3 44.9 %all-to-all-done = bf16[64,16,1024]{2,1,0:T(8,128)(2,1)} async-done(((bf16[64,16,1024]{2,1,0:T(8,128)(2,1)}), bf16[64,16,1024]{2,1,0:T(8,128)(2,1)}, u32[]{:S(2)}, u32[]{:S(2)}) %all-to-all-start) | async-done | bytes 2097184 | tf_op jit(solution)/shard_map/all_to_all | solution.py:285
  76.2 4.1 %copy.37 = bf16[64,16,1024]{2,0,1:T(8,128)(2,1)} copy(bf16[64,16,1024]{2,1,0:T(8,128)(2,1)} %all-to-all-done) | data formatting | bytes 4194304 | tf_op jit(solution)/shard_map/all_to_all | solution.py:285
  80.3 10.4 %shard_map.114 = bf16[1024,512]{1,0:T(8,128)(2,1)} custom-call(bf16[1024,1024]{1,0:T(8,128)(2,1)} %bitcast.36, s32[1024,1]{1,0:T(8,128)} %add.210.refs_1_, s32[1,1024]{1,0:T(1,128)} %compare_select_fusion.refs_2_), custom_call_target="tpu_custom_call" | custom-call | flops 1342177280 | bytes 3145728 | tf_op jit(solution)/shard_map/pallas_call | solution.py:222
  90.7 2.8 %copy.36 = bf16[16,64,512]{2,0,1:T(8,128)(2,1)} copy(bf16[16,64,512]{2,1,0:T(8,128)(2,1)} %bitcast.40) | data formatting | bytes 2097152 | tf_op jit(solution)/shard_map/reshape | solution.py:301
  93.5 7.0 %all-to-all-start.1 = ((bf16[64,16,512]{2,1,0:T(8,128)(2,1)}), bf16[64,16,512]{2,1,0:T(8,128)(2,1)S(1)}, u32[]{:S(2)}, u32[]{:S(2)}) async-start(bf16[64,16,512]{2,1,0:T(8,128)(2,1)} %bitcast.39), calls=%async_computation.1 | async-start | bytes 2097152 | tf_op jit(solution)/shard_map/all_to_all | solution.py:300
  102.5 0.8 scatter_custom_fusion
  103.3 0.1 multiply_reduce_fusion
  103.5 1.3 slice.14
  104.8 0.8 fusion.2
  105.6 1.1 slice_bitcast_fusion.1
  106.6 22.0 %all-to-all-done.1 = bf16[64,16,512]{2,1,0:T(8,128)(2,1)S(1)} async-done(((bf16[64,16,512]{2,1,0:T(8,128)(2,1)}), bf16[64,16,512]{2,1,0:T(8,128)(2,1)S(1)}, u32[]{:S(2)}, u32[]{:S(2)}) %all-to-all-start.1) | async-done | bytes 1048608 | tf_op jit(solution)/shard_map/all_to_all | solution.py:300
  128.7 1.2 gather_fusion
  129.8 0.1 broadcast_select_fusion
  129.9 3.0 %collective-permute-start.2 = (bf16[256,512]{1,0:T(8,128)(2,1)S(1)}, bf16[256,512]{1,0:T(8,128)(2,1)S(1)}, u32[]{:S(2)}, u32[]{:S(2)}) collective-permute-start(bf16[256,512]{1,0:T(8,128)(2,1)S(1)} %broadcast_select_fusion), channel_id=1, source_target_pairs={{0,3},{1,0},{2,1},{3,2},{4,7},{5,4},{6,5},{7,6},{8,11},{9,8},{10,9... | collective-permute-start | bytes 786440 | tf_op jit(solution)/shard_map/ppermute | solution.py:318
  133.0 2.3 %maximum_bitcast_fusion = bf16[2,1,1024,256]{3,2,1,0:T(8,128)(2,1)} fusion(bf16[1,1024,256]{2,1,0:T(8,128)(2,1)} %get-tuple-element.21, bf16[1,1024,256]{2,1,0:T(8,128)(2,1)} %get-tuple-element.20), kind=kLoop, calls=%fused_computation.9 | loop fusion | flops 524288 | bytes 2097152
  135.2 0.3 collective-permute-start.1
  135.6 0.7 collective-permute-start
  136.3 0.0 copy-done
  136.3 0.3 fusion.7
  136.6 1.4 collective-permute-done.2
  138.0 0.3 fusion.3
  138.3 12.3 %collective-permute-done = bf16[256,512]{1,0:T(8,128)(2,1)S(1)} collective-permute-done((bf16[256,512]{1,0:T(8,128)(2,1)S(1)}, bf16[256,512]{1,0:T(8,128)(2,1)S(1)}, u32[]{:S(2)}, u32[]{:S(2)}) %collective-permute-start) | collective-permute-done | bytes 262176 | tf_op jit(solution)/shard_map/ppermute | solution.py:318
  150.6 0.3 convolution_add_fusion.1
  150.9 0.0 collective-permute-done.1
  150.9 0.3 fusion.1
  151.2 1.7 %add_convert_fusion = bf16[256,512]{1,0:T(8,128)(2,1)} fusion(bf16[256,512]{1,0:T(8,128)(2,1)S(1)} %fusion.1, bf16[256,2048]{1,0:T(8,128)(2,1)} %refs_3_.1, s32[]{:T(128)S(6)} %select_n.117), kind=kLoop, calls=%fused_computation.13 | loop fusion | flops 524288 | bytes 786436 | tf_op jit(solution)/shard_map/convert_element_type | solution.py:329
  (13 shorter events, 0.1 us)
Async XLA Ops:
  0.6 135.6 %copy-start = (bf16[2048,512]{1,0:T(8,128)(2,1)S(1)}, bf16[2048,512]{1,0:T(8,128)(2,1)}, u32[]{:S(2)}) copy-start(bf16[2048,512]{1,0:T(8,128)(2,1)} %param.19) | copy-start | bytes 6291460
  13.3 13.3 %copy-start.1 = (s32[64]{0:T(128)S(1)}, s32[64]{0:T(128)}, u32[]{:S(2)}) copy-start(s32[64]{0:T(128)} %refs_0_.1) | copy-start | bytes 772
  13.3 13.3 %copy-start.2 = (s32[64]{0:T(128)S(1)}, s32[64]{0:T(128)}, u32[]{:S(2)}) copy-start(s32[64]{0:T(128)} %refs_1_.1) | copy-start | bytes 772
  13.3 62.9 %all-to-all-start = ((bf16[64,16,1024]{2,1,0:T(8,128)(2,1)}), bf16[64,16,1024]{2,1,0:T(8,128)(2,1)}, u32[]{:S(2)}, u32[]{:S(2)}) async-start(bf16[64,16,1024]{2,1,0:T(8,128)(2,1)} %bitcast.35), calls=%async_computation | async-start | bytes 4194304 | tf_op jit(solution)/shard_map/all_to_all | solution.py:285
  93.5 35.1 %all-to-all-start.1 = ((bf16[64,16,512]{2,1,0:T(8,128)(2,1)}), bf16[64,16,512]{2,1,0:T(8,128)(2,1)S(1)}, u32[]{:S(2)}, u32[]{:S(2)}) async-start(bf16[64,16,512]{2,1,0:T(8,128)(2,1)} %bitcast.39), calls=%async_computation.1 | async-start | bytes 2097152 | tf_op jit(solution)/shard_map/all_to_all | solution.py:300
  129.9 8.0 %collective-permute-start.2 = (bf16[256,512]{1,0:T(8,128)(2,1)S(1)}, bf16[256,512]{1,0:T(8,128)(2,1)S(1)}, u32[]{:S(2)}, u32[]{:S(2)}) collective-permute-start(bf16[256,512]{1,0:T(8,128)(2,1)S(1)} %broadcast_select_fusion), channel_id=1, source_target_pairs={{0,3},{1,0},{2,1},{3,2},{4,7},{5,4},{6,5},{7,6},{8,11},{9,8},{10,9... | collective-permute-start | bytes 786440 | tf_op jit(solution)/shard_map/ppermute | solution.py:318
  135.2 15.7 %collective-permute-start.1 = (bf16[256,512]{1,0:T(8,128)(2,1)S(1)}, bf16[256,512]{1,0:T(8,128)(2,1)S(1)}, u32[]{:S(2)}, u32[]{:S(2)}) collective-permute-start(bf16[256,512]{1,0:T(8,128)(2,1)S(1)} %broadcast_select_fusion), channel_id=1, source_target_pairs={{0,2},{1,3},{2,0},{3,1},{4,6},{5,7},{6,4},{7,5},{8,10},{9,11},{10,... | collective-permute-start | bytes 786440 | tf_op jit(solution)/shard_map/ppermute | solution.py:318
  135.6 15.0 %collective-permute-start = (bf16[256,512]{1,0:T(8,128)(2,1)S(1)}, bf16[256,512]{1,0:T(8,128)(2,1)S(1)}, u32[]{:S(2)}, u32[]{:S(2)}) collective-permute-start(bf16[256,512]{1,0:T(8,128)(2,1)S(1)} %broadcast_select_fusion), channel_id=1, source_target_pairs={{0,1},{1,2},{2,3},{3,0},{4,5},{5,6},{6,7},{7,4},{8,9},{9,10},{10,1... | collective-permute-start | bytes 786440 | tf_op jit(solution)/shard_map/ppermute | solution.py:318

commit v9 on v8

--- a/solution.py
+++ b/solution.py
@@ -101,7 +101,9 @@
     lax.fori_loop(0, devices, pick_rows, 0)
     values = hidden_ref[...].astype(jnp.float32)
     inv_rms = lax.rsqrt(jnp.mean(values * values, axis=-1, keepdims=True) + EPS)
-    normed = (values * inv_rms * norm_gain_ref[...].astype(jnp.float32)).astype(jnp.bfloat16)
+    normed = (values * inv_rms * norm_gain_ref[...].astype(jnp.float32)[None, :]).astype(
+        jnp.bfloat16
+    )
     cosine = cos_ref[...]
     sine = sin_ref[...]
     column = 0
@@ -169,7 +171,7 @@
         dealing,
         home,
         hidden,
-        norm_gain[None, :],
+        norm_gain,
         w_query,
         w_key,
         w_value,

time: 153 us -> 152 us (level)
  no operation moved by 1% of the time
where the time goes in v9:
time: 152 us
  waiting for transfers between devices  80.6 us (53%)
  starting transfers between devices  24.4 us (16%)
  Pallas kernels  18.5 us (12%)
  local copies, waits for them, and re-layouts  14.6 us (10%)
  other arithmetic  9.6 us (6%)
  between operations  2.81 us (2%)
    all_to_all x1, waiting for transfers between devices, on_device(): lax.all_to_all(picked.reshape(devices, capacity, picked.shape[1]), 'req',...  44.9 us
    all_to_all x1, waiting for transfers between devices, on_device(): lax.all_to_all(mixture.reshape(capacity, devices, mixture.shape[1]).trans...  22 us
    ppermute x3, waiting for transfers between devices, on_device(): lax.ppermute(attended, 'tp', perm=[(i, (i + shift) % tp_size) for i in ra...  13.7 us
    all_to_all x1, starting transfers between devices, on_device(): lax.all_to_all(picked.reshape(devices, capacity, picked.shape[1]), 'req',...  13.3 us
    pallas_call x1, Pallas kernels, attend(): pl.pallas_call(lambda *refs: attention_kernel(*refs, q_width=q_width, k_w...  10.4 us
    pallas_call x1, Pallas kernels, prepare(): pl.pallas_call(lambda *refs: prep_kernel(*refs, head_dim=head_dim, capaci...  8.02 us
    all_to_all x1, starting transfers between devices, on_device(): lax.all_to_all(mixture.reshape(capacity, devices, mixture.shape[1]).trans...  6.96 us
    all_to_all x1, local copies, waits for them, and re-layouts, on_device(): lax.all_to_all(picked.reshape(devices, capacity, picked.shape[1]), 'req',...  4.09 us
  transfers between devices with their start and end apart: 5, of which 4 were waited for; matrix products, arithmetic and copies ran while one was open for 8% of the time, Pallas kernels for 0%

profile of v9, /device:TPU:1, one launch (start us, length us, event | category | flops | bytes accessed | tf_op | source)
XLA Modules:
  0.0 151.6 jit_solution(16425602259600862920)
XLA Ops:
  0.6 0.0 copy-start
  0.7 0.1 compare_select_fusion.9
  0.7 0.9 copy.28
  1.6 0.1 reduce-window.8
  1.7 0.1 reduce
  1.8 0.7 sub.52
  2.5 0.1 convert_reduce_fusion
  2.6 0.1 select_reduce_fusion
  2.7 1.2 fusion.9
  3.9 8.0 %shard_map.113 = bf16[1024,1024]{1,0:T(8,128)(2,1)} custom-call(s32[64]{0:T(128)} %refs_0_.1, s32[64]{0:T(128)} %refs_1_.1, s32[1]{0:T(128)} %bitcast.refs_2_, bf16[256,2048]{1,0:T(8,128)(2,1)} %refs_3_.1, bf16[2048]{0:T(1024)(128)(2,1)} %refs_4_.1, bf16[2048,512]{1,0:T(8,128)(2,1)} %refs_5_.1, bf16[2048,256]{1,0:T(8,128)(2,1)} %refs_6_.1, ...), custom_call_target="tpu_custom_call" | custom-call | flops 1610612736 | bytes 7340032 | tf_op jit(solution)/shard_map/pallas_call | solution.py:154
  12.0 0.0 copy-start.1
  12.0 13.3 %all-to-all-start = ((bf16[64,16,1024]{2,1,0:T(8,128)(2,1)}), bf16[64,16,1024]{2,1,0:T(8,128)(2,1)}, u32[]{:S(2)}, u32[]{:S(2)}) async-start(bf16[64,16,1024]{2,1,0:T(8,128)(2,1)} %bitcast.35), calls=%async_computation | async-start | bytes 4194304 | tf_op jit(solution)/shard_map/all_to_all | solution.py:287
  25.3 0.0 copy-done.1
  25.3 0.0 copy-done.2
  25.3 0.2 select_reduce_fusion.1
  25.5 0.7 dynamic_slice.27
  26.2 0.6 and_select_fusion.1
  26.8 0.1 broadcast_add_fusion
  26.9 0.1 add.191
  27.0 1.3 add.210.refs_1_
  28.2 0.6 dynamic_slice.28
  28.8 1.2 compare_select_fusion.refs_2_
  30.1 44.9 %all-to-all-done = bf16[64,16,1024]{2,1,0:T(8,128)(2,1)} async-done(((bf16[64,16,1024]{2,1,0:T(8,128)(2,1)}), bf16[64,16,1024]{2,1,0:T(8,128)(2,1)}, u32[]{:S(2)}, u32[]{:S(2)}) %all-to-all-start) | async-done | bytes 2097184 | tf_op jit(solution)/shard_map/all_to_all | solution.py:287
  74.9 4.1 %copy.37 = bf16[64,16,1024]{2,0,1:T(8,128)(2,1)} copy(bf16[64,16,1024]{2,1,0:T(8,128)(2,1)} %all-to-all-done) | data formatting | bytes 4194304 | tf_op jit(solution)/shard_map/all_to_all | solution.py:287
  79.0 10.4 %shard_map.114 = bf16[1024,512]{1,0:T(8,128)(2,1)} custom-call(bf16[1024,1024]{1,0:T(8,128)(2,1)} %bitcast.36, s32[1024,1]{1,0:T(8,128)} %add.210.refs_1_, s32[1,1024]{1,0:T(1,128)} %compare_select_fusion.refs_2_), custom_call_target="tpu_custom_call" | custom-call | flops 1342177280 | bytes 3145728 | tf_op jit(solution)/shard_map/pallas_call | solution.py:224
  89.5 2.8 %copy.36 = bf16[16,64,512]{2,0,1:T(8,128)(2,1)} copy(bf16[16,64,512]{2,1,0:T(8,128)(2,1)} %bitcast.40) | data formatting | bytes 2097152 | tf_op jit(solution)/shard_map/reshape | solution.py:303
  92.2 7.0 %all-to-all-start.1 = ((bf16[64,16,512]{2,1,0:T(8,128)(2,1)}), bf16[64,16,512]{2,1,0:T(8,128)(2,1)S(1)}, u32[]{:S(2)}, u32[]{:S(2)}) async-start(bf16[64,16,512]{2,1,0:T(8,128)(2,1)} %bitcast.39), calls=%async_computation.1 | async-start | bytes 2097152 | tf_op jit(solution)/shard_map/all_to_all | solution.py:302
  101.2 0.8 scatter_custom_fusion
  102.0 0.1 multiply_reduce_fusion
  102.2 1.3 slice.14
  103.5 0.8 fusion.2
  104.3 1.1 slice_bitcast_fusion.1
  105.4 22.0 %all-to-all-done.1 = bf16[64,16,512]{2,1,0:T(8,128)(2,1)S(1)} async-done(((bf16[64,16,512]{2,1,0:T(8,128)(2,1)}), bf16[64,16,512]{2,1,0:T(8,128)(2,1)S(1)}, u32[]{:S(2)}, u32[]{:S(2)}) %all-to-all-start.1) | async-done | bytes 1048608 | tf_op jit(solution)/shard_map/all_to_all | solution.py:302
  127.4 1.2 gather_fusion
  128.5 0.1 broadcast_select_fusion
  128.6 3.0 %collective-permute-start.2 = (bf16[256,512]{1,0:T(8,128)(2,1)S(1)}, bf16[256,512]{1,0:T(8,128)(2,1)S(1)}, u32[]{:S(2)}, u32[]{:S(2)}) collective-permute-start(bf16[256,512]{1,0:T(8,128)(2,1)S(1)} %broadcast_select_fusion), channel_id=1, source_target_pairs={{0,3},{1,0},{2,1},{3,2},{4,7},{5,4},{6,5},{7,6},{8,11},{9,8},{10,9... | collective-permute-start | bytes 786440 | tf_op jit(solution)/shard_map/ppermute | solution.py:320
  131.7 2.3 %maximum_bitcast_fusion = bf16[2,1,1024,256]{3,2,1,0:T(8,128)(2,1)} fusion(bf16[1,1024,256]{2,1,0:T(8,128)(2,1)} %get-tuple-element.21, bf16[1,1024,256]{2,1,0:T(8,128)(2,1)} %get-tuple-element.20), kind=kLoop, calls=%fused_computation.9 | loop fusion | flops 524288 | bytes 2097152
  133.9 0.4 collective-permute-start.1
  134.3 0.7 collective-permute-start
  135.0 0.0 copy-done
  135.0 0.3 fusion.7
  135.3 1.4 collective-permute-done.2
  136.7 0.3 fusion.3
  137.0 12.3 %collective-permute-done = bf16[256,512]{1,0:T(8,128)(2,1)S(1)} collective-permute-done((bf16[256,512]{1,0:T(8,128)(2,1)S(1)}, bf16[256,512]{1,0:T(8,128)(2,1)S(1)}, u32[]{:S(2)}, u32[]{:S(2)}) %collective-permute-start) | collective-permute-done | bytes 262176 | tf_op jit(solution)/shard_map/ppermute | solution.py:320
  149.3 0.3 convolution_add_fusion.1
  149.6 0.0 collective-permute-done.1
  149.6 0.3 fusion.1
  149.9 1.7 %add_convert_fusion = bf16[256,512]{1,0:T(8,128)(2,1)} fusion(bf16[256,512]{1,0:T(8,128)(2,1)S(1)} %fusion.1, bf16[256,2048]{1,0:T(8,128)(2,1)} %refs_3_.1, s32[]{:T(128)S(6)} %select_n.117), kind=kLoop, calls=%fused_computation.13 | loop fusion | flops 524288 | bytes 786436 | tf_op jit(solution)/shard_map/convert_element_type | solution.py:331
  (12 shorter events, 0.1 us)
Async XLA Ops:
  0.6 134.3 %copy-start = (bf16[2048,512]{1,0:T(8,128)(2,1)S(1)}, bf16[2048,512]{1,0:T(8,128)(2,1)}, u32[]{:S(2)}) copy-start(bf16[2048,512]{1,0:T(8,128)(2,1)} %param.19) | copy-start | bytes 6291460
  12.0 13.3 %copy-start.1 = (s32[64]{0:T(128)S(1)}, s32[64]{0:T(128)}, u32[]{:S(2)}) copy-start(s32[64]{0:T(128)} %refs_0_.1) | copy-start | bytes 772
  12.0 13.3 %copy-start.2 = (s32[64]{0:T(128)S(1)}, s32[64]{0:T(128)}, u32[]{:S(2)}) copy-start(s32[64]{0:T(128)} %refs_1_.1) | copy-start | bytes 772
  12.0 62.9 %all-to-all-start = ((bf16[64,16,1024]{2,1,0:T(8,128)(2,1)}), bf16[64,16,1024]{2,1,0:T(8,128)(2,1)}, u32[]{:S(2)}, u32[]{:S(2)}) async-start(bf16[64,16,1024]{2,1,0:T(8,128)(2,1)} %bitcast.35), calls=%async_computation | async-start | bytes 4194304 | tf_op jit(solution)/shard_map/all_to_all | solution.py:287
  92.2 35.1 %all-to-all-start.1 = ((bf16[64,16,512]{2,1,0:T(8,128)(2,1)}), bf16[64,16,512]{2,1,0:T(8,128)(2,1)S(1)}, u32[]{:S(2)}, u32[]{:S(2)}) async-start(bf16[64,16,512]{2,1,0:T(8,128)(2,1)} %bitcast.39), calls=%async_computation.1 | async-start | bytes 2097152 | tf_op jit(solution)/shard_map/all_to_all | solution.py:302
  128.6 8.0 %collective-permute-start.2 = (bf16[256,512]{1,0:T(8,128)(2,1)S(1)}, bf16[256,512]{1,0:T(8,128)(2,1)S(1)}, u32[]{:S(2)}, u32[]{:S(2)}) collective-permute-start(bf16[256,512]{1,0:T(8,128)(2,1)S(1)} %broadcast_select_fusion), channel_id=1, source_target_pairs={{0,3},{1,0},{2,1},{3,2},{4,7},{5,4},{6,5},{7,6},{8,11},{9,8},{10,9... | collective-permute-start | bytes 786440 | tf_op jit(solution)/shard_map/ppermute | solution.py:320
  133.9 15.7 %collective-permute-start.1 = (bf16[256,512]{1,0:T(8,128)(2,1)S(1)}, bf16[256,512]{1,0:T(8,128)(2,1)S(1)}, u32[]{:S(2)}, u32[]{:S(2)}) collective-permute-start(bf16[256,512]{1,0:T(8,128)(2,1)S(1)} %broadcast_select_fusion), channel_id=1, source_target_pairs={{0,2},{1,3},{2,0},{3,1},{4,6},{5,7},{6,4},{7,5},{8,10},{9,11},{10,... | collective-permute-start | bytes 786440 | tf_op jit(solution)/shard_map/ppermute | solution.py:320
  134.3 15.0 %collective-permute-start = (bf16[256,512]{1,0:T(8,128)(2,1)S(1)}, bf16[256,512]{1,0:T(8,128)(2,1)S(1)}, u32[]{:S(2)}, u32[]{:S(2)}) collective-permute-start(bf16[256,512]{1,0:T(8,128)(2,1)S(1)} %broadcast_select_fusion), channel_id=1, source_target_pairs={{0,1},{1,2},{2,3},{3,0},{4,5},{5,6},{6,7},{7,4},{8,9},{9,10},{10,1... | collective-permute-start | bytes 786440 | tf_op jit(solution)/shard_map/ppermute | solution.py:320

commit v10 on v9

--- a/solution.py
+++ b/solution.py
@@ -216,7 +216,7 @@
 
 def attend(qkv_slot, query_pos, key_pos, q_width, k_width, head_dim):
     rows = qkv_slot.shape[0]
-    blocks = 4
+    blocks = 8
     heads = q_width // head_dim
     causal_pairs = blocks * (blocks + 1) // 2
     pair_flops = 4 * (rows // blocks) ** 2 * head_dim

time: 152 us -> 156 us (1.026)
  Pallas kernels: 18.5 us -> 22.6 us
    pallas_call x1, Pallas kernels: 10.4 us -> 14.6 us  [attend(): pl.pallas_call(lambda *refs: attention_kernel(*refs, q_width=q_width, k_w...]
where the time goes in v10:
time: 156 us
  waiting for transfers between devices  80.4 us (52%)
  starting transfers between devices  24.1 us (15%)
  Pallas kernels  22.6 us (14%)
  local copies, waits for them, and re-layouts  14.9 us (10%)
  other arithmetic  9.59 us (6%)
  between operations  2.81 us (2%)
    all_to_all x1, waiting for transfers between devices, on_device(): lax.all_to_all(picked.reshape(devices, capacity, picked.shape[1]), 'req',...  44.9 us
    all_to_all x1, waiting for transfers between devices, on_device(): lax.all_to_all(mixture.reshape(capacity, devices, mixture.shape[1]).trans...  21.8 us
    pallas_call x1, Pallas kernels, attend(): pl.pallas_call(lambda *refs: attention_kernel(*refs, q_width=q_width, k_w...  14.6 us
    ppermute x3, waiting for transfers between devices, on_device(): lax.ppermute(attended, 'tp', perm=[(i, (i + shift) % tp_size) for i in ra...  13.7 us
    all_to_all x1, starting transfers between devices, on_device(): lax.all_to_all(picked.reshape(devices, capacity, picked.shape[1]), 'req',...  13.3 us
    pallas_call x1, Pallas kernels, prepare(): pl.pallas_call(lambda *refs: prep_kernel(*refs, head_dim=head_dim, capaci...  8.02 us
    all_to_all x1, starting transfers between devices, on_device(): lax.all_to_all(mixture.reshape(capacity, devices, mixture.shape[1]).trans...  6.95 us
    all_to_all x1, local copies, waits for them, and re-layouts, on_device(): lax.all_to_all(picked.reshape(devices, capacity, picked.shape[1]), 'req',...  4.09 us
  transfers between devices with their start and end apart: 5, of which 4 were waited for; matrix products, arithmetic and copies ran while one was open for 8% of the time, Pallas kernels for 0%

profile of v10, /device:TPU:1, one launch (start us, length us, event | category | flops | bytes accessed | tf_op | source)
XLA Modules:
  0.0 155.5 jit_solution(3126093305635509758)
XLA Ops:
  0.6 0.0 copy-start
  0.7 0.1 compare_select_fusion.9
  0.7 0.9 copy.28
  1.6 0.1 reduce-window.8
  1.7 0.1 reduce
  1.8 0.7 sub.52
  2.5 0.1 convert_reduce_fusion
  2.6 0.1 select_reduce_fusion
  2.7 1.2 fusion.9
  3.9 8.0 %shard_map.113 = bf16[1024,1024]{1,0:T(8,128)(2,1)} custom-call(s32[64]{0:T(128)} %refs_0_.1, s32[64]{0:T(128)} %refs_1_.1, s32[1]{0:T(128)} %bitcast.refs_2_, bf16[256,2048]{1,0:T(8,128)(2,1)} %refs_3_.1, bf16[2048]{0:T(1024)(128)(2,1)} %refs_4_.1, bf16[2048,512]{1,0:T(8,128)(2,1)} %refs_5_.1, bf16[2048,256]{1,0:T(8,128)(2,1)} %refs_6_.1, ...), custom_call_target="tpu_custom_call" | custom-call | flops 1610612736 | bytes 7340032 | tf_op jit(solution)/shard_map/pallas_call | solution.py:154
  12.0 0.0 copy-start.1
  12.0 13.3 %all-to-all-start = ((bf16[64,16,1024]{2,1,0:T(8,128)(2,1)}), bf16[64,16,1024]{2,1,0:T(8,128)(2,1)}, u32[]{:S(2)}, u32[]{:S(2)}) async-start(bf16[64,16,1024]{2,1,0:T(8,128)(2,1)} %bitcast.35), calls=%async_computation | async-start | bytes 4194304 | tf_op jit(solution)/shard_map/all_to_all | solution.py:287
  25.3 0.0 copy-done.1
  25.3 0.0 copy-done.2
  25.3 0.2 select_reduce_fusion.1
  25.5 0.7 dynamic_slice.27
  26.2 0.6 and_select_fusion.1
  26.8 0.1 broadcast_add_fusion
  26.9 0.1 add.191
  27.0 1.3 add.210.refs_1_
  28.2 0.6 dynamic_slice.28
  28.8 1.2 compare_select_fusion.refs_2_
  30.1 44.9 %all-to-all-done = bf16[64,16,1024]{2,1,0:T(8,128)(2,1)} async-done(((bf16[64,16,1024]{2,1,0:T(8,128)(2,1)}), bf16[64,16,1024]{2,1,0:T(8,128)(2,1)}, u32[]{:S(2)}, u32[]{:S(2)}) %all-to-all-start) | async-done | bytes 2097184 | tf_op jit(solution)/shard_map/all_to_all | solution.py:287
  74.9 4.1 %copy.37 = bf16[64,16,1024]{2,0,1:T(8,128)(2,1)} copy(bf16[64,16,1024]{2,1,0:T(8,128)(2,1)} %all-to-all-done) | data formatting | bytes 4194304 | tf_op jit(solution)/shard_map/all_to_all | solution.py:287
  79.0 14.6 %shard_map.114 = bf16[1024,512]{1,0:T(8,128)(2,1)} custom-call(bf16[1024,1024]{1,0:T(8,128)(2,1)} %bitcast.36, s32[1024,1]{1,0:T(8,128)} %add.210.refs_1_, s32[1,1024]{1,0:T(1,128)} %compare_select_fusion.refs_2_), custom_call_target="tpu_custom_call" | custom-call | flops 1207959552 | bytes 3145728 | tf_op jit(solution)/shard_map/pallas_call | solution.py:224
  93.6 2.8 %copy.36 = bf16[16,64,512]{2,0,1:T(8,128)(2,1)} copy(bf16[16,64,512]{2,1,0:T(8,128)(2,1)} %bitcast.40) | data formatting | bytes 2097152 | tf_op jit(solution)/shard_map/reshape | solution.py:303
  96.4 6.9 %all-to-all-start.1 = ((bf16[64,16,512]{2,1,0:T(8,128)(2,1)}), bf16[64,16,512]{2,1,0:T(8,128)(2,1)S(1)}, u32[]{:S(2)}, u32[]{:S(2)}) async-start(bf16[64,16,512]{2,1,0:T(8,128)(2,1)} %bitcast.39), calls=%async_computation.1 | async-start | bytes 2097152 | tf_op jit(solution)/shard_map/all_to_all | solution.py:302
  105.3 1.0 scatter_custom_fusion
  106.4 0.1 multiply_reduce_fusion
  106.5 1.3 slice.14
  107.8 0.8 fusion.2
  108.6 1.1 slice_bitcast_fusion.1
  109.7 21.8 %all-to-all-done.1 = bf16[64,16,512]{2,1,0:T(8,128)(2,1)S(1)} async-done(((bf16[64,16,512]{2,1,0:T(8,128)(2,1)}), bf16[64,16,512]{2,1,0:T(8,128)(2,1)S(1)}, u32[]{:S(2)}, u32[]{:S(2)}) %all-to-all-start.1) | async-done | bytes 1048608 | tf_op jit(solution)/shard_map/all_to_all | solution.py:302
  131.5 1.2 gather_fusion
  132.7 0.1 broadcast_select_fusion
  132.8 2.8 %collective-permute-start.2 = (bf16[256,512]{1,0:T(8,128)(2,1)S(1)}, bf16[256,512]{1,0:T(8,128)(2,1)S(1)}, u32[]{:S(2)}, u32[]{:S(2)}) collective-permute-start(bf16[256,512]{1,0:T(8,128)(2,1)S(1)} %broadcast_select_fusion), channel_id=1, source_target_pairs={{0,3},{1,0},{2,1},{3,2},{4,7},{5,4},{6,5},{7,6},{8,11},{9,8},{10,9... | collective-permute-start | bytes 786440 | tf_op jit(solution)/shard_map/ppermute | solution.py:320
  135.6 2.3 %maximum_bitcast_fusion = bf16[2,1,1024,256]{3,2,1,0:T(8,128)(2,1)} fusion(bf16[1,1024,256]{2,1,0:T(8,128)(2,1)} %get-tuple-element.21, bf16[1,1024,256]{2,1,0:T(8,128)(2,1)} %get-tuple-element.20), kind=kLoop, calls=%fused_computation.9 | loop fusion | flops 524288 | bytes 2097152
  137.8 0.4 collective-permute-start.1
  138.2 0.7 collective-permute-start
  138.9 0.0 copy-done
  138.9 0.3 fusion.7
  139.2 1.4 collective-permute-done.2
  140.6 0.3 fusion.3
  140.9 12.3 %collective-permute-done = bf16[256,512]{1,0:T(8,128)(2,1)S(1)} collective-permute-done((bf16[256,512]{1,0:T(8,128)(2,1)S(1)}, bf16[256,512]{1,0:T(8,128)(2,1)S(1)}, u32[]{:S(2)}, u32[]{:S(2)}) %collective-permute-start) | collective-permute-done | bytes 262176 | tf_op jit(solution)/shard_map/ppermute | solution.py:320
  153.2 0.3 convolution_add_fusion.1
  153.5 0.0 collective-permute-done.1
  153.5 0.3 fusion.1
  153.8 1.7 %add_convert_fusion = bf16[256,512]{1,0:T(8,128)(2,1)} fusion(bf16[256,512]{1,0:T(8,128)(2,1)S(1)} %fusion.1, bf16[256,2048]{1,0:T(8,128)(2,1)} %refs_3_.1, s32[]{:T(128)S(6)} %select_n.117), kind=kLoop, calls=%fused_computation.13 | loop fusion | flops 524288 | bytes 786436 | tf_op jit(solution)/shard_map/convert_element_type | solution.py:331
  (12 shorter events, 0.1 us)
Async XLA Ops:
  0.6 138.2 %copy-start = (bf16[2048,512]{1,0:T(8,128)(2,1)S(1)}, bf16[2048,512]{1,0:T(8,128)(2,1)}, u32[]{:S(2)}) copy-start(bf16[2048,512]{1,0:T(8,128)(2,1)} %param.19) | copy-start | bytes 6291460
  12.0 13.3 %copy-start.1 = (s32[64]{0:T(128)S(1)}, s32[64]{0:T(128)}, u32[]{:S(2)}) copy-start(s32[64]{0:T(128)} %refs_0_.1) | copy-start | bytes 772
  12.0 13.3 %copy-start.2 = (s32[64]{0:T(128)S(1)}, s32[64]{0:T(128)}, u32[]{:S(2)}) copy-start(s32[64]{0:T(128)} %refs_1_.1) | copy-start | bytes 772
  12.0 62.9 %all-to-all-start = ((bf16[64,16,1024]{2,1,0:T(8,128)(2,1)}), bf16[64,16,1024]{2,1,0:T(8,128)(2,1)}, u32[]{:S(2)}, u32[]{:S(2)}) async-start(bf16[64,16,1024]{2,1,0:T(8,128)(2,1)} %bitcast.35), calls=%async_computation | async-start | bytes 4194304 | tf_op jit(solution)/shard_map/all_to_all | solution.py:287
  96.4 35.1 %all-to-all-start.1 = ((bf16[64,16,512]{2,1,0:T(8,128)(2,1)}), bf16[64,16,512]{2,1,0:T(8,128)(2,1)S(1)}, u32[]{:S(2)}, u32[]{:S(2)}) async-start(bf16[64,16,512]{2,1,0:T(8,128)(2,1)} %bitcast.39), calls=%async_computation.1 | async-start | bytes 2097152 | tf_op jit(solution)/shard_map/all_to_all | solution.py:302
  132.8 7.8 %collective-permute-start.2 = (bf16[256,512]{1,0:T(8,128)(2,1)S(1)}, bf16[256,512]{1,0:T(8,128)(2,1)S(1)}, u32[]{:S(2)}, u32[]{:S(2)}) collective-permute-start(bf16[256,512]{1,0:T(8,128)(2,1)S(1)} %broadcast_select_fusion), channel_id=1, source_target_pairs={{0,3},{1,0},{2,1},{3,2},{4,7},{5,4},{6,5},{7,6},{8,11},{9,8},{10,9... | collective-permute-start | bytes 786440 | tf_op jit(solution)/shard_map/ppermute | solution.py:320
  137.8 15.7 %collective-permute-start.1 = (bf16[256,512]{1,0:T(8,128)(2,1)S(1)}, bf16[256,512]{1,0:T(8,128)(2,1)S(1)}, u32[]{:S(2)}, u32[]{:S(2)}) collective-permute-start(bf16[256,512]{1,0:T(8,128)(2,1)S(1)} %broadcast_select_fusion), channel_id=1, source_target_pairs={{0,2},{1,3},{2,0},{3,1},{4,6},{5,7},{6,4},{7,5},{8,10},{9,11},{10,... | collective-permute-start | bytes 786440 | tf_op jit(solution)/shard_map/ppermute | solution.py:320
  138.2 15.0 %collective-permute-start = (bf16[256,512]{1,0:T(8,128)(2,1)S(1)}, bf16[256,512]{1,0:T(8,128)(2,1)S(1)}, u32[]{:S(2)}, u32[]{:S(2)}) collective-permute-start(bf16[256,512]{1,0:T(8,128)(2,1)S(1)} %broadcast_select_fusion), channel_id=1, source_target_pairs={{0,1},{1,2},{2,3},{3,0},{4,5},{5,6},{6,7},{7,4},{8,9},{9,10},{10,1... | collective-permute-start | bytes 786440 | tf_op jit(solution)/shard_map/ppermute | solution.py:320

commit v11 on v10

--- a/solution.py
+++ b/solution.py
@@ -216,7 +216,7 @@
 
 def attend(qkv_slot, query_pos, key_pos, q_width, k_width, head_dim):
     rows = qkv_slot.shape[0]
-    blocks = 8
+    blocks = 2
     heads = q_width // head_dim
     causal_pairs = blocks * (blocks + 1) // 2
     pair_flops = 4 * (rows // blocks) ** 2 * head_dim

time: 156 us -> 151 us (0.968)
  Pallas kernels: 22.6 us -> 17.1 us
    pallas_call x1, Pallas kernels: 14.6 us -> 9.07 us  [attend(): pl.pallas_call(lambda *refs: attention_kernel(*refs, q_width=q_width, k_w...]
where the time goes in v11:
time: 151 us; the launch traced here: 150 us
  waiting for transfers between devices  80.6 us (53%)
  starting transfers between devices  24.1 us (16%)
  Pallas kernels  17.1 us (11%)
  local copies, waits for them, and re-layouts  14.6 us (10%)
  other arithmetic  9.59 us (6%)
  between operations  2.81 us (2%)
    all_to_all x1, waiting for transfers between devices, on_device(): lax.all_to_all(picked.reshape(devices, capacity, picked.shape[1]), 'req',...  44.9 us
    all_to_all x1, waiting for transfers between devices, on_device(): lax.all_to_all(mixture.reshape(capacity, devices, mixture.shape[1]).trans...  22 us
    ppermute x3, waiting for transfers between devices, on_device(): lax.ppermute(attended, 'tp', perm=[(i, (i + shift) % tp_size) for i in ra...  13.7 us
    all_to_all x1, starting transfers between devices, on_device(): lax.all_to_all(picked.reshape(devices, capacity, picked.shape[1]), 'req',...  13.3 us
    pallas_call x1, Pallas kernels, attend(): pl.pallas_call(lambda *refs: attention_kernel(*refs, q_width=q_width, k_w...  9.07 us
    pallas_call x1, Pallas kernels, prepare(): pl.pallas_call(lambda *refs: prep_kernel(*refs, head_dim=head_dim, capaci...  8.02 us
    all_to_all x1, starting transfers between devices, on_device(): lax.all_to_all(mixture.reshape(capacity, devices, mixture.shape[1]).trans...  6.96 us
    all_to_all x1, local copies, waits for them, and re-layouts, on_device(): lax.all_to_all(picked.reshape(devices, capacity, picked.shape[1]), 'req',...  4.09 us
  transfers between devices with their start and end apart: 5, of which 4 were waited for; matrix products, arithmetic and copies ran while one was open for 8% of the time, Pallas kernels for 0%

profile of v11, /device:TPU:1, one launch (start us, length us, event | category | flops | bytes accessed | tf_op | source)
XLA Modules:
  0.0 150.0 jit_solution(4549538282619270589)
XLA Ops:
  0.6 0.0 copy-start
  0.7 0.1 compare_select_fusion.9
  0.7 0.9 copy.28
  1.6 0.1 reduce-window.8
  1.7 0.1 reduce
  1.8 0.7 sub.52
  2.5 0.1 convert_reduce_fusion
  2.6 0.1 select_reduce_fusion
  2.7 1.2 fusion.9
  3.9 8.0 %shard_map.113 = bf16[1024,1024]{1,0:T(8,128)(2,1)} custom-call(s32[64]{0:T(128)} %refs_0_.1, s32[64]{0:T(128)} %refs_1_.1, s32[1]{0:T(128)} %bitcast.refs_2_, bf16[256,2048]{1,0:T(8,128)(2,1)} %refs_3_.1, bf16[2048]{0:T(1024)(128)(2,1)} %refs_4_.1, bf16[2048,512]{1,0:T(8,128)(2,1)} %refs_5_.1, bf16[2048,256]{1,0:T(8,128)(2,1)} %refs_6_.1, ...), custom_call_target="tpu_custom_call" | custom-call | flops 1610612736 | bytes 7340032 | tf_op jit(solution)/shard_map/pallas_call | solution.py:154
  12.0 0.0 copy-start.1
  12.0 13.3 %all-to-all-start = ((bf16[64,16,1024]{2,1,0:T(8,128)(2,1)}), bf16[64,16,1024]{2,1,0:T(8,128)(2,1)}, u32[]{:S(2)}, u32[]{:S(2)}) async-start(bf16[64,16,1024]{2,1,0:T(8,128)(2,1)} %bitcast.35), calls=%async_computation | async-start | bytes 4194304 | tf_op jit(solution)/shard_map/all_to_all | solution.py:287
  25.3 0.0 copy-done.1
  25.3 0.0 copy-done.2
  25.3 0.2 select_reduce_fusion.1
  25.5 0.7 dynamic_slice.27
  26.2 0.6 and_select_fusion.1
  26.8 0.1 broadcast_add_fusion
  26.9 0.1 add.191
  27.0 1.3 add.210.refs_1_
  28.2 0.6 dynamic_slice.28
  28.8 1.2 compare_select_fusion.refs_2_
  30.1 44.9 %all-to-all-done = bf16[64,16,1024]{2,1,0:T(8,128)(2,1)} async-done(((bf16[64,16,1024]{2,1,0:T(8,128)(2,1)}), bf16[64,16,1024]{2,1,0:T(8,128)(2,1)}, u32[]{:S(2)}, u32[]{:S(2)}) %all-to-all-start) | async-done | bytes 2097184 | tf_op jit(solution)/shard_map/all_to_all | solution.py:287
  74.9 4.1 %copy.37 = bf16[64,16,1024]{2,0,1:T(8,128)(2,1)} copy(bf16[64,16,1024]{2,1,0:T(8,128)(2,1)} %all-to-all-done) | data formatting | bytes 4194304 | tf_op jit(solution)/shard_map/all_to_all | solution.py:287
  79.0 9.1 %shard_map.114 = bf16[1024,512]{1,0:T(8,128)(2,1)} custom-call(bf16[1024,1024]{1,0:T(8,128)(2,1)} %bitcast.36, s32[1024,1]{1,0:T(8,128)} %add.210.refs_1_, s32[1,1024]{1,0:T(1,128)} %compare_select_fusion.refs_2_), custom_call_target="tpu_custom_call" | custom-call | flops 1610612736 | bytes 3145728 | tf_op jit(solution)/shard_map/pallas_call | solution.py:224
  88.1 2.8 %copy.36 = bf16[16,64,512]{2,0,1:T(8,128)(2,1)} copy(bf16[16,64,512]{2,1,0:T(8,128)(2,1)} %bitcast.40) | data formatting | bytes 2097152 | tf_op jit(solution)/shard_map/reshape | solution.py:303
  90.9 7.0 %all-to-all-start.1 = ((bf16[64,16,512]{2,1,0:T(8,128)(2,1)}), bf16[64,16,512]{2,1,0:T(8,128)(2,1)S(1)}, u32[]{:S(2)}, u32[]{:S(2)}) async-start(bf16[64,16,512]{2,1,0:T(8,128)(2,1)} %bitcast.39), calls=%async_computation.1 | async-start | bytes 2097152 | tf_op jit(solution)/shard_map/all_to_all | solution.py:302
  99.9 0.8 scatter_custom_fusion
  100.6 0.1 multiply_reduce_fusion
  100.8 1.3 slice.14
  102.1 0.8 fusion.2
  102.9 1.1 slice_bitcast_fusion.1
  104.0 22.0 %all-to-all-done.1 = bf16[64,16,512]{2,1,0:T(8,128)(2,1)S(1)} async-done(((bf16[64,16,512]{2,1,0:T(8,128)(2,1)}), bf16[64,16,512]{2,1,0:T(8,128)(2,1)S(1)}, u32[]{:S(2)}, u32[]{:S(2)}) %all-to-all-start.1) | async-done | bytes 1048608 | tf_op jit(solution)/shard_map/all_to_all | solution.py:302
  126.0 1.2 gather_fusion
  127.2 0.1 broadcast_select_fusion
  127.3 2.8 %collective-permute-start.2 = (bf16[256,512]{1,0:T(8,128)(2,1)S(1)}, bf16[256,512]{1,0:T(8,128)(2,1)S(1)}, u32[]{:S(2)}, u32[]{:S(2)}) collective-permute-start(bf16[256,512]{1,0:T(8,128)(2,1)S(1)} %broadcast_select_fusion), channel_id=1, source_target_pairs={{0,3},{1,0},{2,1},{3,2},{4,7},{5,4},{6,5},{7,6},{8,11},{9,8},{10,9... | collective-permute-start | bytes 786440 | tf_op jit(solution)/shard_map/ppermute | solution.py:320
  130.1 2.3 %maximum_bitcast_fusion = bf16[2,1,1024,256]{3,2,1,0:T(8,128)(2,1)} fusion(bf16[1,1024,256]{2,1,0:T(8,128)(2,1)} %get-tuple-element.21, bf16[1,1024,256]{2,1,0:T(8,128)(2,1)} %get-tuple-element.20), kind=kLoop, calls=%fused_computation.9 | loop fusion | flops 524288 | bytes 2097152
  132.3 0.4 collective-permute-start.1
  132.7 0.7 collective-permute-start
  133.4 0.0 copy-done
  133.4 0.3 fusion.7
  133.7 1.4 collective-permute-done.2
  135.1 0.3 fusion.3
  135.4 12.3 %collective-permute-done = bf16[256,512]{1,0:T(8,128)(2,1)S(1)} collective-permute-done((bf16[256,512]{1,0:T(8,128)(2,1)S(1)}, bf16[256,512]{1,0:T(8,128)(2,1)S(1)}, u32[]{:S(2)}, u32[]{:S(2)}) %collective-permute-start) | collective-permute-done | bytes 262176 | tf_op jit(solution)/shard_map/ppermute | solution.py:320
  147.7 0.3 convolution_add_fusion.1
  148.0 0.0 collective-permute-done.1
  148.0 0.3 fusion.1
  148.3 1.7 %add_convert_fusion = bf16[256,512]{1,0:T(8,128)(2,1)} fusion(bf16[256,512]{1,0:T(8,128)(2,1)S(1)} %fusion.1, bf16[256,2048]{1,0:T(8,128)(2,1)} %refs_3_.1, s32[]{:T(128)S(6)} %select_n.117), kind=kLoop, calls=%fused_computation.13 | loop fusion | flops 524288 | bytes 786436 | tf_op jit(solution)/shard_map/convert_element_type | solution.py:331
  (12 shorter events, 0.1 us)
Async XLA Ops:
  0.6 132.7 %copy-start = (bf16[2048,512]{1,0:T(8,128)(2,1)S(1)}, bf16[2048,512]{1,0:T(8,128)(2,1)}, u32[]{:S(2)}) copy-start(bf16[2048,512]{1,0:T(8,128)(2,1)} %param.19) | copy-start | bytes 6291460
  12.0 13.3 %copy-start.1 = (s32[64]{0:T(128)S(1)}, s32[64]{0:T(128)}, u32[]{:S(2)}) copy-start(s32[64]{0:T(128)} %refs_0_.1) | copy-start | bytes 772
  12.0 13.3 %copy-start.2 = (s32[64]{0:T(128)S(1)}, s32[64]{0:T(128)}, u32[]{:S(2)}) copy-start(s32[64]{0:T(128)} %refs_1_.1) | copy-start | bytes 772
  12.0 62.9 %all-to-all-start = ((bf16[64,16,1024]{2,1,0:T(8,128)(2,1)}), bf16[64,16,1024]{2,1,0:T(8,128)(2,1)}, u32[]{:S(2)}, u32[]{:S(2)}) async-start(bf16[64,16,1024]{2,1,0:T(8,128)(2,1)} %bitcast.35), calls=%async_computation | async-start | bytes 4194304 | tf_op jit(solution)/shard_map/all_to_all | solution.py:287
  90.9 35.1 %all-to-all-start.1 = ((bf16[64,16,512]{2,1,0:T(8,128)(2,1)}), bf16[64,16,512]{2,1,0:T(8,128)(2,1)S(1)}, u32[]{:S(2)}, u32[]{:S(2)}) async-start(bf16[64,16,512]{2,1,0:T(8,128)(2,1)} %bitcast.39), calls=%async_computation.1 | async-start | bytes 2097152 | tf_op jit(solution)/shard_map/all_to_all | solution.py:302
  127.3 7.8 %collective-permute-start.2 = (bf16[256,512]{1,0:T(8,128)(2,1)S(1)}, bf16[256,512]{1,0:T(8,128)(2,1)S(1)}, u32[]{:S(2)}, u32[]{:S(2)}) collective-permute-start(bf16[256,512]{1,0:T(8,128)(2,1)S(1)} %broadcast_select_fusion), channel_id=1, source_target_pairs={{0,3},{1,0},{2,1},{3,2},{4,7},{5,4},{6,5},{7,6},{8,11},{9,8},{10,9... | collective-permute-start | bytes 786440 | tf_op jit(solution)/shard_map/ppermute | solution.py:320
  132.3 15.7 %collective-permute-start.1 = (bf16[256,512]{1,0:T(8,128)(2,1)S(1)}, bf16[256,512]{1,0:T(8,128)(2,1)S(1)}, u32[]{:S(2)}, u32[]{:S(2)}) collective-permute-start(bf16[256,512]{1,0:T(8,128)(2,1)S(1)} %broadcast_select_fusion), channel_id=1, source_target_pairs={{0,2},{1,3},{2,0},{3,1},{4,6},{5,7},{6,4},{7,5},{8,10},{9,11},{10,... | collective-permute-start | bytes 786440 | tf_op jit(solution)/shard_map/ppermute | solution.py:320
  132.7 15.0 %collective-permute-start = (bf16[256,512]{1,0:T(8,128)(2,1)S(1)}, bf16[256,512]{1,0:T(8,128)(2,1)S(1)}, u32[]{:S(2)}, u32[]{:S(2)}) collective-permute-start(bf16[256,512]{1,0:T(8,128)(2,1)S(1)} %broadcast_select_fusion), channel_id=1, source_target_pairs={{0,1},{1,2},{2,3},{3,0},{4,5},{5,6},{6,7},{7,4},{8,9},{9,10},{10,1... | collective-permute-start | bytes 786440 | tf_op jit(solution)/shard_map/ppermute | solution.py:320

commit v12 on v11

--- a/solution.py
+++ b/solution.py
@@ -216,7 +216,7 @@
 
 def attend(qkv_slot, query_pos, key_pos, q_width, k_width, head_dim):
     rows = qkv_slot.shape[0]
-    blocks = 2
+    blocks = 1
     heads = q_width // head_dim
     causal_pairs = blocks * (blocks + 1) // 2
     pair_flops = 4 * (rows // blocks) ** 2 * head_dim

time: 151 us -> 153 us (1.013)
  Pallas kernels: 17.1 us -> 19.1 us
    pallas_call x1, Pallas kernels: 9.07 us -> 11 us  [attend(): pl.pallas_call(lambda *refs: attention_kernel(*refs, q_width=q_width, k_w...]
where the time goes in v12:
time: 153 us; the launch traced here: 152 us
  waiting for transfers between devices  80.4 us (53%)
  starting transfers between devices  24.1 us (16%)
  Pallas kernels  19.1 us (12%)
  local copies, waits for them, and re-layouts  14.9 us (10%)
  other arithmetic  9.6 us (6%)
  between operations  2.81 us (2%)
    all_to_all x1, waiting for transfers between devices, on_device(): lax.all_to_all(picked.reshape(devices, capacity, picked.shape[1]), 'req',...  44.9 us
    all_to_all x1, waiting for transfers between devices, on_device(): lax.all_to_all(mixture.reshape(capacity, devices, mixture.shape[1]).trans...  21.8 us
    ppermute x3, waiting for transfers between devices, on_device(): lax.ppermute(attended, 'tp', perm=[(i, (i + shift) % tp_size) for i in ra...  13.7 us
    all_to_all x1, starting transfers between devices, on_device(): lax.all_to_all(picked.reshape(devices, capacity, picked.shape[1]), 'req',...  13.3 us
    pallas_call x1, Pallas kernels, attend(): pl.pallas_call(lambda *refs: attention_kernel(*refs, q_width=q_width, k_w...  11 us
    pallas_call x1, Pallas kernels, prepare(): pl.pallas_call(lambda *refs: prep_kernel(*refs, head_dim=head_dim, capaci...  8.02 us
    all_to_all x1, starting transfers between devices, on_device(): lax.all_to_all(mixture.reshape(capacity, devices, mixture.shape[1]).trans...  6.96 us
    all_to_all x1, local copies, waits for them, and re-layouts, on_device(): lax.all_to_all(picked.reshape(devices, capacity, picked.shape[1]), 'req',...  4.09 us
  transfers between devices with their start and end apart: 5, of which 4 were waited for; matrix products, arithmetic and copies ran while one was open for 8% of the time, Pallas kernels for 0%

profile of v12, /device:TPU:1, one launch (start us, length us, event | category | flops | bytes accessed | tf_op | source)
XLA Modules:
  0.0 152.0 jit_solution(9545126774833597826)
XLA Ops:
  0.6 0.0 copy-start
  0.7 0.1 compare_select_fusion.9
  0.7 0.9 copy.28
  1.6 0.1 reduce-window.8
  1.7 0.1 reduce
  1.8 0.7 sub.52
  2.5 0.1 convert_reduce_fusion
  2.6 0.1 select_reduce_fusion
  2.7 1.2 fusion.9
  3.9 8.0 %shard_map.113 = bf16[1024,1024]{1,0:T(8,128)(2,1)} custom-call(s32[64]{0:T(128)} %refs_0_.1, s32[64]{0:T(128)} %refs_1_.1, s32[1]{0:T(128)} %bitcast.refs_2_, bf16[256,2048]{1,0:T(8,128)(2,1)} %refs_3_.1, bf16[2048]{0:T(1024)(128)(2,1)} %refs_4_.1, bf16[2048,512]{1,0:T(8,128)(2,1)} %refs_5_.1, bf16[2048,256]{1,0:T(8,128)(2,1)} %refs_6_.1, ...), custom_call_target="tpu_custom_call" | custom-call | flops 1610612736 | bytes 7340032 | tf_op jit(solution)/shard_map/pallas_call | solution.py:154
  12.0 0.0 copy-start.1
  12.0 13.3 %all-to-all-start = ((bf16[64,16,1024]{2,1,0:T(8,128)(2,1)}), bf16[64,16,1024]{2,1,0:T(8,128)(2,1)}, u32[]{:S(2)}, u32[]{:S(2)}) async-start(bf16[64,16,1024]{2,1,0:T(8,128)(2,1)} %bitcast.35), calls=%async_computation | async-start | bytes 4194304 | tf_op jit(solution)/shard_map/all_to_all | solution.py:287
  25.3 0.0 copy-done.1
  25.3 0.0 copy-done.2
  25.3 0.2 select_reduce_fusion.1
  25.5 0.7 dynamic_slice.27
  26.2 0.6 and_select_fusion.1
  26.8 0.1 broadcast_add_fusion
  26.9 0.1 add.191
  27.0 1.3 add.210.refs_1_
  28.2 0.6 dynamic_slice.28
  28.8 1.2 compare_select_fusion.refs_2_
  30.1 44.9 %all-to-all-done = bf16[64,16,1024]{2,1,0:T(8,128)(2,1)} async-done(((bf16[64,16,1024]{2,1,0:T(8,128)(2,1)}), bf16[64,16,1024]{2,1,0:T(8,128)(2,1)}, u32[]{:S(2)}, u32[]{:S(2)}) %all-to-all-start) | async-done | bytes 2097184 | tf_op jit(solution)/shard_map/all_to_all | solution.py:287
  74.9 4.1 %copy.37 = bf16[64,16,1024]{2,0,1:T(8,128)(2,1)} copy(bf16[64,16,1024]{2,1,0:T(8,128)(2,1)} %all-to-all-done) | data formatting | bytes 4194304 | tf_op jit(solution)/shard_map/all_to_all | solution.py:287
  79.0 11.0 %shard_map.114 = bf16[1024,512]{1,0:T(8,128)(2,1)} custom-call(bf16[1024,1024]{1,0:T(8,128)(2,1)} %bitcast.36, s32[1024,1]{1,0:T(8,128)} %add.210.refs_1_, s32[1,1024]{1,0:T(1,128)} %compare_select_fusion.refs_2_), custom_call_target="tpu_custom_call" | custom-call | flops 2147483648 | bytes 3145728 | tf_op jit(solution)/shard_map/pallas_call | solution.py:224
  90.0 2.8 %copy.36 = bf16[16,64,512]{2,0,1:T(8,128)(2,1)} copy(bf16[16,64,512]{2,1,0:T(8,128)(2,1)} %bitcast.40) | data formatting | bytes 2097152 | tf_op jit(solution)/shard_map/reshape | solution.py:303
  92.8 7.0 %all-to-all-start.1 = ((bf16[64,16,512]{2,1,0:T(8,128)(2,1)}), bf16[64,16,512]{2,1,0:T(8,128)(2,1)S(1)}, u32[]{:S(2)}, u32[]{:S(2)}) async-start(bf16[64,16,512]{2,1,0:T(8,128)(2,1)} %bitcast.39), calls=%async_computation.1 | async-start | bytes 2097152 | tf_op jit(solution)/shard_map/all_to_all | solution.py:302
  101.8 1.0 scatter_custom_fusion
  102.8 0.1 multiply_reduce_fusion
  103.0 1.3 slice.14
  104.3 0.8 fusion.2
  105.1 1.1 slice_bitcast_fusion.1
  106.2 21.8 %all-to-all-done.1 = bf16[64,16,512]{2,1,0:T(8,128)(2,1)S(1)} async-done(((bf16[64,16,512]{2,1,0:T(8,128)(2,1)}), bf16[64,16,512]{2,1,0:T(8,128)(2,1)S(1)}, u32[]{:S(2)}, u32[]{:S(2)}) %all-to-all-start.1) | async-done | bytes 1048608 | tf_op jit(solution)/shard_map/all_to_all | solution.py:302
  128.0 1.2 gather_fusion
  129.1 0.1 broadcast_select_fusion
  129.2 2.8 %collective-permute-start.2 = (bf16[256,512]{1,0:T(8,128)(2,1)S(1)}, bf16[256,512]{1,0:T(8,128)(2,1)S(1)}, u32[]{:S(2)}, u32[]{:S(2)}) collective-permute-start(bf16[256,512]{1,0:T(8,128)(2,1)S(1)} %broadcast_select_fusion), channel_id=1, source_target_pairs={{0,3},{1,0},{2,1},{3,2},{4,7},{5,4},{6,5},{7,6},{8,11},{9,8},{10,9... | collective-permute-start | bytes 786440 | tf_op jit(solution)/shard_map/ppermute | solution.py:320
  132.0 2.3 %maximum_bitcast_fusion = bf16[2,1,1024,256]{3,2,1,0:T(8,128)(2,1)} fusion(bf16[1,1024,256]{2,1,0:T(8,128)(2,1)} %get-tuple-element.21, bf16[1,1024,256]{2,1,0:T(8,128)(2,1)} %get-tuple-element.20), kind=kLoop, calls=%fused_computation.9 | loop fusion | flops 524288 | bytes 2097152
  134.3 0.4 collective-permute-start.1
  134.7 0.7 collective-permute-start
  135.3 0.0 copy-done
  135.3 0.3 fusion.7
  135.6 1.4 collective-permute-done.2
  137.0 0.3 fusion.3
  137.3 12.3 %collective-permute-done = bf16[256,512]{1,0:T(8,128)(2,1)S(1)} collective-permute-done((bf16[256,512]{1,0:T(8,128)(2,1)S(1)}, bf16[256,512]{1,0:T(8,128)(2,1)S(1)}, u32[]{:S(2)}, u32[]{:S(2)}) %collective-permute-start) | collective-permute-done | bytes 262176 | tf_op jit(solution)/shard_map/ppermute | solution.py:320
  149.6 0.3 convolution_add_fusion.1
  150.0 0.0 collective-permute-done.1
  150.0 0.3 fusion.1
  150.3 1.7 %add_convert_fusion = bf16[256,512]{1,0:T(8,128)(2,1)} fusion(bf16[256,512]{1,0:T(8,128)(2,1)S(1)} %fusion.1, bf16[256,2048]{1,0:T(8,128)(2,1)} %refs_3_.1, s32[]{:T(128)S(6)} %select_n.117), kind=kLoop, calls=%fused_computation.13 | loop fusion | flops 524288 | bytes 786436 | tf_op jit(solution)/shard_map/convert_element_type | solution.py:331
  (12 shorter events, 0.1 us)
Async XLA Ops:
  0.6 134.7 %copy-start = (bf16[2048,512]{1,0:T(8,128)(2,1)S(1)}, bf16[2048,512]{1,0:T(8,128)(2,1)}, u32[]{:S(2)}) copy-start(bf16[2048,512]{1,0:T(8,128)(2,1)} %param.19) | copy-start | bytes 6291460
  12.0 13.3 %copy-start.1 = (s32[64]{0:T(128)S(1)}, s32[64]{0:T(128)}, u32[]{:S(2)}) copy-start(s32[64]{0:T(128)} %refs_0_.1) | copy-start | bytes 772
  12.0 13.3 %copy-start.2 = (s32[64]{0:T(128)S(1)}, s32[64]{0:T(128)}, u32[]{:S(2)}) copy-start(s32[64]{0:T(128)} %refs_1_.1) | copy-start | bytes 772
  12.0 62.9 %all-to-all-start = ((bf16[64,16,1024]{2,1,0:T(8,128)(2,1)}), bf16[64,16,1024]{2,1,0:T(8,128)(2,1)}, u32[]{:S(2)}, u32[]{:S(2)}) async-start(bf16[64,16,1024]{2,1,0:T(8,128)(2,1)} %bitcast.35), calls=%async_computation | async-start | bytes 4194304 | tf_op jit(solution)/shard_map/all_to_all | solution.py:287
  92.8 35.1 %all-to-all-start.1 = ((bf16[64,16,512]{2,1,0:T(8,128)(2,1)}), bf16[64,16,512]{2,1,0:T(8,128)(2,1)S(1)}, u32[]{:S(2)}, u32[]{:S(2)}) async-start(bf16[64,16,512]{2,1,0:T(8,128)(2,1)} %bitcast.39), calls=%async_computation.1 | async-start | bytes 2097152 | tf_op jit(solution)/shard_map/all_to_all | solution.py:302
  129.2 7.8 %collective-permute-start.2 = (bf16[256,512]{1,0:T(8,128)(2,1)S(1)}, bf16[256,512]{1,0:T(8,128)(2,1)S(1)}, u32[]{:S(2)}, u32[]{:S(2)}) collective-permute-start(bf16[256,512]{1,0:T(8,128)(2,1)S(1)} %broadcast_select_fusion), channel_id=1, source_target_pairs={{0,3},{1,0},{2,1},{3,2},{4,7},{5,4},{6,5},{7,6},{8,11},{9,8},{10,9... | collective-permute-start | bytes 786440 | tf_op jit(solution)/shard_map/ppermute | solution.py:320
  134.3 15.7 %collective-permute-start.1 = (bf16[256,512]{1,0:T(8,128)(2,1)S(1)}, bf16[256,512]{1,0:T(8,128)(2,1)S(1)}, u32[]{:S(2)}, u32[]{:S(2)}) collective-permute-start(bf16[256,512]{1,0:T(8,128)(2,1)S(1)} %broadcast_select_fusion), channel_id=1, source_target_pairs={{0,2},{1,3},{2,0},{3,1},{4,6},{5,7},{6,4},{7,5},{8,10},{9,11},{10,... | collective-permute-start | bytes 786440 | tf_op jit(solution)/shard_map/ppermute | solution.py:320
  134.7 15.0 %collective-permute-start = (bf16[256,512]{1,0:T(8,128)(2,1)S(1)}, bf16[256,512]{1,0:T(8,128)(2,1)S(1)}, u32[]{:S(2)}, u32[]{:S(2)}) collective-permute-start(bf16[256,512]{1,0:T(8,128)(2,1)S(1)} %broadcast_select_fusion), channel_id=1, source_target_pairs={{0,1},{1,2},{2,3},{3,0},{4,5},{5,6},{6,7},{7,4},{8,9},{9,10},{10,1... | collective-permute-start | bytes 786440 | tf_op jit(solution)/shard_map/ppermute | solution.py:320

commit v13 on v11

--- a/solution.py
+++ b/solution.py
@@ -197,21 +197,25 @@
             v_col = q_width + k_width + h * head_dim
             keys = qkv_ref[:key_rows, k_col : k_col + head_dim]
             values = qkv_ref[:key_rows, v_col : v_col + head_dim]
-            for g in range(group):
-                q_col = (h * group + g) * head_dim
-                queries = qkv_ref[rows_here, q_col : q_col + head_dim]
-                scores = lax.dot_general(
-                    queries,
-                    keys,
-                    (((1,), (1,)), ((), ())),
-                    preferred_element_type=jnp.float32,
-                ) * scale
-                scores = jnp.where(allowed, scores, -jnp.inf)
-                row_max = jnp.max(scores, axis=-1, keepdims=True)
-                weights = jnp.exp(scores - row_max)
-                weights = (weights / jnp.sum(weights, axis=-1, keepdims=True)).astype(jnp.bfloat16)
-                mixed = jnp.dot(weights, values, preferred_element_type=jnp.float32)
-                out_ref[rows_here, q_col : q_col + head_dim] = mixed.astype(out_ref.dtype)
+            q_cols = [(h * group + g) * head_dim for g in range(group)]
+            queries = jnp.concatenate(
+                [qkv_ref[rows_here, c : c + head_dim] for c in q_cols], axis=0
+            )
+            scores = lax.dot_general(
+                queries,
+                keys,
+                (((1,), (1,)), ((), ())),
+                preferred_element_type=jnp.float32,
+            ) * scale
+            scores = jnp.where(jnp.concatenate([allowed] * group, axis=0), scores, -jnp.inf)
+            row_max = jnp.max(scores, axis=-1, keepdims=True)
+            weights = jnp.exp(scores - row_max)
+            weights = (weights / jnp.sum(weights, axis=-1, keepdims=True)).astype(jnp.bfloat16)
+            mixed = jnp.dot(weights, values, preferred_element_type=jnp.float32)
+            for g, c in enumerate(q_cols):
+                out_ref[rows_here, c : c + head_dim] = mixed[g * block : (g + 1) * block].astype(
+                    out_ref.dtype
+                )
 
 
 def attend(qkv_slot, query_pos, key_pos, q_width, k_width, head_dim):

time: 151 us -> 151 us (level)
  no operation moved by 1% of the time
where the time goes in v13:
time: 151 us
  waiting for transfers between devices  80.6 us (53%)
  starting transfers between devices  24.3 us (16%)
  Pallas kernels  17.6 us (12%)
  local copies, waits for them, and re-layouts  14.6 us (10%)
  other arithmetic  9.59 us (6%)
  between operations  2.81 us (2%)
    all_to_all x1, waiting for transfers between devices, on_device(): lax.all_to_all(picked.reshape(devices, capacity, picked.shape[1]), 'req',...  44.9 us
    all_to_all x1, waiting for transfers between devices, on_device(): lax.all_to_all(mixture.reshape(capacity, devices, mixture.shape[1]).trans...  22 us
    ppermute x3, waiting for transfers between devices, on_device(): lax.ppermute(attended, 'tp', perm=[(i, (i + shift) % tp_size) for i in ra...  13.7 us
    all_to_all x1, starting transfers between devices, on_device(): lax.all_to_all(picked.reshape(devices, capacity, picked.shape[1]), 'req',...  13.3 us
    pallas_call x1, Pallas kernels, attend(): pl.pallas_call(lambda *refs: attention_kernel(*refs, q_width=q_width, k_w...  9.55 us
    pallas_call x1, Pallas kernels, prepare(): pl.pallas_call(lambda *refs: prep_kernel(*refs, head_dim=head_dim, capaci...  8.02 us
    all_to_all x1, starting transfers between devices, on_device(): lax.all_to_all(mixture.reshape(capacity, devices, mixture.shape[1]).trans...  6.96 us
    all_to_all x1, local copies, waits for them, and re-layouts, on_device(): lax.all_to_all(picked.reshape(devices, capacity, picked.shape[1]), 'req',...  4.09 us
  transfers between devices with their start and end apart: 5, of which 4 were waited for; matrix products, arithmetic and copies ran while one was open for 8% of the time, Pallas kernels for 0%

profile of v13, /device:TPU:1, one launch (start us, length us, event | category | flops | bytes accessed | tf_op | source)
XLA Modules:
  0.0 150.7 jit_solution(8924849966837517934)
XLA Ops:
  0.6 0.0 copy-start
  0.7 0.1 compare_select_fusion.9
  0.7 0.9 copy.28
  1.6 0.1 reduce-window.8
  1.7 0.1 reduce
  1.8 0.7 sub.52
  2.5 0.1 convert_reduce_fusion
  2.6 0.1 select_reduce_fusion
  2.7 1.2 fusion.9
  3.9 8.0 %shard_map.113 = bf16[1024,1024]{1,0:T(8,128)(2,1)} custom-call(s32[64]{0:T(128)} %refs_0_.1, s32[64]{0:T(128)} %refs_1_.1, s32[1]{0:T(128)} %bitcast.refs_2_, bf16[256,2048]{1,0:T(8,128)(2,1)} %refs_3_.1, bf16[2048]{0:T(1024)(128)(2,1)} %refs_4_.1, bf16[2048,512]{1,0:T(8,128)(2,1)} %refs_5_.1, bf16[2048,256]{1,0:T(8,128)(2,1)} %refs_6_.1, ...), custom_call_target="tpu_custom_call" | custom-call | flops 1610612736 | bytes 7340032 | tf_op jit(solution)/shard_map/pallas_call | solution.py:154
  12.0 0.0 copy-start.1
  12.0 13.3 %all-to-all-start = ((bf16[64,16,1024]{2,1,0:T(8,128)(2,1)}), bf16[64,16,1024]{2,1,0:T(8,128)(2,1)}, u32[]{:S(2)}, u32[]{:S(2)}) async-start(bf16[64,16,1024]{2,1,0:T(8,128)(2,1)} %bitcast.35), calls=%async_computation | async-start | bytes 4194304 | tf_op jit(solution)/shard_map/all_to_all | solution.py:291
  25.3 0.0 copy-done.1
  25.3 0.0 copy-done.2
  25.3 0.2 select_reduce_fusion.1
  25.5 0.7 dynamic_slice.27
  26.2 0.6 and_select_fusion.1
  26.8 0.1 broadcast_add_fusion
  26.9 0.1 add.191
  27.0 1.3 add.210.refs_1_
  28.2 0.6 dynamic_slice.28
  28.8 1.2 compare_select_fusion.refs_2_
  30.1 44.9 %all-to-all-done = bf16[64,16,1024]{2,1,0:T(8,128)(2,1)} async-done(((bf16[64,16,1024]{2,1,0:T(8,128)(2,1)}), bf16[64,16,1024]{2,1,0:T(8,128)(2,1)}, u32[]{:S(2)}, u32[]{:S(2)}) %all-to-all-start) | async-done | bytes 2097184 | tf_op jit(solution)/shard_map/all_to_all | solution.py:291
  74.9 4.1 %copy.37 = bf16[64,16,1024]{2,0,1:T(8,128)(2,1)} copy(bf16[64,16,1024]{2,1,0:T(8,128)(2,1)} %all-to-all-done) | data formatting | bytes 4194304 | tf_op jit(solution)/shard_map/all_to_all | solution.py:291
  79.0 9.6 %shard_map.114 = bf16[1024,512]{1,0:T(8,128)(2,1)} custom-call(bf16[1024,1024]{1,0:T(8,128)(2,1)} %bitcast.36, s32[1024,1]{1,0:T(8,128)} %add.210.refs_1_, s32[1,1024]{1,0:T(1,128)} %compare_select_fusion.refs_2_), custom_call_target="tpu_custom_call" | custom-call | flops 1610612736 | bytes 3145728 | tf_op jit(solution)/shard_map/pallas_call | solution.py:228
  88.6 2.8 %copy.36 = bf16[16,64,512]{2,0,1:T(8,128)(2,1)} copy(bf16[16,64,512]{2,1,0:T(8,128)(2,1)} %bitcast.40) | data formatting | bytes 2097152 | tf_op jit(solution)/shard_map/reshape | solution.py:307
  91.4 7.0 %all-to-all-start.1 = ((bf16[64,16,512]{2,1,0:T(8,128)(2,1)}), bf16[64,16,512]{2,1,0:T(8,128)(2,1)S(1)}, u32[]{:S(2)}, u32[]{:S(2)}) async-start(bf16[64,16,512]{2,1,0:T(8,128)(2,1)} %bitcast.39), calls=%async_computation.1 | async-start | bytes 2097152 | tf_op jit(solution)/shard_map/all_to_all | solution.py:306
  100.3 0.8 scatter_custom_fusion
  101.1 0.1 multiply_reduce_fusion
  101.3 1.3 slice.14
  102.6 0.8 fusion.2
  103.4 1.1 slice_bitcast_fusion.1
  104.4 22.0 %all-to-all-done.1 = bf16[64,16,512]{2,1,0:T(8,128)(2,1)S(1)} async-done(((bf16[64,16,512]{2,1,0:T(8,128)(2,1)}), bf16[64,16,512]{2,1,0:T(8,128)(2,1)S(1)}, u32[]{:S(2)}, u32[]{:S(2)}) %all-to-all-start.1) | async-done | bytes 1048608 | tf_op jit(solution)/shard_map/all_to_all | solution.py:306
  126.5 1.2 gather_fusion
  127.6 0.1 broadcast_select_fusion
  127.7 3.0 %collective-permute-start.2 = (bf16[256,512]{1,0:T(8,128)(2,1)S(1)}, bf16[256,512]{1,0:T(8,128)(2,1)S(1)}, u32[]{:S(2)}, u32[]{:S(2)}) collective-permute-start(bf16[256,512]{1,0:T(8,128)(2,1)S(1)} %broadcast_select_fusion), channel_id=1, source_target_pairs={{0,3},{1,0},{2,1},{3,2},{4,7},{5,4},{6,5},{7,6},{8,11},{9,8},{10,9... | collective-permute-start | bytes 786440 | tf_op jit(solution)/shard_map/ppermute | solution.py:324
  130.8 2.3 %maximum_bitcast_fusion = bf16[2,1,1024,256]{3,2,1,0:T(8,128)(2,1)} fusion(bf16[1,1024,256]{2,1,0:T(8,128)(2,1)} %get-tuple-element.21, bf16[1,1024,256]{2,1,0:T(8,128)(2,1)} %get-tuple-element.20), kind=kLoop, calls=%fused_computation.9 | loop fusion | flops 524288 | bytes 2097152
  133.0 0.4 collective-permute-start.1
  133.4 0.7 collective-permute-start
  134.1 0.0 copy-done
  134.1 0.3 fusion.7
  134.4 1.4 collective-permute-done.2
  135.8 0.3 fusion.3
  136.1 12.3 %collective-permute-done = bf16[256,512]{1,0:T(8,128)(2,1)S(1)} collective-permute-done((bf16[256,512]{1,0:T(8,128)(2,1)S(1)}, bf16[256,512]{1,0:T(8,128)(2,1)S(1)}, u32[]{:S(2)}, u32[]{:S(2)}) %collective-permute-start) | collective-permute-done | bytes 262176 | tf_op jit(solution)/shard_map/ppermute | solution.py:324
  148.4 0.3 convolution_add_fusion.1
  148.7 0.0 collective-permute-done.1
  148.7 0.3 fusion.1
  149.0 1.7 %add_convert_fusion = bf16[256,512]{1,0:T(8,128)(2,1)} fusion(bf16[256,512]{1,0:T(8,128)(2,1)S(1)} %fusion.1, bf16[256,2048]{1,0:T(8,128)(2,1)} %refs_3_.1, s32[]{:T(128)S(6)} %select_n.117), kind=kLoop, calls=%fused_computation.13 | loop fusion | flops 524288 | bytes 786436 | tf_op jit(solution)/shard_map/convert_element_type | solution.py:335
  (12 shorter events, 0.1 us)
Async XLA Ops:
  0.6 133.5 %copy-start = (bf16[2048,512]{1,0:T(8,128)(2,1)S(1)}, bf16[2048,512]{1,0:T(8,128)(2,1)}, u32[]{:S(2)}) copy-start(bf16[2048,512]{1,0:T(8,128)(2,1)} %param.19) | copy-start | bytes 6291460
  12.0 13.3 %copy-start.1 = (s32[64]{0:T(128)S(1)}, s32[64]{0:T(128)}, u32[]{:S(2)}) copy-start(s32[64]{0:T(128)} %refs_0_.1) | copy-start | bytes 772
  12.0 13.3 %copy-start.2 = (s32[64]{0:T(128)S(1)}, s32[64]{0:T(128)}, u32[]{:S(2)}) copy-start(s32[64]{0:T(128)} %refs_1_.1) | copy-start | bytes 772
  12.0 62.9 %all-to-all-start = ((bf16[64,16,1024]{2,1,0:T(8,128)(2,1)}), bf16[64,16,1024]{2,1,0:T(8,128)(2,1)}, u32[]{:S(2)}, u32[]{:S(2)}) async-start(bf16[64,16,1024]{2,1,0:T(8,128)(2,1)} %bitcast.35), calls=%async_computation | async-start | bytes 4194304 | tf_op jit(solution)/shard_map/all_to_all | solution.py:291
  91.4 35.1 %all-to-all-start.1 = ((bf16[64,16,512]{2,1,0:T(8,128)(2,1)}), bf16[64,16,512]{2,1,0:T(8,128)(2,1)S(1)}, u32[]{:S(2)}, u32[]{:S(2)}) async-start(bf16[64,16,512]{2,1,0:T(8,128)(2,1)} %bitcast.39), calls=%async_computation.1 | async-start | bytes 2097152 | tf_op jit(solution)/shard_map/all_to_all | solution.py:306
  127.7 8.0 %collective-permute-start.2 = (bf16[256,512]{1,0:T(8,128)(2,1)S(1)}, bf16[256,512]{1,0:T(8,128)(2,1)S(1)}, u32[]{:S(2)}, u32[]{:S(2)}) collective-permute-start(bf16[256,512]{1,0:T(8,128)(2,1)S(1)} %broadcast_select_fusion), channel_id=1, source_target_pairs={{0,3},{1,0},{2,1},{3,2},{4,7},{5,4},{6,5},{7,6},{8,11},{9,8},{10,9... | collective-permute-start | bytes 786440 | tf_op jit(solution)/shard_map/ppermute | solution.py:324
  133.0 15.7 %collective-permute-start.1 = (bf16[256,512]{1,0:T(8,128)(2,1)S(1)}, bf16[256,512]{1,0:T(8,128)(2,1)S(1)}, u32[]{:S(2)}, u32[]{:S(2)}) collective-permute-start(bf16[256,512]{1,0:T(8,128)(2,1)S(1)} %broadcast_select_fusion), channel_id=1, source_target_pairs={{0,2},{1,3},{2,0},{3,1},{4,6},{5,7},{6,4},{7,5},{8,10},{9,11},{10,... | collective-permute-start | bytes 786440 | tf_op jit(solution)/shard_map/ppermute | solution.py:324
  133.4 15.0 %collective-permute-start = (bf16[256,512]{1,0:T(8,128)(2,1)S(1)}, bf16[256,512]{1,0:T(8,128)(2,1)S(1)}, u32[]{:S(2)}, u32[]{:S(2)}) collective-permute-start(bf16[256,512]{1,0:T(8,128)(2,1)S(1)} %broadcast_select_fusion), channel_id=1, source_target_pairs={{0,1},{1,2},{2,3},{3,0},{4,5},{5,6},{6,7},{7,4},{8,9},{9,10},{10,1... | collective-permute-start | bytes 786440 | tf_op jit(solution)/shard_map/ppermute | solution.py:324

commit v14 on v11

--- a/solution.py
+++ b/solution.py
@@ -125,8 +125,8 @@
     ).astype(jnp.bfloat16)
     qkv = qkv_ref[...]
     out_rows = out_ref.shape[0]
-    block = out_rows // 4
-    for b in range(4):
+    block = out_rows // 2
+    for b in range(2):
         rows_here = pl.ds(b * block, block)
         out_ref[rows_here, :] = jnp.dot(
             pick_ref[rows_here, :], qkv, preferred_element_type=jnp.float32

time: 151 us -> 150 us (level)
  no operation moved by 1% of the time
where the time goes in v14:
time: 150 us
  waiting for transfers between devices  80.6 us (54%)
  starting transfers between devices  24.1 us (16%)
  Pallas kernels  17 us (11%)
  local copies, waits for them, and re-layouts  14.6 us (10%)
  other arithmetic  9.6 us (6%)
  between operations  2.81 us (2%)
    all_to_all x1, waiting for transfers between devices, on_device(): lax.all_to_all(picked.reshape(devices, capacity, picked.shape[1]), 'req',...  44.9 us
    all_to_all x1, waiting for transfers between devices, on_device(): lax.all_to_all(mixture.reshape(capacity, devices, mixture.shape[1]).trans...  22 us
    ppermute x3, waiting for transfers between devices, on_device(): lax.ppermute(attended, 'tp', perm=[(i, (i + shift) % tp_size) for i in ra...  13.7 us
    all_to_all x1, starting transfers between devices, on_device(): lax.all_to_all(picked.reshape(devices, capacity, picked.shape[1]), 'req',...  13.3 us
    pallas_call x1, Pallas kernels, attend(): pl.pallas_call(lambda *refs: attention_kernel(*refs, q_width=q_width, k_w...  9.07 us
    pallas_call x1, Pallas kernels, prepare(): pl.pallas_call(lambda *refs: prep_kernel(*refs, head_dim=head_dim, capaci...  7.92 us
    all_to_all x1, starting transfers between devices, on_device(): lax.all_to_all(mixture.reshape(capacity, devices, mixture.shape[1]).trans...  6.96 us
    all_to_all x1, local copies, waits for them, and re-layouts, on_device(): lax.all_to_all(picked.reshape(devices, capacity, picked.shape[1]), 'req',...  4.09 us
  transfers between devices with their start and end apart: 5, of which 4 were waited for; matrix products, arithmetic and copies ran while one was open for 8% of the time, Pallas kernels for 0%

profile of v14, /device:TPU:1, one launch (start us, length us, event | category | flops | bytes accessed | tf_op | source)
XLA Modules:
  0.0 149.9 jit_solution(2943679638165253020)
XLA Ops:
  0.6 0.0 copy-start
  0.7 0.1 compare_select_fusion.9
  0.7 0.9 copy.28
  1.6 0.1 reduce-window.8
  1.7 0.1 reduce
  1.8 0.7 sub.52
  2.5 0.1 convert_reduce_fusion
  2.6 0.1 select_reduce_fusion
  2.7 1.2 fusion.9
  3.9 7.9 %shard_map.113 = bf16[1024,1024]{1,0:T(8,128)(2,1)} custom-call(s32[64]{0:T(128)} %refs_0_.1, s32[64]{0:T(128)} %refs_1_.1, s32[1]{0:T(128)} %bitcast.refs_2_, bf16[256,2048]{1,0:T(8,128)(2,1)} %refs_3_.1, bf16[2048]{0:T(1024)(128)(2,1)} %refs_4_.1, bf16[2048,512]{1,0:T(8,128)(2,1)} %refs_5_.1, bf16[2048,256]{1,0:T(8,128)(2,1)} %refs_6_.1, ...), custom_call_target="tpu_custom_call" | custom-call | flops 1610612736 | bytes 7340032 | tf_op jit(solution)/shard_map/pallas_call | solution.py:154
  11.9 0.0 copy-start.1
  11.9 13.3 %all-to-all-start = ((bf16[64,16,1024]{2,1,0:T(8,128)(2,1)}), bf16[64,16,1024]{2,1,0:T(8,128)(2,1)}, u32[]{:S(2)}, u32[]{:S(2)}) async-start(bf16[64,16,1024]{2,1,0:T(8,128)(2,1)} %bitcast.35), calls=%async_computation | async-start | bytes 4194304 | tf_op jit(solution)/shard_map/all_to_all | solution.py:287
  25.2 0.0 copy-done.1
  25.2 0.0 copy-done.2
  25.2 0.2 select_reduce_fusion.1
  25.4 0.7 dynamic_slice.27
  26.1 0.6 and_select_fusion.1
  26.7 0.1 broadcast_add_fusion
  26.8 0.1 add.191
  26.9 1.3 add.210.refs_1_
  28.1 0.6 dynamic_slice.28
  28.7 1.2 compare_select_fusion.refs_2_
  30.0 44.9 %all-to-all-done = bf16[64,16,1024]{2,1,0:T(8,128)(2,1)} async-done(((bf16[64,16,1024]{2,1,0:T(8,128)(2,1)}), bf16[64,16,1024]{2,1,0:T(8,128)(2,1)}, u32[]{:S(2)}, u32[]{:S(2)}) %all-to-all-start) | async-done | bytes 2097184 | tf_op jit(solution)/shard_map/all_to_all | solution.py:287
  74.8 4.1 %copy.37 = bf16[64,16,1024]{2,0,1:T(8,128)(2,1)} copy(bf16[64,16,1024]{2,1,0:T(8,128)(2,1)} %all-to-all-done) | data formatting | bytes 4194304 | tf_op jit(solution)/shard_map/all_to_all | solution.py:287
  78.9 9.1 %shard_map.114 = bf16[1024,512]{1,0:T(8,128)(2,1)} custom-call(bf16[1024,1024]{1,0:T(8,128)(2,1)} %bitcast.36, s32[1024,1]{1,0:T(8,128)} %add.210.refs_1_, s32[1,1024]{1,0:T(1,128)} %compare_select_fusion.refs_2_), custom_call_target="tpu_custom_call" | custom-call | flops 1610612736 | bytes 3145728 | tf_op jit(solution)/shard_map/pallas_call | solution.py:224
  88.0 2.8 %copy.36 = bf16[16,64,512]{2,0,1:T(8,128)(2,1)} copy(bf16[16,64,512]{2,1,0:T(8,128)(2,1)} %bitcast.40) | data formatting | bytes 2097152 | tf_op jit(solution)/shard_map/reshape | solution.py:303
  90.8 7.0 %all-to-all-start.1 = ((bf16[64,16,512]{2,1,0:T(8,128)(2,1)}), bf16[64,16,512]{2,1,0:T(8,128)(2,1)S(1)}, u32[]{:S(2)}, u32[]{:S(2)}) async-start(bf16[64,16,512]{2,1,0:T(8,128)(2,1)} %bitcast.39), calls=%async_computation.1 | async-start | bytes 2097152 | tf_op jit(solution)/shard_map/all_to_all | solution.py:302
  99.8 0.8 scatter_custom_fusion
  100.5 0.1 multiply_reduce_fusion
  100.7 1.3 slice.14
  102.0 0.8 fusion.2
  102.8 1.1 slice_bitcast_fusion.1
  103.9 22.0 %all-to-all-done.1 = bf16[64,16,512]{2,1,0:T(8,128)(2,1)S(1)} async-done(((bf16[64,16,512]{2,1,0:T(8,128)(2,1)}), bf16[64,16,512]{2,1,0:T(8,128)(2,1)S(1)}, u32[]{:S(2)}, u32[]{:S(2)}) %all-to-all-start.1) | async-done | bytes 1048608 | tf_op jit(solution)/shard_map/all_to_all | solution.py:302
  125.9 1.2 gather_fusion
  127.1 0.1 broadcast_select_fusion
  127.2 2.8 %collective-permute-start.2 = (bf16[256,512]{1,0:T(8,128)(2,1)S(1)}, bf16[256,512]{1,0:T(8,128)(2,1)S(1)}, u32[]{:S(2)}, u32[]{:S(2)}) collective-permute-start(bf16[256,512]{1,0:T(8,128)(2,1)S(1)} %broadcast_select_fusion), channel_id=1, source_target_pairs={{0,3},{1,0},{2,1},{3,2},{4,7},{5,4},{6,5},{7,6},{8,11},{9,8},{10,9... | collective-permute-start | bytes 786440 | tf_op jit(solution)/shard_map/ppermute | solution.py:320
  130.0 2.3 %maximum_bitcast_fusion = bf16[2,1,1024,256]{3,2,1,0:T(8,128)(2,1)} fusion(bf16[1,1024,256]{2,1,0:T(8,128)(2,1)} %get-tuple-element.21, bf16[1,1024,256]{2,1,0:T(8,128)(2,1)} %get-tuple-element.20), kind=kLoop, calls=%fused_computation.9 | loop fusion | flops 524288 | bytes 2097152
  132.2 0.4 collective-permute-start.1
  132.6 0.7 collective-permute-start
  133.3 0.0 copy-done
  133.3 0.3 fusion.7
  133.6 1.4 collective-permute-done.2
  135.0 0.3 fusion.3
  135.3 12.3 %collective-permute-done = bf16[256,512]{1,0:T(8,128)(2,1)S(1)} collective-permute-done((bf16[256,512]{1,0:T(8,128)(2,1)S(1)}, bf16[256,512]{1,0:T(8,128)(2,1)S(1)}, u32[]{:S(2)}, u32[]{:S(2)}) %collective-permute-start) | collective-permute-done | bytes 262176 | tf_op jit(solution)/shard_map/ppermute | solution.py:320
  147.6 0.3 convolution_add_fusion.1
  147.9 0.0 collective-permute-done.1
  147.9 0.3 fusion.1
  148.2 1.7 %add_convert_fusion = bf16[256,512]{1,0:T(8,128)(2,1)} fusion(bf16[256,512]{1,0:T(8,128)(2,1)S(1)} %fusion.1, bf16[256,2048]{1,0:T(8,128)(2,1)} %refs_3_.1, s32[]{:T(128)S(6)} %select_n.117), kind=kLoop, calls=%fused_computation.13 | loop fusion | flops 524288 | bytes 786436 | tf_op jit(solution)/shard_map/convert_element_type | solution.py:331
  (12 shorter events, 0.1 us)
Async XLA Ops:
  0.6 132.7 %copy-start = (bf16[2048,512]{1,0:T(8,128)(2,1)S(1)}, bf16[2048,512]{1,0:T(8,128)(2,1)}, u32[]{:S(2)}) copy-start(bf16[2048,512]{1,0:T(8,128)(2,1)} %param.19) | copy-start | bytes 6291460
  11.9 13.3 %copy-start.1 = (s32[64]{0:T(128)S(1)}, s32[64]{0:T(128)}, u32[]{:S(2)}) copy-start(s32[64]{0:T(128)} %refs_0_.1) | copy-start | bytes 772
  11.9 13.3 %copy-start.2 = (s32[64]{0:T(128)S(1)}, s32[64]{0:T(128)}, u32[]{:S(2)}) copy-start(s32[64]{0:T(128)} %refs_1_.1) | copy-start | bytes 772
  11.9 62.9 %all-to-all-start = ((bf16[64,16,1024]{2,1,0:T(8,128)(2,1)}), bf16[64,16,1024]{2,1,0:T(8,128)(2,1)}, u32[]{:S(2)}, u32[]{:S(2)}) async-start(bf16[64,16,1024]{2,1,0:T(8,128)(2,1)} %bitcast.35), calls=%async_computation | async-start | bytes 4194304 | tf_op jit(solution)/shard_map/all_to_all | solution.py:287
  90.8 35.1 %all-to-all-start.1 = ((bf16[64,16,512]{2,1,0:T(8,128)(2,1)}), bf16[64,16,512]{2,1,0:T(8,128)(2,1)S(1)}, u32[]{:S(2)}, u32[]{:S(2)}) async-start(bf16[64,16,512]{2,1,0:T(8,128)(2,1)} %bitcast.39), calls=%async_computation.1 | async-start | bytes 2097152 | tf_op jit(solution)/shard_map/all_to_all | solution.py:302
  127.2 7.8 %collective-permute-start.2 = (bf16[256,512]{1,0:T(8,128)(2,1)S(1)}, bf16[256,512]{1,0:T(8,128)(2,1)S(1)}, u32[]{:S(2)}, u32[]{:S(2)}) collective-permute-start(bf16[256,512]{1,0:T(8,128)(2,1)S(1)} %broadcast_select_fusion), channel_id=1, source_target_pairs={{0,3},{1,0},{2,1},{3,2},{4,7},{5,4},{6,5},{7,6},{8,11},{9,8},{10,9... | collective-permute-start | bytes 786440 | tf_op jit(solution)/shard_map/ppermute | solution.py:320
  132.2 15.7 %collective-permute-start.1 = (bf16[256,512]{1,0:T(8,128)(2,1)S(1)}, bf16[256,512]{1,0:T(8,128)(2,1)S(1)}, u32[]{:S(2)}, u32[]{:S(2)}) collective-permute-start(bf16[256,512]{1,0:T(8,128)(2,1)S(1)} %broadcast_select_fusion), channel_id=1, source_target_pairs={{0,2},{1,3},{2,0},{3,1},{4,6},{5,7},{6,4},{7,5},{8,10},{9,11},{10,... | collective-permute-start | bytes 786440 | tf_op jit(solution)/shard_map/ppermute | solution.py:320
  132.6 15.0 %collective-permute-start = (bf16[256,512]{1,0:T(8,128)(2,1)S(1)}, bf16[256,512]{1,0:T(8,128)(2,1)S(1)}, u32[]{:S(2)}, u32[]{:S(2)}) collective-permute-start(bf16[256,512]{1,0:T(8,128)(2,1)S(1)} %broadcast_select_fusion), channel_id=1, source_target_pairs={{0,1},{1,2},{2,3},{3,0},{4,5},{5,6},{6,7},{7,4},{8,9},{9,10},{10,1... | collective-permute-start | bytes 786440 | tf_op jit(solution)/shard_map/ppermute | solution.py:320

commit v15 on v12

--- a/solution.py
+++ b/solution.py
@@ -290,24 +290,28 @@
         split_axis=0,
         concat_axis=0,
         tiled=True,
-    ).transpose(1, 0, 2)
+    )
     source_ids = jnp.arange(devices, dtype=jnp.int32)
     arrived_pos = (
-        ranks[:, None] * devices + jnp.mod(source_ids[None, :] - my_start, devices)
+        ranks[None, :] * devices + jnp.mod(source_ids[:, None] - my_start, devices)
     ).reshape(-1)
     key_pos = jnp.where(arrived_pos < my_length, arrived_pos, 1 << 30)
     mixture = attend(
         arrived.reshape(slot_len, arrived.shape[2]), arrived_pos, key_pos, q_width, k_width, head_dim
     )
     returned = lax.all_to_all(
-        mixture.reshape(capacity, devices, mixture.shape[1]).transpose(1, 0, 2),
+        mixture.reshape(devices, capacity, mixture.shape[1]),
         "req",
         split_axis=0,
         concat_axis=0,
         tiled=True,
     )
     attended = jnp.take(returned.reshape(capacity * devices, -1), back_rows, axis=0)
-    kv_rows = jnp.roll(arrived[:, :, q_width:], -roll_shift, axis=1).reshape(slot_len, -1)
+    kv_rows = (
+        jnp.roll(arrived[:, :, q_width:], -roll_shift, axis=0)
+        .transpose(1, 0, 2)
+        .reshape(slot_len, -1)
+    )
     kv_cache = jnp.stack([kv_rows[:, :k_width], kv_rows[:, k_width:]])[:, None]
     tp_size = lax.axis_size("tp")
     w_rows = w_out.shape[0] // tp_size

time: 153 us -> 146 us (0.954)
  local copies, waits for them, and re-layouts: 14.9 us -> 8.18 us
    all_to_all x1 -> x0, local copies, waits for them, and re-layouts: 4.09 us -> none  [on_device(): lax.all_to_all(picked.reshape(devices, capacity, picked.shape[1]), 'req',...]
    reshape x1 -> x0, local copies, waits for them, and re-layouts: 2.79 us -> none  [on_device(): mixture.reshape(capacity, devices, mixture.shape[1]).transpose(1, 0, 2)]
    broadcast_in_dim x0 -> x1, other arithmetic: none -> 2.27 us  [on_device(): kv_cache = jnp.stack([kv_rows[:, :k_width], kv_rows[:, k_width:]])[:, None]]
    unnamed x1 -> x0, other arithmetic: 2.27 us -> none
where the time goes in v15:
time: 146 us; the launch traced here: 145 us
  waiting for transfers between devices  80.5 us (55%)
  starting transfers between devices  24.3 us (17%)
  Pallas kernels  19 us (13%)
  other arithmetic  9.26 us (6%)
  local copies, waits for them, and re-layouts  8.18 us (6%)
  between operations  2.81 us (2%)
    all_to_all x1, waiting for transfers between devices, on_device(): lax.all_to_all(picked.reshape(devices, capacity, picked.shape[1]), 'req',...  45 us
    all_to_all x1, waiting for transfers between devices, on_device(): lax.all_to_all(mixture.reshape(devices, capacity, mixture.shape[1]), 'req...  21.8 us
    ppermute x3, waiting for transfers between devices, on_device(): lax.ppermute(attended, 'tp', perm=[(i, (i + shift) % tp_size) for i in ra...  13.7 us
    all_to_all x1, starting transfers between devices, on_device(): lax.all_to_all(picked.reshape(devices, capacity, picked.shape[1]), 'req',...  13.3 us
    pallas_call x1, Pallas kernels, attend(): pl.pallas_call(lambda *refs: attention_kernel(*refs, q_width=q_width, k_w...  11 us
    pallas_call x1, Pallas kernels, prepare(): pl.pallas_call(lambda *refs: prep_kernel(*refs, head_dim=head_dim, capaci...  7.96 us
    all_to_all x1, starting transfers between devices, on_device(): lax.all_to_all(mixture.reshape(devices, capacity, mixture.shape[1]), 'req...  6.96 us
    ppermute x3, starting transfers between devices, on_device(): lax.ppermute(attended, 'tp', perm=[(i, (i + shift) % tp_size) for i in ra...  4.06 us
  transfers between devices with their start and end apart: 5, of which 4 were waited for; matrix products, arithmetic and copies ran while one was open for 8% of the time, Pallas kernels for 0%

profile of v15, /device:TPU:1, one launch (start us, length us, event | category | flops | bytes accessed | tf_op | source)
XLA Modules:
  0.0 145.3 jit_solution(12872330092611379678)
XLA Ops:
  0.6 0.0 copy-start
  0.7 0.1 compare_select_fusion.9
  0.7 0.9 copy.17
  1.6 0.1 reduce-window.8
  1.7 0.1 reduce
  1.8 0.7 sub.52
  2.5 0.1 convert_reduce_fusion
  2.6 0.1 select_reduce_fusion
  2.7 1.2 fusion.10
  3.9 8.0 %shard_map.113 = bf16[1024,1024]{1,0:T(8,128)(2,1)} custom-call(s32[64]{0:T(128)} %refs_0_.1, s32[64]{0:T(128)} %refs_1_.1, s32[1]{0:T(128)} %bitcast.refs_2_, bf16[256,2048]{1,0:T(8,128)(2,1)} %refs_3_.1, bf16[2048]{0:T(1024)(128)(2,1)} %refs_4_.1, bf16[2048,512]{1,0:T(8,128)(2,1)} %refs_5_.1, bf16[2048,256]{1,0:T(8,128)(2,1)} %refs_6_.1, ...), custom_call_target="tpu_custom_call" | custom-call | flops 1610612736 | bytes 7340032 | tf_op jit(solution)/shard_map/pallas_call | solution.py:154
  11.9 0.0 copy-start.1
  11.9 0.0 copy-start.2
  11.9 13.3 %all-to-all-start = ((bf16[64,16,1024]{2,1,0:T(8,128)(2,1)}), bf16[64,16,1024]{2,1,0:T(8,128)(2,1)}, u32[]{:S(2)}, u32[]{:S(2)}) async-start(bf16[64,16,1024]{2,1,0:T(8,128)(2,1)} %bitcast.28), calls=%async_computation | async-start | bytes 4194304 | tf_op jit(solution)/shard_map/all_to_all | solution.py:287
  25.2 0.0 copy-done.1
  25.3 0.0 copy-done.2
  25.3 0.2 select_reduce_fusion.1
  25.4 0.7 dynamic_slice.27
  26.1 0.6 and_select_fusion.1
  26.8 0.1 broadcast_add_fusion
  26.8 0.1 add.191
  26.9 1.1 add.210.refs_1_
  28.0 0.6 dynamic_slice.28
  28.6 1.2 compare_select_fusion.refs_2_
  29.8 45.0 %all-to-all-done = bf16[64,16,1024]{2,1,0:T(8,128)(2,1)} async-done(((bf16[64,16,1024]{2,1,0:T(8,128)(2,1)}), bf16[64,16,1024]{2,1,0:T(8,128)(2,1)}, u32[]{:S(2)}, u32[]{:S(2)}) %all-to-all-start) | async-done | bytes 2097184 | tf_op jit(solution)/shard_map/all_to_all | solution.py:287
  74.9 11.0 %shard_map.114 = bf16[1024,512]{1,0:T(8,128)(2,1)} custom-call(bf16[1024,1024]{1,0:T(8,128)(2,1)} %bitcast.5.refs_0_, s32[1024,1]{1,0:T(8,128)} %add.210.refs_1_, s32[1,1024]{1,0:T(1,128)} %compare_select_fusion.refs_2_), custom_call_target="tpu_custom_call" | custom-call | flops 2147483648 | bytes 3145728 | tf_op jit(solution)/shard_map/pallas_call | solution.py:224
  85.9 7.0 %all-to-all-start.1 = ((bf16[64,16,512]{2,1,0:T(8,128)(2,1)}), bf16[64,16,512]{2,1,0:T(8,128)(2,1)S(1)}, u32[]{:S(2)}, u32[]{:S(2)}) async-start(bf16[64,16,512]{2,1,0:T(8,128)(2,1)} %bitcast.30), calls=%async_computation.1 | async-start | bytes 2097152 | tf_op jit(solution)/shard_map/all_to_all | solution.py:302
  94.9 0.8 scatter_custom_fusion
  95.7 0.1 multiply_reduce_fusion
  95.8 1.3 slice.14
  97.1 0.5 fusion.3
  97.6 0.6 copy.19
  98.2 1.1 slice_bitcast_fusion.1
  99.3 21.8 %all-to-all-done.1 = bf16[64,16,512]{2,1,0:T(8,128)(2,1)S(1)} async-done(((bf16[64,16,512]{2,1,0:T(8,128)(2,1)}), bf16[64,16,512]{2,1,0:T(8,128)(2,1)S(1)}, u32[]{:S(2)}, u32[]{:S(2)}) %all-to-all-start.1) | async-done | bytes 1048608 | tf_op jit(solution)/shard_map/all_to_all | solution.py:302
  121.0 1.2 gather_fusion
  122.2 0.1 broadcast_select_fusion
  122.3 3.0 %collective-permute-start.2 = (bf16[256,512]{1,0:T(8,128)(2,1)S(1)}, bf16[256,512]{1,0:T(8,128)(2,1)S(1)}, u32[]{:S(2)}, u32[]{:S(2)}) collective-permute-start(bf16[256,512]{1,0:T(8,128)(2,1)S(1)} %broadcast_select_fusion), channel_id=1, source_target_pairs={{0,3},{1,0},{2,1},{3,2},{4,7},{5,4},{6,5},{7,6},{8,11},{9,8},{10,9... | collective-permute-start | bytes 786440 | tf_op jit(solution)/shard_map/ppermute | solution.py:324
  125.3 2.3 %maximum_bitcast_fusion = bf16[2,1,1024,256]{3,2,1,0:T(8,128)(2,1)} fusion(bf16[1,1024,256]{2,1,0:T(8,128)(2,1)} %get-tuple-element.15, bf16[1,1024,256]{2,1,0:T(8,128)(2,1)} %get-tuple-element.14), kind=kLoop, calls=%fused_computation.10 | loop fusion | flops 524288 | bytes 2097152 | tf_op jit(solution)/shard_map/broadcast_in_dim | solution.py:315
  127.6 0.4 collective-permute-start.1
  128.0 0.7 collective-permute-start
  128.6 0.0 copy-done
  128.6 0.3 fusion.8
  128.9 1.4 collective-permute-done.2
  130.3 0.3 fusion.4
  130.6 12.3 %collective-permute-done = bf16[256,512]{1,0:T(8,128)(2,1)S(1)} collective-permute-done((bf16[256,512]{1,0:T(8,128)(2,1)S(1)}, bf16[256,512]{1,0:T(8,128)(2,1)S(1)}, u32[]{:S(2)}, u32[]{:S(2)}) %collective-permute-start) | collective-permute-done | bytes 262176 | tf_op jit(solution)/shard_map/ppermute | solution.py:324
  142.9 0.3 convolution_add_fusion.1
  143.2 0.0 collective-permute-done.1
  143.2 0.3 fusion.1
  143.6 1.7 %add_convert_fusion = bf16[256,512]{1,0:T(8,128)(2,1)} fusion(bf16[256,512]{1,0:T(8,128)(2,1)S(1)} %fusion.1, bf16[256,2048]{1,0:T(8,128)(2,1)} %refs_3_.1, s32[]{:T(128)S(6)} %select_n.117), kind=kLoop, calls=%fused_computation.13 | loop fusion | flops 524288 | bytes 786436 | tf_op jit(solution)/shard_map/convert_element_type | solution.py:335
  (11 shorter events, 0.1 us)
Async XLA Ops:
  0.6 128.0 %copy-start = (bf16[2048,512]{1,0:T(8,128)(2,1)S(1)}, bf16[2048,512]{1,0:T(8,128)(2,1)}, u32[]{:S(2)}) copy-start(bf16[2048,512]{1,0:T(8,128)(2,1)} %param.19) | copy-start | bytes 6291460
  11.9 13.3 %copy-start.1 = (s32[64]{0:T(128)S(1)}, s32[64]{0:T(128)}, u32[]{:S(2)}) copy-start(s32[64]{0:T(128)} %refs_0_.1) | copy-start | bytes 772
  11.9 13.3 %copy-start.2 = (s32[64]{0:T(128)S(1)}, s32[64]{0:T(128)}, u32[]{:S(2)}) copy-start(s32[64]{0:T(128)} %refs_1_.1) | copy-start | bytes 772
  11.9 62.9 %all-to-all-start = ((bf16[64,16,1024]{2,1,0:T(8,128)(2,1)}), bf16[64,16,1024]{2,1,0:T(8,128)(2,1)}, u32[]{:S(2)}, u32[]{:S(2)}) async-start(bf16[64,16,1024]{2,1,0:T(8,128)(2,1)} %bitcast.28), calls=%async_computation | async-start | bytes 4194304 | tf_op jit(solution)/shard_map/all_to_all | solution.py:287
  85.9 35.1 %all-to-all-start.1 = ((bf16[64,16,512]{2,1,0:T(8,128)(2,1)}), bf16[64,16,512]{2,1,0:T(8,128)(2,1)S(1)}, u32[]{:S(2)}, u32[]{:S(2)}) async-start(bf16[64,16,512]{2,1,0:T(8,128)(2,1)} %bitcast.30), calls=%async_computation.1 | async-start | bytes 2097152 | tf_op jit(solution)/shard_map/all_to_all | solution.py:302
  122.3 8.0 %collective-permute-start.2 = (bf16[256,512]{1,0:T(8,128)(2,1)S(1)}, bf16[256,512]{1,0:T(8,128)(2,1)S(1)}, u32[]{:S(2)}, u32[]{:S(2)}) collective-permute-start(bf16[256,512]{1,0:T(8,128)(2,1)S(1)} %broadcast_select_fusion), channel_id=1, source_target_pairs={{0,3},{1,0},{2,1},{3,2},{4,7},{5,4},{6,5},{7,6},{8,11},{9,8},{10,9... | collective-permute-start | bytes 786440 | tf_op jit(solution)/shard_map/ppermute | solution.py:324
  127.6 15.7 %collective-permute-start.1 = (bf16[256,512]{1,0:T(8,128)(2,1)S(1)}, bf16[256,512]{1,0:T(8,128)(2,1)S(1)}, u32[]{:S(2)}, u32[]{:S(2)}) collective-permute-start(bf16[256,512]{1,0:T(8,128)(2,1)S(1)} %broadcast_select_fusion), channel_id=1, source_target_pairs={{0,2},{1,3},{2,0},{3,1},{4,6},{5,7},{6,4},{7,5},{8,10},{9,11},{10,... | collective-permute-start | bytes 786440 | tf_op jit(solution)/shard_map/ppermute | solution.py:324
  128.0 15.0 %collective-permute-start = (bf16[256,512]{1,0:T(8,128)(2,1)S(1)}, bf16[256,512]{1,0:T(8,128)(2,1)S(1)}, u32[]{:S(2)}, u32[]{:S(2)}) collective-permute-start(bf16[256,512]{1,0:T(8,128)(2,1)S(1)} %broadcast_select_fusion), channel_id=1, source_target_pairs={{0,1},{1,2},{2,3},{3,0},{4,5},{5,6},{6,7},{7,4},{8,9},{9,10},{10,1... | collective-permute-start | bytes 786440 | tf_op jit(solution)/shard_map/ppermute | solution.py:324

commit v16 on v15

--- a/solution.py
+++ b/solution.py
@@ -189,7 +189,7 @@
     group = q_width // head_dim // kv_heads
     scale = head_dim ** (-0.5)
     for i in range(blocks):
-        key_rows = block * (i + 1)
+        key_rows = rows
         rows_here = pl.ds(i * block, block)
         allowed = kpos_ref[:, :key_rows] <= qpos_ref[rows_here, :]
         for h in range(kv_heads):
@@ -216,9 +216,9 @@
 
 def attend(qkv_slot, query_pos, key_pos, q_width, k_width, head_dim):
     rows = qkv_slot.shape[0]
-    blocks = 1
+    blocks = 2
     heads = q_width // head_dim
-    causal_pairs = blocks * (blocks + 1) // 2
+    causal_pairs = blocks * blocks
     pair_flops = 4 * (rows // blocks) ** 2 * head_dim
     vmem = pl.BlockSpec(memory_space=pltpu.VMEM)
     return pl.pallas_call(

time: 146 us -> 145 us (level)
  no operation moved by 1% of the time
where the time goes in v16:
time: 145 us; the launch traced here: 144 us
  waiting for transfers between devices  80.5 us (56%)
  starting transfers between devices  24.3 us (17%)
  Pallas kernels  18.1 us (12%)
  other arithmetic  9.26 us (6%)
  local copies, waits for them, and re-layouts  8.18 us (6%)
  between operations  2.81 us (2%)
    all_to_all x1, waiting for transfers between devices, on_device(): lax.all_to_all(picked.reshape(devices, capacity, picked.shape[1]), 'req',...  45 us
    all_to_all x1, waiting for transfers between devices, on_device(): lax.all_to_all(mixture.reshape(devices, capacity, mixture.shape[1]), 'req...  21.8 us
    ppermute x3, waiting for transfers between devices, on_device(): lax.ppermute(attended, 'tp', perm=[(i, (i + shift) % tp_size) for i in ra...  13.7 us
    all_to_all x1, starting transfers between devices, on_device(): lax.all_to_all(picked.reshape(devices, capacity, picked.shape[1]), 'req',...  13.3 us
    pallas_call x1, Pallas kernels, attend(): pl.pallas_call(lambda *refs: attention_kernel(*refs, q_width=q_width, k_w...  10.1 us
    pallas_call x1, Pallas kernels, prepare(): pl.pallas_call(lambda *refs: prep_kernel(*refs, head_dim=head_dim, capaci...  7.96 us
    all_to_all x1, starting transfers between devices, on_device(): lax.all_to_all(mixture.reshape(devices, capacity, mixture.shape[1]), 'req...  7.14 us
    ppermute x3, starting transfers between devices, on_device(): lax.ppermute(attended, 'tp', perm=[(i, (i + shift) % tp_size) for i in ra...  3.84 us
  transfers between devices with their start and end apart: 5, of which 4 were waited for; matrix products, arithmetic and copies ran while one was open for 8% of the time, Pallas kernels for 0%

profile of v16, /device:TPU:1, one launch (start us, length us, event | category | flops | bytes accessed | tf_op | source)
XLA Modules:
  0.0 144.3 jit_solution(36126423364820342)
XLA Ops:
  0.6 0.0 copy-start
  0.7 0.1 compare_select_fusion.9
  0.7 0.9 copy.17
  1.6 0.1 reduce-window.8
  1.7 0.1 reduce
  1.8 0.7 sub.52
  2.5 0.1 convert_reduce_fusion
  2.6 0.1 select_reduce_fusion
  2.7 1.2 fusion.10
  3.9 8.0 %shard_map.113 = bf16[1024,1024]{1,0:T(8,128)(2,1)} custom-call(s32[64]{0:T(128)} %refs_0_.1, s32[64]{0:T(128)} %refs_1_.1, s32[1]{0:T(128)} %bitcast.refs_2_, bf16[256,2048]{1,0:T(8,128)(2,1)} %refs_3_.1, bf16[2048]{0:T(1024)(128)(2,1)} %refs_4_.1, bf16[2048,512]{1,0:T(8,128)(2,1)} %refs_5_.1, bf16[2048,256]{1,0:T(8,128)(2,1)} %refs_6_.1, ...), custom_call_target="tpu_custom_call" | custom-call | flops 1610612736 | bytes 7340032 | tf_op jit(solution)/shard_map/pallas_call | solution.py:154
  11.9 0.0 copy-start.1
  11.9 0.0 copy-start.2
  11.9 13.3 %all-to-all-start = ((bf16[64,16,1024]{2,1,0:T(8,128)(2,1)}), bf16[64,16,1024]{2,1,0:T(8,128)(2,1)}, u32[]{:S(2)}, u32[]{:S(2)}) async-start(bf16[64,16,1024]{2,1,0:T(8,128)(2,1)} %bitcast.28), calls=%async_computation | async-start | bytes 4194304 | tf_op jit(solution)/shard_map/all_to_all | solution.py:287
  25.2 0.0 copy-done.1
  25.2 0.0 copy-done.2
  25.3 0.2 select_reduce_fusion.1
  25.4 0.7 dynamic_slice.27
  26.1 0.6 and_select_fusion.1
  26.7 0.1 broadcast_add_fusion
  26.8 0.1 add.191
  26.9 1.1 add.210.refs_1_
  28.0 0.6 dynamic_slice.28
  28.6 1.2 compare_select_fusion.refs_2_
  29.8 45.0 %all-to-all-done = bf16[64,16,1024]{2,1,0:T(8,128)(2,1)} async-done(((bf16[64,16,1024]{2,1,0:T(8,128)(2,1)}), bf16[64,16,1024]{2,1,0:T(8,128)(2,1)}, u32[]{:S(2)}, u32[]{:S(2)}) %all-to-all-start) | async-done | bytes 2097184 | tf_op jit(solution)/shard_map/all_to_all | solution.py:287
  74.9 10.1 %shard_map.114 = bf16[1024,512]{1,0:T(8,128)(2,1)} custom-call(bf16[1024,1024]{1,0:T(8,128)(2,1)} %bitcast.5.refs_0_, s32[1024,1]{1,0:T(8,128)} %add.210.refs_1_, s32[1,1024]{1,0:T(1,128)} %compare_select_fusion.refs_2_), custom_call_target="tpu_custom_call" | custom-call | flops 2147483648 | bytes 3145728 | tf_op jit(solution)/shard_map/pallas_call | solution.py:224
  85.0 7.1 %all-to-all-start.1 = ((bf16[64,16,512]{2,1,0:T(8,128)(2,1)}), bf16[64,16,512]{2,1,0:T(8,128)(2,1)S(1)}, u32[]{:S(2)}, u32[]{:S(2)}) async-start(bf16[64,16,512]{2,1,0:T(8,128)(2,1)} %bitcast.30), calls=%async_computation.1 | async-start | bytes 2097152 | tf_op jit(solution)/shard_map/all_to_all | solution.py:302
  94.2 0.8 scatter_custom_fusion
  94.9 0.1 multiply_reduce_fusion
  95.1 1.3 slice.14
  96.4 0.5 fusion.3
  96.9 0.6 copy.19
  97.5 1.1 slice_bitcast_fusion.1
  98.5 21.8 %all-to-all-done.1 = bf16[64,16,512]{2,1,0:T(8,128)(2,1)S(1)} async-done(((bf16[64,16,512]{2,1,0:T(8,128)(2,1)}), bf16[64,16,512]{2,1,0:T(8,128)(2,1)S(1)}, u32[]{:S(2)}, u32[]{:S(2)}) %all-to-all-start.1) | async-done | bytes 1048608 | tf_op jit(solution)/shard_map/all_to_all | solution.py:302
  120.3 1.2 gather_fusion
  121.5 0.1 broadcast_select_fusion
  121.6 2.8 %collective-permute-start.2 = (bf16[256,512]{1,0:T(8,128)(2,1)S(1)}, bf16[256,512]{1,0:T(8,128)(2,1)S(1)}, u32[]{:S(2)}, u32[]{:S(2)}) collective-permute-start(bf16[256,512]{1,0:T(8,128)(2,1)S(1)} %broadcast_select_fusion), channel_id=1, source_target_pairs={{0,3},{1,0},{2,1},{3,2},{4,7},{5,4},{6,5},{7,6},{8,11},{9,8},{10,9... | collective-permute-start | bytes 786440 | tf_op jit(solution)/shard_map/ppermute | solution.py:324
  124.4 2.3 %maximum_bitcast_fusion = bf16[2,1,1024,256]{3,2,1,0:T(8,128)(2,1)} fusion(bf16[1,1024,256]{2,1,0:T(8,128)(2,1)} %get-tuple-element.15, bf16[1,1024,256]{2,1,0:T(8,128)(2,1)} %get-tuple-element.14), kind=kLoop, calls=%fused_computation.10 | loop fusion | flops 524288 | bytes 2097152 | tf_op jit(solution)/shard_map/broadcast_in_dim | solution.py:315
  126.6 0.4 collective-permute-start.1
  127.0 0.7 collective-permute-start
  127.7 0.0 copy-done
  127.7 0.3 fusion.8
  128.0 1.4 collective-permute-done.2
  129.4 0.3 fusion.4
  129.7 12.3 %collective-permute-done = bf16[256,512]{1,0:T(8,128)(2,1)S(1)} collective-permute-done((bf16[256,512]{1,0:T(8,128)(2,1)S(1)}, bf16[256,512]{1,0:T(8,128)(2,1)S(1)}, u32[]{:S(2)}, u32[]{:S(2)}) %collective-permute-start) | collective-permute-done | bytes 262176 | tf_op jit(solution)/shard_map/ppermute | solution.py:324
  142.0 0.3 convolution_add_fusion.1
  142.3 0.0 collective-permute-done.1
  142.3 0.3 fusion.1
  142.6 1.7 %add_convert_fusion = bf16[256,512]{1,0:T(8,128)(2,1)} fusion(bf16[256,512]{1,0:T(8,128)(2,1)S(1)} %fusion.1, bf16[256,2048]{1,0:T(8,128)(2,1)} %refs_3_.1, s32[]{:T(128)S(6)} %select_n.117), kind=kLoop, calls=%fused_computation.13 | loop fusion | flops 524288 | bytes 786436 | tf_op jit(solution)/shard_map/convert_element_type | solution.py:335
  (11 shorter events, 0.1 us)
Async XLA Ops:
  0.6 127.0 %copy-start = (bf16[2048,512]{1,0:T(8,128)(2,1)S(1)}, bf16[2048,512]{1,0:T(8,128)(2,1)}, u32[]{:S(2)}) copy-start(bf16[2048,512]{1,0:T(8,128)(2,1)} %param.19) | copy-start | bytes 6291460
  11.9 13.3 %copy-start.1 = (s32[64]{0:T(128)S(1)}, s32[64]{0:T(128)}, u32[]{:S(2)}) copy-start(s32[64]{0:T(128)} %refs_0_.1) | copy-start | bytes 772
  11.9 13.3 %copy-start.2 = (s32[64]{0:T(128)S(1)}, s32[64]{0:T(128)}, u32[]{:S(2)}) copy-start(s32[64]{0:T(128)} %refs_1_.1) | copy-start | bytes 772
  11.9 62.9 %all-to-all-start = ((bf16[64,16,1024]{2,1,0:T(8,128)(2,1)}), bf16[64,16,1024]{2,1,0:T(8,128)(2,1)}, u32[]{:S(2)}, u32[]{:S(2)}) async-start(bf16[64,16,1024]{2,1,0:T(8,128)(2,1)} %bitcast.28), calls=%async_computation | async-start | bytes 4194304 | tf_op jit(solution)/shard_map/all_to_all | solution.py:287
  85.0 35.3 %all-to-all-start.1 = ((bf16[64,16,512]{2,1,0:T(8,128)(2,1)}), bf16[64,16,512]{2,1,0:T(8,128)(2,1)S(1)}, u32[]{:S(2)}, u32[]{:S(2)}) async-start(bf16[64,16,512]{2,1,0:T(8,128)(2,1)} %bitcast.30), calls=%async_computation.1 | async-start | bytes 2097152 | tf_op jit(solution)/shard_map/all_to_all | solution.py:302
  121.6 7.8 %collective-permute-start.2 = (bf16[256,512]{1,0:T(8,128)(2,1)S(1)}, bf16[256,512]{1,0:T(8,128)(2,1)S(1)}, u32[]{:S(2)}, u32[]{:S(2)}) collective-permute-start(bf16[256,512]{1,0:T(8,128)(2,1)S(1)} %broadcast_select_fusion), channel_id=1, source_target_pairs={{0,3},{1,0},{2,1},{3,2},{4,7},{5,4},{6,5},{7,6},{8,11},{9,8},{10,9... | collective-permute-start | bytes 786440 | tf_op jit(solution)/shard_map/ppermute | solution.py:324
  126.6 15.7 %collective-permute-start.1 = (bf16[256,512]{1,0:T(8,128)(2,1)S(1)}, bf16[256,512]{1,0:T(8,128)(2,1)S(1)}, u32[]{:S(2)}, u32[]{:S(2)}) collective-permute-start(bf16[256,512]{1,0:T(8,128)(2,1)S(1)} %broadcast_select_fusion), channel_id=1, source_target_pairs={{0,2},{1,3},{2,0},{3,1},{4,6},{5,7},{6,4},{7,5},{8,10},{9,11},{10,... | collective-permute-start | bytes 786440 | tf_op jit(solution)/shard_map/ppermute | solution.py:324
  127.0 15.0 %collective-permute-start = (bf16[256,512]{1,0:T(8,128)(2,1)S(1)}, bf16[256,512]{1,0:T(8,128)(2,1)S(1)}, u32[]{:S(2)}, u32[]{:S(2)}) collective-permute-start(bf16[256,512]{1,0:T(8,128)(2,1)S(1)} %broadcast_select_fusion), channel_id=1, source_target_pairs={{0,1},{1,2},{2,3},{3,0},{4,5},{5,6},{6,7},{7,4},{8,9},{9,10},{10,1... | collective-permute-start | bytes 786440 | tf_op jit(solution)/shard_map/ppermute | solution.py:324

commit v17 on v16

--- a/solution.py
+++ b/solution.py
@@ -216,7 +216,7 @@
 
 def attend(qkv_slot, query_pos, key_pos, q_width, k_width, head_dim):
     rows = qkv_slot.shape[0]
-    blocks = 2
+    blocks = 4
     heads = q_width // head_dim
     causal_pairs = blocks * blocks
     pair_flops = 4 * (rows // blocks) ** 2 * head_dim

time: 145 us -> 148 us (1.021)
  Pallas kernels: 18.1 us -> 21.2 us
    pallas_call x1, Pallas kernels: 10.1 us -> 13.3 us  [attend(): pl.pallas_call(lambda *refs: attention_kernel(*refs, q_width=q_width, k_w...]
where the time goes in v17:
time: 148 us; the launch traced here: 147 us
  waiting for transfers between devices  80.3 us (54%)
  starting transfers between devices  24.1 us (16%)
  Pallas kernels  21.2 us (14%)
  other arithmetic  9.26 us (6%)
  local copies, waits for them, and re-layouts  8.4 us (6%)
  between operations  2.81 us (2%)
    all_to_all x1, waiting for transfers between devices, on_device(): lax.all_to_all(picked.reshape(devices, capacity, picked.shape[1]), 'req',...  45 us
    all_to_all x1, waiting for transfers between devices, on_device(): lax.all_to_all(mixture.reshape(devices, capacity, mixture.shape[1]), 'req...  21.6 us
    ppermute x3, waiting for transfers between devices, on_device(): lax.ppermute(attended, 'tp', perm=[(i, (i + shift) % tp_size) for i in ra...  13.7 us
    all_to_all x1, starting transfers between devices, on_device(): lax.all_to_all(picked.reshape(devices, capacity, picked.shape[1]), 'req',...  13.3 us
    pallas_call x1, Pallas kernels, attend(): pl.pallas_call(lambda *refs: attention_kernel(*refs, q_width=q_width, k_w...  13.3 us
    pallas_call x1, Pallas kernels, prepare(): pl.pallas_call(lambda *refs: prep_kernel(*refs, head_dim=head_dim, capaci...  7.96 us
    all_to_all x1, starting transfers between devices, on_device(): lax.all_to_all(mixture.reshape(devices, capacity, mixture.shape[1]), 'req...  7 us
    ppermute x3, starting transfers between devices, on_device(): lax.ppermute(attended, 'tp', perm=[(i, (i + shift) % tp_size) for i in ra...  3.81 us
  transfers between devices with their start and end apart: 5, of which 4 were waited for; matrix products, arithmetic and copies ran while one was open for 8% of the time, Pallas kernels for 0%

profile of v17, /device:TPU:1, one launch (start us, length us, event | category | flops | bytes accessed | tf_op | source)
XLA Modules:
  0.0 147.3 jit_solution(16635296760838816631)
XLA Ops:
  0.6 0.0 copy-start
  0.7 0.1 compare_select_fusion.9
  0.7 0.9 copy.17
  1.6 0.1 reduce-window.8
  1.7 0.1 reduce
  1.8 0.7 sub.52
  2.5 0.1 convert_reduce_fusion
  2.6 0.1 select_reduce_fusion
  2.7 1.2 fusion.10
  3.9 8.0 %shard_map.113 = bf16[1024,1024]{1,0:T(8,128)(2,1)} custom-call(s32[64]{0:T(128)} %refs_0_.1, s32[64]{0:T(128)} %refs_1_.1, s32[1]{0:T(128)} %bitcast.refs_2_, bf16[256,2048]{1,0:T(8,128)(2,1)} %refs_3_.1, bf16[2048]{0:T(1024)(128)(2,1)} %refs_4_.1, bf16[2048,512]{1,0:T(8,128)(2,1)} %refs_5_.1, bf16[2048,256]{1,0:T(8,128)(2,1)} %refs_6_.1, ...), custom_call_target="tpu_custom_call" | custom-call | flops 1610612736 | bytes 7340032 | tf_op jit(solution)/shard_map/pallas_call | solution.py:154
  11.9 0.0 copy-start.1
  11.9 0.0 copy-start.2
  11.9 13.3 %all-to-all-start = ((bf16[64,16,1024]{2,1,0:T(8,128)(2,1)}), bf16[64,16,1024]{2,1,0:T(8,128)(2,1)}, u32[]{:S(2)}, u32[]{:S(2)}) async-start(bf16[64,16,1024]{2,1,0:T(8,128)(2,1)} %bitcast.28), calls=%async_computation | async-start | bytes 4194304 | tf_op jit(solution)/shard_map/all_to_all | solution.py:287
  25.2 0.0 copy-done.1
  25.3 0.0 copy-done.2
  25.3 0.2 select_reduce_fusion.1
  25.4 0.7 dynamic_slice.27
  26.1 0.6 and_select_fusion.1
  26.8 0.1 broadcast_add_fusion
  26.8 0.1 add.191
  26.9 1.1 add.210.refs_1_
  28.0 0.6 dynamic_slice.28
  28.6 1.2 compare_select_fusion.refs_2_
  29.8 45.0 %all-to-all-done = bf16[64,16,1024]{2,1,0:T(8,128)(2,1)} async-done(((bf16[64,16,1024]{2,1,0:T(8,128)(2,1)}), bf16[64,16,1024]{2,1,0:T(8,128)(2,1)}, u32[]{:S(2)}, u32[]{:S(2)}) %all-to-all-start) | async-done | bytes 2097184 | tf_op jit(solution)/shard_map/all_to_all | solution.py:287
  74.9 13.3 %shard_map.114 = bf16[1024,512]{1,0:T(8,128)(2,1)} custom-call(bf16[1024,1024]{1,0:T(8,128)(2,1)} %bitcast.5.refs_0_, s32[1024,1]{1,0:T(8,128)} %add.210.refs_1_, s32[1,1024]{1,0:T(1,128)} %compare_select_fusion.refs_2_), custom_call_target="tpu_custom_call" | custom-call | flops 2147483648 | bytes 3145728 | tf_op jit(solution)/shard_map/pallas_call | solution.py:224
  88.1 7.0 %all-to-all-start.1 = ((bf16[64,16,512]{2,1,0:T(8,128)(2,1)}), bf16[64,16,512]{2,1,0:T(8,128)(2,1)S(1)}, u32[]{:S(2)}, u32[]{:S(2)}) async-start(bf16[64,16,512]{2,1,0:T(8,128)(2,1)} %bitcast.30), calls=%async_computation.1 | async-start | bytes 2097152 | tf_op jit(solution)/shard_map/all_to_all | solution.py:302
  97.1 1.0 scatter_custom_fusion
  98.1 0.1 multiply_reduce_fusion
  98.3 1.3 slice.14
  99.6 0.5 fusion.3
  100.1 0.6 copy.19
  100.7 1.1 slice_bitcast_fusion.1
  101.7 21.6 %all-to-all-done.1 = bf16[64,16,512]{2,1,0:T(8,128)(2,1)S(1)} async-done(((bf16[64,16,512]{2,1,0:T(8,128)(2,1)}), bf16[64,16,512]{2,1,0:T(8,128)(2,1)S(1)}, u32[]{:S(2)}, u32[]{:S(2)}) %all-to-all-start.1) | async-done | bytes 1048608 | tf_op jit(solution)/shard_map/all_to_all | solution.py:302
  123.3 1.2 gather_fusion
  124.4 0.1 broadcast_select_fusion
  124.6 2.8 %collective-permute-start.2 = (bf16[256,512]{1,0:T(8,128)(2,1)S(1)}, bf16[256,512]{1,0:T(8,128)(2,1)S(1)}, u32[]{:S(2)}, u32[]{:S(2)}) collective-permute-start(bf16[256,512]{1,0:T(8,128)(2,1)S(1)} %broadcast_select_fusion), channel_id=1, source_target_pairs={{0,3},{1,0},{2,1},{3,2},{4,7},{5,4},{6,5},{7,6},{8,11},{9,8},{10,9... | collective-permute-start | bytes 786440 | tf_op jit(solution)/shard_map/ppermute | solution.py:324
  127.3 2.3 %maximum_bitcast_fusion = bf16[2,1,1024,256]{3,2,1,0:T(8,128)(2,1)} fusion(bf16[1,1024,256]{2,1,0:T(8,128)(2,1)} %get-tuple-element.15, bf16[1,1024,256]{2,1,0:T(8,128)(2,1)} %get-tuple-element.14), kind=kLoop, calls=%fused_computation.10 | loop fusion | flops 524288 | bytes 2097152 | tf_op jit(solution)/shard_map/broadcast_in_dim | solution.py:315
  129.6 0.4 collective-permute-start.1
  130.0 0.6 collective-permute-start
  130.6 0.0 copy-done
  130.6 0.3 fusion.8
  130.9 1.4 collective-permute-done.2
  132.3 0.3 fusion.4
  132.6 12.3 %collective-permute-done = bf16[256,512]{1,0:T(8,128)(2,1)S(1)} collective-permute-done((bf16[256,512]{1,0:T(8,128)(2,1)S(1)}, bf16[256,512]{1,0:T(8,128)(2,1)S(1)}, u32[]{:S(2)}, u32[]{:S(2)}) %collective-permute-start) | collective-permute-done | bytes 262176 | tf_op jit(solution)/shard_map/ppermute | solution.py:324
  144.9 0.3 convolution_add_fusion.1
  145.2 0.0 collective-permute-done.1
  145.3 0.3 fusion.1
  145.6 1.7 %add_convert_fusion = bf16[256,512]{1,0:T(8,128)(2,1)} fusion(bf16[256,512]{1,0:T(8,128)(2,1)S(1)} %fusion.1, bf16[256,2048]{1,0:T(8,128)(2,1)} %refs_3_.1, s32[]{:T(128)S(6)} %select_n.117), kind=kLoop, calls=%fused_computation.13 | loop fusion | flops 524288 | bytes 786436 | tf_op jit(solution)/shard_map/convert_element_type | solution.py:335
  (11 shorter events, 0.1 us)
Async XLA Ops:
  0.6 130.0 %copy-start = (bf16[2048,512]{1,0:T(8,128)(2,1)S(1)}, bf16[2048,512]{1,0:T(8,128)(2,1)}, u32[]{:S(2)}) copy-start(bf16[2048,512]{1,0:T(8,128)(2,1)} %param.19) | copy-start | bytes 6291460
  11.9 13.3 %copy-start.1 = (s32[64]{0:T(128)S(1)}, s32[64]{0:T(128)}, u32[]{:S(2)}) copy-start(s32[64]{0:T(128)} %refs_0_.1) | copy-start | bytes 772
  11.9 13.3 %copy-start.2 = (s32[64]{0:T(128)S(1)}, s32[64]{0:T(128)}, u32[]{:S(2)}) copy-start(s32[64]{0:T(128)} %refs_1_.1) | copy-start | bytes 772
  11.9 62.9 %all-to-all-start = ((bf16[64,16,1024]{2,1,0:T(8,128)(2,1)}), bf16[64,16,1024]{2,1,0:T(8,128)(2,1)}, u32[]{:S(2)}, u32[]{:S(2)}) async-start(bf16[64,16,1024]{2,1,0:T(8,128)(2,1)} %bitcast.28), calls=%async_computation | async-start | bytes 4194304 | tf_op jit(solution)/shard_map/all_to_all | solution.py:287
  88.1 35.2 %all-to-all-start.1 = ((bf16[64,16,512]{2,1,0:T(8,128)(2,1)}), bf16[64,16,512]{2,1,0:T(8,128)(2,1)S(1)}, u32[]{:S(2)}, u32[]{:S(2)}) async-start(bf16[64,16,512]{2,1,0:T(8,128)(2,1)} %bitcast.30), calls=%async_computation.1 | async-start | bytes 2097152 | tf_op jit(solution)/shard_map/all_to_all | solution.py:302
  124.6 7.8 %collective-permute-start.2 = (bf16[256,512]{1,0:T(8,128)(2,1)S(1)}, bf16[256,512]{1,0:T(8,128)(2,1)S(1)}, u32[]{:S(2)}, u32[]{:S(2)}) collective-permute-start(bf16[256,512]{1,0:T(8,128)(2,1)S(1)} %broadcast_select_fusion), channel_id=1, source_target_pairs={{0,3},{1,0},{2,1},{3,2},{4,7},{5,4},{6,5},{7,6},{8,11},{9,8},{10,9... | collective-permute-start | bytes 786440 | tf_op jit(solution)/shard_map/ppermute | solution.py:324
  129.6 15.7 %collective-permute-start.1 = (bf16[256,512]{1,0:T(8,128)(2,1)S(1)}, bf16[256,512]{1,0:T(8,128)(2,1)S(1)}, u32[]{:S(2)}, u32[]{:S(2)}) collective-permute-start(bf16[256,512]{1,0:T(8,128)(2,1)S(1)} %broadcast_select_fusion), channel_id=1, source_target_pairs={{0,2},{1,3},{2,0},{3,1},{4,6},{5,7},{6,4},{7,5},{8,10},{9,11},{10,... | collective-permute-start | bytes 786440 | tf_op jit(solution)/shard_map/ppermute | solution.py:324
  130.0 14.9 %collective-permute-start = (bf16[256,512]{1,0:T(8,128)(2,1)S(1)}, bf16[256,512]{1,0:T(8,128)(2,1)S(1)}, u32[]{:S(2)}, u32[]{:S(2)}) collective-permute-start(bf16[256,512]{1,0:T(8,128)(2,1)S(1)} %broadcast_select_fusion), channel_id=1, source_target_pairs={{0,1},{1,2},{2,3},{3,0},{4,5},{5,6},{6,7},{7,4},{8,9},{9,10},{10,1... | collective-permute-start | bytes 786440 | tf_op jit(solution)/shard_map/ppermute | solution.py:324

commit v18 on v16

--- a/solution.py
+++ b/solution.py
@@ -320,7 +320,7 @@
         lax.dynamic_slice_in_dim(w_out, slice_index * w_rows, w_rows, 0),
         preferred_element_type=jnp.float32,
     )
-    for shift in range(1, tp_size):
+    for shift in sorted(range(1, tp_size), key=lambda s: min(s, tp_size - s)):
         passed = lax.ppermute(
             attended, "tp", perm=[(i, (i + shift) % tp_size) for i in range(tp_size)]
         )

time: 145 us -> 139 us (0.959)
  waiting for transfers between devices: 80.5 us -> 74.1 us
    ppermute x3, waiting for transfers between devices: 13.7 us -> 7.27 us  [on_device(): lax.ppermute(attended, 'tp', perm=[(i, (i + shift) % tp_size) for i in ra...]
  transfers between devices with their start and end apart: 5 -> 5, of which waited for: 4 -> 4; matrix products, arithmetic and copies ran while one was open for 8% -> 9% of each run, Pallas kernels for 0% -> 0%
where the time goes in v18:
time: 139 us
  waiting for transfers between devices  74.1 us (53%)
  starting transfers between devices  24.9 us (18%)
  Pallas kernels  18.1 us (13%)
  other arithmetic  9.26 us (7%)
  local copies, waits for them, and re-layouts  8.18 us (6%)
  between operations  2.81 us (2%)
    all_to_all x1, waiting for transfers between devices, on_device(): lax.all_to_all(picked.reshape(devices, capacity, picked.shape[1]), 'req',...  45 us
    all_to_all x1, waiting for transfers between devices, on_device(): lax.all_to_all(mixture.reshape(devices, capacity, mixture.shape[1]), 'req...  21.8 us
    all_to_all x1, starting transfers between devices, on_device(): lax.all_to_all(picked.reshape(devices, capacity, picked.shape[1]), 'req',...  13.3 us
    pallas_call x1, Pallas kernels, attend(): pl.pallas_call(lambda *refs: attention_kernel(*refs, q_width=q_width, k_w...  10.1 us
    pallas_call x1, Pallas kernels, prepare(): pl.pallas_call(lambda *refs: prep_kernel(*refs, head_dim=head_dim, capaci...  7.96 us
    ppermute x3, waiting for transfers between devices, on_device(): lax.ppermute(attended, 'tp', perm=[(i, (i + shift) % tp_size) for i in ra...  7.27 us
    all_to_all x1, starting transfers between devices, on_device(): lax.all_to_all(mixture.reshape(devices, capacity, mixture.shape[1]), 'req...  7.14 us
    ppermute x3, starting transfers between devices, on_device(): lax.ppermute(attended, 'tp', perm=[(i, (i + shift) % tp_size) for i in ra...  4.45 us
  transfers between devices with their start and end apart: 5, of which 4 were waited for; matrix products, arithmetic and copies ran while one was open for 9% of the time, Pallas kernels for 0%

profile of v18, /device:TPU:1, one launch (start us, length us, event | category | flops | bytes accessed | tf_op | source)
XLA Modules:
  0.0 138.5 jit_solution(12776643447142145636)
XLA Ops:
  0.6 0.0 copy-start
  0.7 0.1 compare_select_fusion.9
  0.7 0.9 copy.17
  1.6 0.1 reduce-window.8
  1.7 0.1 reduce
  1.8 0.7 sub.52
  2.5 0.1 convert_reduce_fusion
  2.6 0.1 select_reduce_fusion
  2.7 1.2 fusion.10
  3.9 8.0 %shard_map.113 = bf16[1024,1024]{1,0:T(8,128)(2,1)} custom-call(s32[64]{0:T(128)} %refs_0_.1, s32[64]{0:T(128)} %refs_1_.1, s32[1]{0:T(128)} %bitcast.refs_2_, bf16[256,2048]{1,0:T(8,128)(2,1)} %refs_3_.1, bf16[2048]{0:T(1024)(128)(2,1)} %refs_4_.1, bf16[2048,512]{1,0:T(8,128)(2,1)} %refs_5_.1, bf16[2048,256]{1,0:T(8,128)(2,1)} %refs_6_.1, ...), custom_call_target="tpu_custom_call" | custom-call | flops 1610612736 | bytes 7340032 | tf_op jit(solution)/shard_map/pallas_call | solution.py:154
  11.9 0.0 copy-start.1
  11.9 0.0 copy-start.2
  11.9 13.3 %all-to-all-start = ((bf16[64,16,1024]{2,1,0:T(8,128)(2,1)}), bf16[64,16,1024]{2,1,0:T(8,128)(2,1)}, u32[]{:S(2)}, u32[]{:S(2)}) async-start(bf16[64,16,1024]{2,1,0:T(8,128)(2,1)} %bitcast.28), calls=%async_computation | async-start | bytes 4194304 | tf_op jit(solution)/shard_map/all_to_all | solution.py:287
  25.2 0.0 copy-done.1
  25.2 0.0 copy-done.2
  25.3 0.2 select_reduce_fusion.1
  25.4 0.7 dynamic_slice.27
  26.1 0.6 and_select_fusion.1
  26.7 0.1 broadcast_add_fusion
  26.8 0.1 add.191
  26.9 1.1 add.210.refs_1_
  28.0 0.6 dynamic_slice.28
  28.6 1.2 compare_select_fusion.refs_2_
  29.8 45.0 %all-to-all-done = bf16[64,16,1024]{2,1,0:T(8,128)(2,1)} async-done(((bf16[64,16,1024]{2,1,0:T(8,128)(2,1)}), bf16[64,16,1024]{2,1,0:T(8,128)(2,1)}, u32[]{:S(2)}, u32[]{:S(2)}) %all-to-all-start) | async-done | bytes 2097184 | tf_op jit(solution)/shard_map/all_to_all | solution.py:287
  74.9 10.1 %shard_map.114 = bf16[1024,512]{1,0:T(8,128)(2,1)} custom-call(bf16[1024,1024]{1,0:T(8,128)(2,1)} %bitcast.5.refs_0_, s32[1024,1]{1,0:T(8,128)} %add.210.refs_1_, s32[1,1024]{1,0:T(1,128)} %compare_select_fusion.refs_2_), custom_call_target="tpu_custom_call" | custom-call | flops 2147483648 | bytes 3145728 | tf_op jit(solution)/shard_map/pallas_call | solution.py:224
  85.0 7.1 %all-to-all-start.1 = ((bf16[64,16,512]{2,1,0:T(8,128)(2,1)}), bf16[64,16,512]{2,1,0:T(8,128)(2,1)S(1)}, u32[]{:S(2)}, u32[]{:S(2)}) async-start(bf16[64,16,512]{2,1,0:T(8,128)(2,1)} %bitcast.30), calls=%async_computation.1 | async-start | bytes 2097152 | tf_op jit(solution)/shard_map/all_to_all | solution.py:302
  94.2 0.8 scatter_custom_fusion
  94.9 0.1 multiply_reduce_fusion
  95.1 1.3 slice.14
  96.4 0.5 fusion.3
  96.9 0.6 copy.19
  97.5 1.1 slice_bitcast_fusion.1
  98.5 21.8 %all-to-all-done.1 = bf16[64,16,512]{2,1,0:T(8,128)(2,1)S(1)} async-done(((bf16[64,16,512]{2,1,0:T(8,128)(2,1)}), bf16[64,16,512]{2,1,0:T(8,128)(2,1)S(1)}, u32[]{:S(2)}, u32[]{:S(2)}) %all-to-all-start.1) | async-done | bytes 1048608 | tf_op jit(solution)/shard_map/all_to_all | solution.py:302
  120.3 1.2 gather_fusion
  121.5 0.1 broadcast_select_fusion
  121.6 3.0 %collective-permute-start.2 = (bf16[256,512]{1,0:T(8,128)(2,1)S(1)}, bf16[256,512]{1,0:T(8,128)(2,1)S(1)}, u32[]{:S(2)}, u32[]{:S(2)}) collective-permute-start(bf16[256,512]{1,0:T(8,128)(2,1)S(1)} %broadcast_select_fusion), channel_id=1, source_target_pairs={{0,2},{1,3},{2,0},{3,1},{4,6},{5,7},{6,4},{7,5},{8,10},{9,11},{10,... | collective-permute-start | bytes 786440 | tf_op jit(solution)/shard_map/ppermute | solution.py:324
  124.6 2.3 %maximum_bitcast_fusion = bf16[2,1,1024,256]{3,2,1,0:T(8,128)(2,1)} fusion(bf16[1,1024,256]{2,1,0:T(8,128)(2,1)} %get-tuple-element.15, bf16[1,1024,256]{2,1,0:T(8,128)(2,1)} %get-tuple-element.14), kind=kLoop, calls=%fused_computation.10 | loop fusion | flops 524288 | bytes 2097152 | tf_op jit(solution)/shard_map/broadcast_in_dim | solution.py:315
  126.8 0.8 collective-permute-start.1
  127.6 0.7 collective-permute-start
  128.3 0.0 copy-done
  128.3 0.3 fusion.8
  128.6 1.3 collective-permute-done.2
  129.9 0.3 fusion.4
  130.2 6.0 %collective-permute-done = bf16[256,512]{1,0:T(8,128)(2,1)S(1)} collective-permute-done((bf16[256,512]{1,0:T(8,128)(2,1)S(1)}, bf16[256,512]{1,0:T(8,128)(2,1)S(1)}, u32[]{:S(2)}, u32[]{:S(2)}) %collective-permute-start) | collective-permute-done | bytes 262176 | tf_op jit(solution)/shard_map/ppermute | solution.py:324
  136.2 0.3 convolution_add_fusion.1
  136.5 0.0 collective-permute-done.1
  136.5 0.3 fusion.1
  136.8 1.7 %add_convert_fusion = bf16[256,512]{1,0:T(8,128)(2,1)} fusion(bf16[256,512]{1,0:T(8,128)(2,1)S(1)} %fusion.1, bf16[256,2048]{1,0:T(8,128)(2,1)} %refs_3_.1, s32[]{:T(128)S(6)} %select_n.117), kind=kLoop, calls=%fused_computation.13 | loop fusion | flops 524288 | bytes 786436 | tf_op jit(solution)/shard_map/convert_element_type | solution.py:335
  (11 shorter events, 0.1 us)
Async XLA Ops:
  0.6 127.7 %copy-start = (bf16[2048,512]{1,0:T(8,128)(2,1)S(1)}, bf16[2048,512]{1,0:T(8,128)(2,1)}, u32[]{:S(2)}) copy-start(bf16[2048,512]{1,0:T(8,128)(2,1)} %param.19) | copy-start | bytes 6291460
  11.9 13.3 %copy-start.1 = (s32[64]{0:T(128)S(1)}, s32[64]{0:T(128)}, u32[]{:S(2)}) copy-start(s32[64]{0:T(128)} %refs_0_.1) | copy-start | bytes 772
  11.9 13.3 %copy-start.2 = (s32[64]{0:T(128)S(1)}, s32[64]{0:T(128)}, u32[]{:S(2)}) copy-start(s32[64]{0:T(128)} %refs_1_.1) | copy-start | bytes 772
  11.9 62.9 %all-to-all-start = ((bf16[64,16,1024]{2,1,0:T(8,128)(2,1)}), bf16[64,16,1024]{2,1,0:T(8,128)(2,1)}, u32[]{:S(2)}, u32[]{:S(2)}) async-start(bf16[64,16,1024]{2,1,0:T(8,128)(2,1)} %bitcast.28), calls=%async_computation | async-start | bytes 4194304 | tf_op jit(solution)/shard_map/all_to_all | solution.py:287
  85.0 35.3 %all-to-all-start.1 = ((bf16[64,16,512]{2,1,0:T(8,128)(2,1)}), bf16[64,16,512]{2,1,0:T(8,128)(2,1)S(1)}, u32[]{:S(2)}, u32[]{:S(2)}) async-start(bf16[64,16,512]{2,1,0:T(8,128)(2,1)} %bitcast.30), calls=%async_computation.1 | async-start | bytes 2097152 | tf_op jit(solution)/shard_map/all_to_all | solution.py:302
  121.6 8.3 %collective-permute-start.2 = (bf16[256,512]{1,0:T(8,128)(2,1)S(1)}, bf16[256,512]{1,0:T(8,128)(2,1)S(1)}, u32[]{:S(2)}, u32[]{:S(2)}) collective-permute-start(bf16[256,512]{1,0:T(8,128)(2,1)S(1)} %broadcast_select_fusion), channel_id=1, source_target_pairs={{0,2},{1,3},{2,0},{3,1},{4,6},{5,7},{6,4},{7,5},{8,10},{9,11},{10,... | collective-permute-start | bytes 786440 | tf_op jit(solution)/shard_map/ppermute | solution.py:324
  126.8 9.6 %collective-permute-start.1 = (bf16[256,512]{1,0:T(8,128)(2,1)S(1)}, bf16[256,512]{1,0:T(8,128)(2,1)S(1)}, u32[]{:S(2)}, u32[]{:S(2)}) collective-permute-start(bf16[256,512]{1,0:T(8,128)(2,1)S(1)} %broadcast_select_fusion), channel_id=1, source_target_pairs={{0,3},{1,0},{2,1},{3,2},{4,7},{5,4},{6,5},{7,6},{8,11},{9,8},{10,9... | collective-permute-start | bytes 786440 | tf_op jit(solution)/shard_map/ppermute | solution.py:324
  127.6 8.5 %collective-permute-start = (bf16[256,512]{1,0:T(8,128)(2,1)S(1)}, bf16[256,512]{1,0:T(8,128)(2,1)S(1)}, u32[]{:S(2)}, u32[]{:S(2)}) collective-permute-start(bf16[256,512]{1,0:T(8,128)(2,1)S(1)} %broadcast_select_fusion), channel_id=1, source_target_pairs={{0,1},{1,2},{2,3},{3,0},{4,5},{5,6},{6,7},{7,4},{8,9},{9,10},{10,1... | collective-permute-start | bytes 786440 | tf_op jit(solution)/shard_map/ppermute | solution.py:324

commit v19 on v18

--- a/solution.py
+++ b/solution.py
@@ -320,7 +320,7 @@
         lax.dynamic_slice_in_dim(w_out, slice_index * w_rows, w_rows, 0),
         preferred_element_type=jnp.float32,
     )
-    for shift in sorted(range(1, tp_size), key=lambda s: min(s, tp_size - s)):
+    for shift in sorted(range(1, tp_size), key=lambda s: (min(s, tp_size - s), -s)):
         passed = lax.ppermute(
             attended, "tp", perm=[(i, (i + shift) % tp_size) for i in range(tp_size)]
         )

time: 139 us -> 139 us (level)
  transfers between devices with their start and end apart: 5 -> 5, of which waited for: 4 -> 5; matrix products, arithmetic and copies ran while one was open for 9% -> 9% of each run, Pallas kernels for 0% -> 0%
where the time goes in v19:
time: 139 us
  waiting for transfers between devices  72.9 us (52%)
  starting transfers between devices  26.1 us (19%)
  Pallas kernels  18.1 us (13%)
  other arithmetic  9.26 us (7%)
  local copies, waits for them, and re-layouts  8.18 us (6%)
  between operations  2.81 us (2%)
    all_to_all x1, waiting for transfers between devices, on_device(): lax.all_to_all(picked.reshape(devices, capacity, picked.shape[1]), 'req',...  45 us
    all_to_all x1, waiting for transfers between devices, on_device(): lax.all_to_all(mixture.reshape(devices, capacity, mixture.shape[1]), 'req...  21.8 us
    all_to_all x1, starting transfers between devices, on_device(): lax.all_to_all(picked.reshape(devices, capacity, picked.shape[1]), 'req',...  13.3 us
    pallas_call x1, Pallas kernels, attend(): pl.pallas_call(lambda *refs: attention_kernel(*refs, q_width=q_width, k_w...  10.1 us
    pallas_call x1, Pallas kernels, prepare(): pl.pallas_call(lambda *refs: prep_kernel(*refs, head_dim=head_dim, capaci...  7.96 us
    all_to_all x1, starting transfers between devices, on_device(): lax.all_to_all(mixture.reshape(devices, capacity, mixture.shape[1]), 'req...  7.14 us
    ppermute x3, waiting for transfers between devices, on_device(): lax.ppermute(attended, 'tp', perm=[(i, (i + shift) % tp_size) for i in ra...  6.09 us
    ppermute x3, starting transfers between devices, on_device(): lax.ppermute(attended, 'tp', perm=[(i, (i + shift) % tp_size) for i in ra...  5.67 us
  transfers between devices with their start and end apart: 5, of which 5 were waited for; matrix products, arithmetic and copies ran while one was open for 9% of the time, Pallas kernels for 0%

profile of v19, /device:TPU:1, one launch (start us, length us, event | category | flops | bytes accessed | tf_op | source)
XLA Modules:
  0.0 138.5 jit_solution(15988383577714310830)
XLA Ops:
  0.6 0.0 copy-start
  0.7 0.1 compare_select_fusion.9
  0.7 0.9 copy.17
  1.6 0.1 reduce-window.8
  1.7 0.1 reduce
  1.8 0.7 sub.52
  2.5 0.1 convert_reduce_fusion
  2.6 0.1 select_reduce_fusion
  2.7 1.2 fusion.10
  3.9 8.0 %shard_map.113 = bf16[1024,1024]{1,0:T(8,128)(2,1)} custom-call(s32[64]{0:T(128)} %refs_0_.1, s32[64]{0:T(128)} %refs_1_.1, s32[1]{0:T(128)} %bitcast.refs_2_, bf16[256,2048]{1,0:T(8,128)(2,1)} %refs_3_.1, bf16[2048]{0:T(1024)(128)(2,1)} %refs_4_.1, bf16[2048,512]{1,0:T(8,128)(2,1)} %refs_5_.1, bf16[2048,256]{1,0:T(8,128)(2,1)} %refs_6_.1, ...), custom_call_target="tpu_custom_call" | custom-call | flops 1610612736 | bytes 7340032 | tf_op jit(solution)/shard_map/pallas_call | solution.py:154
  11.9 0.0 copy-start.1
  11.9 0.0 copy-start.2
  11.9 13.3 %all-to-all-start = ((bf16[64,16,1024]{2,1,0:T(8,128)(2,1)}), bf16[64,16,1024]{2,1,0:T(8,128)(2,1)}, u32[]{:S(2)}, u32[]{:S(2)}) async-start(bf16[64,16,1024]{2,1,0:T(8,128)(2,1)} %bitcast.28), calls=%async_computation | async-start | bytes 4194304 | tf_op jit(solution)/shard_map/all_to_all | solution.py:287
  25.2 0.0 copy-done.1
  25.2 0.0 copy-done.2
  25.3 0.2 select_reduce_fusion.1
  25.4 0.7 dynamic_slice.27
  26.1 0.6 and_select_fusion.1
  26.7 0.1 broadcast_add_fusion
  26.8 0.1 add.191
  26.9 1.1 add.210.refs_1_
  28.0 0.6 dynamic_slice.28
  28.6 1.2 compare_select_fusion.refs_2_
  29.8 45.0 %all-to-all-done = bf16[64,16,1024]{2,1,0:T(8,128)(2,1)} async-done(((bf16[64,16,1024]{2,1,0:T(8,128)(2,1)}), bf16[64,16,1024]{2,1,0:T(8,128)(2,1)}, u32[]{:S(2)}, u32[]{:S(2)}) %all-to-all-start) | async-done | bytes 2097184 | tf_op jit(solution)/shard_map/all_to_all | solution.py:287
  74.9 10.1 %shard_map.114 = bf16[1024,512]{1,0:T(8,128)(2,1)} custom-call(bf16[1024,1024]{1,0:T(8,128)(2,1)} %bitcast.5.refs_0_, s32[1024,1]{1,0:T(8,128)} %add.210.refs_1_, s32[1,1024]{1,0:T(1,128)} %compare_select_fusion.refs_2_), custom_call_target="tpu_custom_call" | custom-call | flops 2147483648 | bytes 3145728 | tf_op jit(solution)/shard_map/pallas_call | solution.py:224
  85.0 7.1 %all-to-all-start.1 = ((bf16[64,16,512]{2,1,0:T(8,128)(2,1)}), bf16[64,16,512]{2,1,0:T(8,128)(2,1)S(1)}, u32[]{:S(2)}, u32[]{:S(2)}) async-start(bf16[64,16,512]{2,1,0:T(8,128)(2,1)} %bitcast.30), calls=%async_computation.1 | async-start | bytes 2097152 | tf_op jit(solution)/shard_map/all_to_all | solution.py:302
  94.2 0.8 scatter_custom_fusion
  94.9 0.1 multiply_reduce_fusion
  95.1 1.3 slice.14
  96.4 0.5 fusion.3
  96.9 0.6 copy.19
  97.5 1.1 slice_bitcast_fusion.1
  98.5 21.8 %all-to-all-done.1 = bf16[64,16,512]{2,1,0:T(8,128)(2,1)S(1)} async-done(((bf16[64,16,512]{2,1,0:T(8,128)(2,1)}), bf16[64,16,512]{2,1,0:T(8,128)(2,1)S(1)}, u32[]{:S(2)}, u32[]{:S(2)}) %all-to-all-start.1) | async-done | bytes 1048608 | tf_op jit(solution)/shard_map/all_to_all | solution.py:302
  120.3 1.2 gather_fusion
  121.5 0.1 broadcast_select_fusion
  121.6 3.0 %collective-permute-start.2 = (bf16[256,512]{1,0:T(8,128)(2,1)S(1)}, bf16[256,512]{1,0:T(8,128)(2,1)S(1)}, u32[]{:S(2)}, u32[]{:S(2)}) collective-permute-start(bf16[256,512]{1,0:T(8,128)(2,1)S(1)} %broadcast_select_fusion), channel_id=1, source_target_pairs={{0,2},{1,3},{2,0},{3,1},{4,6},{5,7},{6,4},{7,5},{8,10},{9,11},{10,... | collective-permute-start | bytes 786440 | tf_op jit(solution)/shard_map/ppermute | solution.py:324
  124.6 2.3 %maximum_bitcast_fusion = bf16[2,1,1024,256]{3,2,1,0:T(8,128)(2,1)} fusion(bf16[1,1024,256]{2,1,0:T(8,128)(2,1)} %get-tuple-element.15, bf16[1,1024,256]{2,1,0:T(8,128)(2,1)} %get-tuple-element.14), kind=kLoop, calls=%fused_computation.10 | loop fusion | flops 524288 | bytes 2097152 | tf_op jit(solution)/shard_map/broadcast_in_dim | solution.py:315
  126.8 0.4 collective-permute-start.1
  127.2 2.3 %collective-permute-start = (bf16[256,512]{1,0:T(8,128)(2,1)S(1)}, bf16[256,512]{1,0:T(8,128)(2,1)S(1)}, u32[]{:S(2)}, u32[]{:S(2)}) collective-permute-start(bf16[256,512]{1,0:T(8,128)(2,1)S(1)} %broadcast_select_fusion), channel_id=1, source_target_pairs={{0,3},{1,0},{2,1},{3,2},{4,7},{5,4},{6,5},{7,6},{8,11},{9,8},{10,9... | collective-permute-start | bytes 786440 | tf_op jit(solution)/shard_map/ppermute | solution.py:324
  129.5 0.0 copy-done
  129.5 0.3 fusion.8
  129.8 0.1 collective-permute-done.2
  129.9 0.3 fusion.4
  130.2 5.6 %collective-permute-done = bf16[256,512]{1,0:T(8,128)(2,1)S(1)} collective-permute-done((bf16[256,512]{1,0:T(8,128)(2,1)S(1)}, bf16[256,512]{1,0:T(8,128)(2,1)S(1)}, u32[]{:S(2)}, u32[]{:S(2)}) %collective-permute-start) | collective-permute-done | bytes 262176 | tf_op jit(solution)/shard_map/ppermute | solution.py:324
  135.8 0.3 convolution_add_fusion.1
  136.1 0.4 collective-permute-done.1
  136.5 0.3 fusion.1
  136.8 1.7 %add_convert_fusion = bf16[256,512]{1,0:T(8,128)(2,1)} fusion(bf16[256,512]{1,0:T(8,128)(2,1)S(1)} %fusion.1, bf16[256,2048]{1,0:T(8,128)(2,1)} %refs_3_.1, s32[]{:T(128)S(6)} %select_n.117), kind=kLoop, calls=%fused_computation.13 | loop fusion | flops 524288 | bytes 786436 | tf_op jit(solution)/shard_map/convert_element_type | solution.py:335
  (11 shorter events, 0.1 us)
Async XLA Ops:
  0.6 128.9 %copy-start = (bf16[2048,512]{1,0:T(8,128)(2,1)S(1)}, bf16[2048,512]{1,0:T(8,128)(2,1)}, u32[]{:S(2)}) copy-start(bf16[2048,512]{1,0:T(8,128)(2,1)} %param.19) | copy-start | bytes 6291460
  11.9 13.3 %copy-start.1 = (s32[64]{0:T(128)S(1)}, s32[64]{0:T(128)}, u32[]{:S(2)}) copy-start(s32[64]{0:T(128)} %refs_0_.1) | copy-start | bytes 772
  11.9 13.3 %copy-start.2 = (s32[64]{0:T(128)S(1)}, s32[64]{0:T(128)}, u32[]{:S(2)}) copy-start(s32[64]{0:T(128)} %refs_1_.1) | copy-start | bytes 772
  11.9 62.9 %all-to-all-start = ((bf16[64,16,1024]{2,1,0:T(8,128)(2,1)}), bf16[64,16,1024]{2,1,0:T(8,128)(2,1)}, u32[]{:S(2)}, u32[]{:S(2)}) async-start(bf16[64,16,1024]{2,1,0:T(8,128)(2,1)} %bitcast.28), calls=%async_computation | async-start | bytes 4194304 | tf_op jit(solution)/shard_map/all_to_all | solution.py:287
  85.0 35.3 %all-to-all-start.1 = ((bf16[64,16,512]{2,1,0:T(8,128)(2,1)}), bf16[64,16,512]{2,1,0:T(8,128)(2,1)S(1)}, u32[]{:S(2)}, u32[]{:S(2)}) async-start(bf16[64,16,512]{2,1,0:T(8,128)(2,1)} %bitcast.30), calls=%async_computation.1 | async-start | bytes 2097152 | tf_op jit(solution)/shard_map/all_to_all | solution.py:302
  121.6 8.3 %collective-permute-start.2 = (bf16[256,512]{1,0:T(8,128)(2,1)S(1)}, bf16[256,512]{1,0:T(8,128)(2,1)S(1)}, u32[]{:S(2)}, u32[]{:S(2)}) collective-permute-start(bf16[256,512]{1,0:T(8,128)(2,1)S(1)} %broadcast_select_fusion), channel_id=1, source_target_pairs={{0,2},{1,3},{2,0},{3,1},{4,6},{5,7},{6,4},{7,5},{8,10},{9,11},{10,... | collective-permute-start | bytes 786440 | tf_op jit(solution)/shard_map/ppermute | solution.py:324
  126.8 9.7 %collective-permute-start.1 = (bf16[256,512]{1,0:T(8,128)(2,1)S(1)}, bf16[256,512]{1,0:T(8,128)(2,1)S(1)}, u32[]{:S(2)}, u32[]{:S(2)}) collective-permute-start(bf16[256,512]{1,0:T(8,128)(2,1)S(1)} %broadcast_select_fusion), channel_id=1, source_target_pairs={{0,1},{1,2},{2,3},{3,0},{4,5},{5,6},{6,7},{7,4},{8,9},{9,10},{10,1... | collective-permute-start | bytes 786440 | tf_op jit(solution)/shard_map/ppermute | solution.py:324
  127.2 8.6 %collective-permute-start = (bf16[256,512]{1,0:T(8,128)(2,1)S(1)}, bf16[256,512]{1,0:T(8,128)(2,1)S(1)}, u32[]{:S(2)}, u32[]{:S(2)}) collective-permute-start(bf16[256,512]{1,0:T(8,128)(2,1)S(1)} %broadcast_select_fusion), channel_id=1, source_target_pairs={{0,3},{1,0},{2,1},{3,2},{4,7},{5,4},{6,5},{7,6},{8,11},{9,8},{10,9... | collective-permute-start | bytes 786440 | tf_op jit(solution)/shard_map/ppermute | solution.py:324

commit v20 on v18

--- a/solution.py
+++ b/solution.py
@@ -315,21 +315,21 @@
     kv_cache = jnp.stack([kv_rows[:, :k_width], kv_rows[:, k_width:]])[:, None]
     tp_size = lax.axis_size("tp")
     w_rows = w_out.shape[0] // tp_size
-    summed = jnp.dot(
-        attended,
-        lax.dynamic_slice_in_dim(w_out, slice_index * w_rows, w_rows, 0),
-        preferred_element_type=jnp.float32,
-    )
+    passes = []
     for shift in sorted(range(1, tp_size), key=lambda s: min(s, tp_size - s)):
         passed = lax.ppermute(
             attended, "tp", perm=[(i, (i + shift) % tp_size) for i in range(tp_size)]
         )
-        source = jnp.mod(slice_index - shift, tp_size)
-        summed = summed + jnp.dot(
+        passes.append((passed, jnp.mod(slice_index - shift, tp_size)))
+    passes.append((attended, slice_index))
+    summed = None
+    for passed, source in passes:
+        product = jnp.dot(
             passed,
             lax.dynamic_slice_in_dim(w_out, source * w_rows, w_rows, 0),
             preferred_element_type=jnp.float32,
         )
+        summed = product if summed is None else summed + product
     branch = lax.optimization_barrier(summed.astype(jnp.bfloat16))
     residual = lax.dynamic_slice_in_dim(hidden, slice_index * out_width, out_width, 1)
     hidden_out = (residual.astype(jnp.float32) + branch.astype(jnp.float32)).astype(jnp.bfloat16)

time: 139 us -> 139 us (level)
  no operation moved by 1% of the time
where the time goes in v20:
time: 139 us; the launch traced here: 138 us
  waiting for transfers between devices  73.9 us (53%)
  starting transfers between devices  24.9 us (18%)
  Pallas kernels  18.1 us (13%)
  other arithmetic  9.26 us (7%)
  local copies, waits for them, and re-layouts  8.18 us (6%)
  between operations  2.82 us (2%)
    all_to_all x1, waiting for transfers between devices, on_device(): lax.all_to_all(picked.reshape(devices, capacity, picked.shape[1]), 'req',...  45 us
    all_to_all x1, waiting for transfers between devices, on_device(): lax.all_to_all(mixture.reshape(devices, capacity, mixture.shape[1]), 'req...  21.8 us
    all_to_all x1, starting transfers between devices, on_device(): lax.all_to_all(picked.reshape(devices, capacity, picked.shape[1]), 'req',...  13.3 us
    pallas_call x1, Pallas kernels, attend(): pl.pallas_call(lambda *refs: attention_kernel(*refs, q_width=q_width, k_w...  10.1 us
    pallas_call x1, Pallas kernels, prepare(): pl.pallas_call(lambda *refs: prep_kernel(*refs, head_dim=head_dim, capaci...  7.96 us
    all_to_all x1, starting transfers between devices, on_device(): lax.all_to_all(mixture.reshape(devices, capacity, mixture.shape[1]), 'req...  7.14 us
    ppermute x3, waiting for transfers between devices, on_device(): lax.ppermute(attended, 'tp', perm=[(i, (i + shift) % tp_size) for i in ra...  7.11 us
    ppermute x3, starting transfers between devices, on_device(): lax.ppermute(attended, 'tp', perm=[(i, (i + shift) % tp_size) for i in ra...  4.45 us
  transfers between devices with their start and end apart: 5, of which 4 were waited for; matrix products, arithmetic and copies ran while one was open for 9% of the time, Pallas kernels for 0%

profile of v20, /device:TPU:1, one launch (start us, length us, event | category | flops | bytes accessed | tf_op | source)
XLA Modules:
  0.0 138.4 jit_solution(7911810040241498317)
XLA Ops:
  0.6 0.0 copy-start
  0.7 0.1 compare_select_fusion.9
  0.7 0.9 copy.17
  1.6 0.1 reduce-window.8
  1.7 0.1 reduce
  1.8 0.7 sub.52
  2.5 0.1 convert_reduce_fusion
  2.6 0.1 select_reduce_fusion
  2.7 1.2 fusion.12
  3.9 8.0 %shard_map.113 = bf16[1024,1024]{1,0:T(8,128)(2,1)} custom-call(s32[64]{0:T(128)} %refs_0_.1, s32[64]{0:T(128)} %refs_1_.1, s32[1]{0:T(128)} %bitcast.refs_2_, bf16[256,2048]{1,0:T(8,128)(2,1)} %refs_3_.1, bf16[2048]{0:T(1024)(128)(2,1)} %refs_4_.1, bf16[2048,512]{1,0:T(8,128)(2,1)} %refs_5_.1, bf16[2048,256]{1,0:T(8,128)(2,1)} %refs_6_.1, ...), custom_call_target="tpu_custom_call" | custom-call | flops 1610612736 | bytes 7340032 | tf_op jit(solution)/shard_map/pallas_call | solution.py:154
  11.9 0.0 copy-start.1
  11.9 0.0 copy-start.2
  11.9 13.3 %all-to-all-start = ((bf16[64,16,1024]{2,1,0:T(8,128)(2,1)}), bf16[64,16,1024]{2,1,0:T(8,128)(2,1)}, u32[]{:S(2)}, u32[]{:S(2)}) async-start(bf16[64,16,1024]{2,1,0:T(8,128)(2,1)} %bitcast.28), calls=%async_computation | async-start | bytes 4194304 | tf_op jit(solution)/shard_map/all_to_all | solution.py:287
  25.2 0.0 copy-done.1
  25.2 0.0 copy-done.2
  25.3 0.2 select_reduce_fusion.1
  25.4 0.7 dynamic_slice.27
  26.1 0.6 and_select_fusion.1
  26.7 0.1 broadcast_add_fusion
  26.8 0.1 add.191
  26.9 1.1 add.210.refs_1_
  28.0 0.6 dynamic_slice.28
  28.6 1.2 compare_select_fusion.refs_2_
  29.8 45.0 %all-to-all-done = bf16[64,16,1024]{2,1,0:T(8,128)(2,1)} async-done(((bf16[64,16,1024]{2,1,0:T(8,128)(2,1)}), bf16[64,16,1024]{2,1,0:T(8,128)(2,1)}, u32[]{:S(2)}, u32[]{:S(2)}) %all-to-all-start) | async-done | bytes 2097184 | tf_op jit(solution)/shard_map/all_to_all | solution.py:287
  74.9 10.1 %shard_map.114 = bf16[1024,512]{1,0:T(8,128)(2,1)} custom-call(bf16[1024,1024]{1,0:T(8,128)(2,1)} %bitcast.5.refs_0_, s32[1024,1]{1,0:T(8,128)} %add.210.refs_1_, s32[1,1024]{1,0:T(1,128)} %compare_select_fusion.refs_2_), custom_call_target="tpu_custom_call" | custom-call | flops 2147483648 | bytes 3145728 | tf_op jit(solution)/shard_map/pallas_call | solution.py:224
  85.0 7.1 %all-to-all-start.1 = ((bf16[64,16,512]{2,1,0:T(8,128)(2,1)}), bf16[64,16,512]{2,1,0:T(8,128)(2,1)S(1)}, u32[]{:S(2)}, u32[]{:S(2)}) async-start(bf16[64,16,512]{2,1,0:T(8,128)(2,1)} %bitcast.30), calls=%async_computation.1 | async-start | bytes 2097152 | tf_op jit(solution)/shard_map/all_to_all | solution.py:302
  94.2 0.8 scatter_custom_fusion
  94.9 0.1 multiply_reduce_fusion
  95.1 1.3 slice.14
  96.4 0.5 fusion.4
  96.9 0.6 copy.19
  97.5 1.1 slice_bitcast_fusion.1
  98.5 21.8 %all-to-all-done.1 = bf16[64,16,512]{2,1,0:T(8,128)(2,1)S(1)} async-done(((bf16[64,16,512]{2,1,0:T(8,128)(2,1)}), bf16[64,16,512]{2,1,0:T(8,128)(2,1)S(1)}, u32[]{:S(2)}, u32[]{:S(2)}) %all-to-all-start.1) | async-done | bytes 1048608 | tf_op jit(solution)/shard_map/all_to_all | solution.py:302
  120.3 1.2 gather_fusion
  121.5 0.1 broadcast_select_fusion
  121.6 3.0 %collective-permute-start.2 = (bf16[256,512]{1,0:T(8,128)(2,1)S(1)}, bf16[256,512]{1,0:T(8,128)(2,1)S(1)}, u32[]{:S(2)}, u32[]{:S(2)}) collective-permute-start(bf16[256,512]{1,0:T(8,128)(2,1)S(1)} %broadcast_select_fusion), channel_id=1, source_target_pairs={{0,2},{1,3},{2,0},{3,1},{4,6},{5,7},{6,4},{7,5},{8,10},{9,11},{10,... | collective-permute-start | bytes 786440 | tf_op jit(solution)/shard_map/ppermute | solution.py:320
  124.6 2.3 %maximum_bitcast_fusion = bf16[2,1,1024,256]{3,2,1,0:T(8,128)(2,1)} fusion(bf16[1,1024,256]{2,1,0:T(8,128)(2,1)} %get-tuple-element.15, bf16[1,1024,256]{2,1,0:T(8,128)(2,1)} %get-tuple-element.14), kind=kLoop, calls=%fused_computation.10 | loop fusion | flops 524288 | bytes 2097152 | tf_op jit(solution)/shard_map/broadcast_in_dim | solution.py:315
  126.8 0.8 collective-permute-start.1
  127.6 0.7 collective-permute-start
  128.3 0.0 copy-done
  128.3 0.3 fusion.5
  128.6 1.3 collective-permute-done.2
  129.9 0.3 fusion.7
  130.2 5.8 %collective-permute-done.1 = bf16[256,512]{1,0:T(8,128)(2,1)S(1)} collective-permute-done((bf16[256,512]{1,0:T(8,128)(2,1)S(1)}, bf16[256,512]{1,0:T(8,128)(2,1)S(1)}, u32[]{:S(2)}, u32[]{:S(2)}) %collective-permute-start.1) | collective-permute-done | bytes 262176 | tf_op jit(solution)/shard_map/ppermute | solution.py:320
  136.0 0.3 fusion.9
  136.3 0.0 collective-permute-done
  136.3 0.3 fusion.2
  136.6 1.7 %add_convert_fusion = bf16[256,512]{1,0:T(8,128)(2,1)} fusion(bf16[256,512]{1,0:T(8,128)(2,1)S(1)} %fusion.2, bf16[256,2048]{1,0:T(8,128)(2,1)} %refs_3_.1, s32[]{:T(128)S(6)} %select_n.117), kind=kLoop, calls=%fused_computation.13 | loop fusion | flops 524288 | bytes 786436 | tf_op jit(solution)/shard_map/convert_element_type | solution.py:335
  (11 shorter events, 0.1 us)
Async XLA Ops:
  0.6 127.7 %copy-start = (bf16[2048,512]{1,0:T(8,128)(2,1)S(1)}, bf16[2048,512]{1,0:T(8,128)(2,1)}, u32[]{:S(2)}) copy-start(bf16[2048,512]{1,0:T(8,128)(2,1)} %param.19) | copy-start | bytes 6291460
  11.9 13.3 %copy-start.1 = (s32[64]{0:T(128)S(1)}, s32[64]{0:T(128)}, u32[]{:S(2)}) copy-start(s32[64]{0:T(128)} %refs_0_.1) | copy-start | bytes 772
  11.9 13.3 %copy-start.2 = (s32[64]{0:T(128)S(1)}, s32[64]{0:T(128)}, u32[]{:S(2)}) copy-start(s32[64]{0:T(128)} %refs_1_.1) | copy-start | bytes 772
  11.9 62.9 %all-to-all-start = ((bf16[64,16,1024]{2,1,0:T(8,128)(2,1)}), bf16[64,16,1024]{2,1,0:T(8,128)(2,1)}, u32[]{:S(2)}, u32[]{:S(2)}) async-start(bf16[64,16,1024]{2,1,0:T(8,128)(2,1)} %bitcast.28), calls=%async_computation | async-start | bytes 4194304 | tf_op jit(solution)/shard_map/all_to_all | solution.py:287
  85.0 35.3 %all-to-all-start.1 = ((bf16[64,16,512]{2,1,0:T(8,128)(2,1)}), bf16[64,16,512]{2,1,0:T(8,128)(2,1)S(1)}, u32[]{:S(2)}, u32[]{:S(2)}) async-start(bf16[64,16,512]{2,1,0:T(8,128)(2,1)} %bitcast.30), calls=%async_computation.1 | async-start | bytes 2097152 | tf_op jit(solution)/shard_map/all_to_all | solution.py:302
  121.6 8.3 %collective-permute-start.2 = (bf16[256,512]{1,0:T(8,128)(2,1)S(1)}, bf16[256,512]{1,0:T(8,128)(2,1)S(1)}, u32[]{:S(2)}, u32[]{:S(2)}) collective-permute-start(bf16[256,512]{1,0:T(8,128)(2,1)S(1)} %broadcast_select_fusion), channel_id=1, source_target_pairs={{0,2},{1,3},{2,0},{3,1},{4,6},{5,7},{6,4},{7,5},{8,10},{9,11},{10,... | collective-permute-start | bytes 786440 | tf_op jit(solution)/shard_map/ppermute | solution.py:320
  126.8 9.2 %collective-permute-start.1 = (bf16[256,512]{1,0:T(8,128)(2,1)S(1)}, bf16[256,512]{1,0:T(8,128)(2,1)S(1)}, u32[]{:S(2)}, u32[]{:S(2)}) collective-permute-start(bf16[256,512]{1,0:T(8,128)(2,1)S(1)} %broadcast_select_fusion), channel_id=1, source_target_pairs={{0,3},{1,0},{2,1},{3,2},{4,7},{5,4},{6,5},{7,6},{8,11},{9,8},{10,9... | collective-permute-start | bytes 786440 | tf_op jit(solution)/shard_map/ppermute | solution.py:320
  127.6 8.7 %collective-permute-start = (bf16[256,512]{1,0:T(8,128)(2,1)S(1)}, bf16[256,512]{1,0:T(8,128)(2,1)S(1)}, u32[]{:S(2)}, u32[]{:S(2)}) collective-permute-start(bf16[256,512]{1,0:T(8,128)(2,1)S(1)} %broadcast_select_fusion), channel_id=1, source_target_pairs={{0,1},{1,2},{2,3},{3,0},{4,5},{5,6},{6,7},{7,4},{8,9},{9,10},{10,1... | collective-permute-start | bytes 786440 | tf_op jit(solution)/shard_map/ppermute | solution.py:320

commit v21 on v20

--- a/solution.py
+++ b/solution.py
@@ -306,7 +306,12 @@
         concat_axis=0,
         tiled=True,
     )
-    attended = jnp.take(returned.reshape(capacity * devices, -1), back_rows, axis=0)
+    back_hot = (
+        back_rows[:, None] == jnp.arange(capacity * devices, dtype=jnp.int32)[None, :]
+    ).astype(returned.dtype)
+    attended = jnp.dot(
+        back_hot, returned.reshape(capacity * devices, -1), preferred_element_type=jnp.float32
+    ).astype(returned.dtype)
     kv_rows = (
         jnp.roll(arrived[:, :, q_width:], -roll_shift, axis=0)
         .transpose(1, 0, 2)

time: 139 us -> 140 us (level)
  waiting for transfers between devices: 73.9 us -> 76.4 us
  local copies, waits for them, and re-layouts: 8.18 us -> 6.04 us
  matrix products: 1.19 us -> 2.89 us
    dot_general x0 -> x1, matrix products: none -> 1.7 us  [on_device(): jnp.dot(back_hot, returned.reshape(capacity * devices, -1), preferred_ele...]
    ppermute x3, waiting for transfers between devices: 7.11 us -> 8.63 us  [on_device(): lax.ppermute(attended, 'tp', perm=[(i, (i + shift) % tp_size) for i in ra...]
  transfers between devices with their start and end apart: 5 -> 5, of which waited for: 4 -> 4; matrix products, arithmetic and copies ran while one was open for 9% -> 7% of each run, Pallas kernels for 0% -> 0%
where the time goes in v21:
time: 140 us; the launch traced here: 139 us
  waiting for transfers between devices  76.4 us (55%)
  starting transfers between devices  25.1 us (18%)
  Pallas kernels  18.1 us (13%)
  other arithmetic  7.91 us (6%)
  local copies, waits for them, and re-layouts  6.04 us (4%)
  matrix products  2.89 us (2%)
  between operations  2.81 us (2%)
    all_to_all x1, waiting for transfers between devices, on_device(): lax.all_to_all(picked.reshape(devices, capacity, picked.shape[1]), 'req',...  45 us
    all_to_all x1, waiting for transfers between devices, on_device(): lax.all_to_all(mixture.reshape(devices, capacity, mixture.shape[1]), 'req...  22.7 us
    all_to_all x1, starting transfers between devices, on_device(): lax.all_to_all(picked.reshape(devices, capacity, picked.shape[1]), 'req',...  13.3 us
    pallas_call x1, Pallas kernels, attend(): pl.pallas_call(lambda *refs: attention_kernel(*refs, q_width=q_width, k_w...  10.1 us
    ppermute x3, waiting for transfers between devices, on_device(): lax.ppermute(attended, 'tp', perm=[(i, (i + shift) % tp_size) for i in ra...  8.63 us
    pallas_call x1, Pallas kernels, prepare(): pl.pallas_call(lambda *refs: prep_kernel(*refs, head_dim=head_dim, capaci...  7.96 us
    all_to_all x1, starting transfers between devices, on_device(): lax.all_to_all(mixture.reshape(devices, capacity, mixture.shape[1]), 'req...  7.33 us
    ppermute x3, starting transfers between devices, on_device(): lax.ppermute(attended, 'tp', perm=[(i, (i + shift) % tp_size) for i in ra...  4.45 us
  transfers between devices with their start and end apart: 5, of which 4 were waited for; matrix products, arithmetic and copies ran while one was open for 7% of the time, Pallas kernels for 0%

profile of v21, /device:TPU:1, one launch (start us, length us, event | category | flops | bytes accessed | tf_op | source)
XLA Modules:
  0.0 139.2 jit_solution(3773676789335676965)
XLA Ops:
  0.6 0.0 copy-start
  0.7 0.1 compare_select_fusion.4
  0.7 0.9 copy.17
  1.6 0.1 reduce-window.8
  1.7 0.1 reduce
  1.8 0.7 sub.43
  2.5 0.1 convert_reduce_fusion
  2.6 0.1 select_reduce_fusion
  2.7 1.2 fusion.13
  3.9 8.0 %shard_map.113 = bf16[1024,1024]{1,0:T(8,128)(2,1)} custom-call(s32[64]{0:T(128)} %refs_0_.1, s32[64]{0:T(128)} %refs_1_.1, s32[1]{0:T(128)} %bitcast.refs_2_, bf16[256,2048]{1,0:T(8,128)(2,1)} %refs_3_.1, bf16[2048]{0:T(1024)(128)(2,1)} %refs_4_.1, bf16[2048,512]{1,0:T(8,128)(2,1)} %refs_5_.1, bf16[2048,256]{1,0:T(8,128)(2,1)} %refs_6_.1, ...), custom_call_target="tpu_custom_call" | custom-call | flops 1610612736 | bytes 7340032 | tf_op jit(solution)/shard_map/pallas_call | solution.py:154
  11.9 0.0 copy-start.1
  11.9 0.0 copy-start.2
  11.9 13.3 %all-to-all-start = ((bf16[64,16,1024]{2,1,0:T(8,128)(2,1)}), bf16[64,16,1024]{2,1,0:T(8,128)(2,1)}, u32[]{:S(2)}, u32[]{:S(2)}) async-start(bf16[64,16,1024]{2,1,0:T(8,128)(2,1)} %bitcast.25), calls=%async_computation | async-start | bytes 4194304 | tf_op jit(solution)/shard_map/all_to_all | solution.py:287
  25.2 0.0 copy-done.1
  25.2 0.0 copy-done.2
  25.3 0.2 select_reduce_fusion.1
  25.4 0.7 dynamic_slice.27
  26.1 0.6 and_select_fusion
  26.7 0.1 broadcast_add_fusion
  26.8 0.1 add.147
  26.9 1.1 add.161.refs_1_
  28.0 0.6 dynamic_slice.28
  28.6 1.2 compare_select_fusion.refs_2_
  29.8 45.0 %all-to-all-done = bf16[64,16,1024]{2,1,0:T(8,128)(2,1)} async-done(((bf16[64,16,1024]{2,1,0:T(8,128)(2,1)}), bf16[64,16,1024]{2,1,0:T(8,128)(2,1)}, u32[]{:S(2)}, u32[]{:S(2)}) %all-to-all-start) | async-done | bytes 2097184 | tf_op jit(solution)/shard_map/all_to_all | solution.py:287
  74.9 10.1 %shard_map.114 = bf16[1024,512]{1,0:T(8,128)(2,1)} custom-call(bf16[1024,1024]{1,0:T(8,128)(2,1)} %bitcast.5.refs_0_, s32[1024,1]{1,0:T(8,128)} %add.161.refs_1_, s32[1,1024]{1,0:T(1,128)} %compare_select_fusion.refs_2_), custom_call_target="tpu_custom_call" | custom-call | flops 2147483648 | bytes 3145728 | tf_op jit(solution)/shard_map/pallas_call | solution.py:224
  85.0 7.3 %all-to-all-start.1 = ((bf16[64,16,512]{2,1,0:T(8,128)(2,1)}), bf16[64,16,512]{2,1,0:T(8,128)(2,1)}, u32[]{:S(2)}, u32[]{:S(2)}) async-start(bf16[64,16,512]{2,1,0:T(8,128)(2,1)} %bitcast.27), calls=%async_computation.1 | async-start | bytes 2097152 | tf_op jit(solution)/shard_map/all_to_all | solution.py:302
  94.3 0.8 scatter_custom_fusion
  95.1 0.1 multiply_reduce_fusion
  95.2 1.3 slice.12
  96.5 0.5 fusion.4
  97.0 0.6 copy.19
  97.6 0.1 slice_bitcast_fusion.1
  97.7 22.7 %all-to-all-done.1 = bf16[64,16,512]{2,1,0:T(8,128)(2,1)} async-done(((bf16[64,16,512]{2,1,0:T(8,128)(2,1)}), bf16[64,16,512]{2,1,0:T(8,128)(2,1)}, u32[]{:S(2)}, u32[]{:S(2)}) %all-to-all-start.1) | async-done | bytes 1048608 | tf_op jit(solution)/shard_map/all_to_all | solution.py:302
  120.4 1.7 %convolution_convert_fusion = bf16[256,512]{1,0:T(8,128)(2,1)S(1)} fusion(bf16[1024,512]{1,0:T(8,128)(2,1)} %bitcast.9, s32[256]{0:T(256)S(1)} %fusion.19), kind=kOutput, calls=%fused_computation.7 | convolution fusion | flops 268828672 | bytes 1311744 | tf_op jit(solution)/shard_map/dot_general | solution.py:312
  122.1 3.0 %collective-permute-start.2 = (bf16[256,512]{1,0:T(8,128)(2,1)S(1)}, bf16[256,512]{1,0:T(8,128)(2,1)S(1)}, u32[]{:S(2)}, u32[]{:S(2)}) collective-permute-start(bf16[256,512]{1,0:T(8,128)(2,1)S(1)} %convolution_convert_fusion), channel_id=1, source_target_pairs={{0,2},{1,3},{2,0},{3,1},{4,6},{5,7},{6,4},{7,5},{8,10},{9,11},{10,... | collective-permute-start | bytes 786440 | tf_op jit(solution)/shard_map/ppermute | solution.py:325
  125.1 1.1 maximum_bitcast_fusion
  126.2 0.8 collective-permute-start.1
  127.0 0.7 collective-permute-start
  127.6 0.0 copy-done
  127.6 0.3 fusion.5
  127.9 2.5 %collective-permute-done.2 = bf16[256,512]{1,0:T(8,128)(2,1)S(1)} collective-permute-done((bf16[256,512]{1,0:T(8,128)(2,1)S(1)}, bf16[256,512]{1,0:T(8,128)(2,1)S(1)}, u32[]{:S(2)}, u32[]{:S(2)}) %collective-permute-start.2) | collective-permute-done | bytes 262176 | tf_op jit(solution)/shard_map/ppermute | solution.py:325
  130.4 0.3 fusion.7
  130.7 6.1 %collective-permute-done.1 = bf16[256,512]{1,0:T(8,128)(2,1)S(1)} collective-permute-done((bf16[256,512]{1,0:T(8,128)(2,1)S(1)}, bf16[256,512]{1,0:T(8,128)(2,1)S(1)}, u32[]{:S(2)}, u32[]{:S(2)}) %collective-permute-start.1) | collective-permute-done | bytes 262176 | tf_op jit(solution)/shard_map/ppermute | solution.py:325
  136.9 0.3 fusion.9
  137.2 0.0 collective-permute-done
  137.2 0.3 fusion.2
  137.5 1.7 %add_convert_fusion = bf16[256,512]{1,0:T(8,128)(2,1)} fusion(bf16[256,512]{1,0:T(8,128)(2,1)S(1)} %fusion.2, bf16[256,2048]{1,0:T(8,128)(2,1)} %refs_3_.1, s32[]{:T(128)S(6)} %select_n.91), kind=kLoop, calls=%fused_computation.14 | loop fusion | flops 524288 | bytes 786436 | tf_op jit(solution)/shard_map/convert_element_type | solution.py:340
  (8 shorter events, 0.1 us)
Async XLA Ops:
  0.6 127.0 %copy-start = (bf16[2048,512]{1,0:T(8,128)(2,1)S(1)}, bf16[2048,512]{1,0:T(8,128)(2,1)}, u32[]{:S(2)}) copy-start(bf16[2048,512]{1,0:T(8,128)(2,1)} %param.19) | copy-start | bytes 6291460
  11.9 13.3 %copy-start.1 = (s32[64]{0:T(128)S(1)}, s32[64]{0:T(128)}, u32[]{:S(2)}) copy-start(s32[64]{0:T(128)} %refs_0_.1) | copy-start | bytes 772
  11.9 13.3 %copy-start.2 = (s32[64]{0:T(128)S(1)}, s32[64]{0:T(128)}, u32[]{:S(2)}) copy-start(s32[64]{0:T(128)} %refs_1_.1) | copy-start | bytes 772
  11.9 62.9 %all-to-all-start = ((bf16[64,16,1024]{2,1,0:T(8,128)(2,1)}), bf16[64,16,1024]{2,1,0:T(8,128)(2,1)}, u32[]{:S(2)}, u32[]{:S(2)}) async-start(bf16[64,16,1024]{2,1,0:T(8,128)(2,1)} %bitcast.25), calls=%async_computation | async-start | bytes 4194304 | tf_op jit(solution)/shard_map/all_to_all | solution.py:287
  85.0 35.4 %all-to-all-start.1 = ((bf16[64,16,512]{2,1,0:T(8,128)(2,1)}), bf16[64,16,512]{2,1,0:T(8,128)(2,1)}, u32[]{:S(2)}, u32[]{:S(2)}) async-start(bf16[64,16,512]{2,1,0:T(8,128)(2,1)} %bitcast.27), calls=%async_computation.1 | async-start | bytes 2097152 | tf_op jit(solution)/shard_map/all_to_all | solution.py:302
  122.1 8.3 %collective-permute-start.2 = (bf16[256,512]{1,0:T(8,128)(2,1)S(1)}, bf16[256,512]{1,0:T(8,128)(2,1)S(1)}, u32[]{:S(2)}, u32[]{:S(2)}) collective-permute-start(bf16[256,512]{1,0:T(8,128)(2,1)S(1)} %convolution_convert_fusion), channel_id=1, source_target_pairs={{0,2},{1,3},{2,0},{3,1},{4,6},{5,7},{6,4},{7,5},{8,10},{9,11},{10,... | collective-permute-start | bytes 786440 | tf_op jit(solution)/shard_map/ppermute | solution.py:325
  126.2 10.7 %collective-permute-start.1 = (bf16[256,512]{1,0:T(8,128)(2,1)S(1)}, bf16[256,512]{1,0:T(8,128)(2,1)S(1)}, u32[]{:S(2)}, u32[]{:S(2)}) collective-permute-start(bf16[256,512]{1,0:T(8,128)(2,1)S(1)} %convolution_convert_fusion), channel_id=1, source_target_pairs={{0,3},{1,0},{2,1},{3,2},{4,7},{5,4},{6,5},{7,6},{8,11},{9,8},{10,9... | collective-permute-start | bytes 786440 | tf_op jit(solution)/shard_map/ppermute | solution.py:325
  127.0 10.2 %collective-permute-start = (bf16[256,512]{1,0:T(8,128)(2,1)S(1)}, bf16[256,512]{1,0:T(8,128)(2,1)S(1)}, u32[]{:S(2)}, u32[]{:S(2)}) collective-permute-start(bf16[256,512]{1,0:T(8,128)(2,1)S(1)} %convolution_convert_fusion), channel_id=1, source_target_pairs={{0,1},{1,2},{2,3},{3,0},{4,5},{5,6},{6,7},{7,4},{8,9},{9,10},{10,1... | collective-permute-start | bytes 786440 | tf_op jit(solution)/shard_map/ppermute | solution.py:325

commit v22 on v13

--- a/solution.py
+++ b/solution.py
@@ -189,7 +189,7 @@
     group = q_width // head_dim // kv_heads
     scale = head_dim ** (-0.5)
     for i in range(blocks):
-        key_rows = block * (i + 1)
+        key_rows = rows
         rows_here = pl.ds(i * block, block)
         allowed = kpos_ref[:, :key_rows] <= qpos_ref[rows_here, :]
         for h in range(kv_heads):
@@ -222,7 +222,7 @@
     rows = qkv_slot.shape[0]
     blocks = 2
     heads = q_width // head_dim
-    causal_pairs = blocks * (blocks + 1) // 2
+    causal_pairs = blocks * blocks
     pair_flops = 4 * (rows // blocks) ** 2 * head_dim
     vmem = pl.BlockSpec(memory_space=pltpu.VMEM)
     return pl.pallas_call(
@@ -294,42 +294,46 @@
         split_axis=0,
         concat_axis=0,
         tiled=True,
-    ).transpose(1, 0, 2)
+    )
     source_ids = jnp.arange(devices, dtype=jnp.int32)
     arrived_pos = (
-        ranks[:, None] * devices + jnp.mod(source_ids[None, :] - my_start, devices)
+        ranks[None, :] * devices + jnp.mod(source_ids[:, None] - my_start, devices)
     ).reshape(-1)
     key_pos = jnp.where(arrived_pos < my_length, arrived_pos, 1 << 30)
     mixture = attend(
         arrived.reshape(slot_len, arrived.shape[2]), arrived_pos, key_pos, q_width, k_width, head_dim
     )
     returned = lax.all_to_all(
-        mixture.reshape(capacity, devices, mixture.shape[1]).transpose(1, 0, 2),
+        mixture.reshape(devices, capacity, mixture.shape[1]),
         "req",
         split_axis=0,
         concat_axis=0,
         tiled=True,
     )
     attended = jnp.take(returned.reshape(capacity * devices, -1), back_rows, axis=0)
-    kv_rows = jnp.roll(arrived[:, :, q_width:], -roll_shift, axis=1).reshape(slot_len, -1)
+    kv_rows = (
+        jnp.roll(arrived[:, :, q_width:], -roll_shift, axis=0)
+        .transpose(1, 0, 2)
+        .reshape(slot_len, -1)
+    )
     kv_cache = jnp.stack([kv_rows[:, :k_width], kv_rows[:, k_width:]])[:, None]
     tp_size = lax.axis_size("tp")
     w_rows = w_out.shape[0] // tp_size
-    summed = jnp.dot(
-        attended,
-        lax.dynamic_slice_in_dim(w_out, slice_index * w_rows, w_rows, 0),
-        preferred_element_type=jnp.float32,
-    )
-    for shift in range(1, tp_size):
+    passes = []
+    for shift in sorted(range(1, tp_size), key=lambda s: min(s, tp_size - s)):
         passed = lax.ppermute(
             attended, "tp", perm=[(i, (i + shift) % tp_size) for i in range(tp_size)]
         )
-        source = jnp.mod(slice_index - shift, tp_size)
-        summed = summed + jnp.dot(
+        passes.append((passed, jnp.mod(slice_index - shift, tp_size)))
+    passes.append((attended, slice_index))
+    summed = None
+    for passed, source in passes:
+        product = jnp.dot(
             passed,
             lax.dynamic_slice_in_dim(w_out, source * w_rows, w_rows, 0),
             preferred_element_type=jnp.float32,
         )
+        summed = product if summed is None else summed + product
     branch = lax.optimization_barrier(summed.astype(jnp.bfloat16))
     residual = lax.dynamic_slice_in_dim(hidden, slice_index * out_width, out_width, 1)
     hidden_out = (residual.astype(jnp.float32) + branch.astype(jnp.float32)).astype(jnp.bfloat16)

time: 151 us -> 140 us (0.927)
  waiting for transfers between devices: 80.6 us -> 73.9 us
  local copies, waits for them, and re-layouts: 14.6 us -> 8.18 us
    ppermute x3, waiting for transfers between devices: 13.7 us -> 7.11 us  [on_device(): lax.ppermute(attended, 'tp', perm=[(i, (i + shift) % tp_size) for i in ra...]
    all_to_all x1 -> x0, local copies, waits for them, and re-layouts: 4.09 us -> none  [on_device(): lax.all_to_all(picked.reshape(devices, capacity, picked.shape[1]), 'req',...]
    reshape x1 -> x0, local copies, waits for them, and re-layouts: 2.79 us -> none  [on_device(): mixture.reshape(capacity, devices, mixture.shape[1]).transpose(1, 0, 2)]
    unnamed x1 -> x0, other arithmetic: 2.27 us -> none
    broadcast_in_dim x0 -> x1, other arithmetic: none -> 2.27 us  [on_device(): kv_cache = jnp.stack([kv_rows[:, :k_width], kv_rows[:, k_width:]])[:, None]]
  transfers between devices with their start and end apart: 5 -> 5, of which waited for: 4 -> 4; matrix products, arithmetic and copies ran while one was open for 8% -> 9% of each run, Pallas kernels for 0% -> 0%
where the time goes in v22:
time: 140 us; the launch traced here: 139 us
  waiting for transfers between devices  73.9 us (53%)
  starting transfers between devices  25 us (18%)
  Pallas kernels  19 us (14%)
  other arithmetic  9.26 us (7%)
  local copies, waits for them, and re-layouts  8.18 us (6%)
  between operations  2.82 us (2%)
    all_to_all x1, waiting for transfers between devices, on_device(): lax.all_to_all(picked.reshape(devices, capacity, picked.shape[1]), 'req',...  45 us
    all_to_all x1, waiting for transfers between devices, on_device(): lax.all_to_all(mixture.reshape(devices, capacity, mixture.shape[1]), 'req...  21.8 us
    all_to_all x1, starting transfers between devices, on_device(): lax.all_to_all(picked.reshape(devices, capacity, picked.shape[1]), 'req',...  13.3 us
    pallas_call x1, Pallas kernels, attend(): pl.pallas_call(lambda *refs: attention_kernel(*refs, q_width=q_width, k_w...  11 us
    pallas_call x1, Pallas kernels, prepare(): pl.pallas_call(lambda *refs: prep_kernel(*refs, head_dim=head_dim, capaci...  7.96 us
    ppermute x3, waiting for transfers between devices, on_device(): lax.ppermute(attended, 'tp', perm=[(i, (i + shift) % tp_size) for i in ra...  7.11 us
    all_to_all x1, starting transfers between devices, on_device(): lax.all_to_all(mixture.reshape(devices, capacity, mixture.shape[1]), 'req...  6.96 us
    ppermute x3, starting transfers between devices, on_device(): lax.ppermute(attended, 'tp', perm=[(i, (i + shift) % tp_size) for i in ra...  4.68 us
  transfers between devices with their start and end apart: 5, of which 4 were waited for; matrix products, arithmetic and copies ran while one was open for 9% of the time, Pallas kernels for 0%

profile of v22, /device:TPU:1, one launch (start us, length us, event | category | flops | bytes accessed | tf_op | source)
XLA Modules:
  0.0 139.3 jit_solution(7245556756409842637)
XLA Ops:
  0.6 0.0 copy-start
  0.7 0.1 compare_select_fusion.9
  0.7 0.9 copy.17
  1.6 0.1 reduce-window.8
  1.7 0.1 reduce
  1.8 0.7 sub.52
  2.5 0.1 convert_reduce_fusion
  2.6 0.1 select_reduce_fusion
  2.7 1.2 fusion.12
  3.9 8.0 %shard_map.113 = bf16[1024,1024]{1,0:T(8,128)(2,1)} custom-call(s32[64]{0:T(128)} %refs_0_.1, s32[64]{0:T(128)} %refs_1_.1, s32[1]{0:T(128)} %bitcast.refs_2_, bf16[256,2048]{1,0:T(8,128)(2,1)} %refs_3_.1, bf16[2048]{0:T(1024)(128)(2,1)} %refs_4_.1, bf16[2048,512]{1,0:T(8,128)(2,1)} %refs_5_.1, bf16[2048,256]{1,0:T(8,128)(2,1)} %refs_6_.1, ...), custom_call_target="tpu_custom_call" | custom-call | flops 1610612736 | bytes 7340032 | tf_op jit(solution)/shard_map/pallas_call | solution.py:154
  11.9 0.0 copy-start.1
  11.9 0.0 copy-start.2
  11.9 13.3 %all-to-all-start = ((bf16[64,16,1024]{2,1,0:T(8,128)(2,1)}), bf16[64,16,1024]{2,1,0:T(8,128)(2,1)}, u32[]{:S(2)}, u32[]{:S(2)}) async-start(bf16[64,16,1024]{2,1,0:T(8,128)(2,1)} %bitcast.28), calls=%async_computation | async-start | bytes 4194304 | tf_op jit(solution)/shard_map/all_to_all | solution.py:291
  25.2 0.0 copy-done.1
  25.3 0.0 copy-done.2
  25.3 0.2 select_reduce_fusion.1
  25.4 0.7 dynamic_slice.27
  26.1 0.6 and_select_fusion.1
  26.8 0.1 broadcast_add_fusion
  26.8 0.1 add.191
  26.9 1.1 add.210.refs_1_
  28.0 0.6 dynamic_slice.28
  28.6 1.2 compare_select_fusion.refs_2_
  29.8 45.0 %all-to-all-done = bf16[64,16,1024]{2,1,0:T(8,128)(2,1)} async-done(((bf16[64,16,1024]{2,1,0:T(8,128)(2,1)}), bf16[64,16,1024]{2,1,0:T(8,128)(2,1)}, u32[]{:S(2)}, u32[]{:S(2)}) %all-to-all-start) | async-done | bytes 2097184 | tf_op jit(solution)/shard_map/all_to_all | solution.py:291
  74.9 11.0 %shard_map.114 = bf16[1024,512]{1,0:T(8,128)(2,1)} custom-call(bf16[1024,1024]{1,0:T(8,128)(2,1)} %bitcast.5.refs_0_, s32[1024,1]{1,0:T(8,128)} %add.210.refs_1_, s32[1,1024]{1,0:T(1,128)} %compare_select_fusion.refs_2_), custom_call_target="tpu_custom_call" | custom-call | flops 2147483648 | bytes 3145728 | tf_op jit(solution)/shard_map/pallas_call | solution.py:228
  85.9 7.0 %all-to-all-start.1 = ((bf16[64,16,512]{2,1,0:T(8,128)(2,1)}), bf16[64,16,512]{2,1,0:T(8,128)(2,1)S(1)}, u32[]{:S(2)}, u32[]{:S(2)}) async-start(bf16[64,16,512]{2,1,0:T(8,128)(2,1)} %bitcast.30), calls=%async_computation.1 | async-start | bytes 2097152 | tf_op jit(solution)/shard_map/all_to_all | solution.py:306
  94.9 0.8 scatter_custom_fusion
  95.7 0.1 multiply_reduce_fusion
  95.8 1.3 slice.14
  97.1 0.5 fusion.4
  97.6 0.6 copy.19
  98.2 1.1 slice_bitcast_fusion.1
  99.3 21.8 %all-to-all-done.1 = bf16[64,16,512]{2,1,0:T(8,128)(2,1)S(1)} async-done(((bf16[64,16,512]{2,1,0:T(8,128)(2,1)}), bf16[64,16,512]{2,1,0:T(8,128)(2,1)S(1)}, u32[]{:S(2)}, u32[]{:S(2)}) %all-to-all-start.1) | async-done | bytes 1048608 | tf_op jit(solution)/shard_map/all_to_all | solution.py:306
  121.0 1.2 gather_fusion
  122.2 0.1 broadcast_select_fusion
  122.3 3.2 %collective-permute-start.2 = (bf16[256,512]{1,0:T(8,128)(2,1)S(1)}, bf16[256,512]{1,0:T(8,128)(2,1)S(1)}, u32[]{:S(2)}, u32[]{:S(2)}) collective-permute-start(bf16[256,512]{1,0:T(8,128)(2,1)S(1)} %broadcast_select_fusion), channel_id=1, source_target_pairs={{0,2},{1,3},{2,0},{3,1},{4,6},{5,7},{6,4},{7,5},{8,10},{9,11},{10,... | collective-permute-start | bytes 786440 | tf_op jit(solution)/shard_map/ppermute | solution.py:324
  125.5 2.3 %maximum_bitcast_fusion = bf16[2,1,1024,256]{3,2,1,0:T(8,128)(2,1)} fusion(bf16[1,1024,256]{2,1,0:T(8,128)(2,1)} %get-tuple-element.15, bf16[1,1024,256]{2,1,0:T(8,128)(2,1)} %get-tuple-element.14), kind=kLoop, calls=%fused_computation.10 | loop fusion | flops 524288 | bytes 2097152 | tf_op jit(solution)/shard_map/broadcast_in_dim | solution.py:319
  127.8 0.8 collective-permute-start.1
  128.6 0.7 collective-permute-start
  129.2 0.0 copy-done
  129.2 0.3 fusion.5
  129.5 1.3 collective-permute-done.2
  130.8 0.3 fusion.7
  131.1 5.8 %collective-permute-done.1 = bf16[256,512]{1,0:T(8,128)(2,1)S(1)} collective-permute-done((bf16[256,512]{1,0:T(8,128)(2,1)S(1)}, bf16[256,512]{1,0:T(8,128)(2,1)S(1)}, u32[]{:S(2)}, u32[]{:S(2)}) %collective-permute-start.1) | collective-permute-done | bytes 262176 | tf_op jit(solution)/shard_map/ppermute | solution.py:324
  136.9 0.3 fusion.9
  137.2 0.0 collective-permute-done
  137.3 0.3 fusion.2
  137.6 1.7 %add_convert_fusion = bf16[256,512]{1,0:T(8,128)(2,1)} fusion(bf16[256,512]{1,0:T(8,128)(2,1)S(1)} %fusion.2, bf16[256,2048]{1,0:T(8,128)(2,1)} %refs_3_.1, s32[]{:T(128)S(6)} %select_n.117), kind=kLoop, calls=%fused_computation.13 | loop fusion | flops 524288 | bytes 786436 | tf_op jit(solution)/shard_map/convert_element_type | solution.py:339
  (11 shorter events, 0.1 us)
Async XLA Ops:
  0.6 128.6 %copy-start = (bf16[2048,512]{1,0:T(8,128)(2,1)S(1)}, bf16[2048,512]{1,0:T(8,128)(2,1)}, u32[]{:S(2)}) copy-start(bf16[2048,512]{1,0:T(8,128)(2,1)} %param.19) | copy-start | bytes 6291460
  11.9 13.3 %copy-start.1 = (s32[64]{0:T(128)S(1)}, s32[64]{0:T(128)}, u32[]{:S(2)}) copy-start(s32[64]{0:T(128)} %refs_0_.1) | copy-start | bytes 772
  11.9 13.3 %copy-start.2 = (s32[64]{0:T(128)S(1)}, s32[64]{0:T(128)}, u32[]{:S(2)}) copy-start(s32[64]{0:T(128)} %refs_1_.1) | copy-start | bytes 772
  11.9 62.9 %all-to-all-start = ((bf16[64,16,1024]{2,1,0:T(8,128)(2,1)}), bf16[64,16,1024]{2,1,0:T(8,128)(2,1)}, u32[]{:S(2)}, u32[]{:S(2)}) async-start(bf16[64,16,1024]{2,1,0:T(8,128)(2,1)} %bitcast.28), calls=%async_computation | async-start | bytes 4194304 | tf_op jit(solution)/shard_map/all_to_all | solution.py:291
  85.9 35.1 %all-to-all-start.1 = ((bf16[64,16,512]{2,1,0:T(8,128)(2,1)}), bf16[64,16,512]{2,1,0:T(8,128)(2,1)S(1)}, u32[]{:S(2)}, u32[]{:S(2)}) async-start(bf16[64,16,512]{2,1,0:T(8,128)(2,1)} %bitcast.30), calls=%async_computation.1 | async-start | bytes 2097152 | tf_op jit(solution)/shard_map/all_to_all | solution.py:306
  122.3 8.5 %collective-permute-start.2 = (bf16[256,512]{1,0:T(8,128)(2,1)S(1)}, bf16[256,512]{1,0:T(8,128)(2,1)S(1)}, u32[]{:S(2)}, u32[]{:S(2)}) collective-permute-start(bf16[256,512]{1,0:T(8,128)(2,1)S(1)} %broadcast_select_fusion), channel_id=1, source_target_pairs={{0,2},{1,3},{2,0},{3,1},{4,6},{5,7},{6,4},{7,5},{8,10},{9,11},{10,... | collective-permute-start | bytes 786440 | tf_op jit(solution)/shard_map/ppermute | solution.py:324
  127.8 9.2 %collective-permute-start.1 = (bf16[256,512]{1,0:T(8,128)(2,1)S(1)}, bf16[256,512]{1,0:T(8,128)(2,1)S(1)}, u32[]{:S(2)}, u32[]{:S(2)}) collective-permute-start(bf16[256,512]{1,0:T(8,128)(2,1)S(1)} %broadcast_select_fusion), channel_id=1, source_target_pairs={{0,3},{1,0},{2,1},{3,2},{4,7},{5,4},{6,5},{7,6},{8,11},{9,8},{10,9... | collective-permute-start | bytes 786440 | tf_op jit(solution)/shard_map/ppermute | solution.py:324
  128.6 8.7 %collective-permute-start = (bf16[256,512]{1,0:T(8,128)(2,1)S(1)}, bf16[256,512]{1,0:T(8,128)(2,1)S(1)}, u32[]{:S(2)}, u32[]{:S(2)}) collective-permute-start(bf16[256,512]{1,0:T(8,128)(2,1)S(1)} %broadcast_select_fusion), channel_id=1, source_target_pairs={{0,1},{1,2},{2,3},{3,0},{4,5},{5,6},{6,7},{7,4},{8,9},{9,10},{10,1... | collective-permute-start | bytes 786440 | tf_op jit(solution)/shard_map/ppermute | solution.py:324
